TPU v7x, 32 devices: a whole 2x2x4 slice. The times are simulated.
32 devices in a mesh: mem: 8 (over z, x), tp: 4 (over y, core).
Axes of the slice: x: 2, y: 2, z: 4, core: 2. Of those that a mesh axis runs over, the one named last changes fastest.
Arguments:
- tokens: bfloat16 [3072, 2560], P(('mem', 'tp')), may hold values from -48 to 48
- input_weight: bfloat16 [2560, 6144], P(None, 'tp'), may hold values from -0.125 to 0.125
- output_weight: bfloat16 [2048, 2560], P('tp'), may hold values from -0.125 to 0.125
- gate_logit: float32 [16], P('tp'), may hold values from -2 to 2
- memory: bfloat16 [2, 32768, 2048], P(None, 'mem', 'tp'), may hold values from -48 to 48
- retrieved: int32 [24, 16], P('mem'), may hold values from 0 to 255, as said below
- block_home: int32 [256], replicated, may hold values from 0 to 255, as said below
Outputs:
- mixed: bfloat16 [3072, 2560], P(('mem', 'tp'))
Inputs may be any that keep to these rules, and one draw needn't show every extreme that they name: `block_home`: A permutation: each logical block names one stored block; stored block s lies with index s // 32 of mem, as its block s % 32. `retrieved`: each row names 16 different logical blocks; rows i * 3 to i * 3 + 2 are the query blocks of index i of mem. A row names at most 2 blocks held by one index of mem, and all rows of one index of mem together name at most 2 different blocks held by one index of mem.
All inputs are finite; a program needn't handle non-finite values.
Results may differ from a plain program's by a relative error of at most 0.023.
Values may be sent and summed in bfloat16 or wider, within the bound.
No kernel may reach another device: no remote copies, remote signals or barrier semaphores. Data moves between devices by JAX's collectives and lax.ppermute only.
A program may use at most 128 MiB of HBM per device.

v0:
```python
import jax
import jax.numpy as jnp
from jax import lax
from jax.sharding import PartitionSpec as P

HD = 128
BLK = 128
TOPB = 16
CAP = 2


NEG_FILL = -1e30


def from_behind(value, axis, steps):
    count = lax.axis_size(axis)
    initial, last = (max(0, -steps), min(count, count - steps))
    return lax.ppermute(value, axis, [(source, source + steps) for source in range(initial, last)])


def softmax_rows(scores, allowed):
    row_peak = jnp.max(jnp.where(allowed, scores, NEG_FILL), axis=-1, keepdims=True)
    weights = jnp.where(allowed, jnp.exp(scores - row_peak), 0.0)
    return (weights / jnp.sum(weights, axis=-1, keepdims=True)).astype(jnp.bfloat16)


def local(tokens, input_weight, output_weight, gate_logit, memory, retrieved, block_home):
    holder_count = lax.axis_size("mem")
    share_rows = tokens.shape[0]
    local_rows = share_rows * lax.axis_size("tp")
    groups = output_weight.shape[0] // HD
    score_scale = HD ** (-0.5)
    projected = jnp.dot(
        lax.all_gather(tokens, "tp", axis=0, tiled=True),
        input_weight,
        preferred_element_type=jnp.float32,
    )
    projected = projected.astype(jnp.bfloat16).reshape(local_rows, groups, 3, HD)
    queries = projected[:, :, 0]
    key_rows = projected[:, :, 1]
    value_rows = projected[:, :, 2]
    last_rows = jnp.stack([key_rows[-BLK:], value_rows[-BLK:]]).reshape(2, BLK, groups * HD)
    before = from_behind(last_rows, "mem", 1).reshape(2, BLK, groups, HD)
    near_keys = jnp.concatenate([before[0], key_rows], axis=0)
    near_values = jnp.concatenate([before[1], value_rows], axis=0)
    near_scores = (
        jnp.einsum("qgd,kgd->gqk", queries, near_keys, preferred_element_type=jnp.float32)
        * score_scale
    )
    query_index = lax.broadcasted_iota(jnp.int32, (local_rows, local_rows + BLK), 0)
    key_index = lax.broadcasted_iota(jnp.int32, (local_rows, local_rows + BLK), 1)
    first_key = lax.axis_index("mem") * local_rows - BLK
    allowed = (
        (key_index > query_index) & (key_index <= query_index + BLK) & (key_index + first_key >= 0)
    )
    near_probs = softmax_rows(near_scores, allowed[None])
    near_out = jnp.einsum(
        "gqk,kgd->qgd", near_probs, near_values, preferred_element_type=jnp.float32
    )
    blocks_here = retrieved.shape[0]
    entries = blocks_here * TOPB
    local_blocks = memory.shape[1] // BLK
    flat_blocks = retrieved.reshape(entries)
    home_slot = jnp.take(block_home, flat_blocks)
    holder = home_slot // local_blocks
    local_block = home_slot % local_blocks
    local_store = memory.reshape(2, local_blocks, BLK, groups * HD)
    entry_order = jnp.arange(entries)
    earlier = entry_order[None, :] < entry_order[:, None]
    same_owner = holder[:, None] == holder[None, :]
    slot_count = blocks_here * CAP
    slot_of = jnp.sum(same_owner & earlier, axis=1)
    wanted_ids = (
        jnp.zeros((holder_count, slot_count), jnp.int32).at[holder, slot_of].set(local_block)
    )
    picked = jnp.take(
        local_store,
        lax.all_to_all(wanted_ids, "mem", split_axis=0, concat_axis=0, tiled=True),
        axis=1,
    )
    fetched = lax.all_to_all(picked, "mem", split_axis=1, concat_axis=1, tiled=True)
    gathered = fetched[:, holder, slot_of]
    far_pairs = gathered.reshape(2, blocks_here, TOPB * BLK, groups, HD)
    block_queries = queries.reshape(blocks_here, BLK, groups, HD)
    far_scores = (
        jnp.einsum(
            "bqgd,bkgd->bgqk", block_queries, far_pairs[0], preferred_element_type=jnp.float32
        )
        * score_scale
    )
    far_probs = softmax_rows(far_scores, True)
    far_out = jnp.einsum(
        "bgqk,bkgd->bqgd", far_probs, far_pairs[1], preferred_element_type=jnp.float32
    )
    far_out = far_out.reshape(local_rows, groups, HD)
    mixing = jax.nn.sigmoid(gate_logit)[None, :, None]
    attended = (
        (mixing * far_out + (1.0 - mixing) * near_out)
        .astype(jnp.bfloat16)
        .reshape(local_rows, groups * HD)
    )
    return lax.psum_scatter(
        jnp.dot(attended, output_weight, preferred_element_type=jnp.float32).astype(jnp.bfloat16),
        "tp",
        scatter_dimension=0,
        tiled=True,
    )


def solution(mesh):
    placed = (
        P(("mem", "tp"), None),
        P(None, "tp"),
        P("tp", None),
        P("tp"),
        P(None, "mem", "tp"),
        P("mem", None),
        P(),
    )
    return jax.shard_map(
        local, mesh=mesh, in_specs=placed, out_specs=P(("mem", "tp"), None), check_vma=False
    )
```

profile of v0, /device:TPU:16, one launch (start us, length us, event | category | flops | bytes accessed | tf_op | source)
XLA Modules:
  0.0 462.3 jit_solution(4355462425641250528)
XLA Ops:
  6.5 0.0 copy-start
  6.5 0.9 reshape.292
  7.4 0.8 reshape.293
  8.2 1.5 gather_fusion
  9.7 0.2 convert_reduce_fusion
  10.0 2.7 scatter_fusion
  12.7 10.0 %all_to_all.20 = s32[8,1,6]{2,1,0:T(1,128)S(1)} all-to-all(s32[8,1,6]{2,1,0:T(1,128)S(1)} %bitcast.71), channel_id=1, replica_groups=mesh['mem'=8,'tp'=4] {'mem'}, dimensions={0} | all-to-all | bytes 384 | tf_op jit(solution)/shard_map/all_to_all | solution.py:78
  22.7 0.1 copy.68
  22.8 0.1 copy.69
  22.9 0.1 reshape.308
  23.0 9.7 %gather_fusion.1 = bf16[48,2,128,512]{3,2,1,0:T(8,128)(2,1)} fusion(bf16[2,32,128,512]{3,2,1,0:T(8,128)(2,1)} %bitcast.74, s32[1024]{0:T(1024)S(1)} %pad_clamp_fusion), kind=kCustom, calls=%fused_computation.1 | custom fusion | bytes 25166016 | tf_op jit(solution)/shard_map/jit(_take)/gather | solution.py:76
  32.7 10.8 %fusion.2 = bf16[2,8,6,128,512]{4,3,2,0,1:T(8,128)(2,1)} fusion(bf16[8,6,2,128,512]{4,3,2,1,0:T(8,128)(2,1)} %bitcast.73, pred[8,6]{1,0:T(8,128)(4,1)S(1)} %compare_and_fusion), kind=kLoop, calls=%fused_computation.7 | loop fusion | flops 6291456 | bytes 25165872 | tf_op jit(solution)/shard_map/jit(_take)/select_n | solution.py:76
  43.5 7.6 %all-to-all-start.1 = ((bf16[2,8,6,128,512]{4,3,2,0,1:T(8,128)(2,1)}), bf16[2,8,6,128,512]{4,3,2,0,1:T(8,128)(2,1)}, u32[]{:S(2)}, u32[]{:S(2)}) async-start(bf16[2,8,6,128,512]{4,3,2,0,1:T(8,128)(2,1)} %fusion.2), calls=%async_computation.1 | async-start | bytes 25165824 | tf_op jit(solution)/shard_map/all_to_all | solution.py:81
  51.1 0.0 all-gather.2.cloned.1.call-start
  51.1 0.7 all-gather.2.cloned.1.call-update
  51.9 0.0 reduce-scatter.2.cloned.1.call-start
  51.9 0.9 fusion.27
  52.8 0.0 copy-start.2
  52.8 23.6 %all-gather.2.cloned.1.call-done = bf16[384,2560]{1,0:T(8,128)(2,1)} async-done(((bf16[96,2560]{1,0:T(8,128)(2,1)}), bf16[384,2560]{1,0:T(8,128)(2,1)}) %all-gather.2.cloned.1.call-update) | async-done | bytes 1966096 | tf_op jit(solution)/shard_map/all_gather | solution.py:34
  76.4 8.0 %convolution_convert_fusion.1 = bf16[384,1536]{1,0:T(8,128)(2,1)} fusion(bf16[384,2560]{1,0:T(8,128)(2,1)} %all-gather.2.cloned.1.call-done, bf16[2560,1536]{1,0:T(8,128)(2,1)} %param.8), kind=kOutput, calls=%fused_computation.22 | convolution fusion | flops 3020488704 | bytes 11010048 | tf_op jit(solution)/shard_map/dot_general | solution.py:33
  84.4 2.4 copy.72
  86.8 1.0 fusion.49
  87.8 0.7 pad_maximum_fusion
  88.5 3.4 collective-permute-start
  91.9 0.0 copy-done.2
  91.9 2.1 slice_bitcast_fusion
  94.1 0.9 copy.82
  95.0 0.2 copy.84
  95.2 231.9 %collective-permute-done = bf16[2,128,512]{1,2,0:T(8,128)(2,1)} collective-permute-done((bf16[2,128,512]{1,2,0:T(8,128)(2,1)}, bf16[2,128,512]{1,2,0:T(8,128)(2,1)}, u32[]{:S(2)}, u32[]{:S(2)}) %collective-permute-start) | collective-permute-done | bytes 262176 | tf_op jit(solution)/shard_map/ppermute | solution.py:18
  327.2 1.0 fusion.50
  328.2 0.1 copy.81
  328.3 1.6 fusion.31
  329.9 4.7 %fusion.51 = (f32[4,384]{1,0:T(4,128)}, f32[4,384,512]{2,1,0:T(8,128)}) fusion(f32[4,384,512]{2,1,0:T(8,128)S(1)} %fusion.31, pred[384,512]{1,0:T(8,128)(4,1)} %fusion.27), kind=kOutput, calls=%fused_computation.91 | output fusion | flops 4719103 | bytes 6494208 | tf_op jit(solution)/shard_map/sub | solution.py:23
  334.6 0.0 all-to-all-done.1
  334.6 10.6 %copy.71 = bf16[2,8,6,128,512]{4,3,2,1,0:T(8,128)(2,1)} copy(bf16[2,8,6,128,512]{4,3,2,0,1:T(8,128)(2,1)} %all-to-all-done.1) | data formatting | bytes 25165824 | tf_op jit(solution)/shard_map/all_to_all | solution.py:81
  345.2 11.1 %gather_fusion.2 = bf16[48,2,128,512]{3,2,1,0:T(8,128)(2,1)} fusion(bf16[2,8,6,128,512]{4,3,2,1,0:T(8,128)(2,1)} %copy.71, s32[48]{0:T(128)S(1)} %get-tuple-element.7), kind=kCustom, calls=%fused_computation.2 | custom fusion | bytes 25166208 | tf_op jit(solution)/shard_map/gather | solution.py:82
  356.3 10.5 %fusion.48 = (bf16[1,48,128,512]{3,2,0,1:T(8,128)(2,1)}, bf16[1,48,128,512]{3,2,0,1:T(8,128)(2,1)}) fusion(bf16[2,48,128,512]{3,2,0,1:T(8,128)(2,1)} %bitcast.72), kind=kLoop, calls=%fused_computation.88 | loop fusion | bytes 25165824 | tf_op jit(solution)/shard_map/slice | solution.py:87
  366.7 0.0 copy-start.1
  366.7 9.8 %squeeze.22 = bf16[3,2048,4,128]{3,2,1,0:T(4,128)(2,1)} reshape(bf16[1,48,128,512]{3,2,0,1:T(8,128)(2,1)} %get-tuple-element.11) | data formatting | bytes 12582912 | tf_op jit(solution)/shard_map/squeeze | solution.py:87
  376.5 0.0 copy-done.1
  376.5 9.1 %fusion.8 = f32[3,4,128,2048]{3,2,1,0:T(8,128)} fusion(bf16[3,2048,4,128]{3,2,1,0:T(4,128)(2,1)} %squeeze.22, bf16[3,128,4,128]{3,1,0,2:T(8,128)(2,1)S(1)} %bitcast.79), kind=kOutput, calls=%fused_computation.14 | convolution fusion | flops 805306368 | bytes 19267584 | tf_op jit(solution)/shard_map/bqgd,bkgd->bgqk/dot_general | solution.py:86
  385.6 15.7 %fusion.52 = (f32[3,4,128]{2,1,0:T(4,128)S(1)}, f32[3,4,128,2048]{3,2,1,0:T(8,128)}) fusion(f32[3,4,128,2048]{3,2,1,0:T(8,128)} %fusion.8), kind=kOutput, calls=%fused_computation.92 | output fusion | flops 12584959 | bytes 25171968 | tf_op jit(solution)/shard_map/sub | solution.py:23
  401.3 9.7 %squeeze.21 = bf16[3,2048,4,128]{3,2,1,0:T(4,128)(2,1)} reshape(bf16[1,48,128,512]{3,2,0,1:T(8,128)(2,1)} %get-tuple-element.12) | data formatting | bytes 12582912 | tf_op jit(solution)/shard_map/squeeze | solution.py:93
  411.0 7.9 %fusion.19 = f32[3,128,4,128]{3,1,2,0:T(8,128)S(1)} fusion(bf16[3,2048,4,128]{3,2,1,0:T(4,128)(2,1)} %squeeze.21, f32[3,4,128,2048]{3,2,1,0:T(8,128)} %get-tuple-element.23, f32[3,4,128]{2,1,0:T(4,128)S(1)} %get-tuple-element.22), kind=kOutput, calls=%fused_computation.28 | convolution fusion | flops 811597824 | bytes 19666944 | tf_op jit(solution)/shard_map/bgqk,bkgd->bqgd/dot_general | solution.py:92
  418.9 0.1 copy.77
  419.0 1.1 copy.78
  420.1 2.9 fusion.25
  423.0 0.0 copy-done
  423.1 2.5 convolution_convert_fusion
  425.6 0.0 reduce-scatter.2.cloned.1.call-update
  425.6 29.9 %reduce-scatter.2.cloned.1.call-done = bf16[96,2560]{1,0:T(8,128)(2,1)} async-done(((bf16[384,2560]{1,0:T(8,128)(2,1)}), bf16[96,2560]{1,0:T(8,128)(2,1)}) %reduce-scatter.2.cloned.1.call-update) | async-done | bytes 491536 | tf_op jit(solution)/shard_map/reduce_scatter | solution.py:102
  (13 shorter events, 0.1 us)
Async XLA Ops:
  6.5 416.5 %copy-start = (bf16[512,2560]{1,0:T(8,128)(2,1)S(1)}, bf16[512,2560]{1,0:T(8,128)(2,1)}, u32[]{:S(2)}) copy-start(bf16[512,2560]{1,0:T(8,128)(2,1)} %param.9) | copy-start | bytes 7864324
  43.5 291.1 %all-to-all-start.1 = ((bf16[2,8,6,128,512]{4,3,2,0,1:T(8,128)(2,1)}), bf16[2,8,6,128,512]{4,3,2,0,1:T(8,128)(2,1)}, u32[]{:S(2)}, u32[]{:S(2)}) async-start(bf16[2,8,6,128,512]{4,3,2,0,1:T(8,128)(2,1)} %fusion.2), calls=%async_computation.1 | async-start | bytes 25165824 | tf_op jit(solution)/shard_map/all_to_all | solution.py:81
  51.1 25.2 %all-gather.2.cloned.1.call-start = ((), (), s32[]{:S(2)}) async-start(), calls=%async_computation.3 | async-start | bytes 2457600 | tf_op jit(solution)/shard_map/all_gather | solution.py:34
  51.9 403.6 %reduce-scatter.2.cloned.1.call-start = ((), (), s32[]{:S(2)}) async-start(), calls=%async_computation.4 | async-start | bytes 2457600 | tf_op jit(solution)/shard_map/reduce_scatter | solution.py:102
  52.8 39.1 %copy-start.2 = (f32[4]{0:T(128)S(1)}, f32[4]{0:T(128)}, u32[]{:S(2)}) copy-start(f32[4]{0:T(128)} %param.10) | copy-start | bytes 52
  88.5 238.6 %collective-permute-start = (bf16[2,128,512]{1,2,0:T(8,128)(2,1)}, bf16[2,128,512]{1,2,0:T(8,128)(2,1)}, u32[]{:S(2)}, u32[]{:S(2)}) collective-permute-start(bf16[2,128,512]{1,2,0:T(8,128)(2,1)} %pad_maximum_fusion), channel_id=1, source_target_pairs={{0,4},{4,8},{8,12},{12,16},{16,20},{20,24},{24,28},{1,5},{5,9},{9,... | collective-permute-start | bytes 786440 | tf_op jit(solution)/shard_map/ppermute | solution.py:18
  366.7 9.8 %copy-start.1 = (bf16[384,4,1,128]{3,0,1,2:T(8,128)(2,1)S(1)}, bf16[384,4,1,128]{3,0,1,2:T(8,128)(2,1)}, u32[]{:S(2)}) copy-start(bf16[384,4,1,128]{3,0,1,2:T(8,128)(2,1)} %copy.82) | copy-start | bytes 1179652
Sparse Core Ops, SparseCore 0:
  53.5 22.7 all-gather.1
  425.7 29.7 reduce-scatter.1
where the time goes:
time: 465 us; the launch traced here: 462 us
  waiting for transfers between devices  286 us (62%)
  local copies, waits for them, and re-layouts  76.5 us (16%)
  other arithmetic  33.1 us (7%)
  matrix products  32 us (7%)
  between operations  13.6 us (3%)
  starting transfers between devices  11 us (2%)
  blocking collectives  10 us (2%)
    ppermute x1, waiting for transfers between devices, from_behind(): lax.ppermute(value, axis, [(source, source + steps) for source in range(i...  232 us
    reduce_scatter x1, waiting for transfers between devices, local(): lax.psum_scatter(jnp.dot(attended, output_weight, preferred_element_type=...  29.9 us
    all_gather x1, waiting for transfers between devices, local(): lax.all_gather(tokens, 'tp', axis=0, tiled=True)  23.6 us
    sub x2, other arithmetic, softmax_rows(): weights = jnp.where(allowed, jnp.exp(scores - row_peak), 0.0)  20.4 us
    gather x1, local copies, waits for them, and re-layouts, local(): gathered = fetched[:, holder, slot_of]  11.1 us
    select_n x2, other arithmetic, local(): jnp.take(local_store, lax.all_to_all(wanted_ids, 'mem', split_axis=0, con...  10.8 us
    all_to_all x1, local copies, waits for them, and re-layouts, local(): lax.all_to_all(picked, 'mem', split_axis=1, concat_axis=1, tiled=True)  10.6 us
    slice x1, local copies, waits for them, and re-layouts, local(): far_pairs[0]  10.5 us
  transfers between devices with their start and end apart: 4, of which 3 were waited for; matrix products, arithmetic and copies ran while one was open for 5% of the time, Pallas kernels for 0%

commit v1 on v0

--- a/solution.py
+++ b/solution.py
@@ -68,29 +68,40 @@
     entry_order = jnp.arange(entries)
     earlier = entry_order[None, :] < entry_order[:, None]
     same_owner = holder[:, None] == holder[None, :]
-    slot_count = blocks_here * CAP
-    slot_of = jnp.sum(same_owner & earlier, axis=1)
+    same_block = home_slot[:, None] == home_slot[None, :]
+    first = jnp.sum(same_block & earlier, axis=1) == 0
+    first_entry = jnp.argmax(same_block, axis=1)
+    before_first = entry_order[None, :] < first_entry[:, None]
+    slot_of = jnp.sum(same_owner & before_first & first[None, :], axis=1)
     wanted_ids = (
-        jnp.zeros((holder_count, slot_count), jnp.int32).at[holder, slot_of].set(local_block)
+        jnp.zeros((holder_count, CAP), jnp.int32).at[holder, slot_of].set(local_block)
     )
     picked = jnp.take(
         local_store,
-        lax.all_to_all(wanted_ids, "mem", split_axis=0, concat_axis=0, tiled=True),
+        lax.all_to_all(wanted_ids, "mem", split_axis=0, concat_axis=0, tiled=True).reshape(
+            holder_count * CAP
+        ),
         axis=1,
     )
     fetched = lax.all_to_all(picked, "mem", split_axis=1, concat_axis=1, tiled=True)
-    gathered = fetched[:, holder, slot_of]
-    far_pairs = gathered.reshape(2, blocks_here, TOPB * BLK, groups, HD)
+    pool = holder_count * CAP
+    far_keys = fetched[0].reshape(pool * BLK, groups, HD)
+    far_values = fetched[1].reshape(pool * BLK, groups, HD)
+    row_of = entry_order // TOPB
+    member = (
+        jnp.zeros((blocks_here, pool), jnp.bool_).at[row_of, holder * CAP + slot_of].set(True)
+    )
+    far_allowed = jnp.repeat(member, BLK, axis=1)[:, None, None, :]
     block_queries = queries.reshape(blocks_here, BLK, groups, HD)
     far_scores = (
         jnp.einsum(
-            "bqgd,bkgd->bgqk", block_queries, far_pairs[0], preferred_element_type=jnp.float32
+            "bqgd,kgd->bgqk", block_queries, far_keys, preferred_element_type=jnp.float32
         )
         * score_scale
     )
-    far_probs = softmax_rows(far_scores, True)
+    far_probs = softmax_rows(far_scores, far_allowed)
     far_out = jnp.einsum(
-        "bgqk,bkgd->bqgd", far_probs, far_pairs[1], preferred_element_type=jnp.float32
+        "bgqk,kgd->bqgd", far_probs, far_values, preferred_element_type=jnp.float32
     )
     far_out = far_out.reshape(local_rows, groups, HD)
     mixing = jax.nn.sigmoid(gate_logit)[None, :, None]

time: 465 us -> 222 us (0.48)
  waiting for transfers between devices: 286 us -> 103 us
  local copies, waits for them, and re-layouts: 76.5 us -> 37.6 us
  other arithmetic: 33.1 us -> 18.7 us
  matrix products: 32 us -> 26.2 us
    ppermute x1, waiting for transfers between devices: 232 us -> 51.9 us  [from_behind(): lax.ppermute(value, axis, [(source, source + steps) for source in range(i...]
    squeeze x2 -> x0, local copies, waits for them, and re-layouts: 19.5 us -> none  [the longest x1 9.75 us: local(): far_pairs[0]]
    gather x1 -> x0, local copies, waits for them, and re-layouts: 11.1 us -> none  [local(): gathered = fetched[:, holder, slot_of]]
    all_to_all x1 -> x0, local copies, waits for them, and re-layouts: 10.6 us -> none  [local(): lax.all_to_all(picked, 'mem', split_axis=1, concat_axis=1, tiled=True)]
    sub x2, other arithmetic: 20.4 us -> 10.6 us  [softmax_rows(): weights = jnp.where(allowed, jnp.exp(scores - row_peak), 0.0)]
    another operation x0 -> x3, local copies, waits for them, and re-layouts: none -> 7.99 us  [the longest x1 4.02 us: local(): far_values = fetched[1].reshape(pool * BLK, groups, HD)]
    select_n x2, other arithmetic: 10.8 us -> 4.63 us  [local(): jnp.take(local_store, lax.all_to_all(wanted_ids, 'mem', split_axis=0, con...]
    slice x1, local copies, waits for them, and re-layouts: 10.5 us -> 4.63 us  [local(): far_values = fetched[1].reshape(pool * BLK, groups, HD)]
  transfers between devices with their start and end apart: 4 -> 4, of which waited for: 3 -> 3; matrix products, arithmetic and copies ran while one was open for 5% -> 12% of each run, Pallas kernels for 0% -> 0%
where the time goes in v1:
time: 222 us; the launch traced here: 220 us
  waiting for transfers between devices  103 us (46%)
  local copies, waits for them, and re-layouts  37.6 us (17%)
  matrix products  26.2 us (12%)
  other arithmetic  18.7 us (8%)
  between operations  13.6 us (6%)
  starting transfers between devices  10.4 us (5%)
  blocking collectives  10 us (5%)
    ppermute x1, waiting for transfers between devices, from_behind(): lax.ppermute(value, axis, [(source, source + steps) for source in range(i...  51.9 us
    reduce_scatter x1, waiting for transfers between devices, local(): lax.psum_scatter(jnp.dot(attended, output_weight, preferred_element_type=...  29.9 us
    all_gather x1, waiting for transfers between devices, local(): lax.all_gather(tokens, 'tp', axis=0, tiled=True)  20.6 us
    sub x2, other arithmetic, softmax_rows(): weights = jnp.where(allowed, jnp.exp(scores - row_peak), 0.0)  10.6 us
    all_to_all x1, blocking collectives, local(): lax.all_to_all(wanted_ids, 'mem', split_axis=0, concat_axis=0, tiled=True)  10 us
    dot_general x1, matrix products, local(): jnp.dot(lax.all_gather(tokens, 'tp', axis=0, tiled=True), input_weight, p...  8.05 us
    dot_general x1, matrix products, local(): jnp.einsum('bgqk,kgd->bqgd', far_probs, far_values, preferred_element_typ...  7.92 us
    all_to_all x1, starting transfers between devices, local(): lax.all_to_all(picked, 'mem', split_axis=1, concat_axis=1, tiled=True)  6.8 us
  transfers between devices with their start and end apart: 4, of which 3 were waited for; matrix products, arithmetic and copies ran while one was open for 12% of the time, Pallas kernels for 0%

profile of v1, /device:TPU:16, one launch (start us, length us, event | category | flops | bytes accessed | tf_op | source)
XLA Modules:
  0.0 219.8 jit_solution(2529680987774456837)
XLA Ops:
  6.5 0.0 copy-start
  6.5 0.9 reshape.393
  7.4 0.8 reshape.394
  8.2 1.5 gather_fusion
  9.7 0.7 compare_reduce_fusion
  10.4 0.2 convert_reduce_fusion.1
  10.6 0.2 convert_reduce_fusion
  10.9 2.8 %scatter_fusion = s32[8,2]{0,1:T(2,128)S(1)} fusion(s32[8,2]{0,1:T(2,128)S(1)} %broadcast.458, s32[48]{0:T(128)S(1)} %fusion.41, s32[48]{0:T(128)S(1)} %get-tuple-element.11), kind=kCustom, calls=%fused_computation.2 | custom fusion | bytes 960 | tf_op jit(solution)/shard_map/scatter | solution.py:77
  13.6 0.1 copy.53
  13.7 10.0 %all_to_all.14 = s32[8,1,2]{2,1,0:T(1,128)S(1)} all-to-all(s32[8,1,2]{2,1,0:T(1,128)S(1)} %copy.53), channel_id=1, replica_groups=mesh['mem'=8,'tp'=4] {'mem'}, dimensions={0} | all-to-all | bytes 128 | tf_op jit(solution)/shard_map/all_to_all | solution.py:81
  23.7 0.1 reshape.397
  23.8 0.5 broadcast.518
  24.3 0.7 reduce.24
  25.0 0.1 reshape.395
  25.1 6.2 %gather_fusion.1 = bf16[16,2,128,512]{3,2,1,0:T(8,128)(2,1)} fusion(bf16[2,32,128,512]{3,2,1,0:T(8,128)(2,1)} %bitcast.89, s32[1024]{0:T(1024)S(1)} %pad_clamp_fusion), kind=kCustom, calls=%fused_computation.1 | custom fusion | bytes 8388672 | tf_op jit(solution)/shard_map/jit(_take)/gather | solution.py:79
  31.3 4.6 %select_bitcast_fusion = bf16[2,16,128,512]{3,2,0,1:T(8,128)(2,1)} fusion(bf16[16,2,128,512]{3,2,1,0:T(8,128)(2,1)} %gather_fusion.1, pred[16]{0:T(512)(128)(4,1)S(1)} %compare_and_fusion.1), kind=kLoop, calls=%fused_computation.18 | loop fusion | flops 2097152 | bytes 8388624 | tf_op jit(solution)/shard_map/jit(_take)/select_n | solution.py:79
  35.9 6.8 %all-to-all-start.1 = ((bf16[2,16,128,512]{3,2,0,1:T(8,128)(2,1)}), bf16[2,16,128,512]{3,2,0,1:T(8,128)(2,1)}, u32[]{:S(2)}, u32[]{:S(2)}) async-start(bf16[2,16,128,512]{3,2,0,1:T(8,128)(2,1)} %select_bitcast_fusion), calls=%async_computation.1 | async-start | bytes 8388608 | tf_op jit(solution)/shard_map/all_to_all | solution.py:86
  42.7 0.0 all-gather.2.cloned.1.call-start
  42.7 0.7 all-gather.2.cloned.1.call-update
  43.4 0.0 reduce-scatter.2.cloned.1.call-start
  43.5 2.8 %scatter_fusion.1 = pred[3,16]{1,0:T(4,128)(4,1)S(1)} fusion(pred[3,16]{1,0:T(4,128)(4,1)S(1)} %broadcast_in_dim.88, s32[48]{0:T(128)S(1)} %get-tuple-element.9, pred[48]{0:T(512)(128)(4,1)S(1)} %broadcast.492), kind=kCustom, calls=%fused_computation.3 | custom fusion | bytes 528 | tf_op jit(solution)/shard_map/scatter | solution.py:92
  46.4 0.1 broadcast_bitcast_fusion
  46.4 0.9 fusion.26
  47.3 20.6 %all-gather.2.cloned.1.call-done = bf16[384,2560]{1,0:T(8,128)(2,1)} async-done(((bf16[96,2560]{1,0:T(8,128)(2,1)}), bf16[384,2560]{1,0:T(8,128)(2,1)}) %all-gather.2.cloned.1.call-update) | async-done | bytes 1966096 | tf_op jit(solution)/shard_map/all_gather | solution.py:34
  67.9 8.1 %convolution_convert_fusion.1 = bf16[384,1536]{1,0:T(8,128)(2,1)} fusion(bf16[384,2560]{1,0:T(8,128)(2,1)} %all-gather.2.cloned.1.call-done, bf16[2560,1536]{1,0:T(8,128)(2,1)} %param.8), kind=kOutput, calls=%fused_computation.23 | convolution fusion | flops 3020488704 | bytes 11010048 | tf_op jit(solution)/shard_map/dot_general | solution.py:33
  76.0 0.0 copy-start.4
  76.0 2.4 %copy.56 = bf16[384,1536]{0,1:T(8,128)(2,1)} copy(bf16[384,1536]{1,0:T(8,128)(2,1)} %convolution_convert_fusion.1) | data formatting | bytes 2359296 | tf_op jit(solution)/shard_map/convert_element_type | solution.py:38
  78.4 1.0 fusion.51
  79.4 0.7 pad_maximum_fusion
  80.1 3.5 %collective-permute-start = (bf16[2,128,512]{1,2,0:T(8,128)(2,1)}, bf16[2,128,512]{1,2,0:T(8,128)(2,1)}, u32[]{:S(2)}, u32[]{:S(2)}) collective-permute-start(bf16[2,128,512]{1,2,0:T(8,128)(2,1)} %pad_maximum_fusion), channel_id=1, source_target_pairs={{0,4},{4,8},{8,12},{12,16},{16,20},{20,24},{24,28},{1,5},{5,9},{9,... | collective-permute-start | bytes 786440 | tf_op jit(solution)/shard_map/ppermute | solution.py:18
  83.7 0.0 copy-done.4
  83.7 2.1 slice_bitcast_fusion
  85.9 0.9 copy.76
  86.8 0.2 copy.78
  87.0 51.9 %collective-permute-done = bf16[2,128,512]{1,2,0:T(8,128)(2,1)} collective-permute-done((bf16[2,128,512]{1,2,0:T(8,128)(2,1)}, bf16[2,128,512]{1,2,0:T(8,128)(2,1)}, u32[]{:S(2)}, u32[]{:S(2)}) %collective-permute-start) | collective-permute-done | bytes 262176 | tf_op jit(solution)/shard_map/ppermute | solution.py:18
  139.0 1.0 fusion.52
  140.0 0.1 copy.64
  140.1 0.0 copy-start.3
  140.1 1.7 fusion.30
  141.8 0.0 copy-done.3
  141.8 3.7 %fusion.53 = (f32[4,384]{1,0:T(4,128)}, f32[4,384,512]{2,1,0:T(8,128)}) fusion(f32[4,384,512]{2,1,0:T(8,128)S(1)} %fusion.30, pred[384,512]{1,0:T(8,128)(4,1)S(1)} %copy-done.3), kind=kOutput, calls=%fused_computation.114 | output fusion | flops 4719103 | bytes 6494208 | tf_op jit(solution)/shard_map/sub | solution.py:23
  145.5 0.0 all-to-all-done.1
  145.5 4.6 %fusion.50 = (bf16[1,16,128,512]{3,2,0,1:T(8,128)(2,1)}, bf16[1,16,128,512]{3,2,0,1:T(8,128)(2,1)}) fusion(bf16[2,16,128,512]{3,2,0,1:T(8,128)(2,1)} %all-to-all-done.1), kind=kLoop, calls=%fused_computation.111 | loop fusion | bytes 8388608 | tf_op jit(solution)/shard_map/slice | solution.py:89
  150.1 4.0 %reshape.432 = bf16[2048,4,128]{2,1,0:T(4,128)(2,1)} reshape(bf16[1,16,128,512]{3,2,0,1:T(8,128)(2,1)} %get-tuple-element.14) | data formatting | bytes 4194304 | tf_op jit(solution)/shard_map/reshape;squeeze | solution.py:88
  154.1 0.0 copy-start.2
  154.1 4.0 %reshape.431 = bf16[2048,4,128]{2,1,0:T(4,128)(2,1)} reshape(bf16[1,16,128,512]{3,2,0,1:T(8,128)(2,1)} %get-tuple-element.13) | data formatting | bytes 4194304 | tf_op jit(solution)/shard_map/reshape;squeeze | solution.py:89
  158.1 0.0 copy-done.2
  158.1 3.4 %fusion.14 = f32[4,2048,3,128]{3,1,2,0:T(8,128)S(1)} fusion(bf16[3,128,4,128]{3,1,0,2:T(8,128)(2,1)S(1)} %bitcast.91, bf16[2048,4,128,1]{2,1,0,3:T(4,128)(2,1)} %bitcast.85), kind=kOutput, calls=%fused_computation.25 | convolution fusion | flops 805306368 | bytes 15073280 | tf_op jit(solution)/shard_map/bqgd,kgd->bgqk/dot_general | solution.py:97
  161.5 0.0 copy-start.1
  161.5 6.9 %fusion.54 = (f32[3,4,128]{2,0,1:T(4,128)S(1)}, f32[3,4,128,2048]{2,3,0,1:T(8,128)}) fusion(f32[4,2048,3,128]{3,1,2,0:T(8,128)S(1)} %fusion.14, pred[3,2048]{1,0:T(4,128)(4,1)S(1)} %bitcast.100), kind=kOutput, calls=%fused_computation.115 | output fusion | flops 18876416 | bytes 25178112 | tf_op jit(solution)/shard_map/sub | solution.py:23
  168.4 0.0 copy-done.1
  168.4 0.0 copy-start.5
  168.4 7.9 %fusion.9 = f32[4,128,3,128]{1,3,2,0:T(8,128)} fusion(f32[3,4,128,2048]{2,3,0,1:T(8,128)} %get-tuple-element.25, f32[3,4,128]{2,0,1:T(4,128)S(1)} %get-tuple-element.24, bf16[2048,4,128,1]{2,1,0,3:T(4,128)(2,1)S(1)} %bitcast.90), kind=kOutput, calls=%fused_computation.16 | convolution fusion | flops 811597824 | bytes 15472640 | tf_op jit(solution)/shard_map/bgqk,kgd->bqgd/dot_general | solution.py:103
  176.4 1.4 copy.61
  177.8 0.0 copy-done.5
  177.8 2.7 %fusion.24 = bf16[384,4,128]{0,2,1:T(8,128)(2,1)S(1)} fusion(f32[4,384,512]{2,1,0:T(8,128)} %get-tuple-element.23, f32[4,384]{1,0:T(4,128)S(1)} %copy-done.5, f32[384,4,128]{0,2,1:T(8,128)S(1)} %copy.61, bf16[384,4,128]{0,2,1:T(8,128)(2,1)} %get-tuple-element.15, bf16[128,4,128]{0,2,1:T(8,128)(2,1)S(1)} %bitcast.98, f32[4]{0:T(128)S(1)} %get-tuple-element.7, ...), kind=kOutput, calls=%fused_computation.35 | convolution fusion | flops 204734464 | bytes 4855840 | tf_op jit(solution)/shard_map/gqk,kgd->qgd/dot_general | solution.py:57
  180.5 0.0 copy-done
  180.5 2.5 %convolution_convert_fusion = bf16[384,2560]{1,0:T(8,128)(2,1)} fusion(bf16[384,512]{0,1:T(8,128)(2,1)S(1)} %bitcast.97, bf16[512,2560]{1,0:T(8,128)(2,1)S(1)} %copy-done), kind=kOutput, calls=%fused_computation.17 | convolution fusion | flops 1007616000 | bytes 4980736 | tf_op jit(solution)/shard_map/dot_general | solution.py:114
  183.0 0.0 reduce-scatter.2.cloned.1.call-update
  183.0 29.9 %reduce-scatter.2.cloned.1.call-done = bf16[96,2560]{1,0:T(8,128)(2,1)} async-done(((bf16[384,2560]{1,0:T(8,128)(2,1)}), bf16[96,2560]{1,0:T(8,128)(2,1)}) %reduce-scatter.2.cloned.1.call-update) | async-done | bytes 491536 | tf_op jit(solution)/shard_map/reduce_scatter | solution.py:113
  (17 shorter events, 0.1 us)
Async XLA Ops:
  6.5 174.0 %copy-start = (bf16[512,2560]{1,0:T(8,128)(2,1)S(1)}, bf16[512,2560]{1,0:T(8,128)(2,1)}, u32[]{:S(2)}) copy-start(bf16[512,2560]{1,0:T(8,128)(2,1)} %param.9) | copy-start | bytes 7864324
  35.9 109.6 %all-to-all-start.1 = ((bf16[2,16,128,512]{3,2,0,1:T(8,128)(2,1)}), bf16[2,16,128,512]{3,2,0,1:T(8,128)(2,1)}, u32[]{:S(2)}, u32[]{:S(2)}) async-start(bf16[2,16,128,512]{3,2,0,1:T(8,128)(2,1)} %select_bitcast_fusion), calls=%async_computation.1 | async-start | bytes 8388608 | tf_op jit(solution)/shard_map/all_to_all | solution.py:86
  42.7 25.2 %all-gather.2.cloned.1.call-start = ((), (), s32[]{:S(2)}) async-start(), calls=%async_computation.3 | async-start | bytes 2457600 | tf_op jit(solution)/shard_map/all_gather | solution.py:34
  43.4 169.6 %reduce-scatter.2.cloned.1.call-start = ((), (), s32[]{:S(2)}) async-start(), calls=%async_computation.4 | async-start | bytes 2457600 | tf_op jit(solution)/shard_map/reduce_scatter | solution.py:113
  76.0 7.7 %copy-start.4 = (f32[4]{0:T(128)S(1)}, f32[4]{0:T(128)}, u32[]{:S(2)}) copy-start(f32[4]{0:T(128)} %param.10) | copy-start | bytes 52
  80.1 58.8 %collective-permute-start = (bf16[2,128,512]{1,2,0:T(8,128)(2,1)}, bf16[2,128,512]{1,2,0:T(8,128)(2,1)}, u32[]{:S(2)}, u32[]{:S(2)}) collective-permute-start(bf16[2,128,512]{1,2,0:T(8,128)(2,1)} %pad_maximum_fusion), channel_id=1, source_target_pairs={{0,4},{4,8},{8,12},{12,16},{16,20},{20,24},{24,28},{1,5},{5,9},{9,... | collective-permute-start | bytes 786440 | tf_op jit(solution)/shard_map/ppermute | solution.py:18
  140.1 1.7 copy-start.3
  154.1 4.0 %copy-start.2 = (bf16[384,4,1,128]{3,0,1,2:T(8,128)(2,1)S(1)}, bf16[384,4,1,128]{3,0,1,2:T(8,128)(2,1)}, u32[]{:S(2)}) copy-start(bf16[384,4,1,128]{3,0,1,2:T(8,128)(2,1)} %copy.76) | copy-start | bytes 1179652
  161.5 6.9 %copy-start.1 = (bf16[2048,4,128]{2,1,0:T(4,128)(2,1)S(1)}, bf16[2048,4,128]{2,1,0:T(4,128)(2,1)}, u32[]{:S(2)}) copy-start(bf16[2048,4,128]{2,1,0:T(4,128)(2,1)} %reshape.431) | copy-start | bytes 6291460
  168.4 9.3 %copy-start.5 = (f32[4,384]{1,0:T(4,128)S(1)}, f32[4,384]{1,0:T(4,128)}, u32[]{:S(2)}) copy-start(f32[4,384]{1,0:T(4,128)} %get-tuple-element.22) | copy-start | bytes 18436
Sparse Core Ops, SparseCore 0:
  45.1 22.7 all-gather.1
  183.2 29.7 reduce-scatter.1

commit v2 on v1

--- a/solution.py
+++ b/solution.py
@@ -2,6 +2,8 @@
 import jax.numpy as jnp
 from jax import lax
 from jax.sharding import PartitionSpec as P
+from jax.experimental import pallas as pl
+from jax.experimental.pallas import tpu as pltpu
 
 HD = 128
 BLK = 128
@@ -24,6 +26,45 @@
     return (weights / jnp.sum(weights, axis=-1, keepdims=True)).astype(jnp.bfloat16)
 
 
+def far_kernel(q_ref, k_ref, v_ref, allow_ref, o_ref):
+    pool = k_ref.shape[1]
+    keys = k_ref[0].reshape(pool * BLK, HD)
+    values = v_ref[0].reshape(pool * BLK, HD)
+    scores = lax.dot_general(
+        q_ref[...], keys, (((1,), (1,)), ((), ())), preferred_element_type=jnp.float32
+    ) * (HD ** (-0.5))
+    allowed = allow_ref[0] > 0
+    peak = jnp.max(jnp.where(allowed, scores, NEG_FILL), axis=-1, keepdims=True)
+    weights = jnp.where(allowed, jnp.exp(scores - peak), 0.0)
+    probs = (weights / jnp.sum(weights, axis=-1, keepdims=True)).astype(jnp.bfloat16)
+    o_ref[...] = jnp.dot(probs, values, preferred_element_type=jnp.float32)
+
+
+def far_attention(projected, fetched, allow):
+    rows = projected.shape[0]
+    blocks = rows // BLK
+    pool = fetched.shape[1]
+    groups = fetched.shape[3] // HD
+    steps = groups * blocks
+    return pl.pallas_call(
+        far_kernel,
+        grid=(groups, blocks),
+        in_specs=[
+            pl.BlockSpec((BLK, HD), lambda h, b: (b, h * 3)),
+            pl.BlockSpec((1, pool, BLK, HD), lambda h, b: (0, 0, 0, h)),
+            pl.BlockSpec((1, pool, BLK, HD), lambda h, b: (1, 0, 0, h)),
+            pl.BlockSpec((1, 1, pool * BLK), lambda h, b: (b, 0, 0)),
+        ],
+        out_specs=pl.BlockSpec((BLK, HD), lambda h, b: (b, h)),
+        out_shape=jax.ShapeDtypeStruct((rows, groups * HD), jnp.float32),
+        cost_estimate=pl.CostEstimate(
+            flops=steps * 4 * BLK * pool * BLK * HD,
+            transcendentals=steps * BLK * pool * BLK,
+            bytes_accessed=fetched.size * 2 + rows * groups * HD * 6,
+        ),
+    )(projected, fetched, fetched, allow)
+
+
 def local(tokens, input_weight, output_weight, gate_logit, memory, retrieved, block_home):
     holder_count = lax.axis_size("mem")
     share_rows = tokens.shape[0]
@@ -35,7 +76,8 @@
         input_weight,
         preferred_element_type=jnp.float32,
     )
-    projected = projected.astype(jnp.bfloat16).reshape(local_rows, groups, 3, HD)
+    projected_flat = projected.astype(jnp.bfloat16)
+    projected = projected_flat.reshape(local_rows, groups, 3, HD)
     queries = projected[:, :, 0]
     key_rows = projected[:, :, 1]
     value_rows = projected[:, :, 2]
@@ -82,28 +124,16 @@
             holder_count * CAP
         ),
         axis=1,
+        mode="clip",
     )
     fetched = lax.all_to_all(picked, "mem", split_axis=1, concat_axis=1, tiled=True)
     pool = holder_count * CAP
-    far_keys = fetched[0].reshape(pool * BLK, groups, HD)
-    far_values = fetched[1].reshape(pool * BLK, groups, HD)
     row_of = entry_order // TOPB
     member = (
-        jnp.zeros((blocks_here, pool), jnp.bool_).at[row_of, holder * CAP + slot_of].set(True)
+        jnp.zeros((blocks_here, pool), jnp.float32).at[row_of, holder * CAP + slot_of].set(1.0)
     )
-    far_allowed = jnp.repeat(member, BLK, axis=1)[:, None, None, :]
-    block_queries = queries.reshape(blocks_here, BLK, groups, HD)
-    far_scores = (
-        jnp.einsum(
-            "bqgd,kgd->bgqk", block_queries, far_keys, preferred_element_type=jnp.float32
-        )
-        * score_scale
-    )
-    far_probs = softmax_rows(far_scores, far_allowed)
-    far_out = jnp.einsum(
-        "bgqk,kgd->bqgd", far_probs, far_values, preferred_element_type=jnp.float32
-    )
-    far_out = far_out.reshape(local_rows, groups, HD)
+    allow = jnp.repeat(member, BLK, axis=1).reshape(blocks_here, 1, pool * BLK)
+    far_out = far_attention(projected_flat, fetched, allow).reshape(local_rows, groups, HD)
     mixing = jax.nn.sigmoid(gate_logit)[None, :, None]
     attended = (
         (mixing * far_out + (1.0 - mixing) * near_out)

time: 222 us -> 206 us (0.928)
  Pallas kernels: 0 us -> 14.2 us
  other arithmetic: 18.7 us -> 7.21 us
  matrix products: 26.2 us -> 14.9 us
  local copies, waits for them, and re-layouts: 37.6 us -> 28.9 us
    pallas_call x0 -> x1, Pallas kernels: none -> 14.2 us  [far_attention(): pl.pallas_call(far_kernel, grid=(groups, blocks), in_specs=[pl.BlockSpec(...]
    dot_general x2 -> x0, matrix products: 11.3 us -> none  [the longest x1 7.92 us: local(): jnp.einsum('bgqk,kgd->bqgd', far_probs, far_values, preferred_element_typ...]
    another operation x3 -> x1, local copies, waits for them, and re-layouts: 7.99 us -> 0.01 us  [the longest x1 4.02 us: local(): far_values = fetched[1].reshape(pool * BLK, groups, HD)]
    sub x2 -> x1, other arithmetic: 10.6 us -> 3.81 us  [softmax_rows(): weights = jnp.where(allowed, jnp.exp(scores - row_peak), 0.0)]
    slice x1 -> x0, local copies, waits for them, and re-layouts: 4.63 us -> none  [local(): far_values = fetched[1].reshape(pool * BLK, groups, HD)]
    select_n x2 -> x0, other arithmetic: 4.63 us -> none  [local(): jnp.take(local_store, lax.all_to_all(wanted_ids, 'mem', split_axis=0, con...]
    all_to_all x0 -> x1, local copies, waits for them, and re-layouts: none -> 4.6 us  [local(): lax.all_to_all(picked, 'mem', split_axis=1, concat_axis=1, tiled=True)]
    all_gather x1, waiting for transfers between devices: 20.6 us -> 23.6 us  [local(): lax.all_gather(tokens, 'tp', axis=0, tiled=True)]
where the time goes in v2:
time: 206 us; the launch traced here: 204 us
  waiting for transfers between devices  105 us (51%)
  local copies, waits for them, and re-layouts  28.9 us (14%)
  matrix products  14.9 us (7%)
  Pallas kernels  14.2 us (7%)
  between operations  13.6 us (7%)
  starting transfers between devices  10.2 us (5%)
  blocking collectives  10 us (5%)
  other arithmetic  7.21 us (4%)
    ppermute x1, waiting for transfers between devices, from_behind(): lax.ppermute(value, axis, [(source, source + steps) for source in range(i...  50.5 us
    reduce_scatter x1, waiting for transfers between devices, local(): lax.psum_scatter(jnp.dot(attended, output_weight, preferred_element_type=...  29.9 us
    all_gather x1, waiting for transfers between devices, local(): lax.all_gather(tokens, 'tp', axis=0, tiled=True)  23.6 us
    pallas_call x1, Pallas kernels, far_attention(): pl.pallas_call(far_kernel, grid=(groups, blocks), in_specs=[pl.BlockSpec(...  14.2 us
    all_to_all x1, blocking collectives, local(): lax.all_to_all(wanted_ids, 'mem', split_axis=0, concat_axis=0, tiled=True)  10 us
    dot_general x1, matrix products, local(): jnp.dot(lax.all_gather(tokens, 'tp', axis=0, tiled=True), input_weight, p...  8.07 us
    all_to_all x1, starting transfers between devices, local(): lax.all_to_all(picked, 'mem', split_axis=1, concat_axis=1, tiled=True)  6.8 us
    gather x1, local copies, waits for them, and re-layouts, local(): jnp.take(local_store, lax.all_to_all(wanted_ids, 'mem', split_axis=0, con...  6.17 us
  transfers between devices with their start and end apart: 4, of which 3 were waited for; matrix products, arithmetic and copies ran while one was open for 12% of the time, Pallas kernels for 0%

profile of v2, /device:TPU:16, one launch (start us, length us, event | category | flops | bytes accessed | tf_op | source)
XLA Modules:
  0.0 203.7 jit_solution(7435170070310947738)
XLA Ops:
  6.5 0.0 copy-start
  6.5 0.9 reshape.353
  7.4 0.8 reshape.354
  8.2 1.5 gather_fusion
  9.7 0.7 compare_reduce_fusion
  10.4 0.2 convert_reduce_fusion.1
  10.6 0.2 convert_reduce_fusion
  10.9 2.8 %scatter_fusion = s32[8,2]{0,1:T(2,128)S(1)} fusion(s32[8,2]{0,1:T(2,128)S(1)} %broadcast.422, s32[48]{0:T(128)S(1)} %fusion.27, s32[48]{0:T(128)S(1)} %get-tuple-element.11), kind=kCustom, calls=%fused_computation.2 | custom fusion | bytes 960 | tf_op jit(solution)/shard_map/scatter | solution.py:119
  13.6 0.1 copy.32
  13.7 10.0 %all_to_all.14 = s32[8,1,2]{2,1,0:T(1,128)S(1)} all-to-all(s32[8,1,2]{2,1,0:T(1,128)S(1)} %copy.32), channel_id=1, replica_groups=mesh['mem'=8,'tp'=4] {'mem'}, dimensions={0} | all-to-all | bytes 128 | tf_op jit(solution)/shard_map/all_to_all | solution.py:123
  23.7 0.5 broadcast.475
  24.2 0.7 reduce.22
  24.9 0.1 reshape.368
  25.0 6.2 %gather_fusion.1 = bf16[16,2,128,512]{3,2,1,0:T(8,128)(2,1)} fusion(bf16[2,32,128,512]{3,2,1,0:T(8,128)(2,1)} %bitcast.53, s32[1024]{0:T(1024)S(1)} %pad_clamp_fusion), kind=kCustom, calls=%fused_computation.1 | custom fusion | bytes 8388672 | tf_op jit(solution)/shard_map/jit(_take)/gather | solution.py:121
  31.2 6.8 %all-to-all-start.1 = ((bf16[2,16,128,512]{3,2,0,1:T(8,128)(2,1)}), bf16[2,16,128,512]{3,2,0,1:T(8,128)(2,1)}, u32[]{:S(2)}, u32[]{:S(2)}) async-start(bf16[2,16,128,512]{3,2,0,1:T(8,128)(2,1)} %bitcast.49), calls=%async_computation.1 | async-start | bytes 8388608 | tf_op jit(solution)/shard_map/all_to_all | solution.py:129
  38.0 0.0 all-gather.2.cloned.1.call-start
  38.0 0.7 all-gather.2.cloned.1.call-update
  38.7 0.0 reduce-scatter.2.cloned.1.call-start
  38.8 0.9 fusion.14
  39.6 23.6 %all-gather.2.cloned.1.call-done = bf16[384,2560]{1,0:T(8,128)(2,1)} async-done(((bf16[96,2560]{1,0:T(8,128)(2,1)}), bf16[384,2560]{1,0:T(8,128)(2,1)}) %all-gather.2.cloned.1.call-update) | async-done | bytes 1966096 | tf_op jit(solution)/shard_map/all_gather | solution.py:75
  63.2 8.1 %convolution_convert_fusion.1.q_ref = bf16[384,1536]{1,0:T(8,128)(2,1)} fusion(bf16[384,2560]{1,0:T(8,128)(2,1)} %all-gather.2.cloned.1.call-done, bf16[2560,1536]{1,0:T(8,128)(2,1)} %param.8), kind=kOutput, calls=%fused_computation.10 | convolution fusion | flops 3020488704 | bytes 11010048 | tf_op jit(solution)/shard_map/dot_general | solution.py:74
  71.3 0.0 copy-start.2
  71.3 2.4 %copy.36 = bf16[384,1536]{0,1:T(8,128)(2,1)} copy(bf16[384,1536]{1,0:T(8,128)(2,1)} %convolution_convert_fusion.1.q_ref) | data formatting | bytes 2359296 | tf_op jit(solution)/shard_map/convert_element_type | solution.py:79
  73.7 1.0 fusion.33
  74.7 0.7 pad_maximum_fusion
  75.4 3.4 %collective-permute-start = (bf16[2,128,512]{1,2,0:T(8,128)(2,1)}, bf16[2,128,512]{1,2,0:T(8,128)(2,1)}, u32[]{:S(2)}, u32[]{:S(2)}) collective-permute-start(bf16[2,128,512]{1,2,0:T(8,128)(2,1)} %pad_maximum_fusion), channel_id=1, source_target_pairs={{0,4},{4,8},{8,12},{12,16},{16,20},{20,24},{24,28},{1,5},{5,9},{9,... | collective-permute-start | bytes 786440 | tf_op jit(solution)/shard_map/ppermute | solution.py:20
  78.8 0.0 copy-done.2
  78.8 2.7 %scatter_fusion.1 = f32[3,16]{1,0:T(4,128)S(1)} fusion(f32[3,16]{1,0:T(4,128)S(1)} %broadcast_in_dim.59, s32[48]{0:T(128)S(1)} %get-tuple-element.9, f32[48]{0:T(128)S(1)} %broadcast.456), kind=kCustom, calls=%fused_computation.3 | custom fusion | bytes 960 | tf_op jit(solution)/shard_map/scatter | solution.py:133
  81.6 1.9 slice_bitcast_fusion.2
  83.5 0.2 copy.44
  83.8 50.5 %collective-permute-done = bf16[2,128,512]{1,2,0:T(8,128)(2,1)} collective-permute-done((bf16[2,128,512]{1,2,0:T(8,128)(2,1)}, bf16[2,128,512]{1,2,0:T(8,128)(2,1)}, u32[]{:S(2)}, u32[]{:S(2)}) %collective-permute-start) | collective-permute-done | bytes 262176 | tf_op jit(solution)/shard_map/ppermute | solution.py:20
  134.2 1.0 fusion.34
  135.2 0.1 copy.40
  135.4 0.0 copy-start.1
  135.4 1.7 fusion.18
  137.1 0.0 copy-done.1
  137.1 3.8 %fusion.35 = (f32[4,384]{1,0:T(4,128)}, f32[4,384,512]{2,1,0:T(8,128)}) fusion(f32[4,384,512]{2,1,0:T(8,128)S(1)} %fusion.18, pred[384,512]{1,0:T(8,128)(4,1)S(1)} %copy-done.1), kind=kOutput, calls=%fused_computation.88 | output fusion | flops 4719103 | bytes 6494208 | tf_op jit(solution)/shard_map/sub | solution.py:25
  140.9 0.0 all-to-all-done.1
  140.9 4.6 %copy.33.k_ref.v_ref = bf16[2,16,128,512]{3,2,1,0:T(8,128)(2,1)} copy(bf16[2,16,128,512]{3,2,0,1:T(8,128)(2,1)} %all-to-all-done.1) | data formatting | bytes 8388608 | tf_op jit(solution)/shard_map/all_to_all | solution.py:129
  145.5 0.7 broadcast_in_dim.61
  146.1 14.2 %shard_map.73 = f32[384,512]{1,0:T(8,128)} custom-call(bf16[384,1536]{1,0:T(8,128)(2,1)} %convolution_convert_fusion.1.q_ref, bf16[2,16,128,512]{3,2,1,0:T(8,128)(2,1)} %copy.33.k_ref.v_ref, bf16[2,16,128,512]{3,2,1,0:T(8,128)(2,1)} %copy.33.k_ref.v_ref, f32[3,1,2048]{2,1,0:T(1,128)} %bitcast.61), custom_call_target="tpu_custom_call" | custom-call | flops 1610612736 | bytes 5373952 | tf_op jit(solution)/shard_map/pallas_call | solution.py:49
  160.3 1.4 copy.41
  161.7 2.7 %fusion.12 = bf16[384,4,128]{0,2,1:T(8,128)(2,1)S(1)} fusion(f32[4,384,512]{2,1,0:T(8,128)} %get-tuple-element.20, f32[4,384]{1,0:T(4,128)} %get-tuple-element.19, f32[384,4,128]{0,2,1:T(8,128)S(1)} %bitcast.55, bf16[384,4,128]{0,2,1:T(8,128)(2,1)} %get-tuple-element.13, bf16[128,4,128]{0,2,1:T(8,128)(2,1)S(1)} %bitcast.60, f32[4]{0:T(128)S(1)} %get-tuple-element.7, ...), kind=kOutput, calls=%fused_computation.19 | convolution fusion | flops 204734464 | bytes 4855840 | tf_op jit(solution)/shard_map/gqk,kgd->qgd/dot_general | solution.py:99
  164.4 0.0 copy-done
  164.4 2.5 %convolution_convert_fusion = bf16[384,2560]{1,0:T(8,128)(2,1)} fusion(bf16[384,512]{0,1:T(8,128)(2,1)S(1)} %bitcast.59, bf16[512,2560]{1,0:T(8,128)(2,1)S(1)} %copy-done), kind=kOutput, calls=%fused_computation.5 | convolution fusion | flops 1007616000 | bytes 4980736 | tf_op jit(solution)/shard_map/dot_general | solution.py:144
  166.9 0.0 reduce-scatter.2.cloned.1.call-update
  166.9 29.9 %reduce-scatter.2.cloned.1.call-done = bf16[96,2560]{1,0:T(8,128)(2,1)} async-done(((bf16[384,2560]{1,0:T(8,128)(2,1)}), bf16[96,2560]{1,0:T(8,128)(2,1)}) %reduce-scatter.2.cloned.1.call-update) | async-done | bytes 491536 | tf_op jit(solution)/shard_map/reduce_scatter | solution.py:143
  (14 shorter events, 0.1 us)
Async XLA Ops:
  6.5 157.9 %copy-start = (bf16[512,2560]{1,0:T(8,128)(2,1)S(1)}, bf16[512,2560]{1,0:T(8,128)(2,1)}, u32[]{:S(2)}) copy-start(bf16[512,2560]{1,0:T(8,128)(2,1)} %param.9) | copy-start | bytes 7864324
  31.2 109.7 %all-to-all-start.1 = ((bf16[2,16,128,512]{3,2,0,1:T(8,128)(2,1)}), bf16[2,16,128,512]{3,2,0,1:T(8,128)(2,1)}, u32[]{:S(2)}, u32[]{:S(2)}) async-start(bf16[2,16,128,512]{3,2,0,1:T(8,128)(2,1)} %bitcast.49), calls=%async_computation.1 | async-start | bytes 8388608 | tf_op jit(solution)/shard_map/all_to_all | solution.py:129
  38.0 25.2 %all-gather.2.cloned.1.call-start = ((), (), s32[]{:S(2)}) async-start(), calls=%async_computation.3 | async-start | bytes 2457600 | tf_op jit(solution)/shard_map/all_gather | solution.py:75
  38.7 158.2 %reduce-scatter.2.cloned.1.call-start = ((), (), s32[]{:S(2)}) async-start(), calls=%async_computation.4 | async-start | bytes 2457600 | tf_op jit(solution)/shard_map/reduce_scatter | solution.py:143
  71.3 7.5 %copy-start.2 = (f32[4]{0:T(128)S(1)}, f32[4]{0:T(128)}, u32[]{:S(2)}) copy-start(f32[4]{0:T(128)} %param.10) | copy-start | bytes 52
  75.4 58.8 %collective-permute-start = (bf16[2,128,512]{1,2,0:T(8,128)(2,1)}, bf16[2,128,512]{1,2,0:T(8,128)(2,1)}, u32[]{:S(2)}, u32[]{:S(2)}) collective-permute-start(bf16[2,128,512]{1,2,0:T(8,128)(2,1)} %pad_maximum_fusion), channel_id=1, source_target_pairs={{0,4},{4,8},{8,12},{12,16},{16,20},{20,24},{24,28},{1,5},{5,9},{9,... | collective-permute-start | bytes 786440 | tf_op jit(solution)/shard_map/ppermute | solution.py:20
  135.4 1.7 copy-start.1
Sparse Core Ops, SparseCore 0:
  40.4 22.7 all-gather.1
  167.1 29.7 reduce-scatter.1

commit v3 on v2

--- a/solution.py
+++ b/solution.py
@@ -140,13 +140,30 @@
         .astype(jnp.bfloat16)
         .reshape(local_rows, groups * HD)
     )
-    return lax.psum_scatter(
-        jnp.dot(attended, output_weight, preferred_element_type=jnp.float32).astype(jnp.bfloat16),
-        "tp",
-        scatter_dimension=0,
-        tiled=True,
+    partial = jnp.dot(attended, output_weight, preferred_element_type=jnp.float32)
+    return reduce_over_tp(partial).astype(jnp.bfloat16)
+
+
+def reduce_over_tp(partial):
+    count = lax.axis_size("tp")
+    chips = count // 2
+    share = partial.shape[0] // count
+    me = lax.axis_index("tp")
+    core = me % 2
+    chip = me // 2
+    split = partial.reshape(chips, 2, share, partial.shape[1])
+    mine = lax.dynamic_index_in_dim(split, core, axis=1, keepdims=False)
+    other = lax.dynamic_index_in_dim(split, 1 - core, axis=1, keepdims=False)
+    arrived = lax.ppermute(
+        other.astype(jnp.bfloat16), "tp", [(t, t ^ 1) for t in range(count)]
     )
-
+    chip_sum = mine + arrived.astype(jnp.float32)
+    total = lax.dynamic_index_in_dim(chip_sum, chip, axis=0, keepdims=False)
+    for shift in range(1, chips):
+        outgoing = lax.dynamic_index_in_dim(chip_sum, (chip + shift) % chips, axis=0, keepdims=False)
+        pairs = [(t, ((t // 2 + shift) % chips) * 2 + t % 2) for t in range(count)]
+        total = total + lax.ppermute(outgoing.astype(jnp.bfloat16), "tp", pairs).astype(jnp.float32)
+    return total
 
 def solution(mesh):
     placed = (

time: 206 us -> 200 us (0.971)
  waiting for transfers between devices: 105 us -> 89.5 us
  local copies, waits for them, and re-layouts: 28.9 us -> 34.6 us
  other arithmetic: 7.21 us -> 11.5 us
    reduce_scatter x1 -> x0, waiting for transfers between devices: 29.9 us -> none  [local(): lax.psum_scatter(jnp.dot(attended, output_weight, preferred_element_type=...]
    ppermute x0 -> x2, waiting for transfers between devices: none -> 14.7 us  [the longest x1 11.8 us: reduce_over_tp(): lax.ppermute(outgoing.astype(jnp.bfloat16), 'tp', pairs).astype(jnp.float32)]
    unnamed x7 -> x11, local copies, waits for them, and re-layouts: 0.25 us -> 3.4 us
    convert_element_type x0 -> x3, local copies, waits for them, and re-layouts: none -> 2.36 us  [the longest x1 1.24 us: local(): attended = (mixing * far_out + (1.0 - mixing) * near_out).astype(jnp.bflo...]
    convert_element_type x0 -> x1, other arithmetic: none -> 2.22 us  [local(): return reduce_over_tp(partial).astype(jnp.bfloat16)]
  transfers between devices with their start and end apart: 4 -> 5, of which waited for: 3 -> 4; matrix products, arithmetic and copies ran while one was open for 12% -> 12% of each run, Pallas kernels for 0% -> 0%
where the time goes in v3:
time: 200 us; the launch traced here: 199 us
  waiting for transfers between devices  89.5 us (45%)
  local copies, waits for them, and re-layouts  34.6 us (17%)
  matrix products  14.3 us (7%)
  Pallas kernels  14.2 us (7%)
  between operations  13.6 us (7%)
  starting transfers between devices  11.8 us (6%)
  other arithmetic  11.5 us (6%)
  blocking collectives  10 us (5%)
    ppermute x1, waiting for transfers between devices, from_behind(): lax.ppermute(value, axis, [(source, source + steps) for source in range(i...  50.5 us
    all_gather x1, waiting for transfers between devices, local(): lax.all_gather(tokens, 'tp', axis=0, tiled=True)  23.6 us
    pallas_call x1, Pallas kernels, far_attention(): pl.pallas_call(far_kernel, grid=(groups, blocks), in_specs=[pl.BlockSpec(...  14.2 us
    ppermute x1, waiting for transfers between devices, reduce_over_tp(): lax.ppermute(outgoing.astype(jnp.bfloat16), 'tp', pairs).astype(jnp.float32)  11.8 us
    all_to_all x1, blocking collectives, local(): lax.all_to_all(wanted_ids, 'mem', split_axis=0, concat_axis=0, tiled=True)  10 us
    dot_general x1, matrix products, local(): jnp.dot(lax.all_gather(tokens, 'tp', axis=0, tiled=True), input_weight, p...  8.07 us
    all_to_all x1, starting transfers between devices, local(): lax.all_to_all(picked, 'mem', split_axis=1, concat_axis=1, tiled=True)  6.8 us
    gather x1, local copies, waits for them, and re-layouts, local(): jnp.take(local_store, lax.all_to_all(wanted_ids, 'mem', split_axis=0, con...  6.17 us
  transfers between devices with their start and end apart: 5, of which 4 were waited for; matrix products, arithmetic and copies ran while one was open for 12% of the time, Pallas kernels for 0%

profile of v3, /device:TPU:16, one launch (start us, length us, event | category | flops | bytes accessed | tf_op | source)
XLA Modules:
  0.0 199.5 jit_solution(4079716501421766993)
XLA Ops:
  6.5 0.0 copy-start
  6.5 0.9 reshape.356
  7.4 0.8 reshape.357
  8.2 1.5 gather_fusion
  9.7 0.7 compare_reduce_fusion
  10.4 0.2 convert_reduce_fusion.1
  10.6 0.2 convert_reduce_fusion
  10.9 2.8 %scatter_fusion = s32[8,2]{0,1:T(2,128)S(1)} fusion(s32[8,2]{0,1:T(2,128)S(1)} %broadcast.429, s32[48]{0:T(128)S(1)} %fusion.32, s32[48]{0:T(128)S(1)} %get-tuple-element.11), kind=kCustom, calls=%fused_computation.2 | custom fusion | bytes 960 | tf_op jit(solution)/shard_map/scatter | solution.py:119
  13.6 0.1 copy.35
  13.7 10.0 %all_to_all.14 = s32[8,1,2]{2,1,0:T(1,128)S(1)} all-to-all(s32[8,1,2]{2,1,0:T(1,128)S(1)} %copy.35), channel_id=1, replica_groups=mesh['mem'=8,'tp'=4] {'mem'}, dimensions={0} | all-to-all | bytes 128 | tf_op jit(solution)/shard_map/all_to_all | solution.py:123
  23.7 0.5 broadcast.487
  24.2 0.7 reduce.22
  24.9 0.1 reshape.370
  25.0 6.2 %gather_fusion.1 = bf16[16,2,128,512]{3,2,1,0:T(8,128)(2,1)} fusion(bf16[2,32,128,512]{3,2,1,0:T(8,128)(2,1)} %bitcast.66, s32[1024]{0:T(1024)S(1)} %pad_clamp_fusion), kind=kCustom, calls=%fused_computation.1 | custom fusion | bytes 8388672 | tf_op jit(solution)/shard_map/jit(_take)/gather | solution.py:121
  31.2 6.8 %all-to-all-start.1 = ((bf16[2,16,128,512]{3,2,0,1:T(8,128)(2,1)}), bf16[2,16,128,512]{3,2,0,1:T(8,128)(2,1)}, u32[]{:S(2)}, u32[]{:S(2)}) async-start(bf16[2,16,128,512]{3,2,0,1:T(8,128)(2,1)} %bitcast.62), calls=%async_computation.1 | async-start | bytes 8388608 | tf_op jit(solution)/shard_map/all_to_all | solution.py:129
  38.0 0.0 all-gather.2.cloned.1.call-start
  38.0 0.7 all-gather.2.cloned.1.call-update
  38.7 0.9 fusion.18
  39.6 23.6 %all-gather.2.cloned.1.call-done = bf16[384,2560]{1,0:T(8,128)(2,1)} async-done(((bf16[96,2560]{1,0:T(8,128)(2,1)}), bf16[384,2560]{1,0:T(8,128)(2,1)}) %all-gather.2.cloned.1.call-update) | async-done | bytes 1966096 | tf_op jit(solution)/shard_map/all_gather | solution.py:75
  63.2 8.1 %convolution_convert_fusion.q_ref = bf16[384,1536]{1,0:T(8,128)(2,1)} fusion(bf16[384,2560]{1,0:T(8,128)(2,1)} %all-gather.2.cloned.1.call-done, bf16[2560,1536]{1,0:T(8,128)(2,1)} %param.8), kind=kOutput, calls=%fused_computation.9 | convolution fusion | flops 3020488704 | bytes 11010048 | tf_op jit(solution)/shard_map/dot_general | solution.py:74
  71.3 0.0 copy-start.4
  71.3 2.4 %copy.39 = bf16[384,1536]{0,1:T(8,128)(2,1)} copy(bf16[384,1536]{1,0:T(8,128)(2,1)} %convolution_convert_fusion.q_ref) | data formatting | bytes 2359296 | tf_op jit(solution)/shard_map/convert_element_type | solution.py:79
  73.7 1.0 fusion.38
  74.7 0.7 pad_maximum_fusion
  75.4 3.4 %collective-permute-start = (bf16[2,128,512]{1,2,0:T(8,128)(2,1)}, bf16[2,128,512]{1,2,0:T(8,128)(2,1)}, u32[]{:S(2)}, u32[]{:S(2)}) collective-permute-start(bf16[2,128,512]{1,2,0:T(8,128)(2,1)} %pad_maximum_fusion), channel_id=1, source_target_pairs={{0,4},{4,8},{8,12},{12,16},{16,20},{20,24},{24,28},{1,5},{5,9},{9,... | collective-permute-start | bytes 786440 | tf_op jit(solution)/shard_map/ppermute | solution.py:20
  78.8 0.0 copy-done.4
  78.8 2.7 %scatter_fusion.1 = f32[3,16]{1,0:T(4,128)S(1)} fusion(f32[3,16]{1,0:T(4,128)S(1)} %broadcast_in_dim.59, s32[48]{0:T(128)S(1)} %get-tuple-element.9, f32[48]{0:T(128)S(1)} %broadcast.465), kind=kCustom, calls=%fused_computation.3 | custom fusion | bytes 960 | tf_op jit(solution)/shard_map/scatter | solution.py:133
  81.6 1.9 slice_bitcast_fusion.2
  83.5 0.2 copy.49
  83.8 50.5 %collective-permute-done = bf16[2,128,512]{1,2,0:T(8,128)(2,1)} collective-permute-done((bf16[2,128,512]{1,2,0:T(8,128)(2,1)}, bf16[2,128,512]{1,2,0:T(8,128)(2,1)}, u32[]{:S(2)}, u32[]{:S(2)}) %collective-permute-start) | collective-permute-done | bytes 262176 | tf_op jit(solution)/shard_map/ppermute | solution.py:20
  134.2 1.0 fusion.39
  135.2 0.1 copy.43
  135.4 0.0 copy-start.3
  135.4 1.7 fusion.22
  137.1 0.0 copy-done.3
  137.1 3.8 %fusion.40 = (f32[4,384]{1,0:T(4,128)}, f32[4,384,512]{2,1,0:T(8,128)}) fusion(f32[4,384,512]{2,1,0:T(8,128)S(1)} %fusion.22, pred[384,512]{1,0:T(8,128)(4,1)S(1)} %copy-done.3), kind=kOutput, calls=%fused_computation.96 | output fusion | flops 4719103 | bytes 6494208 | tf_op jit(solution)/shard_map/sub | solution.py:25
  140.9 0.0 all-to-all-done.1
  140.9 4.6 %copy.36.k_ref.v_ref = bf16[2,16,128,512]{3,2,1,0:T(8,128)(2,1)} copy(bf16[2,16,128,512]{3,2,0,1:T(8,128)(2,1)} %all-to-all-done.1) | data formatting | bytes 8388608 | tf_op jit(solution)/shard_map/all_to_all | solution.py:129
  145.5 0.7 broadcast_in_dim.61
  146.1 14.2 %shard_map.73 = f32[384,512]{1,0:T(8,128)} custom-call(bf16[384,1536]{1,0:T(8,128)(2,1)} %convolution_convert_fusion.q_ref, bf16[2,16,128,512]{3,2,1,0:T(8,128)(2,1)} %copy.36.k_ref.v_ref, bf16[2,16,128,512]{3,2,1,0:T(8,128)(2,1)} %copy.36.k_ref.v_ref, f32[3,1,2048]{2,1,0:T(1,128)} %bitcast.73), custom_call_target="tpu_custom_call" | custom-call | flops 1610612736 | bytes 5373952 | tf_op jit(solution)/shard_map/pallas_call | solution.py:49
  160.3 1.4 copy.46
  161.7 3.4 %fusion.14 = bf16[384,4,128]{0,2,1:T(8,128)(2,1)} fusion(f32[4,384,512]{2,1,0:T(8,128)} %get-tuple-element.20, f32[4,384]{1,0:T(4,128)} %get-tuple-element.19, f32[384,4,128]{0,2,1:T(8,128)S(1)} %bitcast.68, bf16[384,4,128]{0,2,1:T(8,128)(2,1)} %get-tuple-element.13, bf16[128,4,128]{0,2,1:T(8,128)(2,1)S(1)} %bitcast.72, f32[4]{0:T(128)S(1)} %get-tuple-element.7, ...), kind=kOutput, calls=%fused_computation.22 | convolution fusion | flops 204734464 | bytes 4855840 | tf_op jit(solution)/shard_map/gqk,kgd->qgd/dot_general | solution.py:99
  165.1 1.2 copy.44
  166.4 0.2 dot_general.17
  166.6 0.0 copy-done
  166.6 1.2 fusion.3
  167.7 0.0 copy-start.1
  167.8 1.9 copy-done.1
  169.6 1.1 fusion.15
  170.7 0.0 collective-permute-start.1
  170.7 2.9 %collective-permute-done.1 = bf16[2,96,2560]{2,1,0:T(8,128)(2,1)} collective-permute-done((bf16[2,96,2560]{2,1,0:T(8,128)(2,1)}, bf16[2,96,2560]{2,1,0:T(8,128)(2,1)}, u32[]{:S(2)}, u32[]{:S(2)}) %collective-permute-start.1) | collective-permute-done | bytes 983072 | tf_op jit(solution)/shard_map/ppermute | solution.py:157
  173.6 2.0 %bitcast_add_fusion = f32[2,96,2560]{2,1,0:T(8,128)S(1)} fusion(bf16[2,96,2560]{2,1,0:T(8,128)(2,1)} %collective-permute-done.1, f32[2,2,96,2560]{3,2,1,0:T(8,128)} %copy-done.1, s32[]{:T(128)S(6)} %select_n.202), kind=kLoop, calls=%fused_computation.13 | loop fusion | flops 983040 | bytes 4915204 | tf_op jit(solution)/shard_map/add | solution.py:160
  175.7 0.0 copy-start.2
  175.7 1.3 copy-done.2
  176.9 0.1 fusion.26
  177.0 1.6 collective-permute-start.2
  178.6 11.8 %collective-permute-done.2 = bf16[96,2560]{1,0:T(8,128)(2,1)} collective-permute-done((bf16[96,2560]{1,0:T(8,128)(2,1)S(1)}, bf16[96,2560]{1,0:T(8,128)(2,1)}, u32[]{:S(2)}, u32[]{:S(2)}) %collective-permute-start.2) | collective-permute-done | bytes 491552 | tf_op jit(solution)/shard_map/ppermute | solution.py:165
  190.4 2.2 %fusion.16 = bf16[96,2560]{1,0:T(8,128)(2,1)} fusion(bf16[96,2560]{1,0:T(8,128)(2,1)} %collective-permute-done.2, f32[2,96,2560]{2,1,0:T(8,128)} %copy-done.2, s32[]{:T(128)S(6)} %select_n.205), kind=kLoop, calls=%fused_computation.25 | loop fusion | flops 737280 | bytes 1966084 | tf_op jit(solution)/shard_map/convert_element_type | solution.py:144
  (14 shorter events, 0.1 us)
Async XLA Ops:
  6.5 160.0 %copy-start = (bf16[512,2560]{1,0:T(8,128)(2,1)S(1)}, bf16[512,2560]{1,0:T(8,128)(2,1)}, u32[]{:S(2)}) copy-start(bf16[512,2560]{1,0:T(8,128)(2,1)} %param.9) | copy-start | bytes 7864324
  31.2 109.7 %all-to-all-start.1 = ((bf16[2,16,128,512]{3,2,0,1:T(8,128)(2,1)}), bf16[2,16,128,512]{3,2,0,1:T(8,128)(2,1)}, u32[]{:S(2)}, u32[]{:S(2)}) async-start(bf16[2,16,128,512]{3,2,0,1:T(8,128)(2,1)} %bitcast.62), calls=%async_computation.1 | async-start | bytes 8388608 | tf_op jit(solution)/shard_map/all_to_all | solution.py:129
  38.0 25.2 %all-gather.2.cloned.1.call-start = ((), (), s32[]{:S(2)}) async-start(), calls=%async_computation.2 | async-start | bytes 2457600 | tf_op jit(solution)/shard_map/all_gather | solution.py:75
  71.3 7.5 %copy-start.4 = (f32[4]{0:T(128)S(1)}, f32[4]{0:T(128)}, u32[]{:S(2)}) copy-start(f32[4]{0:T(128)} %param.10) | copy-start | bytes 52
  75.4 58.8 %collective-permute-start = (bf16[2,128,512]{1,2,0:T(8,128)(2,1)}, bf16[2,128,512]{1,2,0:T(8,128)(2,1)}, u32[]{:S(2)}, u32[]{:S(2)}) collective-permute-start(bf16[2,128,512]{1,2,0:T(8,128)(2,1)} %pad_maximum_fusion), channel_id=1, source_target_pairs={{0,4},{4,8},{8,12},{12,16},{16,20},{20,24},{24,28},{1,5},{5,9},{9,... | collective-permute-start | bytes 786440 | tf_op jit(solution)/shard_map/ppermute | solution.py:20
  135.4 1.7 copy-start.3
  167.7 1.9 copy-start.1
  170.7 2.9 %collective-permute-start.1 = (bf16[2,96,2560]{2,1,0:T(8,128)(2,1)}, bf16[2,96,2560]{2,1,0:T(8,128)(2,1)}, u32[]{:S(2)}, u32[]{:S(2)}) collective-permute-start(bf16[2,96,2560]{2,1,0:T(8,128)(2,1)} %fusion.15), channel_id=1, source_target_pairs={{0,1},{1,0},{2,3},{3,2},{4,5},{5,4},{6,7},{7,6},{8,9},{9,8},{10,11... | collective-permute-start | bytes 2949128 | tf_op jit(solution)/shard_map/ppermute | solution.py:157
  175.7 1.3 copy-start.2
  177.0 13.4 %collective-permute-start.2 = (bf16[96,2560]{1,0:T(8,128)(2,1)S(1)}, bf16[96,2560]{1,0:T(8,128)(2,1)}, u32[]{:S(2)}, u32[]{:S(2)}) collective-permute-start(bf16[96,2560]{1,0:T(8,128)(2,1)S(1)} %fusion.26), channel_id=1, source_target_pairs={{0,2},{1,3},{2,0},{3,1},{4,6},{5,7},{6,4},{7,5},{8,10},{9,11},{10,... | collective-permute-start | bytes 1474568 | tf_op jit(solution)/shard_map/ppermute | solution.py:165
Sparse Core Ops, SparseCore 0:
  40.4 22.7 all-gather.1

commit v4 on v3

--- a/solution.py
+++ b/solution.py
@@ -26,24 +26,24 @@
     return (weights / jnp.sum(weights, axis=-1, keepdims=True)).astype(jnp.bfloat16)
 
 
-def far_kernel(q_ref, k_ref, v_ref, allow_ref, o_ref):
-    pool = k_ref.shape[1]
-    keys = k_ref[0].reshape(pool * BLK, HD)
-    values = v_ref[0].reshape(pool * BLK, HD)
+def far_kernel(q_ref, k_ref, v_ref, bias_ref, o_ref):
+    pool = k_ref.shape[0]
+    keys = k_ref[:, 0].reshape(pool * BLK, HD)
+    values = v_ref[:, 0].reshape(pool * BLK, HD)
     scores = lax.dot_general(
         q_ref[...], keys, (((1,), (1,)), ((), ())), preferred_element_type=jnp.float32
-    ) * (HD ** (-0.5))
-    allowed = allow_ref[0] > 0
-    peak = jnp.max(jnp.where(allowed, scores, NEG_FILL), axis=-1, keepdims=True)
-    weights = jnp.where(allowed, jnp.exp(scores - peak), 0.0)
-    probs = (weights / jnp.sum(weights, axis=-1, keepdims=True)).astype(jnp.bfloat16)
+    ) * (HD ** (-0.5)) + bias_ref[0]
+    peak = jnp.max(scores, axis=-1, keepdims=True)
+    weights = jnp.exp(scores - peak)
+    scale = 1.0 / jnp.sum(weights, axis=-1, keepdims=True)
+    probs = (weights * scale).astype(jnp.bfloat16)
     o_ref[...] = jnp.dot(probs, values, preferred_element_type=jnp.float32)
 
 
-def far_attention(projected, fetched, allow):
+def far_attention(projected, fetched, bias):
     rows = projected.shape[0]
     blocks = rows // BLK
-    pool = fetched.shape[1]
+    pool = fetched.shape[0]
     groups = fetched.shape[3] // HD
     steps = groups * blocks
     return pl.pallas_call(
@@ -51,8 +51,8 @@
         grid=(groups, blocks),
         in_specs=[
             pl.BlockSpec((BLK, HD), lambda h, b: (b, h * 3)),
-            pl.BlockSpec((1, pool, BLK, HD), lambda h, b: (0, 0, 0, h)),
-            pl.BlockSpec((1, pool, BLK, HD), lambda h, b: (1, 0, 0, h)),
+            pl.BlockSpec((pool, 1, BLK, HD), lambda h, b: (0, 0, 0, h)),
+            pl.BlockSpec((pool, 1, BLK, HD), lambda h, b: (0, 1, 0, h)),
             pl.BlockSpec((1, 1, pool * BLK), lambda h, b: (b, 0, 0)),
         ],
         out_specs=pl.BlockSpec((BLK, HD), lambda h, b: (b, h)),
@@ -62,8 +62,20 @@
             transcendentals=steps * BLK * pool * BLK,
             bytes_accessed=fetched.size * 2 + rows * groups * HD * 6,
         ),
-    )(projected, fetched, fetched, allow)
+    )(projected, fetched, fetched, bias)
 
+
+def gather_tp(part):
+    count = lax.axis_size("tp")
+    me = lax.axis_index("tp")
+    arrived = [part] + [
+        lax.ppermute(part, "tp", [(t, (t + shift) % count) for t in range(count)])
+        for shift in range(1, count)
+    ]
+    order = (me - jnp.arange(count)) % count
+    return jnp.take(jnp.stack(arrived), order, axis=0, mode="clip").reshape(
+        count * part.shape[0], part.shape[1]
+    )
 
 def local(tokens, input_weight, output_weight, gate_logit, memory, retrieved, block_home):
     holder_count = lax.axis_size("mem")
@@ -72,7 +84,7 @@
     groups = output_weight.shape[0] // HD
     score_scale = HD ** (-0.5)
     projected = jnp.dot(
-        lax.all_gather(tokens, "tp", axis=0, tiled=True),
+        gather_tp(tokens),
         input_weight,
         preferred_element_type=jnp.float32,
     )
@@ -125,15 +137,17 @@
         ),
         axis=1,
         mode="clip",
-    )
-    fetched = lax.all_to_all(picked, "mem", split_axis=1, concat_axis=1, tiled=True)
+    ).transpose(1, 0, 2, 3)
+    fetched = lax.all_to_all(picked, "mem", split_axis=0, concat_axis=0, tiled=True)
     pool = holder_count * CAP
     row_of = entry_order // TOPB
     member = (
-        jnp.zeros((blocks_here, pool), jnp.float32).at[row_of, holder * CAP + slot_of].set(1.0)
+        jnp.zeros((blocks_here, pool), jnp.bool_).at[row_of, holder * CAP + slot_of].set(True)
     )
-    allow = jnp.repeat(member, BLK, axis=1).reshape(blocks_here, 1, pool * BLK)
-    far_out = far_attention(projected_flat, fetched, allow).reshape(local_rows, groups, HD)
+    bias = jnp.where(jnp.repeat(member, BLK, axis=1), 0.0, NEG_FILL).reshape(
+        blocks_here, 1, pool * BLK
+    )
+    far_out = far_attention(projected_flat, fetched, bias).reshape(local_rows, groups, HD)
     mixing = jax.nn.sigmoid(gate_logit)[None, :, None]
     attended = (
         (mixing * far_out + (1.0 - mixing) * near_out)

time: 200 us -> 182 us (0.910)
  between operations: 13.6 us -> 0.26 us
  waiting for transfers between devices: 89.5 us -> 80 us
  starting transfers between devices: 11.8 us -> 14.9 us
  other arithmetic: 11.5 us -> 14.4 us
    all_gather x1 -> x0, waiting for transfers between devices: 23.6 us -> none  [local(): lax.all_gather(tokens, 'tp', axis=0, tiled=True)]
    ppermute x0 -> x3, waiting for transfers between devices: none -> 16.3 us  [gather_tp(): lax.ppermute(part, 'tp', [(t, (t + shift) % count) for t in range(count)])]
    all_to_all x1 -> x0, local copies, waits for them, and re-layouts: 4.6 us -> none  [local(): lax.all_to_all(picked, 'mem', split_axis=1, concat_axis=1, tiled=True)]
    gather x0 -> x1, local copies, waits for them, and re-layouts: none -> 3.48 us  [gather_tp(): jnp.take(jnp.stack(arrived), order, axis=0, mode='clip')]
    ppermute x0 -> x3, starting transfers between devices: none -> 2.98 us  [gather_tp(): lax.ppermute(part, 'tp', [(t, (t + shift) % count) for t in range(count)])]
    another operation x0 -> x1, other arithmetic: none -> 2.91 us  [gather_tp(): jnp.stack(arrived)]
  transfers between devices with their start and end apart: 5 -> 7, of which waited for: 4 -> 6; matrix products, arithmetic and copies ran while one was open for 12% -> 17% of each run, Pallas kernels for 0% -> 0%
where the time goes in v4:
time: 182 us; the launch traced here: 181 us
  waiting for transfers between devices  80 us (44%)
  local copies, waits for them, and re-layouts  33.5 us (18%)
  starting transfers between devices  14.9 us (8%)
  other arithmetic  14.4 us (8%)
  matrix products  14.4 us (8%)
  Pallas kernels  13.7 us (8%)
  blocking collectives  10 us (5%)
    ppermute x1, waiting for transfers between devices, from_behind(): lax.ppermute(value, axis, [(source, source + steps) for source in range(i...  48.9 us
    ppermute x3, waiting for transfers between devices, gather_tp(): lax.ppermute(part, 'tp', [(t, (t + shift) % count) for t in range(count)])  16.3 us
    pallas_call x1, Pallas kernels, far_attention(): pl.pallas_call(far_kernel, grid=(groups, blocks), in_specs=[pl.BlockSpec(...  13.7 us
    ppermute x1, waiting for transfers between devices, reduce_over_tp(): lax.ppermute(outgoing.astype(jnp.bfloat16), 'tp', pairs).astype(jnp.float32)  11.8 us
    all_to_all x1, blocking collectives, local(): lax.all_to_all(wanted_ids, 'mem', split_axis=0, concat_axis=0, tiled=True)  10 us
    dot_general x1, matrix products, local(): jnp.dot(gather_tp(tokens), input_weight, preferred_element_type=jnp.float32)  8.13 us
    all_to_all x1, starting transfers between devices, local(): lax.all_to_all(picked, 'mem', split_axis=0, concat_axis=0, tiled=True)  6.94 us
    gather x1, local copies, waits for them, and re-layouts, local(): jnp.take(local_store, lax.all_to_all(wanted_ids, 'mem', split_axis=0, con...  6.17 us
  transfers between devices with their start and end apart: 7, of which 6 were waited for; matrix products, arithmetic and copies ran while one was open for 17% of the time, Pallas kernels for 0%

profile of v4, /device:TPU:16, one launch (start us, length us, event | category | flops | bytes accessed | tf_op | source)
XLA Modules:
  0.0 181.1 jit_solution(7109667137641472606)
XLA Ops:
  0.0 0.0 copy-start
  0.0 0.9 reshape.415
  0.9 0.8 reshape.416
  1.7 1.5 gather_fusion.1
  3.2 0.7 compare_reduce_fusion
  3.9 0.2 convert_reduce_fusion.1
  4.1 0.2 convert_reduce_fusion
  4.3 2.8 %scatter_fusion = s32[8,2]{0,1:T(2,128)S(1)} fusion(s32[8,2]{0,1:T(2,128)S(1)} %broadcast.498, s32[48]{0:T(128)S(1)} %fusion.34, s32[48]{0:T(128)S(1)} %get-tuple-element.11), kind=kCustom, calls=%fused_computation.3 | custom fusion | bytes 960 | tf_op jit(solution)/shard_map/scatter | solution.py:131
  7.1 0.1 copy.32
  7.2 10.0 %all_to_all.14 = s32[8,1,2]{2,1,0:T(1,128)S(1)} all-to-all(s32[8,1,2]{2,1,0:T(1,128)S(1)} %copy.32), channel_id=1, replica_groups=mesh['mem'=8,'tp'=4] {'mem'}, dimensions={0} | all-to-all | bytes 128 | tf_op jit(solution)/shard_map/all_to_all | solution.py:135
  17.2 0.5 broadcast.561
  17.7 0.7 reduce.22
  18.4 0.1 reshape.437
  18.5 6.2 %gather_fusion.2 = bf16[16,2,128,512]{3,2,1,0:T(8,128)(2,1)} fusion(bf16[2,32,128,512]{3,2,1,0:T(8,128)(2,1)} %bitcast.71, s32[1024]{0:T(1024)S(1)} %pad_clamp_fusion), kind=kCustom, calls=%fused_computation.2 | custom fusion | bytes 8388672 | tf_op jit(solution)/shard_map/jit(_take)/gather | solution.py:133
  24.6 0.0 copy-start.3
  24.6 6.9 %all-to-all-start.1 = ((bf16[16,2,128,512]{3,2,1,0:T(8,128)(2,1)}), bf16[16,2,128,512]{3,2,1,0:T(8,128)(2,1)}, u32[]{:S(2)}, u32[]{:S(2)}) async-start(bf16[16,2,128,512]{3,2,1,0:T(8,128)(2,1)} %gather_fusion.2), calls=%async_computation.1 | async-start | bytes 8388608 | tf_op jit(solution)/shard_map/all_to_all | solution.py:141
  31.6 0.0 copy-done.3
  31.6 0.0 collective-permute-start
  31.6 1.6 collective-permute-start.1
  33.2 1.4 collective-permute-start.2
  34.6 2.8 %scatter_fusion.1 = pred[3,16]{1,0:T(4,128)(4,1)S(1)} fusion(pred[3,16]{1,0:T(4,128)(4,1)S(1)} %broadcast_in_dim.69, s32[48]{0:T(128)S(1)} %get-tuple-element.9, pred[48]{0:T(512)(128)(4,1)S(1)} %broadcast.534), kind=kCustom, calls=%fused_computation.4 | custom fusion | bytes 528 | tf_op jit(solution)/shard_map/scatter | solution.py:145
  37.5 0.9 fusion.18
  38.4 6.2 %collective-permute-done = bf16[96,2560]{1,0:T(8,128)(2,1)} collective-permute-done((bf16[96,2560]{1,0:T(8,128)(2,1)S(1)}, bf16[96,2560]{1,0:T(8,128)(2,1)}, u32[]{:S(2)}, u32[]{:S(2)}) %collective-permute-start) | collective-permute-done | bytes 491552 | tf_op jit(solution)/shard_map/ppermute | solution.py:72
  44.6 1.2 collective-permute-done.1
  45.8 8.9 %collective-permute-done.2 = bf16[96,2560]{1,0:T(8,128)(2,1)} collective-permute-done((bf16[96,2560]{1,0:T(8,128)(2,1)S(1)}, bf16[96,2560]{1,0:T(8,128)(2,1)}, u32[]{:S(2)}, u32[]{:S(2)}) %collective-permute-start.2) | collective-permute-done | bytes 491552 | tf_op jit(solution)/shard_map/ppermute | solution.py:72
  54.7 2.9 %pad_maximum_fusion = bf16[4,96,2560]{2,1,0:T(8,128)(2,1)} fusion(bf16[1,96,2560]{2,1,0:T(8,128)(2,1)} %bitcast.3, bf16[1,96,2560]{2,1,0:T(8,128)(2,1)} %bitcast.2, bf16[1,96,2560]{2,1,0:T(8,128)(2,1)} %bitcast.1, bf16[1,96,2560]{2,1,0:T(8,128)(2,1)S(1)} %bitcast.78), kind=kLoop, calls=%fused_computation.14 | loop fusion | flops 2949120 | bytes 3932160 | tf_op jit(solution)/shard_map/stack | solution.py:76
  57.6 3.5 %gather_fusion = bf16[4,96,2560]{2,1,0:T(8,128)(2,1)} fusion(bf16[4,96,2560]{2,1,0:T(8,128)(2,1)} %pad_maximum_fusion, s32[1024]{0:T(1024)S(1)} %pad_clamp_fusion.2), kind=kCustom, calls=%fused_computation | custom fusion | bytes 3932176 | tf_op jit(solution)/shard_map/jit(_take)/gather | solution.py:76
  61.1 8.1 %convolution_convert_fusion.q_ref = bf16[384,1536]{1,0:T(8,128)(2,1)} fusion(bf16[384,2560]{1,0:T(8,128)(2,1)} %bitcast.72, bf16[2560,1536]{1,0:T(8,128)(2,1)} %param.8), kind=kOutput, calls=%fused_computation.10 | convolution fusion | flops 3020488704 | bytes 11010048 | tf_op jit(solution)/shard_map/dot_general | solution.py:86
  69.2 0.0 copy-start.5
  69.2 2.4 %copy.34 = bf16[384,1536]{0,1:T(8,128)(2,1)} copy(bf16[384,1536]{1,0:T(8,128)(2,1)} %convolution_convert_fusion.q_ref) | data formatting | bytes 2359296 | tf_op jit(solution)/shard_map/convert_element_type | solution.py:91
  71.6 1.0 fusion.40
  72.6 0.7 pad_maximum_fusion.1
  73.3 3.4 %collective-permute-start.3 = (bf16[2,128,512]{1,2,0:T(8,128)(2,1)}, bf16[2,128,512]{1,2,0:T(8,128)(2,1)}, u32[]{:S(2)}, u32[]{:S(2)}) collective-permute-start(bf16[2,128,512]{1,2,0:T(8,128)(2,1)} %pad_maximum_fusion.1), channel_id=1, source_target_pairs={{0,4},{4,8},{8,12},{12,16},{16,20},{20,24},{24,28},{1,5},{5,9},{9,... | collective-permute-start | bytes 786440 | tf_op jit(solution)/shard_map/ppermute | solution.py:20
  76.7 0.0 copy-done.5
  76.7 2.0 %slice_bitcast_fusion.2 = (bf16[384,4,128]{0,2,1:T(8,128)(2,1)}, bf16[384,4,1,128]{0,3,2,1:T(8,128)(2,1)S(1)}) fusion(bf16[384,4,3,128]{0,3,2,1:T(8,128)(2,1)} %bitcast.69), kind=kLoop, calls=%fused_computation.42 | loop fusion | bytes 1572864 | tf_op jit(solution)/shard_map/squeeze | solution.py:95
  78.7 0.2 copy.44
  78.9 48.9 %collective-permute-done.3 = bf16[2,128,512]{1,2,0:T(8,128)(2,1)} collective-permute-done((bf16[2,128,512]{1,2,0:T(8,128)(2,1)}, bf16[2,128,512]{1,2,0:T(8,128)(2,1)}, u32[]{:S(2)}, u32[]{:S(2)}) %collective-permute-start.3) | collective-permute-done | bytes 262176 | tf_op jit(solution)/shard_map/ppermute | solution.py:20
  127.8 1.0 fusion.41
  128.8 0.1 copy.38
  129.0 0.0 copy-start.4
  129.0 1.7 fusion.22
  130.6 0.0 copy-done.4
  130.7 3.8 %fusion.42 = (f32[4,384]{1,0:T(4,128)}, f32[4,384,512]{2,1,0:T(8,128)}) fusion(f32[4,384,512]{2,1,0:T(8,128)S(1)} %fusion.22, pred[384,512]{1,0:T(8,128)(4,1)S(1)} %copy-done.4), kind=kOutput, calls=%fused_computation.105 | output fusion | flops 4719103 | bytes 6494208 | tf_op jit(solution)/shard_map/sub | solution.py:25
  134.5 0.0 all-to-all-done.1.k_ref.v_ref
  134.5 0.7 broadcast_in_dim.73
  135.1 13.7 %shard_map.73 = f32[384,512]{1,0:T(8,128)} custom-call(bf16[384,1536]{1,0:T(8,128)(2,1)} %convolution_convert_fusion.q_ref, bf16[16,2,128,512]{3,2,1,0:T(8,128)(2,1)} %all-to-all-done.1.k_ref.v_ref, bf16[16,2,128,512]{3,2,1,0:T(8,128)(2,1)} %all-to-all-done.1.k_ref.v_ref, f32[3,1,2048]{2,1,0:T(1,128)} %bitcast.80), custom_call_target="tpu_custom_call" | custom-call | flops 1610612736 | bytes 5373952 | tf_op jit(solution)/shard_map/pallas_call | solution.py:49
  148.8 1.4 copy.41
  150.2 3.4 %fusion.14 = bf16[384,4,128]{0,2,1:T(8,128)(2,1)} fusion(f32[4,384,512]{2,1,0:T(8,128)} %get-tuple-element.20, f32[4,384]{1,0:T(4,128)} %get-tuple-element.19, f32[384,4,128]{0,2,1:T(8,128)S(1)} %bitcast.74, bf16[384,4,128]{0,2,1:T(8,128)(2,1)} %get-tuple-element.13, bf16[128,4,128]{0,2,1:T(8,128)(2,1)S(1)} %bitcast.79, f32[4]{0:T(128)S(1)} %get-tuple-element.7, ...), kind=kOutput, calls=%fused_computation.24 | convolution fusion | flops 204734464 | bytes 4855840 | tf_op jit(solution)/shard_map/gqk,kgd->qgd/dot_general | solution.py:111
  153.6 1.2 copy.39
  154.9 0.2 dot_general.17
  155.0 0.0 copy-done
  155.0 1.2 fusion.3
  156.2 0.0 copy-start.1
  156.2 1.9 %copy-done.1 = f32[2,2,96,2560]{3,2,1,0:T(8,128)} copy-done((f32[2,2,96,2560]{3,2,1,0:T(8,128)}, f32[2,2,96,2560]{3,2,1,0:T(8,128)S(1)}, u32[]{:S(2)}) %copy-start.1) | copy-done | bytes 3932184
  158.1 1.1 fusion.15
  159.2 0.0 collective-permute-start.4
  159.2 2.9 %collective-permute-done.4 = bf16[2,96,2560]{2,1,0:T(8,128)(2,1)} collective-permute-done((bf16[2,96,2560]{2,1,0:T(8,128)(2,1)}, bf16[2,96,2560]{2,1,0:T(8,128)(2,1)}, u32[]{:S(2)}, u32[]{:S(2)}) %collective-permute-start.4) | collective-permute-done | bytes 983072 | tf_op jit(solution)/shard_map/ppermute | solution.py:171
  162.1 2.0 %bitcast_add_fusion = f32[2,96,2560]{2,1,0:T(8,128)S(1)} fusion(bf16[2,96,2560]{2,1,0:T(8,128)(2,1)} %collective-permute-done.4, f32[2,2,96,2560]{3,2,1,0:T(8,128)} %copy-done.1, s32[]{:T(128)S(6)} %select_n.233), kind=kLoop, calls=%fused_computation.15 | loop fusion | flops 983040 | bytes 4915204 | tf_op jit(solution)/shard_map/add | solution.py:174
  164.1 0.0 copy-start.2
  164.1 1.3 copy-done.2
  165.4 0.1 fusion.26
  165.5 1.6 collective-permute-start.5
  167.0 11.8 %collective-permute-done.5 = bf16[96,2560]{1,0:T(8,128)(2,1)} collective-permute-done((bf16[96,2560]{1,0:T(8,128)(2,1)S(1)}, bf16[96,2560]{1,0:T(8,128)(2,1)}, u32[]{:S(2)}, u32[]{:S(2)}) %collective-permute-start.5) | collective-permute-done | bytes 491552 | tf_op jit(solution)/shard_map/ppermute | solution.py:179
  178.9 2.2 %fusion.16 = bf16[96,2560]{1,0:T(8,128)(2,1)} fusion(bf16[96,2560]{1,0:T(8,128)(2,1)} %collective-permute-done.5, f32[2,96,2560]{2,1,0:T(8,128)} %copy-done.2, s32[]{:T(128)S(6)} %select_n.236), kind=kLoop, calls=%fused_computation.27 | loop fusion | flops 737280 | bytes 1966084 | tf_op jit(solution)/shard_map/convert_element_type | solution.py:158
  (17 shorter events, 0.1 us)
Async XLA Ops:
  0.0 155.0 %copy-start = (bf16[512,2560]{1,0:T(8,128)(2,1)S(1)}, bf16[512,2560]{1,0:T(8,128)(2,1)}, u32[]{:S(2)}) copy-start(bf16[512,2560]{1,0:T(8,128)(2,1)} %param.9) | copy-start | bytes 7864324
  24.6 6.9 %copy-start.3 = (bf16[96,2560]{1,0:T(8,128)(2,1)S(1)}, bf16[96,2560]{1,0:T(8,128)(2,1)}, u32[]{:S(2)}) copy-start(bf16[96,2560]{1,0:T(8,128)(2,1)} %param.7) | copy-start | bytes 1474564
  24.6 109.8 %all-to-all-start.1 = ((bf16[16,2,128,512]{3,2,1,0:T(8,128)(2,1)}), bf16[16,2,128,512]{3,2,1,0:T(8,128)(2,1)}, u32[]{:S(2)}, u32[]{:S(2)}) async-start(bf16[16,2,128,512]{3,2,1,0:T(8,128)(2,1)} %gather_fusion.2), calls=%async_computation.1 | async-start | bytes 8388608 | tf_op jit(solution)/shard_map/all_to_all | solution.py:141
  31.6 13.0 %collective-permute-start = (bf16[96,2560]{1,0:T(8,128)(2,1)S(1)}, bf16[96,2560]{1,0:T(8,128)(2,1)}, u32[]{:S(2)}, u32[]{:S(2)}) collective-permute-start(bf16[96,2560]{1,0:T(8,128)(2,1)S(1)} %copy-done.3), channel_id=1, source_target_pairs={{0,1},{1,2},{2,3},{3,0},{4,5},{5,6},{6,7},{7,4},{8,9},{9,10},{10,1... | collective-permute-start | bytes 1474568 | tf_op jit(solution)/shard_map/ppermute | solution.py:72
  31.6 14.2 %collective-permute-start.1 = (bf16[96,2560]{1,0:T(8,128)(2,1)S(1)}, bf16[96,2560]{1,0:T(8,128)(2,1)}, u32[]{:S(2)}, u32[]{:S(2)}) collective-permute-start(bf16[96,2560]{1,0:T(8,128)(2,1)S(1)} %copy-done.3), channel_id=1, source_target_pairs={{0,2},{1,3},{2,0},{3,1},{4,6},{5,7},{6,4},{7,5},{8,10},{9,11},{10,... | collective-permute-start | bytes 1474568 | tf_op jit(solution)/shard_map/ppermute | solution.py:72
  33.2 21.5 %collective-permute-start.2 = (bf16[96,2560]{1,0:T(8,128)(2,1)S(1)}, bf16[96,2560]{1,0:T(8,128)(2,1)}, u32[]{:S(2)}, u32[]{:S(2)}) collective-permute-start(bf16[96,2560]{1,0:T(8,128)(2,1)S(1)} %copy-done.3), channel_id=1, source_target_pairs={{0,3},{1,0},{2,1},{3,2},{4,7},{5,4},{6,5},{7,6},{8,11},{9,8},{10,9... | collective-permute-start | bytes 1474568 | tf_op jit(solution)/shard_map/ppermute | solution.py:72
  69.2 7.5 %copy-start.5 = (f32[4]{0:T(128)S(1)}, f32[4]{0:T(128)}, u32[]{:S(2)}) copy-start(f32[4]{0:T(128)} %param.10) | copy-start | bytes 52
  73.3 54.5 %collective-permute-start.3 = (bf16[2,128,512]{1,2,0:T(8,128)(2,1)}, bf16[2,128,512]{1,2,0:T(8,128)(2,1)}, u32[]{:S(2)}, u32[]{:S(2)}) collective-permute-start(bf16[2,128,512]{1,2,0:T(8,128)(2,1)} %pad_maximum_fusion.1), channel_id=1, source_target_pairs={{0,4},{4,8},{8,12},{12,16},{16,20},{20,24},{24,28},{1,5},{5,9},{9,... | collective-permute-start | bytes 786440 | tf_op jit(solution)/shard_map/ppermute | solution.py:20
  129.0 1.7 copy-start.4
  156.2 1.9 %copy-start.1 = (f32[2,2,96,2560]{3,2,1,0:T(8,128)}, f32[2,2,96,2560]{3,2,1,0:T(8,128)S(1)}, u32[]{:S(2)}) copy-start(f32[2,2,96,2560]{3,2,1,0:T(8,128)S(1)} %fusion.3) | copy-start | bytes 11796484
  159.2 2.9 %collective-permute-start.4 = (bf16[2,96,2560]{2,1,0:T(8,128)(2,1)}, bf16[2,96,2560]{2,1,0:T(8,128)(2,1)}, u32[]{:S(2)}, u32[]{:S(2)}) collective-permute-start(bf16[2,96,2560]{2,1,0:T(8,128)(2,1)} %fusion.15), channel_id=1, source_target_pairs={{0,1},{1,0},{2,3},{3,2},{4,5},{5,4},{6,7},{7,6},{8,9},{9,8},{10,11... | collective-permute-start | bytes 2949128 | tf_op jit(solution)/shard_map/ppermute | solution.py:171
  164.1 1.3 copy-start.2
  165.5 13.4 %collective-permute-start.5 = (bf16[96,2560]{1,0:T(8,128)(2,1)S(1)}, bf16[96,2560]{1,0:T(8,128)(2,1)}, u32[]{:S(2)}, u32[]{:S(2)}) collective-permute-start(bf16[96,2560]{1,0:T(8,128)(2,1)S(1)} %fusion.26), channel_id=1, source_target_pairs={{0,2},{1,3},{2,0},{3,1},{4,6},{5,7},{6,4},{7,5},{8,10},{9,11},{10,... | collective-permute-start | bytes 1474568 | tf_op jit(solution)/shard_map/ppermute | solution.py:179

commit v5 on v4

--- a/solution.py
+++ b/solution.py
@@ -24,6 +24,26 @@
     row_peak = jnp.max(jnp.where(allowed, scores, NEG_FILL), axis=-1, keepdims=True)
     weights = jnp.where(allowed, jnp.exp(scores - row_peak), 0.0)
     return (weights / jnp.sum(weights, axis=-1, keepdims=True)).astype(jnp.bfloat16)
+
+
+def near_part(block_queries, window_keys, window_values, first_key):
+    scores = (
+        jnp.einsum(
+            "nqgd,nkgd->ngqk", block_queries, window_keys, preferred_element_type=jnp.float32
+        )
+        * (HD ** (-0.5))
+    )
+    query_index = lax.broadcasted_iota(jnp.int32, (BLK, 2 * BLK), 0)
+    key_index = lax.broadcasted_iota(jnp.int32, (BLK, 2 * BLK), 1)
+    allowed = (
+        (key_index > query_index)[None]
+        & (key_index <= query_index + BLK)[None]
+        & (key_index[None] + first_key[:, None, None] >= 0)
+    )
+    probs = softmax_rows(scores, allowed[:, None])
+    return jnp.einsum(
+        "ngqk,nkgd->nqgd", probs, window_values, preferred_element_type=jnp.float32
+    )
 
 
 def far_kernel(q_ref, k_ref, v_ref, bias_ref, o_ref):
@@ -95,22 +115,24 @@
     value_rows = projected[:, :, 2]
     last_rows = jnp.stack([key_rows[-BLK:], value_rows[-BLK:]]).reshape(2, BLK, groups * HD)
     before = from_behind(last_rows, "mem", 1).reshape(2, BLK, groups, HD)
-    near_keys = jnp.concatenate([before[0], key_rows], axis=0)
-    near_values = jnp.concatenate([before[1], value_rows], axis=0)
-    near_scores = (
-        jnp.einsum("qgd,kgd->gqk", queries, near_keys, preferred_element_type=jnp.float32)
-        * score_scale
-    )
-    query_index = lax.broadcasted_iota(jnp.int32, (local_rows, local_rows + BLK), 0)
-    key_index = lax.broadcasted_iota(jnp.int32, (local_rows, local_rows + BLK), 1)
-    first_key = lax.axis_index("mem") * local_rows - BLK
-    allowed = (
-        (key_index > query_index) & (key_index <= query_index + BLK) & (key_index + first_key >= 0)
-    )
-    near_probs = softmax_rows(near_scores, allowed[None])
-    near_out = jnp.einsum(
-        "gqk,kgd->qgd", near_probs, near_values, preferred_element_type=jnp.float32
-    )
+    blocks_here = local_rows // BLK
+    query_blocks = queries.reshape(blocks_here, BLK, groups, HD)
+    key_blocks = key_rows.reshape(blocks_here, BLK, groups, HD)
+    value_blocks = value_rows.reshape(blocks_here, BLK, groups, HD)
+    first_row = lax.axis_index("mem") * local_rows + jnp.arange(blocks_here) * BLK
+    later = near_part(
+        query_blocks[1:],
+        jnp.concatenate([key_blocks[:-1], key_blocks[1:]], axis=1),
+        jnp.concatenate([value_blocks[:-1], value_blocks[1:]], axis=1),
+        first_row[1:] - BLK,
+    )
+    opening = near_part(
+        query_blocks[:1],
+        jnp.concatenate([before[0][None], key_blocks[:1]], axis=1),
+        jnp.concatenate([before[1][None], value_blocks[:1]], axis=1),
+        first_row[:1] - BLK,
+    )
+    near_out = jnp.concatenate([opening, later], axis=0).reshape(local_rows, groups, HD)
     blocks_here = retrieved.shape[0]
     entries = blocks_here * TOPB
     local_blocks = memory.shape[1] // BLK

time: 182 us -> 175 us (0.962)
  waiting for transfers between devices: 80 us -> 66.7 us
  local copies, waits for them, and re-layouts: 33.5 us -> 38.5 us
  matrix products: 14.4 us -> 16.8 us
    ppermute x1, waiting for transfers between devices: 48.9 us -> 35.8 us  [from_behind(): lax.ppermute(value, axis, [(source, source + steps) for source in range(i...]
    slice x2 -> x11, local copies, waits for them, and re-layouts: 1.97 us -> 9.78 us  [the longest x2 2.73 us: local(): query_blocks[1:]]
    sub x1 -> x2, other arithmetic: 3.82 us -> 0.67 us  [softmax_rows(): weights = jnp.where(allowed, jnp.exp(scores - row_peak), 0.0)]
    dot_general x2 -> x4, matrix products: 5.06 us -> 7.44 us  [the longest x2 4.77 us: near_part(): jnp.einsum('ngqk,nkgd->nqgd', probs, window_values, preferred_element_typ...]
    squeeze x2 -> x0, local copies, waits for them, and re-layouts: 2.08 us -> none  [the longest x1 1.95 us: local(): value_rows = projected[:, :, 2]]
    unnamed x13 -> x27, local copies, waits for them, and re-layouts: 3.39 us -> 4.29 us
  transfers between devices with their start and end apart: 7 -> 7, of which waited for: 6 -> 6; matrix products, arithmetic and copies ran while one was open for 17% -> 23% of each run, Pallas kernels for 0% -> 0%
where the time goes in v5:
time: 175 us; the launch traced here: 174 us
  waiting for transfers between devices  66.7 us (38%)
  local copies, waits for them, and re-layouts  38.5 us (22%)
  matrix products  16.8 us (10%)
  starting transfers between devices  15.1 us (9%)
  Pallas kernels  13.8 us (8%)
  other arithmetic  12.7 us (7%)
  blocking collectives  10 us (6%)
    ppermute x1, waiting for transfers between devices, from_behind(): lax.ppermute(value, axis, [(source, source + steps) for source in range(i...  35.8 us
    ppermute x3, waiting for transfers between devices, gather_tp(): lax.ppermute(part, 'tp', [(t, (t + shift) % count) for t in range(count)])  16.2 us
    pallas_call x1, Pallas kernels, far_attention(): pl.pallas_call(far_kernel, grid=(groups, blocks), in_specs=[pl.BlockSpec(...  13.8 us
    ppermute x1, waiting for transfers between devices, reduce_over_tp(): lax.ppermute(outgoing.astype(jnp.bfloat16), 'tp', pairs).astype(jnp.float32)  11.8 us
    all_to_all x1, blocking collectives, local(): lax.all_to_all(wanted_ids, 'mem', split_axis=0, concat_axis=0, tiled=True)  10 us
    dot_general x1, matrix products, local(): jnp.dot(gather_tp(tokens), input_weight, preferred_element_type=jnp.float32)  8.14 us
    all_to_all x1, starting transfers between devices, local(): lax.all_to_all(picked, 'mem', split_axis=0, concat_axis=0, tiled=True)  6.94 us
    gather x1, local copies, waits for them, and re-layouts, local(): jnp.take(local_store, lax.all_to_all(wanted_ids, 'mem', split_axis=0, con...  6.17 us
  transfers between devices with their start and end apart: 7, of which 6 were waited for; matrix products, arithmetic and copies ran while one was open for 23% of the time, Pallas kernels for 0%

profile of v5, /device:TPU:16, one launch (start us, length us, event | category | flops | bytes accessed | tf_op | source)
XLA Modules:
  0.0 173.9 jit_solution(12094930025196116463)
XLA Ops:
  0.0 0.9 reshape.479
  0.9 0.8 reshape.480
  1.7 1.5 gather_fusion.1
  3.2 0.7 compare_reduce_fusion
  3.9 0.2 convert_reduce_fusion.1
  4.1 0.2 convert_reduce_fusion
  4.3 2.8 %scatter_fusion = s32[8,2]{0,1:T(2,128)S(1)} fusion(s32[8,2]{0,1:T(2,128)S(1)} %broadcast.537, s32[48]{0:T(128)S(1)} %fusion.51, s32[48]{0:T(128)S(1)} %get-tuple-element.11), kind=kCustom, calls=%fused_computation.3 | custom fusion | bytes 960 | tf_op jit(solution)/shard_map/scatter | solution.py:153
  7.1 0.1 copy.49
  7.2 10.0 %all_to_all.14 = s32[8,1,2]{2,1,0:T(1,128)S(1)} all-to-all(s32[8,1,2]{2,1,0:T(1,128)S(1)} %copy.49), channel_id=1, replica_groups=mesh['mem'=8,'tp'=4] {'mem'}, dimensions={0} | all-to-all | bytes 128 | tf_op jit(solution)/shard_map/all_to_all | solution.py:157
  17.2 0.5 broadcast.606
  17.7 0.7 reduce.26
  18.4 0.1 reshape.504
  18.5 6.2 %gather_fusion.2 = bf16[16,2,128,512]{3,2,1,0:T(8,128)(2,1)} fusion(bf16[2,32,128,512]{3,2,1,0:T(8,128)(2,1)} %bitcast.97, s32[1024]{0:T(1024)S(1)} %pad_clamp_fusion), kind=kCustom, calls=%fused_computation.2 | custom fusion | bytes 8388672 | tf_op jit(solution)/shard_map/jit(_take)/gather | solution.py:155
  24.6 6.9 %all-to-all-start.1 = ((bf16[16,2,128,512]{3,2,1,0:T(8,128)(2,1)}), bf16[16,2,128,512]{3,2,1,0:T(8,128)(2,1)}, u32[]{:S(2)}, u32[]{:S(2)}) async-start(bf16[16,2,128,512]{3,2,1,0:T(8,128)(2,1)} %gather_fusion.2), calls=%async_computation.1 | async-start | bytes 8388608 | tf_op jit(solution)/shard_map/all_to_all | solution.py:163
  31.6 1.6 collective-permute-start.1
  33.2 1.4 collective-permute-start.2
  34.6 2.8 %scatter_fusion.1 = pred[3,16]{1,0:T(4,128)(4,1)S(1)} fusion(pred[3,16]{1,0:T(4,128)(4,1)S(1)} %broadcast_in_dim.98, s32[48]{0:T(128)S(1)} %get-tuple-element.9, pred[48]{0:T(512)(128)(4,1)S(1)} %broadcast.576), kind=kCustom, calls=%fused_computation.4 | custom fusion | bytes 528 | tf_op jit(solution)/shard_map/scatter | solution.py:167
  37.4 0.1 slice_add_fusion
  37.5 0.1 broadcast_bitcast_fusion
  37.7 0.7 fusion.37
  38.4 0.1 fusion.35
  38.5 6.1 %collective-permute-done = bf16[96,2560]{1,0:T(8,128)(2,1)} collective-permute-done((bf16[96,2560]{1,0:T(8,128)(2,1)S(1)}, bf16[96,2560]{1,0:T(8,128)(2,1)}, u32[]{:S(2)}, u32[]{:S(2)}) %collective-permute-start) | collective-permute-done | bytes 491552 | tf_op jit(solution)/shard_map/ppermute | solution.py:92
  44.6 1.2 collective-permute-done.1
  45.8 8.9 %collective-permute-done.2 = bf16[96,2560]{1,0:T(8,128)(2,1)} collective-permute-done((bf16[96,2560]{1,0:T(8,128)(2,1)S(1)}, bf16[96,2560]{1,0:T(8,128)(2,1)}, u32[]{:S(2)}, u32[]{:S(2)}) %collective-permute-start.2) | collective-permute-done | bytes 491552 | tf_op jit(solution)/shard_map/ppermute | solution.py:92
  54.7 2.9 %pad_maximum_fusion = bf16[4,96,2560]{2,1,0:T(8,128)(2,1)} fusion(bf16[1,96,2560]{2,1,0:T(8,128)(2,1)} %bitcast.4, bf16[1,96,2560]{2,1,0:T(8,128)(2,1)} %bitcast.3, bf16[1,96,2560]{2,1,0:T(8,128)(2,1)} %bitcast.2, bf16[1,96,2560]{2,1,0:T(8,128)(2,1)S(1)} %bitcast.109), kind=kLoop, calls=%fused_computation.10 | loop fusion | flops 2949120 | bytes 3932160 | tf_op jit(solution)/shard_map/stack | solution.py:96
  57.6 3.5 %gather_fusion = bf16[4,96,2560]{2,1,0:T(8,128)(2,1)} fusion(bf16[4,96,2560]{2,1,0:T(8,128)(2,1)} %pad_maximum_fusion, s32[1024]{0:T(1024)S(1)} %pad_clamp_fusion.2), kind=kCustom, calls=%fused_computation | custom fusion | bytes 3932176 | tf_op jit(solution)/shard_map/jit(_take)/gather | solution.py:96
  61.1 8.1 %convolution_convert_fusion.q_ref = bf16[384,1536]{1,0:T(8,128)(2,1)} fusion(bf16[384,2560]{1,0:T(8,128)(2,1)} %bitcast.98, bf16[2560,1536]{1,0:T(8,128)(2,1)} %param.8), kind=kOutput, calls=%fused_computation.7 | convolution fusion | flops 3020488704 | bytes 11010048 | tf_op jit(solution)/shard_map/dot_general | solution.py:106
  69.2 2.4 %copy.50 = bf16[384,1536]{0,1:T(8,128)(2,1)} copy(bf16[384,1536]{1,0:T(8,128)(2,1)} %convolution_convert_fusion.q_ref) | data formatting | bytes 2359296 | tf_op jit(solution)/shard_map/convert_element_type | solution.py:111
  71.6 1.9 %slice_bitcast_fusion.2 = (bf16[1,128,4,128]{1,3,2,0:T(8,128)(2,1)}, bf16[128,4,1,128]{0,3,2,1:T(8,128)(2,1)}, bf16[128,4,1,128]{0,3,2,1:T(8,128)(2,1)S(1)}, bf16[128,4,1,128]{0,3,2,1:T(8,128)(2,1)S(1)}) fusion(bf16[384,4,3,128]{0,3,2,1:T(8,128)(2,1)} %bitcast.93), kind=kLoop, calls=%fused_computation.62 | loop fusion | bytes 1048576 | tf_op jit(solution)/shard_map/slice | solution.py:132
  73.5 0.7 pad_maximum_fusion.3
  74.3 3.5 %collective-permute-start.3 = (bf16[2,128,512]{1,2,0:T(8,128)(2,1)}, bf16[2,128,512]{1,2,0:T(8,128)(2,1)}, u32[]{:S(2)}, u32[]{:S(2)}) collective-permute-start(bf16[2,128,512]{1,2,0:T(8,128)(2,1)} %pad_maximum_fusion.3), channel_id=1, source_target_pairs={{0,4},{4,8},{8,12},{12,16},{16,20},{20,24},{24,28},{1,5},{5,9},{9,... | collective-permute-start | bytes 786440 | tf_op jit(solution)/shard_map/ppermute | solution.py:20
  77.8 0.9 fusion.61
  78.8 1.8 %copy.59 = bf16[256,4,1,128]{3,0,1,2:T(8,128)(2,1)} copy(bf16[256,4,1,128]{0,3,2,1:T(8,128)(2,1)} %get-tuple-element.17) | data formatting | bytes 524288 | tf_op jit(solution)/shard_map/slice | solution.py:124
  80.6 1.8 %copy.60 = bf16[256,4,1,128]{3,0,1,2:T(8,128)(2,1)} copy(bf16[256,4,1,128]{0,3,2,1:T(8,128)(2,1)} %get-tuple-element.18) | data formatting | bytes 524288 | tf_op jit(solution)/shard_map/slice | solution.py:125
  82.3 0.8 copy.61
  83.2 1.4 convolution_multiply_fusion
  84.6 1.0 copy-done.5
  85.6 0.4 fusion.63
  86.0 0.1 copy.70
  86.2 0.2 copy.55
  86.4 0.9 copy.57
  87.2 0.2 copy.56
  87.4 0.2 copy.58
  87.6 4.5 %convolution_bitcast_fusion = f32[2,128,4,128]{1,3,2,0:T(8,128)} fusion(bf16[2,128,4,128]{1,3,2,0:T(8,128)(2,1)S(1)} %copy.58, bf16[2,128,4,128]{1,3,2,0:T(8,128)(2,1)} %copy.57, f32[2,4,128]{2,1,0:T(4,128)S(1)} %fusion.63, f32[2,4,128,256]{3,2,1,0:T(8,128)} %copy-done.5, pred[2,128,256]{2,1,0:T(8,128)(4,1)} %copy-done.11), kind=kOutput, calls=%fused_computation.22 | convolution fusion | flops 69469440 | bytes 2166784 | tf_op jit(solution)/shard_map/ngqk,nkgd->nqgd/dot_general | solution.py:44
  92.1 35.8 %collective-permute-done.3 = bf16[2,128,512]{1,2,0:T(8,128)(2,1)} collective-permute-done((bf16[2,128,512]{1,2,0:T(8,128)(2,1)}, bf16[2,128,512]{1,2,0:T(8,128)(2,1)}, u32[]{:S(2)}, u32[]{:S(2)}) %collective-permute-start.3) | collective-permute-done | bytes 262176 | tf_op jit(solution)/shard_map/ppermute | solution.py:20
  127.8 1.0 fusion.62
  128.8 0.1 copy.54
  129.0 1.2 convolution_multiply_fusion.1
  130.2 0.3 fusion.64
  130.5 0.3 convolution_bitcast_fusion.1
  130.8 0.1 pad_maximum_fusion.1
  130.9 1.1 copy.65
  132.0 0.7 broadcast_in_dim.102
  132.7 13.8 %shard_map.73 = f32[384,512]{1,0:T(8,128)} custom-call(bf16[384,1536]{1,0:T(8,128)(2,1)} %convolution_convert_fusion.q_ref, bf16[16,2,128,512]{3,2,1,0:T(8,128)(2,1)} %all-to-all-done.1.k_ref.v_ref, bf16[16,2,128,512]{3,2,1,0:T(8,128)(2,1)} %all-to-all-done.1.k_ref.v_ref, f32[3,1,2048]{2,1,0:T(1,128)} %bitcast.111), custom_call_target="tpu_custom_call" | custom-call | flops 1610612736 | bytes 5373952 | tf_op jit(solution)/shard_map/pallas_call | solution.py:69
  146.5 1.3 fusion.18
  147.8 1.2 fusion.2
  149.0 1.9 %copy-done.1 = f32[2,2,96,2560]{3,2,1,0:T(8,128)} copy-done((f32[2,2,96,2560]{3,2,1,0:T(8,128)}, f32[2,2,96,2560]{3,2,1,0:T(8,128)S(1)}, u32[]{:S(2)}) %copy-start.1) | copy-done | bytes 3932184
  150.9 1.1 fusion.15
  152.0 2.9 %collective-permute-done.4 = bf16[2,96,2560]{2,1,0:T(8,128)(2,1)} collective-permute-done((bf16[2,96,2560]{2,1,0:T(8,128)(2,1)}, bf16[2,96,2560]{2,1,0:T(8,128)(2,1)}, u32[]{:S(2)}, u32[]{:S(2)}) %collective-permute-start.4) | collective-permute-done | bytes 983072 | tf_op jit(solution)/shard_map/ppermute | solution.py:193
  154.9 2.0 %bitcast_add_fusion = f32[2,96,2560]{2,1,0:T(8,128)S(1)} fusion(bf16[2,96,2560]{2,1,0:T(8,128)(2,1)} %collective-permute-done.4, f32[2,2,96,2560]{3,2,1,0:T(8,128)} %copy-done.1, s32[]{:T(128)S(6)} %select_n.244), kind=kLoop, calls=%fused_computation.11 | loop fusion | flops 983040 | bytes 4915204 | tf_op jit(solution)/shard_map/add | solution.py:196
  156.9 1.3 copy-done.3
  158.3 1.6 collective-permute-start.5
  159.9 11.8 %collective-permute-done.5 = bf16[96,2560]{1,0:T(8,128)(2,1)} collective-permute-done((bf16[96,2560]{1,0:T(8,128)(2,1)S(1)}, bf16[96,2560]{1,0:T(8,128)(2,1)}, u32[]{:S(2)}, u32[]{:S(2)}) %collective-permute-start.5) | collective-permute-done | bytes 491552 | tf_op jit(solution)/shard_map/ppermute | solution.py:201
  171.7 2.2 %fusion.16 = bf16[96,2560]{1,0:T(8,128)(2,1)} fusion(bf16[96,2560]{1,0:T(8,128)(2,1)} %collective-permute-done.5, f32[2,96,2560]{2,1,0:T(8,128)} %copy-done.3, s32[]{:T(128)S(6)} %select_n.247), kind=kLoop, calls=%fused_computation.28 | loop fusion | flops 737280 | bytes 1966084 | tf_op jit(solution)/shard_map/convert_element_type | solution.py:180
  (44 shorter events, 0.3 us)
Async XLA Ops:
  0.0 147.8 %copy-start = (bf16[512,2560]{1,0:T(8,128)(2,1)S(1)}, bf16[512,2560]{1,0:T(8,128)(2,1)}, u32[]{:S(2)}) copy-start(bf16[512,2560]{1,0:T(8,128)(2,1)} %param.9) | copy-start | bytes 7864324
  24.6 6.9 %copy-start.8 = (bf16[96,2560]{1,0:T(8,128)(2,1)S(1)}, bf16[96,2560]{1,0:T(8,128)(2,1)}, u32[]{:S(2)}) copy-start(bf16[96,2560]{1,0:T(8,128)(2,1)} %param.7) | copy-start | bytes 1474564
  24.6 12.9 %copy-start.12 = (f32[4]{0:T(128)S(1)}, f32[4]{0:T(128)}, u32[]{:S(2)}) copy-start(f32[4]{0:T(128)} %param.10) | copy-start | bytes 52
  24.6 107.4 %all-to-all-start.1 = ((bf16[16,2,128,512]{3,2,1,0:T(8,128)(2,1)}), bf16[16,2,128,512]{3,2,1,0:T(8,128)(2,1)}, u32[]{:S(2)}, u32[]{:S(2)}) async-start(bf16[16,2,128,512]{3,2,1,0:T(8,128)(2,1)} %gather_fusion.2), calls=%async_computation.1 | async-start | bytes 8388608 | tf_op jit(solution)/shard_map/all_to_all | solution.py:163
  31.6 13.0 %collective-permute-start = (bf16[96,2560]{1,0:T(8,128)(2,1)S(1)}, bf16[96,2560]{1,0:T(8,128)(2,1)}, u32[]{:S(2)}, u32[]{:S(2)}) collective-permute-start(bf16[96,2560]{1,0:T(8,128)(2,1)S(1)} %copy-done.8), channel_id=1, source_target_pairs={{0,1},{1,2},{2,3},{3,0},{4,5},{5,6},{6,7},{7,4},{8,9},{9,10},{10,1... | collective-permute-start | bytes 1474568 | tf_op jit(solution)/shard_map/ppermute | solution.py:92
  31.6 14.2 %collective-permute-start.1 = (bf16[96,2560]{1,0:T(8,128)(2,1)S(1)}, bf16[96,2560]{1,0:T(8,128)(2,1)}, u32[]{:S(2)}, u32[]{:S(2)}) collective-permute-start(bf16[96,2560]{1,0:T(8,128)(2,1)S(1)} %copy-done.8), channel_id=1, source_target_pairs={{0,2},{1,3},{2,0},{3,1},{4,6},{5,7},{6,4},{7,5},{8,10},{9,11},{10,... | collective-permute-start | bytes 1474568 | tf_op jit(solution)/shard_map/ppermute | solution.py:92
  33.2 21.5 %collective-permute-start.2 = (bf16[96,2560]{1,0:T(8,128)(2,1)S(1)}, bf16[96,2560]{1,0:T(8,128)(2,1)}, u32[]{:S(2)}, u32[]{:S(2)}) collective-permute-start(bf16[96,2560]{1,0:T(8,128)(2,1)S(1)} %copy-done.8), channel_id=1, source_target_pairs={{0,3},{1,0},{2,1},{3,2},{4,7},{5,4},{6,5},{7,6},{8,11},{9,8},{10,9... | collective-permute-start | bytes 1474568 | tf_op jit(solution)/shard_map/ppermute | solution.py:92
  38.5 46.1 %copy-start.11 = (pred[2,128,256]{2,1,0:T(8,128)(4,1)}, pred[2,128,256]{2,1,0:T(8,128)(4,1)S(1)}, u32[]{:S(2)}) copy-start(pred[2,128,256]{2,1,0:T(8,128)(4,1)S(1)} %fusion.35) | copy-start | bytes 196612
  71.6 6.2 %copy-start.2 = (bf16[384,1536]{0,1:T(8,128)(2,1)S(1)}, bf16[384,1536]{0,1:T(8,128)(2,1)}, u32[]{:S(2)}) copy-start(bf16[384,1536]{0,1:T(8,128)(2,1)} %copy.50) | copy-start | bytes 3538948
  74.3 53.6 %collective-permute-start.3 = (bf16[2,128,512]{1,2,0:T(8,128)(2,1)}, bf16[2,128,512]{1,2,0:T(8,128)(2,1)}, u32[]{:S(2)}, u32[]{:S(2)}) collective-permute-start(bf16[2,128,512]{1,2,0:T(8,128)(2,1)} %pad_maximum_fusion.3), channel_id=1, source_target_pairs={{0,4},{4,8},{8,12},{12,16},{16,20},{20,24},{24,28},{1,5},{5,9},{9,... | collective-permute-start | bytes 786440 | tf_op jit(solution)/shard_map/ppermute | solution.py:20
  83.2 2.9 %copy-start.7 = (bf16[128,4,1,128]{0,3,2,1:T(8,128)(2,1)S(1)}, bf16[128,4,1,128]{0,3,2,1:T(8,128)(2,1)}, u32[]{:S(2)}) copy-start(bf16[128,4,1,128]{0,3,2,1:T(8,128)(2,1)} %get-tuple-element.14) | copy-start | bytes 393220
  84.6 1.0 copy-start.5
  87.6 42.7 %copy-start.9 = (pred[128,256]{1,0:T(8,128)(4,1)S(1)}, pred[128,256]{1,0:T(8,128)(4,1)}, u32[]{:S(2)}) copy-start(pred[128,256]{1,0:T(8,128)(4,1)} %get-tuple-element.24) | copy-start | bytes 98308
  92.1 38.4 %copy-start.10 = (bf16[1,128,4,128]{1,3,2,0:T(8,128)(2,1)S(1)}, bf16[1,128,4,128]{1,3,2,0:T(8,128)(2,1)}, u32[]{:S(2)}) copy-start(bf16[1,128,4,128]{1,3,2,0:T(8,128)(2,1)} %get-tuple-element.13) | copy-start | bytes 393220
  129.0 1.8 %copy-start.6 = (f32[2,128,4,128]{1,3,2,0:T(8,128)S(1)}, f32[2,128,4,128]{1,3,2,0:T(8,128)}, u32[]{:S(2)}) copy-start(f32[2,128,4,128]{1,3,2,0:T(8,128)} %convolution_bitcast_fusion) | copy-start | bytes 1572868
  132.7 13.8 %copy-start.4 = (f32[3,128,4,128]{3,2,1,0:T(4,128)S(1)}, f32[3,128,4,128]{3,2,1,0:T(4,128)}, u32[]{:S(2)}) copy-start(f32[3,128,4,128]{3,2,1,0:T(4,128)} %copy.65) | copy-start | bytes 2359300
  149.0 1.9 %copy-start.1 = (f32[2,2,96,2560]{3,2,1,0:T(8,128)}, f32[2,2,96,2560]{3,2,1,0:T(8,128)S(1)}, u32[]{:S(2)}) copy-start(f32[2,2,96,2560]{3,2,1,0:T(8,128)S(1)} %fusion.2) | copy-start | bytes 11796484
  152.0 2.9 %collective-permute-start.4 = (bf16[2,96,2560]{2,1,0:T(8,128)(2,1)}, bf16[2,96,2560]{2,1,0:T(8,128)(2,1)}, u32[]{:S(2)}, u32[]{:S(2)}) collective-permute-start(bf16[2,96,2560]{2,1,0:T(8,128)(2,1)} %fusion.15), channel_id=1, source_target_pairs={{0,1},{1,0},{2,3},{3,2},{4,5},{5,4},{6,7},{7,6},{8,9},{9,8},{10,11... | collective-permute-start | bytes 2949128 | tf_op jit(solution)/shard_map/ppermute | solution.py:193
  156.9 1.3 copy-start.3
  158.3 13.4 %collective-permute-start.5 = (bf16[96,2560]{1,0:T(8,128)(2,1)S(1)}, bf16[96,2560]{1,0:T(8,128)(2,1)}, u32[]{:S(2)}, u32[]{:S(2)}) collective-permute-start(bf16[96,2560]{1,0:T(8,128)(2,1)S(1)} %fusion.27), channel_id=1, source_target_pairs={{0,2},{1,3},{2,0},{3,1},{4,6},{5,7},{6,4},{7,5},{8,10},{9,11},{10,... | collective-permute-start | bytes 1474568 | tf_op jit(solution)/shard_map/ppermute | solution.py:201

commit v6 on v5

--- a/solution.py
+++ b/solution.py
@@ -176,30 +176,25 @@
         .astype(jnp.bfloat16)
         .reshape(local_rows, groups * HD)
     )
-    partial = jnp.dot(attended, output_weight, preferred_element_type=jnp.float32)
-    return reduce_over_tp(partial).astype(jnp.bfloat16)
-
-
-def reduce_over_tp(partial):
     count = lax.axis_size("tp")
-    chips = count // 2
-    share = partial.shape[0] // count
+    share = local_rows // count
+    all_weights = gather_tp(output_weight).reshape(count, groups * HD, output_weight.shape[1])
+    owned = exchange_tp(attended.reshape(count, share, groups * HD))
+    mixed = jnp.einsum("jrc,jcd->rd", owned, all_weights, preferred_element_type=jnp.float32)
+    return mixed.astype(jnp.bfloat16)
+
+
+def exchange_tp(pieces):
+    count = lax.axis_size("tp")
     me = lax.axis_index("tp")
-    core = me % 2
-    chip = me // 2
-    split = partial.reshape(chips, 2, share, partial.shape[1])
-    mine = lax.dynamic_index_in_dim(split, core, axis=1, keepdims=False)
-    other = lax.dynamic_index_in_dim(split, 1 - core, axis=1, keepdims=False)
-    arrived = lax.ppermute(
-        other.astype(jnp.bfloat16), "tp", [(t, t ^ 1) for t in range(count)]
-    )
-    chip_sum = mine + arrived.astype(jnp.float32)
-    total = lax.dynamic_index_in_dim(chip_sum, chip, axis=0, keepdims=False)
-    for shift in range(1, chips):
-        outgoing = lax.dynamic_index_in_dim(chip_sum, (chip + shift) % chips, axis=0, keepdims=False)
-        pairs = [(t, ((t // 2 + shift) % chips) * 2 + t % 2) for t in range(count)]
-        total = total + lax.ppermute(outgoing.astype(jnp.bfloat16), "tp", pairs).astype(jnp.float32)
-    return total
+    arrived = [lax.dynamic_index_in_dim(pieces, me, 0, keepdims=False)]
+    for shift in range(1, count):
+        outgoing = lax.dynamic_index_in_dim(pieces, (me + shift) % count, 0, keepdims=False)
+        arrived.append(
+            lax.ppermute(outgoing, "tp", [(t, (t + shift) % count) for t in range(count)])
+        )
+    order = (me - jnp.arange(count)) % count
+    return jnp.take(jnp.stack(arrived), order, axis=0, mode="clip")
 
 def solution(mesh):
     placed = (

time: 175 us -> 223 us (1.27)
  waiting for transfers between devices: 66.7 us -> 94.8 us
  local copies, waits for them, and re-layouts: 38.5 us -> 48.4 us
  other arithmetic: 12.7 us -> 19.8 us
    ppermute x3 -> x6, waiting for transfers between devices: 16.2 us -> 51.3 us  [gather_tp(): lax.ppermute(part, 'tp', [(t, (t + shift) % count) for t in range(count)])]
    gather x1 -> x4, local copies, waits for them, and re-layouts: 3.48 us -> 22 us  [gather_tp(): jnp.take(jnp.stack(arrived), order, axis=0, mode='clip')]
    ppermute x2 -> x3, waiting for transfers between devices: 14.7 us -> 0.01 us  [exchange_tp(): lax.ppermute(outgoing, 'tp', [(t, (t + shift) % count) for t in range(cou...]
    another operation x1 -> x2, other arithmetic: 2.91 us -> 11.2 us  [gather_tp(): jnp.stack(arrived)]
    ppermute x1, waiting for transfers between devices: 35.8 us -> 43.5 us  [from_behind(): lax.ppermute(value, axis, [(source, source + steps) for source in range(i...]
    dot_general x1, matrix products: 1.19 us -> 5.88 us  [local(): jnp.einsum('jrc,jcd->rd', owned, all_weights, preferred_element_type=jnp....]
    unnamed x27 -> x15, local copies, waits for them, and re-layouts: 4.29 us -> 0.94 us
    sub x2, other arithmetic: 0.67 us -> 3.02 us  [softmax_rows(): weights = jnp.where(allowed, jnp.exp(scores - row_peak), 0.0)]
  transfers between devices with their start and end apart: 7 -> 11, of which waited for: 6 -> 5; matrix products, arithmetic and copies ran while one was open for 23% -> 28% of each run, Pallas kernels for 0% -> 0%
where the time goes in v6:
time: 223 us; the launch traced here: 221 us
  waiting for transfers between devices  94.8 us (43%)
  local copies, waits for them, and re-layouts  48.4 us (22%)
  other arithmetic  19.8 us (9%)
  matrix products  17.7 us (8%)
  starting transfers between devices  16.2 us (7%)
  Pallas kernels  13.7 us (6%)
  blocking collectives  10 us (4%)
    ppermute x6, waiting for transfers between devices, gather_tp(): lax.ppermute(part, 'tp', [(t, (t + shift) % count) for t in range(count)])  51.3 us
    ppermute x1, waiting for transfers between devices, from_behind(): lax.ppermute(value, axis, [(source, source + steps) for source in range(i...  43.5 us
    gather x4, local copies, waits for them, and re-layouts, gather_tp(): jnp.take(jnp.stack(arrived), order, axis=0, mode='clip')  22 us
    pallas_call x1, Pallas kernels, far_attention(): pl.pallas_call(far_kernel, grid=(groups, blocks), in_specs=[pl.BlockSpec(...  13.7 us
    another operation x2, other arithmetic, gather_tp(): jnp.stack(arrived)  11.2 us
    all_to_all x1, blocking collectives, local(): lax.all_to_all(wanted_ids, 'mem', split_axis=0, concat_axis=0, tiled=True)  10 us
    dot_general x1, matrix products, local(): jnp.dot(gather_tp(tokens), input_weight, preferred_element_type=jnp.float32)  7.03 us
    all_to_all x1, starting transfers between devices, local(): lax.all_to_all(picked, 'mem', split_axis=0, concat_axis=0, tiled=True)  6.97 us
  transfers between devices with their start and end apart: 11, of which 5 were waited for; matrix products, arithmetic and copies ran while one was open for 28% of the time, Pallas kernels for 0%

profile of v6, /device:TPU:16, one launch (start us, length us, event | category | flops | bytes accessed | tf_op | source)
XLA Modules:
  0.0 221.1 jit_solution(13260156532242893532)
XLA Ops:
  0.0 0.8 reshape.477
  0.8 0.8 reshape.478
  1.6 0.8 gather_fusion.1
  2.4 0.7 compare_reduce_fusion
  3.1 0.2 convert_reduce_fusion.1
  3.3 0.2 convert_reduce_fusion
  3.5 2.8 %scatter_fusion = s32[8,2]{0,1:T(2,128)S(1)} fusion(s32[8,2]{0,1:T(2,128)S(1)} %broadcast.539, s32[48]{0:T(128)S(1)} %fusion.54, s32[48]{0:T(128)S(1)} %get-tuple-element.11), kind=kCustom, calls=%fused_computation.6 | custom fusion | bytes 960 | tf_op jit(solution)/shard_map/scatter | solution.py:153
  6.3 0.1 copy.48
  6.4 10.0 %all_to_all.14 = s32[8,1,2]{2,1,0:T(1,128)S(1)} all-to-all(s32[8,1,2]{2,1,0:T(1,128)S(1)} %copy.48), channel_id=1, replica_groups=mesh['mem'=8,'tp'=4] {'mem'}, dimensions={0} | all-to-all | bytes 128 | tf_op jit(solution)/shard_map/all_to_all | solution.py:157
  16.4 0.5 broadcast.614
  16.9 0.7 reduce.26
  17.6 0.1 reshape.503
  17.7 6.2 %gather_fusion.2 = bf16[16,2,128,512]{3,2,1,0:T(8,128)(2,1)} fusion(bf16[2,32,128,512]{3,2,1,0:T(8,128)(2,1)} %bitcast.91, s32[1024]{0:T(1024)S(1)} %pad_clamp_fusion), kind=kCustom, calls=%fused_computation.2 | custom fusion | bytes 8388672 | tf_op jit(solution)/shard_map/jit(_take)/gather | solution.py:155
  23.8 7.0 %all-to-all-start.1 = ((bf16[16,2,128,512]{3,2,1,0:T(8,128)(2,1)}), bf16[16,2,128,512]{3,2,1,0:T(8,128)(2,1)}, u32[]{:S(2)}, u32[]{:S(2)}) async-start(bf16[16,2,128,512]{3,2,1,0:T(8,128)(2,1)} %gather_fusion.2), calls=%async_computation.1 | async-start | bytes 8388608 | tf_op jit(solution)/shard_map/all_to_all | solution.py:163
  30.8 1.6 collective-permute-start.1
  32.4 1.4 collective-permute-start.2
  33.8 0.5 collective-permute-start.8
  34.4 2.8 %scatter_fusion.1 = pred[3,16]{1,0:T(4,128)(4,1)S(1)} fusion(pred[3,16]{1,0:T(4,128)(4,1)S(1)} %broadcast_in_dim.102, s32[48]{0:T(128)S(1)} %get-tuple-element.9, pred[48]{0:T(512)(128)(4,1)S(1)} %broadcast.578), kind=kCustom, calls=%fused_computation.7 | custom fusion | bytes 528 | tf_op jit(solution)/shard_map/scatter | solution.py:167
  37.2 0.1 slice_add_fusion
  37.4 0.7 fusion.40
  38.2 0.7 fusion.38
  38.9 4.9 %collective-permute-done = bf16[96,2560]{1,0:T(8,128)(2,1)S(1)} collective-permute-done((bf16[96,2560]{1,0:T(8,128)(2,1)S(1)}, bf16[96,2560]{1,0:T(8,128)(2,1)S(1)}, u32[]{:S(2)}, u32[]{:S(2)}) %collective-permute-start) | collective-permute-done | bytes 491552 | tf_op jit(solution)/shard_map/ppermute | solution.py:92
  43.7 1.2 collective-permute-done.1
  44.9 9.6 %collective-permute-done.2 = bf16[96,2560]{1,0:T(8,128)(2,1)S(1)} collective-permute-done((bf16[96,2560]{1,0:T(8,128)(2,1)S(1)}, bf16[96,2560]{1,0:T(8,128)(2,1)S(1)}, u32[]{:S(2)}, u32[]{:S(2)}) %collective-permute-start.2) | collective-permute-done | bytes 491552 | tf_op jit(solution)/shard_map/ppermute | solution.py:92
  54.5 0.8 copy-done.4
  55.3 1.3 pad_maximum_fusion.1
  56.6 2.0 gather_fusion
  58.5 7.0 %convolution_convert_fusion.q_ref = bf16[384,1536]{1,0:T(8,128)(2,1)S(1)} fusion(bf16[384,2560]{1,0:T(8,128)(2,1)} %bitcast.92, bf16[2560,1536]{1,0:T(8,128)(2,1)} %param.8), kind=kOutput, calls=%fused_computation.17 | convolution fusion | flops 3020488704 | bytes 11010048 | tf_op jit(solution)/shard_map/dot_general | solution.py:106
  65.6 0.7 copy.49
  66.3 0.8 slice_bitcast_fusion.2
  67.1 0.7 pad_maximum_fusion.5
  67.8 3.4 %collective-permute-start.3 = (bf16[2,128,512]{1,2,0:T(8,128)(2,1)}, bf16[2,128,512]{1,2,0:T(8,128)(2,1)}, u32[]{:S(2)}, u32[]{:S(2)}) collective-permute-start(bf16[2,128,512]{1,2,0:T(8,128)(2,1)} %pad_maximum_fusion.5), channel_id=1, source_target_pairs={{0,4},{4,8},{8,12},{12,16},{16,20},{20,24},{24,28},{1,5},{5,9},{9,... | collective-permute-start | bytes 786440 | tf_op jit(solution)/shard_map/ppermute | solution.py:20
  71.2 0.9 fusion.66
  72.1 0.8 copy.58
  72.9 0.9 copy.59
  73.8 0.9 copy.60
  74.6 1.4 convolution_multiply_fusion
  76.1 1.9 fusion.68
  78.0 0.1 copy.68
  78.1 1.1 copy.54
  79.3 0.2 copy.56
  79.4 1.1 copy.55
  80.6 0.2 copy.57
  80.8 2.9 %convolution_bitcast_fusion = f32[2,128,4,128]{1,3,2,0:T(8,128)S(1)} fusion(bf16[2,128,4,128]{1,3,2,0:T(8,128)(2,1)S(1)} %copy.57, bf16[2,128,4,128]{1,3,2,0:T(8,128)(2,1)S(1)} %copy.56, f32[2,4,128]{2,1,0:T(4,128)} %fusion.68, f32[2,4,128,256]{3,2,1,0:T(8,128)S(1)} %convolution_multiply_fusion, pred[2,128,256]{2,1,0:T(8,128)(4,1)} %fusion.38), kind=kOutput, calls=%fused_computation.28 | convolution fusion | flops 69469440 | bytes 2166784 | tf_op jit(solution)/shard_map/ngqk,nkgd->nqgd/dot_general | solution.py:44
  83.6 43.5 %collective-permute-done.3 = bf16[2,128,512]{1,2,0:T(8,128)(2,1)} collective-permute-done((bf16[2,128,512]{1,2,0:T(8,128)(2,1)}, bf16[2,128,512]{1,2,0:T(8,128)(2,1)}, u32[]{:S(2)}, u32[]{:S(2)}) %collective-permute-start.3) | collective-permute-done | bytes 262176 | tf_op jit(solution)/shard_map/ppermute | solution.py:20
  127.1 1.0 fusion.67
  128.1 0.1 copy.53
  128.2 0.3 convolution_multiply_fusion.1
  128.5 1.1 fusion.69
  129.6 0.3 convolution_bitcast_fusion.1
  130.0 0.3 copy.64
  130.3 0.3 reshape.484
  130.6 35.7 %collective-permute-done.9 = bf16[512,2560]{1,0:T(8,128)(2,1)} collective-permute-done((bf16[512,2560]{1,0:T(8,128)(2,1)}, bf16[512,2560]{1,0:T(8,128)(2,1)}, u32[]{:S(2)}, u32[]{:S(2)}) %collective-permute-start.9) | collective-permute-done | bytes 2621472 | tf_op jit(solution)/shard_map/ppermute | solution.py:92
  166.4 10.0 %pad_maximum_fusion = bf16[4,512,2560]{2,1,0:T(8,128)(2,1)} fusion(bf16[1,512,2560]{2,1,0:T(8,128)(2,1)} %bitcast.45, bf16[1,512,2560]{2,1,0:T(8,128)(2,1)} %bitcast.44, bf16[1,512,2560]{2,1,0:T(8,128)(2,1)} %bitcast.43, bf16[1,512,2560]{2,1,0:T(8,128)(2,1)} %bitcast.42), kind=kLoop, calls=%fused_computation.10 | loop fusion | flops 15728640 | bytes 20971520 | tf_op jit(solution)/shard_map/stack | solution.py:96
  176.3 0.7 broadcast_in_dim.106
  177.0 13.7 %shard_map.73 = f32[384,512]{1,0:T(8,128)} custom-call(bf16[384,1536]{1,0:T(8,128)(2,1)} %copy-done.2, bf16[16,2,128,512]{3,2,1,0:T(8,128)(2,1)} %all-to-all-done.1.k_ref.v_ref, bf16[16,2,128,512]{3,2,1,0:T(8,128)(2,1)} %all-to-all-done.1.k_ref.v_ref, f32[3,1,2048]{2,1,0:T(1,128)} %bitcast.110), custom_call_target="tpu_custom_call" | custom-call | flops 1610612736 | bytes 5373952 | tf_op jit(solution)/shard_map/pallas_call | solution.py:69
  190.7 1.3 add_convert_fusion
  192.1 0.8 collective-permute-start.4
  192.9 1.5 collective-permute-start.5
  194.4 8.7 %fusion.65 = (bf16[4,512,1280]{2,1,0:T(8,128)(2,1)}, bf16[4,512,1280]{2,1,0:T(8,128)(2,1)}) fusion(bf16[4,512,2560]{2,1,0:T(8,128)(2,1)} %pad_maximum_fusion), kind=kLoop, calls=%fused_computation.137 | loop fusion | bytes 20971520 | tf_op jit(solution)/shard_map/jit(_take)/gather | solution.py:96
  203.1 5.7 %gather_fusion.4 = bf16[4,512,1280]{2,1,0:T(8,128)(2,1)} fusion(bf16[4,512,1280]{2,1,0:T(8,128)(2,1)} %get-tuple-element.13, s32[1024]{0:T(1024)S(1)} %pad_clamp_fusion.2), kind=kCustom, calls=%fused_computation.4 | custom fusion | bytes 10485776 | tf_op jit(solution)/shard_map/jit(_take)/gather | solution.py:96
  208.8 5.7 %gather_fusion.5 = bf16[4,512,1280]{2,1,0:T(8,128)(2,1)} fusion(bf16[4,512,1280]{2,1,0:T(8,128)(2,1)} %get-tuple-element.14, s32[1024]{0:T(1024)S(1)} %pad_clamp_fusion.2), kind=kCustom, calls=%fused_computation.5 | custom fusion | bytes 10485776 | tf_op jit(solution)/shard_map/jit(_take)/gather | solution.py:96
  214.6 0.6 gather_fusion.3
  215.2 5.9 %fusion.9 = bf16[96,2560]{1,0:T(8,128)(2,1)} fusion(bf16[4,96,512]{2,1,0:T(8,128)(2,1)S(1)} %gather_fusion.3, bf16[4,512,1280]{2,1,0:T(8,128)(2,1)} %gather_fusion.5, bf16[4,512,1280]{2,1,0:T(8,128)(2,1)} %gather_fusion.4), kind=kOutput, calls=%fused_computation.16 | convolution fusion | flops 1027850240 | bytes 11370496 | tf_op jit(solution)/shard_map/jrc,jcd->rd/dot_general | solution.py:183
  (44 shorter events, 0.4 us)
Async XLA Ops:
  0.0 1.6 copy-start
  23.8 7.0 %copy-start.3 = (bf16[96,2560]{1,0:T(8,128)(2,1)S(1)}, bf16[96,2560]{1,0:T(8,128)(2,1)}, u32[]{:S(2)}) copy-start(bf16[96,2560]{1,0:T(8,128)(2,1)} %param.7) | copy-start | bytes 1474564
  23.8 13.5 %copy-start.6 = (f32[4]{0:T(128)S(1)}, f32[4]{0:T(128)}, u32[]{:S(2)}) copy-start(f32[4]{0:T(128)} %param.10) | copy-start | bytes 52
  23.8 152.5 %all-to-all-start.1 = ((bf16[16,2,128,512]{3,2,1,0:T(8,128)(2,1)}), bf16[16,2,128,512]{3,2,1,0:T(8,128)(2,1)}, u32[]{:S(2)}, u32[]{:S(2)}) async-start(bf16[16,2,128,512]{3,2,1,0:T(8,128)(2,1)} %gather_fusion.2), calls=%async_computation.1 | async-start | bytes 8388608 | tf_op jit(solution)/shard_map/all_to_all | solution.py:163
  30.8 12.9 %collective-permute-start = (bf16[96,2560]{1,0:T(8,128)(2,1)S(1)}, bf16[96,2560]{1,0:T(8,128)(2,1)S(1)}, u32[]{:S(2)}, u32[]{:S(2)}) collective-permute-start(bf16[96,2560]{1,0:T(8,128)(2,1)S(1)} %copy-done.3), channel_id=1, source_target_pairs={{0,1},{1,2},{2,3},{3,0},{4,5},{5,6},{6,7},{7,4},{8,9},{9,10},{10,1... | collective-permute-start | bytes 1474568 | tf_op jit(solution)/shard_map/ppermute | solution.py:92
  30.8 14.1 %collective-permute-start.1 = (bf16[96,2560]{1,0:T(8,128)(2,1)S(1)}, bf16[96,2560]{1,0:T(8,128)(2,1)S(1)}, u32[]{:S(2)}, u32[]{:S(2)}) collective-permute-start(bf16[96,2560]{1,0:T(8,128)(2,1)S(1)} %copy-done.3), channel_id=1, source_target_pairs={{0,2},{1,3},{2,0},{3,1},{4,6},{5,7},{6,4},{7,5},{8,10},{9,11},{10,... | collective-permute-start | bytes 1474568 | tf_op jit(solution)/shard_map/ppermute | solution.py:92
  32.4 22.1 %collective-permute-start.2 = (bf16[96,2560]{1,0:T(8,128)(2,1)S(1)}, bf16[96,2560]{1,0:T(8,128)(2,1)S(1)}, u32[]{:S(2)}, u32[]{:S(2)}) collective-permute-start(bf16[96,2560]{1,0:T(8,128)(2,1)S(1)} %copy-done.3), channel_id=1, source_target_pairs={{0,3},{1,0},{2,1},{3,2},{4,7},{5,4},{6,5},{7,6},{8,11},{9,8},{10,9... | collective-permute-start | bytes 1474568 | tf_op jit(solution)/shard_map/ppermute | solution.py:92
  33.8 96.8 %collective-permute-start.7 = (bf16[512,2560]{1,0:T(8,128)(2,1)}, bf16[512,2560]{1,0:T(8,128)(2,1)}, u32[]{:S(2)}, u32[]{:S(2)}) collective-permute-start(bf16[512,2560]{1,0:T(8,128)(2,1)} %param.9), channel_id=1, source_target_pairs={{0,1},{1,2},{2,3},{3,0},{4,5},{5,6},{6,7},{7,4},{8,9},{9,10},{10,1... | collective-permute-start | bytes 7864328 | tf_op jit(solution)/shard_map/ppermute | solution.py:92
  33.8 96.8 %collective-permute-start.8 = (bf16[512,2560]{1,0:T(8,128)(2,1)}, bf16[512,2560]{1,0:T(8,128)(2,1)}, u32[]{:S(2)}, u32[]{:S(2)}) collective-permute-start(bf16[512,2560]{1,0:T(8,128)(2,1)} %param.9), channel_id=1, source_target_pairs={{0,2},{1,3},{2,0},{3,1},{4,6},{5,7},{6,4},{7,5},{8,10},{9,11},{10,... | collective-permute-start | bytes 7864328 | tf_op jit(solution)/shard_map/ppermute | solution.py:92
  43.7 122.6 %collective-permute-start.9 = (bf16[512,2560]{1,0:T(8,128)(2,1)}, bf16[512,2560]{1,0:T(8,128)(2,1)}, u32[]{:S(2)}, u32[]{:S(2)}) collective-permute-start(bf16[512,2560]{1,0:T(8,128)(2,1)} %param.9), channel_id=1, source_target_pairs={{0,3},{1,0},{2,1},{3,2},{4,7},{5,4},{6,5},{7,6},{8,11},{9,8},{10,9... | collective-permute-start | bytes 7864328 | tf_op jit(solution)/shard_map/ppermute | solution.py:92
  54.5 0.8 copy-start.4
  65.5 12.4 %copy-start.2 = (bf16[384,1536]{1,0:T(8,128)(2,1)}, bf16[384,1536]{1,0:T(8,128)(2,1)S(1)}, u32[]{:S(2)}) copy-start(bf16[384,1536]{1,0:T(8,128)(2,1)S(1)} %convolution_convert_fusion.q_ref) | copy-start | bytes 3538948
  67.8 59.3 %collective-permute-start.3 = (bf16[2,128,512]{1,2,0:T(8,128)(2,1)}, bf16[2,128,512]{1,2,0:T(8,128)(2,1)}, u32[]{:S(2)}, u32[]{:S(2)}) collective-permute-start(bf16[2,128,512]{1,2,0:T(8,128)(2,1)} %pad_maximum_fusion.5), channel_id=1, source_target_pairs={{0,4},{4,8},{8,12},{12,16},{16,20},{20,24},{24,28},{1,5},{5,9},{9,... | collective-permute-start | bytes 786440 | tf_op jit(solution)/shard_map/ppermute | solution.py:20
  79.2 50.3 %copy-start.5 = (bf16[1,128,4,128]{1,3,2,0:T(8,128)(2,1)S(1)}, bf16[1,128,4,128]{1,3,2,0:T(8,128)(2,1)}, u32[]{:S(2)}) copy-start(bf16[1,128,4,128]{1,3,2,0:T(8,128)(2,1)} %get-tuple-element.15) | copy-start | bytes 393220
  192.1 22.4 %collective-permute-start.4 = (bf16[96,512]{1,0:T(8,128)(2,1)S(1)}, bf16[96,512]{1,0:T(8,128)(2,1)S(1)}, u32[]{:S(2)}, u32[]{:S(2)}) collective-permute-start(bf16[96,512]{1,0:T(8,128)(2,1)S(1)} %get-tuple-element.27), channel_id=1, source_target_pairs={{0,1},{1,2},{2,3},{3,0},{4,5},{5,6},{6,7},{7,4},{8,9},{9,10},{10,1... | collective-permute-start | bytes 294920 | tf_op jit(solution)/shard_map/ppermute | solution.py:194
  192.9 21.6 %collective-permute-start.5 = (bf16[96,512]{1,0:T(8,128)(2,1)S(1)}, bf16[96,512]{1,0:T(8,128)(2,1)S(1)}, u32[]{:S(2)}, u32[]{:S(2)}) collective-permute-start(bf16[96,512]{1,0:T(8,128)(2,1)S(1)} %get-tuple-element.26), channel_id=1, source_target_pairs={{0,2},{1,3},{2,0},{3,1},{4,6},{5,7},{6,4},{7,5},{8,10},{9,11},{10,... | collective-permute-start | bytes 294920 | tf_op jit(solution)/shard_map/ppermute | solution.py:194
  194.4 20.1 %collective-permute-start.6 = (bf16[96,512]{1,0:T(8,128)(2,1)S(1)}, bf16[96,512]{1,0:T(8,128)(2,1)S(1)}, u32[]{:S(2)}, u32[]{:S(2)}) collective-permute-start(bf16[96,512]{1,0:T(8,128)(2,1)S(1)} %get-tuple-element.25), channel_id=1, source_target_pairs={{0,3},{1,0},{2,1},{3,2},{4,7},{5,4},{6,5},{7,6},{8,11},{9,8},{10,9... | collective-permute-start | bytes 294920 | tf_op jit(solution)/shard_map/ppermute | solution.py:194
  214.6 6.5 %copy-start.1 = (s32[256]{0:T(256)S(1)}, s32[256]{0:T(256)}, u32[]{:S(2)}) copy-start(s32[256]{0:T(256)} %param.13) | copy-start | bytes 3076

commit v7 on v5

--- a/solution.py
+++ b/solution.py
@@ -46,44 +46,75 @@
     )
 
 
-def far_kernel(q_ref, k_ref, v_ref, bias_ref, o_ref):
-    pool = k_ref.shape[0]
-    keys = k_ref[:, 0].reshape(pool * BLK, HD)
-    values = v_ref[:, 0].reshape(pool * BLK, HD)
-    scores = lax.dot_general(
-        q_ref[...], keys, (((1,), (1,)), ((), ())), preferred_element_type=jnp.float32
-    ) * (HD ** (-0.5)) + bias_ref[0]
-    peak = jnp.max(scores, axis=-1, keepdims=True)
-    weights = jnp.exp(scores - peak)
-    scale = 1.0 / jnp.sum(weights, axis=-1, keepdims=True)
-    probs = (weights * scale).astype(jnp.bfloat16)
-    o_ref[...] = jnp.dot(probs, values, preferred_element_type=jnp.float32)
-
-
-def far_attention(projected, fetched, bias):
+def far_kernel(*refs):
+    q_ref, bias_ref, o_ref = refs[0], refs[-2], refs[-1]
+    pieces = (len(refs) - 3) // 2
+    span = refs[1].shape[0] * BLK
+    query = q_ref[...]
+    scores = []
+    for piece in range(pieces):
+        keys = refs[1 + piece][:, 0].reshape(span, HD)
+        scores.append(
+            lax.dot_general(
+                query, keys, (((1,), (1,)), ((), ())), preferred_element_type=jnp.float32
+            )
+            * (HD ** (-0.5))
+            + bias_ref[0, :, piece * span:(piece + 1) * span]
+        )
+    peak = scores[0].max(axis=-1, keepdims=True)
+    for piece in range(1, pieces):
+        peak = jnp.maximum(peak, scores[piece].max(axis=-1, keepdims=True))
+    weights = [jnp.exp(part - peak) for part in scores]
+    total = weights[0].sum(axis=-1, keepdims=True)
+    for piece in range(1, pieces):
+        total = total + weights[piece].sum(axis=-1, keepdims=True)
+    scale = 1.0 / total
+    out = None
+    for piece in range(pieces):
+        values = refs[1 + pieces + piece][:, 0].reshape(span, HD)
+        term = jnp.dot(
+            (weights[piece] * scale).astype(jnp.bfloat16), values, preferred_element_type=jnp.float32
+        )
+        out = term if out is None else out + term
+    o_ref[...] = out
+
+
+def far_attention(projected, pieces, bias):
     rows = projected.shape[0]
     blocks = rows // BLK
-    pool = fetched.shape[0]
-    groups = fetched.shape[3] // HD
+    slots = pieces[0].shape[0]
+    groups = pieces[0].shape[3] // HD
     steps = groups * blocks
+    pool = slots * len(pieces)
+    kv_spec = [pl.BlockSpec((slots, 1, BLK, HD), lambda h, b, c=c: (0, c, 0, h)) for c in (0, 1)]
     return pl.pallas_call(
         far_kernel,
         grid=(groups, blocks),
-        in_specs=[
-            pl.BlockSpec((BLK, HD), lambda h, b: (b, h * 3)),
-            pl.BlockSpec((pool, 1, BLK, HD), lambda h, b: (0, 0, 0, h)),
-            pl.BlockSpec((pool, 1, BLK, HD), lambda h, b: (0, 1, 0, h)),
-            pl.BlockSpec((1, 1, pool * BLK), lambda h, b: (b, 0, 0)),
-        ],
+        in_specs=[pl.BlockSpec((BLK, HD), lambda h, b: (b, h * 3))]
+        + [kv_spec[0]] * len(pieces)
+        + [kv_spec[1]] * len(pieces)
+        + [pl.BlockSpec((1, 1, pool * BLK), lambda h, b: (b, 0, 0))],
         out_specs=pl.BlockSpec((BLK, HD), lambda h, b: (b, h)),
         out_shape=jax.ShapeDtypeStruct((rows, groups * HD), jnp.float32),
         cost_estimate=pl.CostEstimate(
             flops=steps * 4 * BLK * pool * BLK * HD,
             transcendentals=steps * BLK * pool * BLK,
-            bytes_accessed=fetched.size * 2 + rows * groups * HD * 6,
+            bytes_accessed=sum(p.size for p in pieces) * 2 + rows * groups * HD * 6,
         ),
-    )(projected, fetched, fetched, bias)
-
+    )(projected, *pieces, *pieces, bias)
+
+
+def exchange_mem(pieces):
+    count = lax.axis_size("mem")
+    me = lax.axis_index("mem")
+    arrived = [pieces(me)]
+    for shift in range(1, count):
+        arrived.append(
+            lax.ppermute(
+                pieces((me + shift) % count), "mem", [(t, (t + shift) % count) for t in range(count)]
+            )
+        )
+    return arrived
 
 def gather_tp(part):
     count = lax.axis_size("tp")
@@ -149,27 +180,39 @@
     first_entry = jnp.argmax(same_block, axis=1)
     before_first = entry_order[None, :] < first_entry[:, None]
     slot_of = jnp.sum(same_owner & before_first & first[None, :], axis=1)
-    wanted_ids = (
-        jnp.zeros((holder_count, CAP), jnp.int32).at[holder, slot_of].set(local_block)
-    )
-    picked = jnp.take(
-        local_store,
-        lax.all_to_all(wanted_ids, "mem", split_axis=0, concat_axis=0, tiled=True).reshape(
-            holder_count * CAP
+    pool = holder_count * CAP
+    slot_index = lax.broadcasted_iota(jnp.int32, (holder_count, CAP, entries), 1)
+    holder_index = lax.broadcasted_iota(jnp.int32, (holder_count, CAP, entries), 0)
+    wanted_ids = jnp.max(
+        jnp.where(
+            (holder_index == holder[None, None, :]) & (slot_index == slot_of[None, None, :]),
+            local_block[None, None, :],
+            0,
         ),
-        axis=1,
-        mode="clip",
-    ).transpose(1, 0, 2, 3)
-    fetched = lax.all_to_all(picked, "mem", split_axis=0, concat_axis=0, tiled=True)
-    pool = holder_count * CAP
+        axis=2,
+    )
+    asked = exchange_mem(lambda target: lax.dynamic_index_in_dim(wanted_ids, target, 0, keepdims=False))
+    me_mem = lax.axis_index("mem")
+    pieces = exchange_mem(
+        lambda target: jnp.take(
+            local_store,
+            lax.dynamic_index_in_dim(jnp.stack(asked), (me_mem - target) % holder_count, 0, keepdims=False),
+            axis=1,
+            mode="clip",
+        ).transpose(1, 0, 2, 3)
+    )
     row_of = entry_order // TOPB
-    member = (
-        jnp.zeros((blocks_here, pool), jnp.bool_).at[row_of, holder * CAP + slot_of].set(True)
+    arrival = (me_mem - holder) % holder_count
+    pool_slot = arrival * CAP + slot_of
+    pool_index = lax.broadcasted_iota(jnp.int32, (blocks_here, pool, entries), 1)
+    row_index = lax.broadcasted_iota(jnp.int32, (blocks_here, pool, entries), 0)
+    member = jnp.any(
+        (pool_index == pool_slot[None, None, :]) & (row_index == row_of[None, None, :]), axis=2
     )
     bias = jnp.where(jnp.repeat(member, BLK, axis=1), 0.0, NEG_FILL).reshape(
         blocks_here, 1, pool * BLK
     )
-    far_out = far_attention(projected_flat, fetched, bias).reshape(local_rows, groups, HD)
+    far_out = far_attention(projected_flat, pieces, bias).reshape(local_rows, groups, HD)
     mixing = jax.nn.sigmoid(gate_logit)[None, :, None]
     attended = (
         (mixing * far_out + (1.0 - mixing) * near_out)

time: 175 us -> 210 us (1.20); the launches traced: 174 us -> 206 us
  local copies, waits for them, and re-layouts: 38.5 us -> 73.3 us
  starting transfers between devices: 15.1 us -> 28.3 us
  blocking collectives: 10 us -> 0 us
  waiting for transfers between devices: 66.7 us -> 59.3 us
    ppermute x0 -> x14, waiting for transfers between devices: none -> 44.6 us  [exchange_mem(): lax.ppermute(pieces((me + shift) % count), 'mem', [(t, (t + shift) % coun...]
    ppermute x1, waiting for transfers between devices: 35.8 us -> 0.01 us  [from_behind(): lax.ppermute(value, axis, [(source, source + steps) for source in range(i...]
    gather x1 -> x8, local copies, waits for them, and re-layouts: 6.17 us -> 38.1 us  [local(): jnp.take(local_store, lax.dynamic_index_in_dim(jnp.stack(asked), (me_mem...]
    ppermute x0 -> x14, starting transfers between devices: none -> 21.4 us  [exchange_mem(): lax.ppermute(pieces((me + shift) % count), 'mem', [(t, (t + shift) % coun...]
    ppermute x3, waiting for transfers between devices: 16.2 us -> 0.01 us  [gather_tp(): lax.ppermute(part, 'tp', [(t, (t + shift) % count) for t in range(count)])]
    all_to_all x1 -> x0, blocking collectives: 10 us -> none  [local(): lax.all_to_all(wanted_ids, 'mem', split_axis=0, concat_axis=0, tiled=True)]
    all_to_all x1 -> x0, starting transfers between devices: 6.94 us -> none  [local(): lax.all_to_all(picked, 'mem', split_axis=0, concat_axis=0, tiled=True)]
    scatter x2 -> x0, local copies, waits for them, and re-layouts: 5.58 us -> none  [the longest x1 2.82 us: local(): jnp.zeros((blocks_here, pool), jnp.bool_).at[row_of, holder * CAP + slot_of]]
  transfers between devices with their start and end apart: 7 -> 20, of which waited for: 6 -> 10; matrix products, arithmetic and copies ran while one was open for 23% -> 42% of each run, Pallas kernels for 0% -> 7%
where the time goes in v7:
time: 210 us; the launch traced here: 206 us
  local copies, waits for them, and re-layouts  73.3 us (35%)
  waiting for transfers between devices  59.3 us (28%)
  starting transfers between devices  28.3 us (13%)
  matrix products  16.8 us (8%)
  Pallas kernels  14.3 us (7%)
  other arithmetic  13.8 us (7%)
    ppermute x14, waiting for transfers between devices, exchange_mem(): lax.ppermute(pieces((me + shift) % count), 'mem', [(t, (t + shift) % coun...  44.6 us
    gather x8, local copies, waits for them, and re-layouts, local(): jnp.take(local_store, lax.dynamic_index_in_dim(jnp.stack(asked), (me_mem...  38.1 us
    ppermute x14, starting transfers between devices, exchange_mem(): lax.ppermute(pieces((me + shift) % count), 'mem', [(t, (t + shift) % coun...  21.4 us
    pallas_call x1, Pallas kernels, far_attention(): pl.pallas_call(far_kernel, grid=(groups, blocks), in_specs=[pl.BlockSpec(...  14.3 us
    ppermute x1, waiting for transfers between devices, reduce_over_tp(): lax.ppermute(outgoing.astype(jnp.bfloat16), 'tp', pairs).astype(jnp.float32)  11.9 us
    dot_general x1, matrix products, local(): jnp.dot(gather_tp(tokens), input_weight, preferred_element_type=jnp.float32)  8.07 us
    dot_general x2, matrix products, near_part(): jnp.einsum('ngqk,nkgd->nqgd', probs, window_values, preferred_element_typ...  4.93 us
  transfers between devices with their start and end apart: 20, of which 10 were waited for; matrix products, arithmetic and copies ran while one was open for 42% of the time, Pallas kernels for 7%

profile of v7, /device:TPU:16, one launch (start us, length us, event | category | flops | bytes accessed | tf_op | source)
XLA Modules:
  0.0 206.2 jit_solution(3322734274923287375)
XLA Ops:
  0.0 1.7 collective-permute-start.2
  1.8 1.5 collective-permute-start.1
  3.3 0.8 reshape.426
  4.0 0.8 reshape.425
  4.8 1.5 gather_fusion.1
  6.5 0.7 compare_reduce_fusion
  7.8 1.4 collective-permute-start.9
  10.8 0.7 fusion.37
  11.5 0.7 fusion.35
  12.2 4.7 %gather_fusion.2 = bf16[2,2,128,512]{3,2,1,0:T(8,128)(2,1)} fusion(bf16[2,32,128,512]{3,2,1,0:T(8,128)(2,1)} %bitcast.86, s32[1024]{0:T(1024)S(1)} %pad_clamp_fusion.7), kind=kCustom, calls=%fused_computation.2 | custom fusion | bytes 1048584 | tf_op jit(solution)/shard_map/jit(_take)/gather | solution.py:197
  17.0 3.6 %collective-permute-start.7 = (s32[2]{0:T(128)S(1)}, s32[2]{0:T(128)S(1)}, u32[]{:S(2)}, u32[]{:S(2)}) collective-permute-start(s32[2]{0:T(128)S(1)} %get-tuple-element.16), channel_id=1, source_target_pairs={{0,20},{4,24},{8,28},{12,0},{16,4},{20,8},{24,12},{28,16},{1,21},{... | collective-permute-start | bytes 32 | tf_op jit(solution)/shard_map/ppermute | solution.py:113
  20.7 1.1 collective-permute-done.7
  21.9 2.6 %collective-permute-start.5 = (s32[2]{0:T(128)S(1)}, s32[2]{0:T(128)S(1)}, u32[]{:S(2)}, u32[]{:S(2)}) collective-permute-start(s32[2]{0:T(128)S(1)} %get-tuple-element.18), channel_id=1, source_target_pairs={{0,12},{4,16},{8,20},{12,24},{16,28},{20,0},{24,4},{28,8},{1,13},{... | collective-permute-start | bytes 32 | tf_op jit(solution)/shard_map/ppermute | solution.py:113
  25.1 2.4 %collective-permute-start.4 = (s32[2]{0:T(128)S(1)}, s32[2]{0:T(128)S(1)}, u32[]{:S(2)}, u32[]{:S(2)}) collective-permute-start(s32[2]{0:T(128)S(1)} %get-tuple-element.19), channel_id=1, source_target_pairs={{0,8},{4,12},{8,16},{12,20},{16,24},{20,28},{24,0},{28,4},{1,9},{5... | collective-permute-start | bytes 32 | tf_op jit(solution)/shard_map/ppermute | solution.py:113
  28.8 3.1 %collective-permute-done.3 = s32[2]{0:T(128)S(1)} collective-permute-done((s32[2]{0:T(128)S(1)}, s32[2]{0:T(128)S(1)}, u32[]{:S(2)}, u32[]{:S(2)}) %collective-permute-start.3) | collective-permute-done | bytes 40 | tf_op jit(solution)/shard_map/ppermute | solution.py:113
  32.5 4.8 %gather_fusion.3 = bf16[2,2,128,512]{3,2,1,0:T(8,128)(2,1)} fusion(bf16[2,32,128,512]{3,2,1,0:T(8,128)(2,1)} %bitcast.87, s32[1024]{0:T(1024)S(1)} %pad_clamp_fusion.6), kind=kCustom, calls=%fused_computation.3 | custom fusion | bytes 1048584 | tf_op jit(solution)/shard_map/jit(_take)/gather | solution.py:197
  37.3 4.8 %gather_fusion.4 = bf16[2,2,128,512]{3,2,1,0:T(8,128)(2,1)} fusion(bf16[2,32,128,512]{3,2,1,0:T(8,128)(2,1)} %bitcast.88, s32[1024]{0:T(1024)S(1)} %pad_clamp_fusion.5), kind=kCustom, calls=%fused_computation.4 | custom fusion | bytes 1048584 | tf_op jit(solution)/shard_map/jit(_take)/gather | solution.py:197
  42.1 4.8 %gather_fusion.5 = bf16[2,2,128,512]{3,2,1,0:T(8,128)(2,1)} fusion(bf16[2,32,128,512]{3,2,1,0:T(8,128)(2,1)} %bitcast.89, s32[1024]{0:T(1024)S(1)} %pad_clamp_fusion.4), kind=kCustom, calls=%fused_computation.5 | custom fusion | bytes 1048584 | tf_op jit(solution)/shard_map/jit(_take)/gather | solution.py:197
  46.9 4.8 %gather_fusion.6 = bf16[2,2,128,512]{3,2,1,0:T(8,128)(2,1)} fusion(bf16[2,32,128,512]{3,2,1,0:T(8,128)(2,1)} %bitcast.90, s32[1024]{0:T(1024)S(1)} %pad_clamp_fusion.3), kind=kCustom, calls=%fused_computation.6 | custom fusion | bytes 1048584 | tf_op jit(solution)/shard_map/jit(_take)/gather | solution.py:197
  51.6 4.8 %gather_fusion.7 = bf16[2,2,128,512]{3,2,1,0:T(8,128)(2,1)} fusion(bf16[2,32,128,512]{3,2,1,0:T(8,128)(2,1)} %bitcast.91, s32[1024]{0:T(1024)S(1)} %pad_clamp_fusion.2), kind=kCustom, calls=%fused_computation.7 | custom fusion | bytes 1048584 | tf_op jit(solution)/shard_map/jit(_take)/gather | solution.py:197
  56.4 4.8 %gather_fusion.8 = bf16[2,2,128,512]{3,2,1,0:T(8,128)(2,1)} fusion(bf16[2,32,128,512]{3,2,1,0:T(8,128)(2,1)} %bitcast.92, s32[1024]{0:T(1024)S(1)} %pad_clamp_fusion.1), kind=kCustom, calls=%fused_computation.8 | custom fusion | bytes 1048584 | tf_op jit(solution)/shard_map/jit(_take)/gather | solution.py:197
  61.2 4.8 %gather_fusion.9 = bf16[2,2,128,512]{3,2,1,0:T(8,128)(2,1)} fusion(bf16[2,32,128,512]{3,2,1,0:T(8,128)(2,1)} %bitcast.93, s32[1024]{0:T(1024)S(1)} %pad_clamp_fusion), kind=kCustom, calls=%fused_computation.9 | custom fusion | bytes 1048584 | tf_op jit(solution)/shard_map/jit(_take)/gather | solution.py:197
  65.9 1.4 collective-permute-start.16
  67.3 2.9 %collective-permute-start.15 = (bf16[2,2,128,512]{3,2,1,0:T(8,128)(2,1)}, bf16[2,2,128,512]{3,2,1,0:T(8,128)(2,1)}, u32[]{:S(2)}, u32[]{:S(2)}) collective-permute-start(bf16[2,2,128,512]{3,2,1,0:T(8,128)(2,1)} %gather_fusion.8), channel_id=1, source_target_pairs={{0,24},{4,28},{8,0},{12,4},{16,8},{20,12},{24,16},{28,20},{1,25},{... | collective-permute-start | bytes 1572872 | tf_op jit(solution)/shard_map/ppermute | solution.py:113
  70.2 2.2 %collective-permute-start.14 = (bf16[2,2,128,512]{3,2,1,0:T(8,128)(2,1)}, bf16[2,2,128,512]{3,2,1,0:T(8,128)(2,1)}, u32[]{:S(2)}, u32[]{:S(2)}) collective-permute-start(bf16[2,2,128,512]{3,2,1,0:T(8,128)(2,1)} %gather_fusion.7), channel_id=1, source_target_pairs={{0,20},{4,24},{8,28},{12,0},{16,4},{20,8},{24,12},{28,16},{1,21},{... | collective-permute-start | bytes 1572872 | tf_op jit(solution)/shard_map/ppermute | solution.py:113
  72.4 0.8 collective-permute-start.13
  73.2 0.9 collective-permute-start.12
  74.0 3.0 %pad_maximum_fusion = bf16[4,96,2560]{2,1,0:T(8,128)(2,1)} fusion(bf16[1,96,2560]{2,1,0:T(8,128)(2,1)} %bitcast.4, bf16[1,96,2560]{2,1,0:T(8,128)(2,1)} %bitcast.3, bf16[1,96,2560]{2,1,0:T(8,128)(2,1)} %bitcast.2, bf16[1,96,2560]{2,1,0:T(8,128)(2,1)} %bitcast.105), kind=kLoop, calls=%fused_computation.15 | loop fusion | flops 2949120 | bytes 3932160 | tf_op jit(solution)/shard_map/stack | solution.py:127
  77.0 3.5 %gather_fusion = bf16[4,96,2560]{2,1,0:T(8,128)(2,1)} fusion(bf16[4,96,2560]{2,1,0:T(8,128)(2,1)} %pad_maximum_fusion, s32[1024]{0:T(1024)S(1)} %pad_clamp_fusion.9), kind=kCustom, calls=%fused_computation | custom fusion | bytes 3932176 | tf_op jit(solution)/shard_map/jit(_take)/gather | solution.py:127
  80.5 8.1 %convolution_convert_fusion.refs_0_ = bf16[384,1536]{1,0:T(8,128)(2,1)} fusion(bf16[384,2560]{1,0:T(8,128)(2,1)} %bitcast.94, bf16[2560,1536]{1,0:T(8,128)(2,1)} %param.8), kind=kOutput, calls=%fused_computation.12 | convolution fusion | flops 3020488704 | bytes 11010048 | tf_op jit(solution)/shard_map/dot_general | solution.py:137
  88.6 2.4 %copy.83 = bf16[384,1536]{0,1:T(8,128)(2,1)} copy(bf16[384,1536]{1,0:T(8,128)(2,1)} %convolution_convert_fusion.refs_0_) | data formatting | bytes 2359296 | tf_op jit(solution)/shard_map/convert_element_type | solution.py:142
  91.0 2.3 %fusion.78 = (bf16[256,4,1,128]{0,3,2,1:T(8,128)(2,1)}, bf16[256,4,1,128]{0,3,2,1:T(8,128)(2,1)}, bf16[256,4,1,128]{0,3,2,1:T(8,128)(2,1)}, bf16[256,4,1,128]{0,3,2,1:T(8,128)(2,1)}, bf16[256,4,1,128]{0,3,2,1:T(8,128)(2,1)}) fusion(bf16[384,4,3,128]{0,3,2,1:T(8,128)(2,1)} %bitcast.82), kind=kLoop, calls=%fused_computation.168 | loop fusion | bytes 2621440 | tf_op jit(solution)/shard_map/slice | solution.py:155
  93.3 1.1 copy.92
  94.4 1.8 copy.93
  96.2 1.8 copy.89
  98.0 1.8 copy.91
  99.8 1.8 copy.88
  101.6 1.8 copy.90
  103.4 1.8 copy.94
  105.1 1.4 convolution_multiply_fusion
  106.5 2.2 %slice_bitcast_fusion.2 = (bf16[1,128,4,128]{1,3,2,0:T(8,128)(2,1)}, bf16[128,4,1,128]{0,3,2,1:T(8,128)(2,1)S(1)}, bf16[128,4,1,128]{0,3,2,1:T(8,128)(2,1)S(1)}, bf16[128,4,1,128]{0,3,2,1:T(8,128)(2,1)S(1)}) fusion(bf16[384,4,3,128]{0,3,2,1:T(8,128)(2,1)} %bitcast.83), kind=kLoop, calls=%fused_computation.67 | loop fusion | bytes 1048576 | tf_op jit(solution)/shard_map/slice | solution.py:163
  108.7 2.3 %collective-permute-start.11 = (bf16[2,2,128,512]{3,2,1,0:T(8,128)(2,1)}, bf16[2,2,128,512]{3,2,1,0:T(8,128)(2,1)}, u32[]{:S(2)}, u32[]{:S(2)}) collective-permute-start(bf16[2,2,128,512]{3,2,1,0:T(8,128)(2,1)} %gather_fusion.4), channel_id=1, source_target_pairs={{0,8},{4,12},{8,16},{12,20},{16,24},{20,28},{24,0},{28,4},{1,9},{5... | collective-permute-start | bytes 1572872 | tf_op jit(solution)/shard_map/ppermute | solution.py:113
  111.0 25.2 %collective-permute-done.15.refs_7_.refs_15_ = bf16[2,2,128,512]{3,2,1,0:T(8,128)(2,1)} collective-permute-done((bf16[2,2,128,512]{3,2,1,0:T(8,128)(2,1)}, bf16[2,2,128,512]{3,2,1,0:T(8,128)(2,1)}, u32[]{:S(2)}, u32[]{:S(2)}) %collective-permute-start.15) | collective-permute-done | bytes 524320 | tf_op jit(solution)/shard_map/ppermute | solution.py:113
  136.6 10.3 %collective-permute-done.14.refs_6_.refs_14_ = bf16[2,2,128,512]{3,2,1,0:T(8,128)(2,1)} collective-permute-done((bf16[2,2,128,512]{3,2,1,0:T(8,128)(2,1)}, bf16[2,2,128,512]{3,2,1,0:T(8,128)(2,1)}, u32[]{:S(2)}, u32[]{:S(2)}) %collective-permute-start.14) | collective-permute-done | bytes 524320 | tf_op jit(solution)/shard_map/ppermute | solution.py:113
  146.9 2.1 %collective-permute-start.17 = (bf16[2,128,512]{1,2,0:T(8,128)(2,1)S(1)}, bf16[2,128,512]{1,2,0:T(8,128)(2,1)}, u32[]{:S(2)}, u32[]{:S(2)}) collective-permute-start(bf16[2,128,512]{1,2,0:T(8,128)(2,1)S(1)} %pad_maximum_fusion.3), channel_id=1, source_target_pairs={{0,4},{4,8},{8,12},{12,16},{16,20},{20,24},{24,28},{1,5},{5,9},{9,... | collective-permute-start | bytes 786440 | tf_op jit(solution)/shard_map/ppermute | solution.py:20
  149.0 4.6 %convolution_bitcast_fusion = f32[2,128,4,128]{1,3,2,0:T(8,128)} fusion(bf16[2,128,4,128]{1,3,2,0:T(8,128)(2,1)} %copy.91, bf16[2,128,4,128]{1,3,2,0:T(8,128)(2,1)} %copy.90, f32[2,4,128]{2,1,0:T(4,128)S(1)} %fusion.80, f32[2,4,128,256]{3,2,1,0:T(8,128)} %copy-done.5, pred[2,128,256]{2,1,0:T(8,128)(4,1)} %fusion.35), kind=kOutput, calls=%fused_computation.27 | convolution fusion | flops 69469440 | bytes 2166784 | tf_op jit(solution)/shard_map/ngqk,nkgd->nqgd/dot_general | solution.py:44
  153.8 2.5 %collective-permute-done.11.refs_3_.refs_11_ = bf16[2,2,128,512]{3,2,1,0:T(8,128)(2,1)} collective-permute-done((bf16[2,2,128,512]{3,2,1,0:T(8,128)(2,1)}, bf16[2,2,128,512]{3,2,1,0:T(8,128)(2,1)}, u32[]{:S(2)}, u32[]{:S(2)}) %collective-permute-start.11) | collective-permute-done | bytes 524320 | tf_op jit(solution)/shard_map/ppermute | solution.py:113
  156.2 1.4 collective-permute-done.10.refs_2_.refs_10_
  157.6 0.7 broadcast_in_dim.134
  158.3 14.3 %shard_map.73 = f32[384,512]{1,0:T(8,128)} custom-call(bf16[384,1536]{1,0:T(8,128)(2,1)} %convolution_convert_fusion.refs_0_, bf16[2,2,128,512]{3,2,1,0:T(8,128)(2,1)} %gather_fusion.2, bf16[2,2,128,512]{3,2,1,0:T(8,128)(2,1)} %collective-permute-done.10.refs_2_.refs_10_, bf16[2,2,128,512]{3,2,1,0:T(8,128)(2,1)} %collective-permute-done.11.refs_3_.refs_11_, ...), custom_call_target="tpu_custom_call" | custom-call | flops 1610612736 | bytes 5373952 | tf_op jit(solution)/shard_map/pallas_call | solution.py:90
  172.6 1.0 fusion.79
  173.7 1.2 convolution_multiply_fusion.1
  175.6 0.9 pad_maximum_fusion.1
  176.5 2.3 %copy.98 = f32[3,128,4,128]{3,2,1,0:T(4,128)} copy(f32[3,128,4,128]{1,3,2,0:T(8,128)} %pad_maximum_fusion.1) | data formatting | bytes 1572864 | tf_op jit(solution)/shard_map/concatenate | solution.py:166
  178.8 1.3 fusion.18
  180.1 1.2 fusion.2
  181.4 1.9 copy-done.1
  183.2 1.1 fusion.15
  184.3 2.9 %collective-permute-done.18 = bf16[2,96,2560]{2,1,0:T(8,128)(2,1)} collective-permute-done((bf16[2,96,2560]{2,1,0:T(8,128)(2,1)}, bf16[2,96,2560]{2,1,0:T(8,128)(2,1)}, u32[]{:S(2)}, u32[]{:S(2)}) %collective-permute-start.18) | collective-permute-done | bytes 983072 | tf_op jit(solution)/shard_map/ppermute | solution.py:236
  187.2 2.0 bitcast_add_fusion
  189.3 1.3 copy-done.2
  190.6 1.6 collective-permute-start.19
  192.2 11.9 %collective-permute-done.19 = bf16[96,2560]{1,0:T(8,128)(2,1)} collective-permute-done((bf16[96,2560]{1,0:T(8,128)(2,1)S(1)}, bf16[96,2560]{1,0:T(8,128)(2,1)}, u32[]{:S(2)}, u32[]{:S(2)}) %collective-permute-start.19) | collective-permute-done | bytes 491552 | tf_op jit(solution)/shard_map/ppermute | solution.py:244
  204.0 2.2 %fusion.16 = bf16[96,2560]{1,0:T(8,128)(2,1)} fusion(bf16[96,2560]{1,0:T(8,128)(2,1)} %collective-permute-done.19, f32[2,96,2560]{2,1,0:T(8,128)} %copy-done.2, s32[]{:T(128)S(6)} %select_n.359), kind=kLoop, calls=%fused_computation.33 | loop fusion | flops 737280 | bytes 1966084 | tf_op jit(solution)/shard_map/convert_element_type | solution.py:223
  (79 shorter events, 6.4 us)
Async XLA Ops:
  0.0 180.1 %copy-start = (bf16[512,2560]{1,0:T(8,128)(2,1)S(1)}, bf16[512,2560]{1,0:T(8,128)(2,1)}, u32[]{:S(2)}) copy-start(bf16[512,2560]{1,0:T(8,128)(2,1)} %param.9) | copy-start | bytes 7864324
  0.0 70.2 %collective-permute-start = (bf16[96,2560]{1,0:T(8,128)(2,1)}, bf16[96,2560]{1,0:T(8,128)(2,1)}, u32[]{:S(2)}, u32[]{:S(2)}) collective-permute-start(bf16[96,2560]{1,0:T(8,128)(2,1)} %param.7), channel_id=1, source_target_pairs={{0,1},{1,2},{2,3},{3,0},{4,5},{5,6},{6,7},{7,4},{8,9},{9,10},{10,1... | collective-permute-start | bytes 1474568 | tf_op jit(solution)/shard_map/ppermute | solution.py:123
  0.0 72.4 %collective-permute-start.2 = (bf16[96,2560]{1,0:T(8,128)(2,1)}, bf16[96,2560]{1,0:T(8,128)(2,1)}, u32[]{:S(2)}, u32[]{:S(2)}) collective-permute-start(bf16[96,2560]{1,0:T(8,128)(2,1)} %param.7), channel_id=1, source_target_pairs={{0,3},{1,0},{2,1},{3,2},{4,7},{5,4},{6,5},{7,6},{8,11},{9,8},{10,9... | collective-permute-start | bytes 1474568 | tf_op jit(solution)/shard_map/ppermute | solution.py:123
  1.8 71.4 %collective-permute-start.1 = (bf16[96,2560]{1,0:T(8,128)(2,1)}, bf16[96,2560]{1,0:T(8,128)(2,1)}, u32[]{:S(2)}, u32[]{:S(2)}) collective-permute-start(bf16[96,2560]{1,0:T(8,128)(2,1)} %param.7), channel_id=1, source_target_pairs={{0,2},{1,3},{2,0},{3,1},{4,6},{5,7},{6,4},{7,5},{8,10},{9,11},{10,... | collective-permute-start | bytes 1474568 | tf_op jit(solution)/shard_map/ppermute | solution.py:123
  7.8 9.2 %collective-permute-start.9 = (s32[2]{0:T(128)S(1)}, s32[2]{0:T(128)S(1)}, u32[]{:S(2)}, u32[]{:S(2)}) collective-permute-start(s32[2]{0:T(128)S(1)} %get-tuple-element.14), channel_id=1, source_target_pairs={{0,28},{4,0},{8,4},{12,8},{16,12},{20,16},{24,20},{28,24},{1,29},{... | collective-permute-start | bytes 32 | tf_op jit(solution)/shard_map/ppermute | solution.py:113
  9.2 11.4 %collective-permute-start.8 = (s32[2]{0:T(128)S(1)}, s32[2]{0:T(128)S(1)}, u32[]{:S(2)}, u32[]{:S(2)}) collective-permute-start(s32[2]{0:T(128)S(1)} %get-tuple-element.15), channel_id=1, source_target_pairs={{0,24},{4,28},{8,0},{12,4},{16,8},{20,12},{24,16},{28,20},{1,25},{... | collective-permute-start | bytes 32 | tf_op jit(solution)/shard_map/ppermute | solution.py:113
  17.0 4.9 %collective-permute-start.7 = (s32[2]{0:T(128)S(1)}, s32[2]{0:T(128)S(1)}, u32[]{:S(2)}, u32[]{:S(2)}) collective-permute-start(s32[2]{0:T(128)S(1)} %get-tuple-element.16), channel_id=1, source_target_pairs={{0,20},{4,24},{8,28},{12,0},{16,4},{20,8},{24,12},{28,16},{1,21},{... | collective-permute-start | bytes 32 | tf_op jit(solution)/shard_map/ppermute | solution.py:113
  20.7 4.4 %collective-permute-start.6 = (s32[2]{0:T(128)S(1)}, s32[2]{0:T(128)S(1)}, u32[]{:S(2)}, u32[]{:S(2)}) collective-permute-start(s32[2]{0:T(128)S(1)} %get-tuple-element.17), channel_id=1, source_target_pairs={{0,16},{4,20},{8,24},{12,28},{16,0},{20,4},{24,8},{28,12},{1,17},{... | collective-permute-start | bytes 32 | tf_op jit(solution)/shard_map/ppermute | solution.py:113
  21.9 5.7 %collective-permute-start.5 = (s32[2]{0:T(128)S(1)}, s32[2]{0:T(128)S(1)}, u32[]{:S(2)}, u32[]{:S(2)}) collective-permute-start(s32[2]{0:T(128)S(1)} %get-tuple-element.18), channel_id=1, source_target_pairs={{0,12},{4,16},{8,20},{12,24},{16,28},{20,0},{24,4},{28,8},{1,13},{... | collective-permute-start | bytes 32 | tf_op jit(solution)/shard_map/ppermute | solution.py:113
  25.1 3.7 %collective-permute-start.4 = (s32[2]{0:T(128)S(1)}, s32[2]{0:T(128)S(1)}, u32[]{:S(2)}, u32[]{:S(2)}) collective-permute-start(s32[2]{0:T(128)S(1)} %get-tuple-element.19), channel_id=1, source_target_pairs={{0,8},{4,12},{8,16},{12,20},{16,24},{20,28},{24,0},{28,4},{1,9},{5... | collective-permute-start | bytes 32 | tf_op jit(solution)/shard_map/ppermute | solution.py:113
  27.6 4.4 %collective-permute-start.3 = (s32[2]{0:T(128)S(1)}, s32[2]{0:T(128)S(1)}, u32[]{:S(2)}, u32[]{:S(2)}) collective-permute-start(s32[2]{0:T(128)S(1)} %get-tuple-element.20), channel_id=1, source_target_pairs={{0,4},{4,8},{8,12},{12,16},{16,20},{20,24},{24,28},{28,0},{1,5},{5... | collective-permute-start | bytes 32 | tf_op jit(solution)/shard_map/ppermute | solution.py:113
  65.9 42.8 %collective-permute-start.16 = (bf16[2,2,128,512]{3,2,1,0:T(8,128)(2,1)}, bf16[2,2,128,512]{3,2,1,0:T(8,128)(2,1)S(1)}, u32[]{:S(2)}, u32[]{:S(2)}) collective-permute-start(bf16[2,2,128,512]{3,2,1,0:T(8,128)(2,1)} %gather_fusion.9), channel_id=1, source_target_pairs={{0,28},{4,0},{8,4},{12,8},{16,12},{20,16},{24,20},{28,24},{1,29},{... | collective-permute-start | bytes 1572872 | tf_op jit(solution)/shard_map/ppermute | solution.py:113
  67.3 68.9 %collective-permute-start.15 = (bf16[2,2,128,512]{3,2,1,0:T(8,128)(2,1)}, bf16[2,2,128,512]{3,2,1,0:T(8,128)(2,1)}, u32[]{:S(2)}, u32[]{:S(2)}) collective-permute-start(bf16[2,2,128,512]{3,2,1,0:T(8,128)(2,1)} %gather_fusion.8), channel_id=1, source_target_pairs={{0,24},{4,28},{8,0},{12,4},{16,8},{20,12},{24,16},{28,20},{1,25},{... | collective-permute-start | bytes 1572872 | tf_op jit(solution)/shard_map/ppermute | solution.py:113
  70.2 76.7 %collective-permute-start.14 = (bf16[2,2,128,512]{3,2,1,0:T(8,128)(2,1)}, bf16[2,2,128,512]{3,2,1,0:T(8,128)(2,1)}, u32[]{:S(2)}, u32[]{:S(2)}) collective-permute-start(bf16[2,2,128,512]{3,2,1,0:T(8,128)(2,1)} %gather_fusion.7), channel_id=1, source_target_pairs={{0,20},{4,24},{8,28},{12,0},{16,4},{20,8},{24,12},{28,16},{1,21},{... | collective-permute-start | bytes 1572872 | tf_op jit(solution)/shard_map/ppermute | solution.py:113
  72.4 81.4 %collective-permute-start.13 = (bf16[2,2,128,512]{3,2,1,0:T(8,128)(2,1)}, bf16[2,2,128,512]{3,2,1,0:T(8,128)(2,1)}, u32[]{:S(2)}, u32[]{:S(2)}) collective-permute-start(bf16[2,2,128,512]{3,2,1,0:T(8,128)(2,1)} %gather_fusion.6), channel_id=1, source_target_pairs={{0,16},{4,20},{8,24},{12,28},{16,0},{20,4},{24,8},{28,12},{1,17},{... | collective-permute-start | bytes 1572872 | tf_op jit(solution)/shard_map/ppermute | solution.py:113
  73.2 80.6 %collective-permute-start.12 = (bf16[2,2,128,512]{3,2,1,0:T(8,128)(2,1)}, bf16[2,2,128,512]{3,2,1,0:T(8,128)(2,1)}, u32[]{:S(2)}, u32[]{:S(2)}) collective-permute-start(bf16[2,2,128,512]{3,2,1,0:T(8,128)(2,1)} %gather_fusion.5), channel_id=1, source_target_pairs={{0,12},{4,16},{8,20},{12,24},{16,28},{20,0},{24,4},{28,8},{1,13},{... | collective-permute-start | bytes 1572872 | tf_op jit(solution)/shard_map/ppermute | solution.py:113
  105.1 31.1 %copy-start.9 = (pred[2,128,256]{2,1,0:T(8,128)(4,1)S(1)}, pred[2,128,256]{2,1,0:T(8,128)(4,1)}, u32[]{:S(2)}) copy-start(pred[2,128,256]{2,1,0:T(8,128)(4,1)} %fusion.35) | copy-start | bytes 196612
  106.5 29.7 %copy-start.5 = (f32[2,4,128,256]{3,2,1,0:T(8,128)}, f32[2,4,128,256]{3,2,1,0:T(8,128)S(1)}, u32[]{:S(2)}) copy-start(f32[2,4,128,256]{3,2,1,0:T(8,128)S(1)} %convolution_multiply_fusion) | copy-start | bytes 3145732
  108.7 44.9 %copy-start.4 = (bf16[2,2,128,512]{3,2,1,0:T(8,128)(2,1)}, bf16[2,2,128,512]{3,2,1,0:T(8,128)(2,1)S(1)}, u32[]{:S(2)}) copy-start(bf16[2,2,128,512]{3,2,1,0:T(8,128)(2,1)S(1)} %collective-permute-done.16.refs_8_.refs_16_) | copy-start | bytes 1572868
  108.7 47.5 %collective-permute-start.11 = (bf16[2,2,128,512]{3,2,1,0:T(8,128)(2,1)}, bf16[2,2,128,512]{3,2,1,0:T(8,128)(2,1)}, u32[]{:S(2)}, u32[]{:S(2)}) collective-permute-start(bf16[2,2,128,512]{3,2,1,0:T(8,128)(2,1)} %gather_fusion.4), channel_id=1, source_target_pairs={{0,8},{4,12},{8,16},{12,20},{16,24},{20,28},{24,0},{28,4},{1,9},{5... | collective-permute-start | bytes 1572872 | tf_op jit(solution)/shard_map/ppermute | solution.py:113
  136.2 21.4 %collective-permute-start.10 = (bf16[2,2,128,512]{3,2,1,0:T(8,128)(2,1)}, bf16[2,2,128,512]{3,2,1,0:T(8,128)(2,1)}, u32[]{:S(2)}, u32[]{:S(2)}) collective-permute-start(bf16[2,2,128,512]{3,2,1,0:T(8,128)(2,1)} %gather_fusion.3), channel_id=1, source_target_pairs={{0,4},{4,8},{8,12},{12,16},{16,20},{20,24},{24,28},{28,0},{1,5},{5... | collective-permute-start | bytes 1572872 | tf_op jit(solution)/shard_map/ppermute | solution.py:113
  146.9 25.7 %collective-permute-start.17 = (bf16[2,128,512]{1,2,0:T(8,128)(2,1)S(1)}, bf16[2,128,512]{1,2,0:T(8,128)(2,1)}, u32[]{:S(2)}, u32[]{:S(2)}) collective-permute-start(bf16[2,128,512]{1,2,0:T(8,128)(2,1)S(1)} %pad_maximum_fusion.3), channel_id=1, source_target_pairs={{0,4},{4,8},{8,12},{12,16},{16,20},{20,24},{24,28},{1,5},{5,9},{9,... | collective-permute-start | bytes 786440 | tf_op jit(solution)/shard_map/ppermute | solution.py:20
  158.3 16.7 %copy-start.7 = (pred[128,256]{1,0:T(8,128)(4,1)S(1)}, pred[128,256]{1,0:T(8,128)(4,1)}, u32[]{:S(2)}) copy-start(pred[128,256]{1,0:T(8,128)(4,1)} %get-tuple-element.40) | copy-start | bytes 98308
  172.6 2.7 %copy-start.8 = (bf16[1,128,4,128]{1,3,2,0:T(8,128)(2,1)S(1)}, bf16[1,128,4,128]{1,3,2,0:T(8,128)(2,1)}, u32[]{:S(2)}) copy-start(bf16[1,128,4,128]{1,3,2,0:T(8,128)(2,1)} %get-tuple-element.27) | copy-start | bytes 393220
  173.7 1.8 copy-start.6
  175.6 3.2 %copy-start.3 = (f32[384,512]{1,0:T(8,128)S(1)}, f32[384,512]{1,0:T(8,128)}, u32[]{:S(2)}) copy-start(f32[384,512]{1,0:T(8,128)} %shard_map.73) | copy-start | bytes 2359300
  181.3 1.9 copy-start.1
  184.3 2.9 %collective-permute-start.18 = (bf16[2,96,2560]{2,1,0:T(8,128)(2,1)}, bf16[2,96,2560]{2,1,0:T(8,128)(2,1)}, u32[]{:S(2)}, u32[]{:S(2)}) collective-permute-start(bf16[2,96,2560]{2,1,0:T(8,128)(2,1)} %fusion.15), channel_id=1, source_target_pairs={{0,1},{1,0},{2,3},{3,2},{4,5},{5,4},{6,7},{7,6},{8,9},{9,8},{10,11... | collective-permute-start | bytes 2949128 | tf_op jit(solution)/shard_map/ppermute | solution.py:236
  189.3 1.3 copy-start.2
  190.6 13.4 %collective-permute-start.19 = (bf16[96,2560]{1,0:T(8,128)(2,1)S(1)}, bf16[96,2560]{1,0:T(8,128)(2,1)}, u32[]{:S(2)}, u32[]{:S(2)}) collective-permute-start(bf16[96,2560]{1,0:T(8,128)(2,1)S(1)} %fusion.27), channel_id=1, source_target_pairs={{0,2},{1,3},{2,0},{3,1},{4,6},{5,7},{6,4},{7,5},{8,10},{9,11},{10,... | collective-permute-start | bytes 1474568 | tf_op jit(solution)/shard_map/ppermute | solution.py:244

commit v8 on v5

--- a/solution.py
+++ b/solution.py
@@ -52,12 +52,12 @@
     values = v_ref[:, 0].reshape(pool * BLK, HD)
     scores = lax.dot_general(
         q_ref[...], keys, (((1,), (1,)), ((), ())), preferred_element_type=jnp.float32
-    ) * (HD ** (-0.5)) + bias_ref[0]
+    ) + bias_ref[0]
     peak = jnp.max(scores, axis=-1, keepdims=True)
-    weights = jnp.exp(scores - peak)
+    weights = jnp.exp((scores - peak) * (HD ** (-0.5)))
     scale = 1.0 / jnp.sum(weights, axis=-1, keepdims=True)
-    probs = (weights * scale).astype(jnp.bfloat16)
-    o_ref[...] = jnp.dot(probs, values, preferred_element_type=jnp.float32)
+    out = jnp.dot(weights.astype(jnp.bfloat16), values, preferred_element_type=jnp.float32)
+    o_ref[...] = out * scale
 
 
 def far_attention(projected, fetched, bias):
@@ -137,7 +137,10 @@
     entries = blocks_here * TOPB
     local_blocks = memory.shape[1] // BLK
     flat_blocks = retrieved.reshape(entries)
-    home_slot = jnp.take(block_home, flat_blocks)
+    block_index = lax.broadcasted_iota(jnp.int32, (entries, block_home.shape[0]), 1)
+    home_slot = jnp.sum(
+        jnp.where(block_index == flat_blocks[:, None], block_home[None, :], 0), axis=1
+    )
     holder = home_slot // local_blocks
     local_block = home_slot % local_blocks
     local_store = memory.reshape(2, local_blocks, BLK, groups * HD)
@@ -149,8 +152,15 @@
     first_entry = jnp.argmax(same_block, axis=1)
     before_first = entry_order[None, :] < first_entry[:, None]
     slot_of = jnp.sum(same_owner & before_first & first[None, :], axis=1)
-    wanted_ids = (
-        jnp.zeros((holder_count, CAP), jnp.int32).at[holder, slot_of].set(local_block)
+    slot_index = lax.broadcasted_iota(jnp.int32, (holder_count, CAP, entries), 1)
+    holder_index = lax.broadcasted_iota(jnp.int32, (holder_count, CAP, entries), 0)
+    wanted_ids = jnp.max(
+        jnp.where(
+            (holder_index == holder[None, None, :]) & (slot_index == slot_of[None, None, :]),
+            local_block[None, None, :],
+            0,
+        ),
+        axis=2,
     )
     picked = jnp.take(
         local_store,

time: 175 us -> 170 us (0.971)
  local copies, waits for them, and re-layouts: 38.5 us -> 33.5 us
    scatter x1 -> x0, local copies, waits for them, and re-layouts: 2.76 us -> none  [local(): jnp.zeros((holder_count, CAP), jnp.int32).at[holder, slot_of]]
  transfers between devices with their start and end apart: 7 -> 7, of which waited for: 6 -> 6; matrix products, arithmetic and copies ran while one was open for 23% -> 24% of each run, Pallas kernels for 0% -> 0%
where the time goes in v8:
time: 170 us; the launch traced here: 169 us
  waiting for transfers between devices  66.9 us (39%)
  local copies, waits for them, and re-layouts  33.5 us (20%)
  matrix products  16.8 us (10%)
  starting transfers between devices  14.9 us (9%)
  other arithmetic  13.6 us (8%)
  Pallas kernels  13.2 us (8%)
  blocking collectives  10 us (6%)
    ppermute x1, waiting for transfers between devices, from_behind(): lax.ppermute(value, axis, [(source, source + steps) for source in range(i...  36 us
    ppermute x3, waiting for transfers between devices, gather_tp(): lax.ppermute(part, 'tp', [(t, (t + shift) % count) for t in range(count)])  16.1 us
    pallas_call x1, Pallas kernels, far_attention(): pl.pallas_call(far_kernel, grid=(groups, blocks), in_specs=[pl.BlockSpec(...  13.2 us
    ppermute x1, waiting for transfers between devices, reduce_over_tp(): lax.ppermute(outgoing.astype(jnp.bfloat16), 'tp', pairs).astype(jnp.float32)  11.8 us
    all_to_all x1, blocking collectives, local(): lax.all_to_all(wanted_ids, 'mem', split_axis=0, concat_axis=0, tiled=True)  10 us
    dot_general x1, matrix products, local(): jnp.dot(gather_tp(tokens), input_weight, preferred_element_type=jnp.float32)  8.14 us
    all_to_all x1, starting transfers between devices, local(): lax.all_to_all(picked, 'mem', split_axis=0, concat_axis=0, tiled=True)  6.94 us
    gather x1, local copies, waits for them, and re-layouts, local(): jnp.take(local_store, lax.all_to_all(wanted_ids, 'mem', split_axis=0, con...  6.17 us
  transfers between devices with their start and end apart: 7, of which 6 were waited for; matrix products, arithmetic and copies ran while one was open for 24% of the time, Pallas kernels for 0%

profile of v8, /device:TPU:16, one launch (start us, length us, event | category | flops | bytes accessed | tf_op | source)
XLA Modules:
  0.0 169.2 jit_solution(530331648294194614)
XLA Ops:
  0.0 0.9 eq.68
  0.9 0.9 select_reduce_fusion.2
  1.8 0.7 compare_reduce_fusion
  2.5 0.2 convert_reduce_fusion.1
  2.7 0.2 convert_reduce_fusion
  2.9 0.1 select_reduce_fusion.3
  3.0 0.1 copy.49
  3.1 10.0 %all_to_all.14 = s32[8,1,2]{2,1,0:T(1,128)S(1)} all-to-all(s32[8,1,2]{2,1,0:T(1,128)S(1)} %copy.49), channel_id=1, replica_groups=mesh['mem'=8,'tp'=4] {'mem'}, dimensions={0} | all-to-all | bytes 128 | tf_op jit(solution)/shard_map/all_to_all | solution.py:167
  13.1 0.5 broadcast.451
  13.6 0.7 reduce.26
  14.3 0.1 reshape.390
  14.4 6.2 %gather_fusion.1 = bf16[16,2,128,512]{3,2,1,0:T(8,128)(2,1)} fusion(bf16[2,32,128,512]{3,2,1,0:T(8,128)(2,1)} %bitcast.94, s32[1024]{0:T(1024)S(1)} %pad_clamp_fusion), kind=kCustom, calls=%fused_computation.1 | custom fusion | bytes 8388672 | tf_op jit(solution)/shard_map/jit(_take)/gather | solution.py:165
  20.5 6.9 %all-to-all-start.1 = ((bf16[16,2,128,512]{3,2,1,0:T(8,128)(2,1)}), bf16[16,2,128,512]{3,2,1,0:T(8,128)(2,1)}, u32[]{:S(2)}, u32[]{:S(2)}) async-start(bf16[16,2,128,512]{3,2,1,0:T(8,128)(2,1)} %gather_fusion.1), calls=%async_computation.1 | async-start | bytes 8388608 | tf_op jit(solution)/shard_map/all_to_all | solution.py:173
  27.5 1.6 collective-permute-start.1
  29.1 1.4 collective-permute-start.2
  30.5 2.8 %scatter_fusion = pred[3,16]{1,0:T(4,128)(4,1)S(1)} fusion(pred[3,16]{1,0:T(4,128)(4,1)S(1)} %broadcast_in_dim.118, s32[48]{0:T(128)S(1)} %fusion.48, pred[48]{0:T(512)(128)(4,1)S(1)} %broadcast.415), kind=kCustom, calls=%fused_computation.2 | custom fusion | bytes 528 | tf_op jit(solution)/shard_map/scatter | solution.py:177
  33.4 0.1 slice_add_fusion
  33.5 0.1 broadcast_bitcast_fusion
  33.6 0.7 fusion.37
  34.3 0.1 fusion.35
  34.4 6.1 %collective-permute-done = bf16[96,2560]{1,0:T(8,128)(2,1)} collective-permute-done((bf16[96,2560]{1,0:T(8,128)(2,1)S(1)}, bf16[96,2560]{1,0:T(8,128)(2,1)}, u32[]{:S(2)}, u32[]{:S(2)}) %collective-permute-start) | collective-permute-done | bytes 491552 | tf_op jit(solution)/shard_map/ppermute | solution.py:92
  40.5 1.2 collective-permute-done.1
  41.7 8.9 %collective-permute-done.2 = bf16[96,2560]{1,0:T(8,128)(2,1)} collective-permute-done((bf16[96,2560]{1,0:T(8,128)(2,1)S(1)}, bf16[96,2560]{1,0:T(8,128)(2,1)}, u32[]{:S(2)}, u32[]{:S(2)}) %collective-permute-start.2) | collective-permute-done | bytes 491552 | tf_op jit(solution)/shard_map/ppermute | solution.py:92
  50.6 2.9 %pad_maximum_fusion = bf16[4,96,2560]{2,1,0:T(8,128)(2,1)} fusion(bf16[1,96,2560]{2,1,0:T(8,128)(2,1)} %bitcast.4, bf16[1,96,2560]{2,1,0:T(8,128)(2,1)} %bitcast.3, bf16[1,96,2560]{2,1,0:T(8,128)(2,1)} %bitcast.2, bf16[1,96,2560]{2,1,0:T(8,128)(2,1)S(1)} %bitcast.106), kind=kLoop, calls=%fused_computation.8 | loop fusion | flops 2949120 | bytes 3932160 | tf_op jit(solution)/shard_map/stack | solution.py:96
  53.5 3.5 %gather_fusion = bf16[4,96,2560]{2,1,0:T(8,128)(2,1)} fusion(bf16[4,96,2560]{2,1,0:T(8,128)(2,1)} %pad_maximum_fusion, s32[1024]{0:T(1024)S(1)} %pad_clamp_fusion.1), kind=kCustom, calls=%fused_computation | custom fusion | bytes 3932176 | tf_op jit(solution)/shard_map/jit(_take)/gather | solution.py:96
  57.0 8.1 %convolution_convert_fusion.q_ref = bf16[384,1536]{1,0:T(8,128)(2,1)} fusion(bf16[384,2560]{1,0:T(8,128)(2,1)} %bitcast.95, bf16[2560,1536]{1,0:T(8,128)(2,1)} %param.8), kind=kOutput, calls=%fused_computation.5 | convolution fusion | flops 3020488704 | bytes 11010048 | tf_op jit(solution)/shard_map/dot_general | solution.py:106
  65.1 2.4 %copy.50 = bf16[384,1536]{0,1:T(8,128)(2,1)} copy(bf16[384,1536]{1,0:T(8,128)(2,1)} %convolution_convert_fusion.q_ref) | data formatting | bytes 2359296 | tf_op jit(solution)/shard_map/convert_element_type | solution.py:111
  67.5 1.9 %slice_bitcast_fusion.2 = (bf16[1,128,4,128]{1,3,2,0:T(8,128)(2,1)}, bf16[128,4,1,128]{0,3,2,1:T(8,128)(2,1)}, bf16[128,4,1,128]{0,3,2,1:T(8,128)(2,1)S(1)}, bf16[128,4,1,128]{0,3,2,1:T(8,128)(2,1)S(1)}) fusion(bf16[384,4,3,128]{0,3,2,1:T(8,128)(2,1)} %bitcast.90), kind=kLoop, calls=%fused_computation.60 | loop fusion | bytes 1048576 | tf_op jit(solution)/shard_map/slice | solution.py:132
  69.4 0.7 pad_maximum_fusion.3
  70.2 3.4 %collective-permute-start.3 = (bf16[2,128,512]{1,2,0:T(8,128)(2,1)}, bf16[2,128,512]{1,2,0:T(8,128)(2,1)}, u32[]{:S(2)}, u32[]{:S(2)}) collective-permute-start(bf16[2,128,512]{1,2,0:T(8,128)(2,1)} %pad_maximum_fusion.3), channel_id=1, source_target_pairs={{0,4},{4,8},{8,12},{12,16},{16,20},{20,24},{24,28},{1,5},{5,9},{9,... | collective-permute-start | bytes 786440 | tf_op jit(solution)/shard_map/ppermute | solution.py:20
  73.6 0.9 fusion.59
  74.5 1.8 %copy.59 = bf16[256,4,1,128]{3,0,1,2:T(8,128)(2,1)} copy(bf16[256,4,1,128]{0,3,2,1:T(8,128)(2,1)} %get-tuple-element.13) | data formatting | bytes 524288 | tf_op jit(solution)/shard_map/slice | solution.py:124
  76.3 1.8 %copy.60 = bf16[256,4,1,128]{3,0,1,2:T(8,128)(2,1)} copy(bf16[256,4,1,128]{0,3,2,1:T(8,128)(2,1)} %get-tuple-element.14) | data formatting | bytes 524288 | tf_op jit(solution)/shard_map/slice | solution.py:125
  78.1 0.8 copy.61
  78.9 1.4 convolution_multiply_fusion
  80.4 1.0 copy-done.5
  81.3 0.4 fusion.61
  81.8 0.1 copy.70
  81.9 0.2 copy.55
  82.1 0.9 copy.57
  82.9 0.2 copy.56
  83.1 0.2 copy.58
  83.3 4.5 %convolution_bitcast_fusion = f32[2,128,4,128]{1,3,2,0:T(8,128)} fusion(bf16[2,128,4,128]{1,3,2,0:T(8,128)(2,1)S(1)} %copy.58, bf16[2,128,4,128]{1,3,2,0:T(8,128)(2,1)} %copy.57, f32[2,4,128]{2,1,0:T(4,128)S(1)} %fusion.61, f32[2,4,128,256]{3,2,1,0:T(8,128)} %copy-done.5, pred[2,128,256]{2,1,0:T(8,128)(4,1)} %copy-done.11), kind=kOutput, calls=%fused_computation.20 | convolution fusion | flops 69469440 | bytes 2166784 | tf_op jit(solution)/shard_map/ngqk,nkgd->nqgd/dot_general | solution.py:44
  87.8 36.0 %collective-permute-done.3 = bf16[2,128,512]{1,2,0:T(8,128)(2,1)} collective-permute-done((bf16[2,128,512]{1,2,0:T(8,128)(2,1)}, bf16[2,128,512]{1,2,0:T(8,128)(2,1)}, u32[]{:S(2)}, u32[]{:S(2)}) %collective-permute-start.3) | collective-permute-done | bytes 262176 | tf_op jit(solution)/shard_map/ppermute | solution.py:20
  123.8 1.0 fusion.60
  124.7 0.1 copy.54
  124.9 1.2 convolution_multiply_fusion.1
  126.1 0.3 fusion.62
  126.4 0.3 convolution_bitcast_fusion.1
  126.7 0.1 pad_maximum_fusion.1
  126.8 1.1 copy.65
  127.9 0.7 broadcast_in_dim.122
  128.6 13.2 %shard_map.73 = f32[384,512]{1,0:T(8,128)} custom-call(bf16[384,1536]{1,0:T(8,128)(2,1)} %convolution_convert_fusion.q_ref, bf16[16,2,128,512]{3,2,1,0:T(8,128)(2,1)} %all-to-all-done.1.k_ref.v_ref, bf16[16,2,128,512]{3,2,1,0:T(8,128)(2,1)} %all-to-all-done.1.k_ref.v_ref, f32[3,1,2048]{2,1,0:T(1,128)} %bitcast.108), custom_call_target="tpu_custom_call" | custom-call | flops 1610612736 | bytes 5373952 | tf_op jit(solution)/shard_map/pallas_call | solution.py:69
  141.8 1.3 fusion.18
  143.1 1.2 fusion.2
  144.3 1.9 %copy-done.1 = f32[2,2,96,2560]{3,2,1,0:T(8,128)} copy-done((f32[2,2,96,2560]{3,2,1,0:T(8,128)}, f32[2,2,96,2560]{3,2,1,0:T(8,128)S(1)}, u32[]{:S(2)}) %copy-start.1) | copy-done | bytes 3932184
  146.2 1.1 fusion.15
  147.3 2.9 %collective-permute-done.4 = bf16[2,96,2560]{2,1,0:T(8,128)(2,1)} collective-permute-done((bf16[2,96,2560]{2,1,0:T(8,128)(2,1)}, bf16[2,96,2560]{2,1,0:T(8,128)(2,1)}, u32[]{:S(2)}, u32[]{:S(2)}) %collective-permute-start.4) | collective-permute-done | bytes 983072 | tf_op jit(solution)/shard_map/ppermute | solution.py:203
  150.2 2.0 %bitcast_add_fusion = f32[2,96,2560]{2,1,0:T(8,128)S(1)} fusion(bf16[2,96,2560]{2,1,0:T(8,128)(2,1)} %collective-permute-done.4, f32[2,2,96,2560]{3,2,1,0:T(8,128)} %copy-done.1, s32[]{:T(128)S(6)} %select_n.166), kind=kLoop, calls=%fused_computation.9 | loop fusion | flops 983040 | bytes 4915204 | tf_op jit(solution)/shard_map/add | solution.py:206
  152.2 1.3 copy-done.3
  153.5 0.1 fusion.27
  153.6 1.6 collective-permute-start.5
  155.2 11.8 %collective-permute-done.5 = bf16[96,2560]{1,0:T(8,128)(2,1)} collective-permute-done((bf16[96,2560]{1,0:T(8,128)(2,1)S(1)}, bf16[96,2560]{1,0:T(8,128)(2,1)}, u32[]{:S(2)}, u32[]{:S(2)}) %collective-permute-start.5) | collective-permute-done | bytes 491552 | tf_op jit(solution)/shard_map/ppermute | solution.py:211
  167.0 2.2 %fusion.16 = bf16[96,2560]{1,0:T(8,128)(2,1)} fusion(bf16[96,2560]{1,0:T(8,128)(2,1)} %collective-permute-done.5, f32[2,96,2560]{2,1,0:T(8,128)} %copy-done.3, s32[]{:T(128)S(6)} %select_n.169), kind=kLoop, calls=%fused_computation.26 | loop fusion | flops 737280 | bytes 1966084 | tf_op jit(solution)/shard_map/convert_element_type | solution.py:190
  (38 shorter events, 0.2 us)
Async XLA Ops:
  0.0 143.1 %copy-start = (bf16[512,2560]{1,0:T(8,128)(2,1)S(1)}, bf16[512,2560]{1,0:T(8,128)(2,1)}, u32[]{:S(2)}) copy-start(bf16[512,2560]{1,0:T(8,128)(2,1)} %param.9) | copy-start | bytes 7864324
  20.5 6.9 %copy-start.8 = (bf16[96,2560]{1,0:T(8,128)(2,1)S(1)}, bf16[96,2560]{1,0:T(8,128)(2,1)}, u32[]{:S(2)}) copy-start(bf16[96,2560]{1,0:T(8,128)(2,1)} %param.7) | copy-start | bytes 1474564
  20.5 12.9 %copy-start.12 = (f32[4]{0:T(128)S(1)}, f32[4]{0:T(128)}, u32[]{:S(2)}) copy-start(f32[4]{0:T(128)} %param.10) | copy-start | bytes 52
  20.5 107.4 %all-to-all-start.1 = ((bf16[16,2,128,512]{3,2,1,0:T(8,128)(2,1)}), bf16[16,2,128,512]{3,2,1,0:T(8,128)(2,1)}, u32[]{:S(2)}, u32[]{:S(2)}) async-start(bf16[16,2,128,512]{3,2,1,0:T(8,128)(2,1)} %gather_fusion.1), calls=%async_computation.1 | async-start | bytes 8388608 | tf_op jit(solution)/shard_map/all_to_all | solution.py:173
  27.5 13.0 %collective-permute-start = (bf16[96,2560]{1,0:T(8,128)(2,1)S(1)}, bf16[96,2560]{1,0:T(8,128)(2,1)}, u32[]{:S(2)}, u32[]{:S(2)}) collective-permute-start(bf16[96,2560]{1,0:T(8,128)(2,1)S(1)} %copy-done.8), channel_id=1, source_target_pairs={{0,1},{1,2},{2,3},{3,0},{4,5},{5,6},{6,7},{7,4},{8,9},{9,10},{10,1... | collective-permute-start | bytes 1474568 | tf_op jit(solution)/shard_map/ppermute | solution.py:92
  27.5 14.2 %collective-permute-start.1 = (bf16[96,2560]{1,0:T(8,128)(2,1)S(1)}, bf16[96,2560]{1,0:T(8,128)(2,1)}, u32[]{:S(2)}, u32[]{:S(2)}) collective-permute-start(bf16[96,2560]{1,0:T(8,128)(2,1)S(1)} %copy-done.8), channel_id=1, source_target_pairs={{0,2},{1,3},{2,0},{3,1},{4,6},{5,7},{6,4},{7,5},{8,10},{9,11},{10,... | collective-permute-start | bytes 1474568 | tf_op jit(solution)/shard_map/ppermute | solution.py:92
  29.1 21.5 %collective-permute-start.2 = (bf16[96,2560]{1,0:T(8,128)(2,1)S(1)}, bf16[96,2560]{1,0:T(8,128)(2,1)}, u32[]{:S(2)}, u32[]{:S(2)}) collective-permute-start(bf16[96,2560]{1,0:T(8,128)(2,1)S(1)} %copy-done.8), channel_id=1, source_target_pairs={{0,3},{1,0},{2,1},{3,2},{4,7},{5,4},{6,5},{7,6},{8,11},{9,8},{10,9... | collective-permute-start | bytes 1474568 | tf_op jit(solution)/shard_map/ppermute | solution.py:92
  34.4 45.9 %copy-start.11 = (pred[2,128,256]{2,1,0:T(8,128)(4,1)}, pred[2,128,256]{2,1,0:T(8,128)(4,1)S(1)}, u32[]{:S(2)}) copy-start(pred[2,128,256]{2,1,0:T(8,128)(4,1)S(1)} %fusion.35) | copy-start | bytes 196612
  67.5 6.0 %copy-start.2 = (bf16[384,1536]{0,1:T(8,128)(2,1)S(1)}, bf16[384,1536]{0,1:T(8,128)(2,1)}, u32[]{:S(2)}) copy-start(bf16[384,1536]{0,1:T(8,128)(2,1)} %copy.50) | copy-start | bytes 3538948
  70.2 53.6 %collective-permute-start.3 = (bf16[2,128,512]{1,2,0:T(8,128)(2,1)}, bf16[2,128,512]{1,2,0:T(8,128)(2,1)}, u32[]{:S(2)}, u32[]{:S(2)}) collective-permute-start(bf16[2,128,512]{1,2,0:T(8,128)(2,1)} %pad_maximum_fusion.3), channel_id=1, source_target_pairs={{0,4},{4,8},{8,12},{12,16},{16,20},{20,24},{24,28},{1,5},{5,9},{9,... | collective-permute-start | bytes 786440 | tf_op jit(solution)/shard_map/ppermute | solution.py:20
  78.9 2.9 %copy-start.7 = (bf16[128,4,1,128]{0,3,2,1:T(8,128)(2,1)S(1)}, bf16[128,4,1,128]{0,3,2,1:T(8,128)(2,1)}, u32[]{:S(2)}) copy-start(bf16[128,4,1,128]{0,3,2,1:T(8,128)(2,1)} %get-tuple-element.10) | copy-start | bytes 393220
  80.4 1.0 copy-start.5
  83.3 42.8 %copy-start.9 = (pred[128,256]{1,0:T(8,128)(4,1)S(1)}, pred[128,256]{1,0:T(8,128)(4,1)}, u32[]{:S(2)}) copy-start(pred[128,256]{1,0:T(8,128)(4,1)} %get-tuple-element.22) | copy-start | bytes 98308
  87.8 38.6 %copy-start.10 = (bf16[1,128,4,128]{1,3,2,0:T(8,128)(2,1)S(1)}, bf16[1,128,4,128]{1,3,2,0:T(8,128)(2,1)}, u32[]{:S(2)}) copy-start(bf16[1,128,4,128]{1,3,2,0:T(8,128)(2,1)} %get-tuple-element.9) | copy-start | bytes 393220
  124.9 1.8 %copy-start.6 = (f32[2,128,4,128]{1,3,2,0:T(8,128)S(1)}, f32[2,128,4,128]{1,3,2,0:T(8,128)}, u32[]{:S(2)}) copy-start(f32[2,128,4,128]{1,3,2,0:T(8,128)} %convolution_bitcast_fusion) | copy-start | bytes 1572868
  128.6 13.2 %copy-start.4 = (f32[3,128,4,128]{3,2,1,0:T(4,128)S(1)}, f32[3,128,4,128]{3,2,1,0:T(4,128)}, u32[]{:S(2)}) copy-start(f32[3,128,4,128]{3,2,1,0:T(4,128)} %copy.65) | copy-start | bytes 2359300
  144.3 1.9 %copy-start.1 = (f32[2,2,96,2560]{3,2,1,0:T(8,128)}, f32[2,2,96,2560]{3,2,1,0:T(8,128)S(1)}, u32[]{:S(2)}) copy-start(f32[2,2,96,2560]{3,2,1,0:T(8,128)S(1)} %fusion.2) | copy-start | bytes 11796484
  147.3 2.9 %collective-permute-start.4 = (bf16[2,96,2560]{2,1,0:T(8,128)(2,1)}, bf16[2,96,2560]{2,1,0:T(8,128)(2,1)}, u32[]{:S(2)}, u32[]{:S(2)}) collective-permute-start(bf16[2,96,2560]{2,1,0:T(8,128)(2,1)} %fusion.15), channel_id=1, source_target_pairs={{0,1},{1,0},{2,3},{3,2},{4,5},{5,4},{6,7},{7,6},{8,9},{9,8},{10,11... | collective-permute-start | bytes 2949128 | tf_op jit(solution)/shard_map/ppermute | solution.py:203
  152.2 1.3 copy-start.3
  153.6 13.4 %collective-permute-start.5 = (bf16[96,2560]{1,0:T(8,128)(2,1)S(1)}, bf16[96,2560]{1,0:T(8,128)(2,1)}, u32[]{:S(2)}, u32[]{:S(2)}) collective-permute-start(bf16[96,2560]{1,0:T(8,128)(2,1)S(1)} %fusion.27), channel_id=1, source_target_pairs={{0,2},{1,3},{2,0},{3,1},{4,6},{5,7},{6,4},{7,5},{8,10},{9,11},{10,... | collective-permute-start | bytes 1474568 | tf_op jit(solution)/shard_map/ppermute | solution.py:211

commit v9 on v8

--- a/solution.py
+++ b/solution.py
@@ -46,44 +46,47 @@
     )
 
 
-def far_kernel(q_ref, k_ref, v_ref, bias_ref, o_ref):
+def far_kernel(q_ref, k_ref, v_ref, bias_ref, near_ref, mix_ref, o_ref):
     pool = k_ref.shape[0]
     keys = k_ref[:, 0].reshape(pool * BLK, HD)
     values = v_ref[:, 0].reshape(pool * BLK, HD)
-    scores = lax.dot_general(
-        q_ref[...], keys, (((1,), (1,)), ((), ())), preferred_element_type=jnp.float32
-    ) + bias_ref[0]
-    peak = jnp.max(scores, axis=-1, keepdims=True)
-    weights = jnp.exp((scores - peak) * (HD ** (-0.5)))
-    scale = 1.0 / jnp.sum(weights, axis=-1, keepdims=True)
-    out = jnp.dot(weights.astype(jnp.bfloat16), values, preferred_element_type=jnp.float32)
-    o_ref[...] = out * scale
-
-
-def far_attention(projected, fetched, bias):
+    mix = mix_ref[...]
+    for block in range(q_ref.shape[0] // BLK):
+        rows = slice(block * BLK, (block + 1) * BLK)
+        scores = lax.dot_general(
+            q_ref[rows, :], keys, (((1,), (1,)), ((), ())), preferred_element_type=jnp.float32
+        ) + bias_ref[block]
+        peak = jnp.max(scores, axis=-1, keepdims=True)
+        weights = jnp.exp((scores - peak) * (HD ** (-0.5)))
+        scale = 1.0 / jnp.sum(weights, axis=-1, keepdims=True)
+        far = jnp.dot(weights.astype(jnp.bfloat16), values, preferred_element_type=jnp.float32)
+        o_ref[rows, :] = (mix * (far * scale) + (1.0 - mix) * near_ref[rows, :]).astype(o_ref.dtype)
+
+
+def far_attention(projected, fetched, bias, near_out, mixing):
     rows = projected.shape[0]
     blocks = rows // BLK
     pool = fetched.shape[0]
     groups = fetched.shape[3] // HD
-    steps = groups * blocks
     return pl.pallas_call(
         far_kernel,
-        grid=(groups, blocks),
+        grid=(groups,),
         in_specs=[
-            pl.BlockSpec((BLK, HD), lambda h, b: (b, h * 3)),
-            pl.BlockSpec((pool, 1, BLK, HD), lambda h, b: (0, 0, 0, h)),
-            pl.BlockSpec((pool, 1, BLK, HD), lambda h, b: (0, 1, 0, h)),
-            pl.BlockSpec((1, 1, pool * BLK), lambda h, b: (b, 0, 0)),
+            pl.BlockSpec((rows, HD), lambda h: (0, h * 3)),
+            pl.BlockSpec((pool, 1, BLK, HD), lambda h: (0, 0, 0, h)),
+            pl.BlockSpec((pool, 1, BLK, HD), lambda h: (0, 1, 0, h)),
+            pl.BlockSpec((blocks, 1, pool * BLK), lambda h: (0, 0, 0)),
+            pl.BlockSpec((rows, HD), lambda h: (0, h)),
+            pl.BlockSpec((1, HD), lambda h: (0, h)),
         ],
-        out_specs=pl.BlockSpec((BLK, HD), lambda h, b: (b, h)),
-        out_shape=jax.ShapeDtypeStruct((rows, groups * HD), jnp.float32),
+        out_specs=pl.BlockSpec((rows, HD), lambda h: (0, h)),
+        out_shape=jax.ShapeDtypeStruct((rows, groups * HD), jnp.bfloat16),
         cost_estimate=pl.CostEstimate(
-            flops=steps * 4 * BLK * pool * BLK * HD,
-            transcendentals=steps * BLK * pool * BLK,
-            bytes_accessed=fetched.size * 2 + rows * groups * HD * 6,
+            flops=groups * blocks * 4 * BLK * pool * BLK * HD,
+            transcendentals=groups * blocks * BLK * pool * BLK,
+            bytes_accessed=fetched.size * 2 + rows * groups * HD * 8,
         ),
-    )(projected, fetched, fetched, bias)
-
+    )(projected, fetched, fetched, bias, near_out, mixing)
 
 def gather_tp(part):
     count = lax.axis_size("tp")
@@ -179,12 +182,9 @@
     bias = jnp.where(jnp.repeat(member, BLK, axis=1), 0.0, NEG_FILL).reshape(
         blocks_here, 1, pool * BLK
     )
-    far_out = far_attention(projected_flat, fetched, bias).reshape(local_rows, groups, HD)
-    mixing = jax.nn.sigmoid(gate_logit)[None, :, None]
-    attended = (
-        (mixing * far_out + (1.0 - mixing) * near_out)
-        .astype(jnp.bfloat16)
-        .reshape(local_rows, groups * HD)
+    mixing = jnp.repeat(jax.nn.sigmoid(gate_logit), HD).reshape(1, groups * HD)
+    attended = far_attention(
+        projected_flat, fetched, bias, near_out.reshape(local_rows, groups * HD), mixing
     )
     partial = jnp.dot(attended, output_weight, preferred_element_type=jnp.float32)
     return reduce_over_tp(partial).astype(jnp.bfloat16)

time: 170 us -> 169 us (level)
  local copies, waits for them, and re-layouts: 33.5 us -> 37.6 us
  Pallas kernels: 13.2 us -> 9.45 us
    pallas_call x1, Pallas kernels: 13.2 us -> 9.45 us  [far_attention(): pl.pallas_call(far_kernel, grid=(groups,), in_specs=[pl.BlockSpec((rows,...]
    ppermute x1, waiting for transfers between devices: 36 us -> 33.5 us  [from_behind(): lax.ppermute(value, axis, [(source, source + steps) for source in range(i...]
    unnamed x27 -> x22, local copies, waits for them, and re-layouts: 4.29 us -> 6.34 us
    ppermute x3, waiting for transfers between devices: 16.1 us -> 18 us  [gather_tp(): lax.ppermute(part, 'tp', [(t, (t + shift) % count) for t in range(count)])]
  transfers between devices with their start and end apart: 7 -> 7, of which waited for: 6 -> 5; matrix products, arithmetic and copies ran while one was open for 24% -> 27% of each run, Pallas kernels for 0% -> 0%
where the time goes in v9:
time: 169 us; the launch traced here: 168 us
  waiting for transfers between devices  66.3 us (39%)
  local copies, waits for them, and re-layouts  37.6 us (22%)
  matrix products  17.7 us (10%)
  starting transfers between devices  13.7 us (8%)
  other arithmetic  12.9 us (8%)
  blocking collectives  10 us (6%)
  Pallas kernels  9.45 us (6%)
    ppermute x1, waiting for transfers between devices, from_behind(): lax.ppermute(value, axis, [(source, source + steps) for source in range(i...  33.5 us
    ppermute x3, waiting for transfers between devices, gather_tp(): lax.ppermute(part, 'tp', [(t, (t + shift) % count) for t in range(count)])  18 us
    ppermute x1, waiting for transfers between devices, reduce_over_tp(): lax.ppermute(outgoing.astype(jnp.bfloat16), 'tp', pairs).astype(jnp.float32)  11.8 us
    all_to_all x1, blocking collectives, local(): lax.all_to_all(wanted_ids, 'mem', split_axis=0, concat_axis=0, tiled=True)  10 us
    pallas_call x1, Pallas kernels, far_attention(): pl.pallas_call(far_kernel, grid=(groups,), in_specs=[pl.BlockSpec((rows,...  9.45 us
    dot_general x1, matrix products, local(): jnp.dot(gather_tp(tokens), input_weight, preferred_element_type=jnp.float32)  8.14 us
    all_to_all x1, starting transfers between devices, local(): lax.all_to_all(picked, 'mem', split_axis=0, concat_axis=0, tiled=True)  6.94 us
    unnamed x22, local copies, waits for them, and re-layouts  6.34 us
  transfers between devices with their start and end apart: 7, of which 5 were waited for; matrix products, arithmetic and copies ran while one was open for 27% of the time, Pallas kernels for 0%

profile of v9, /device:TPU:16, one launch (start us, length us, event | category | flops | bytes accessed | tf_op | source)
XLA Modules:
  0.0 167.9 jit_solution(2081156368501660536)
XLA Ops:
  0.0 0.9 eq.68
  0.9 0.9 select_reduce_fusion.2
  1.8 0.7 compare_reduce_fusion
  2.5 0.2 convert_reduce_fusion.1
  2.7 0.2 convert_reduce_fusion
  2.9 0.1 select_reduce_fusion.3
  3.0 0.1 copy.52
  3.1 10.0 %all_to_all.14 = s32[8,1,2]{2,1,0:T(1,128)S(1)} all-to-all(s32[8,1,2]{2,1,0:T(1,128)S(1)} %copy.52), channel_id=1, replica_groups=mesh['mem'=8,'tp'=4] {'mem'}, dimensions={0} | all-to-all | bytes 128 | tf_op jit(solution)/shard_map/all_to_all | solution.py:170
  13.1 0.5 broadcast.442
  13.6 0.7 reduce.26
  14.3 0.1 reshape.380
  14.4 6.2 %gather_fusion.1 = bf16[16,2,128,512]{3,2,1,0:T(8,128)(2,1)} fusion(bf16[2,32,128,512]{3,2,1,0:T(8,128)(2,1)} %bitcast.91, s32[1024]{0:T(1024)S(1)} %pad_clamp_fusion), kind=kCustom, calls=%fused_computation.1 | custom fusion | bytes 8388672 | tf_op jit(solution)/shard_map/jit(_take)/gather | solution.py:168
  20.5 6.9 %all-to-all-start.1 = ((bf16[16,2,128,512]{3,2,1,0:T(8,128)(2,1)}), bf16[16,2,128,512]{3,2,1,0:T(8,128)(2,1)}, u32[]{:S(2)}, u32[]{:S(2)}) async-start(bf16[16,2,128,512]{3,2,1,0:T(8,128)(2,1)} %gather_fusion.1), calls=%async_computation.1 | async-start | bytes 8388608 | tf_op jit(solution)/shard_map/all_to_all | solution.py:176
  27.5 1.6 collective-permute-start.1
  29.1 0.2 collective-permute-start
  29.3 2.8 %scatter_fusion = pred[3,16]{1,0:T(4,128)(4,1)S(1)} fusion(pred[3,16]{1,0:T(4,128)(4,1)S(1)} %broadcast_in_dim.120, s32[48]{0:T(128)S(1)} %fusion.44, pred[48]{0:T(512)(128)(4,1)S(1)} %broadcast.407), kind=kCustom, calls=%fused_computation.2 | custom fusion | bytes 528 | tf_op jit(solution)/shard_map/scatter | solution.py:180
  32.2 0.1 slice_add_fusion
  32.3 0.7 fusion.33
  33.0 0.7 fusion.31
  33.7 4.3 %collective-permute-done.2 = bf16[96,2560]{1,0:T(8,128)(2,1)} collective-permute-done((bf16[96,2560]{1,0:T(8,128)(2,1)S(1)}, bf16[96,2560]{1,0:T(8,128)(2,1)}, u32[]{:S(2)}, u32[]{:S(2)}) %collective-permute-start.2) | collective-permute-done | bytes 491552 | tf_op jit(solution)/shard_map/ppermute | solution.py:95
  38.0 13.6 %collective-permute-done.1 = bf16[96,2560]{1,0:T(8,128)(2,1)} collective-permute-done((bf16[96,2560]{1,0:T(8,128)(2,1)S(1)}, bf16[96,2560]{1,0:T(8,128)(2,1)}, u32[]{:S(2)}, u32[]{:S(2)}) %collective-permute-start.1) | collective-permute-done | bytes 491552 | tf_op jit(solution)/shard_map/ppermute | solution.py:95
  51.7 0.0 collective-permute-done
  51.7 2.9 %pad_maximum_fusion = bf16[4,96,2560]{2,1,0:T(8,128)(2,1)} fusion(bf16[1,96,2560]{2,1,0:T(8,128)(2,1)} %bitcast.3, bf16[1,96,2560]{2,1,0:T(8,128)(2,1)} %bitcast.2, bf16[1,96,2560]{2,1,0:T(8,128)(2,1)} %bitcast.1, bf16[1,96,2560]{2,1,0:T(8,128)(2,1)S(1)} %bitcast.102), kind=kLoop, calls=%fused_computation.6 | loop fusion | flops 2949120 | bytes 3932160 | tf_op jit(solution)/shard_map/stack | solution.py:99
  54.6 3.5 %gather_fusion = bf16[4,96,2560]{2,1,0:T(8,128)(2,1)} fusion(bf16[4,96,2560]{2,1,0:T(8,128)(2,1)} %pad_maximum_fusion, s32[1024]{0:T(1024)S(1)} %pad_clamp_fusion.1), kind=kCustom, calls=%fused_computation | custom fusion | bytes 3932176 | tf_op jit(solution)/shard_map/jit(_take)/gather | solution.py:99
  58.1 8.1 %convolution_convert_fusion.q_ref = bf16[384,1536]{1,0:T(8,128)(2,1)} fusion(bf16[384,2560]{1,0:T(8,128)(2,1)} %bitcast.92, bf16[2560,1536]{1,0:T(8,128)(2,1)} %param.8), kind=kOutput, calls=%fused_computation.5 | convolution fusion | flops 3020488704 | bytes 11010048 | tf_op jit(solution)/shard_map/dot_general | solution.py:109
  66.3 2.4 %copy.53 = bf16[384,1536]{0,1:T(8,128)(2,1)} copy(bf16[384,1536]{1,0:T(8,128)(2,1)} %convolution_convert_fusion.q_ref) | data formatting | bytes 2359296 | tf_op jit(solution)/shard_map/convert_element_type | solution.py:114
  68.6 2.2 %fusion.55 = (bf16[256,4,1,128]{0,3,2,1:T(8,128)(2,1)}, bf16[256,4,1,128]{0,3,2,1:T(8,128)(2,1)}, bf16[256,4,1,128]{0,3,2,1:T(8,128)(2,1)S(1)}, bf16[256,4,1,128]{0,3,2,1:T(8,128)(2,1)S(1)}, bf16[256,4,1,128]{0,3,2,1:T(8,128)(2,1)}) fusion(bf16[384,4,3,128]{0,3,2,1:T(8,128)(2,1)} %bitcast.86), kind=kLoop, calls=%fused_computation.117 | loop fusion | bytes 2621440 | tf_op jit(solution)/shard_map/slice | solution.py:127
  70.8 1.1 copy.62
  71.9 1.8 %copy.64 = bf16[256,4,1,128]{3,0,1,2:T(8,128)(2,1)} copy(bf16[256,4,1,128]{0,3,2,1:T(8,128)(2,1)} %get-tuple-element.15) | data formatting | bytes 524288 | tf_op jit(solution)/shard_map/slice | solution.py:128
  73.7 1.8 %copy.63 = bf16[256,4,1,128]{3,0,1,2:T(8,128)(2,1)} copy(bf16[256,4,1,128]{0,3,2,1:T(8,128)(2,1)} %get-tuple-element.12) | data formatting | bytes 524288 | tf_op jit(solution)/shard_map/slice | solution.py:128
  75.5 1.8 %slice_bitcast_fusion.2 = (bf16[1,128,4,128]{1,3,2,0:T(8,128)(2,1)}, bf16[128,4,1,128]{0,3,2,1:T(8,128)(2,1)S(1)}, bf16[128,4,1,128]{0,3,2,1:T(8,128)(2,1)S(1)}, bf16[128,4,1,128]{0,3,2,1:T(8,128)(2,1)S(1)}) fusion(bf16[384,4,3,128]{0,3,2,1:T(8,128)(2,1)} %bitcast.87), kind=kLoop, calls=%fused_computation.56 | loop fusion | bytes 1048576 | tf_op jit(solution)/shard_map/slice | solution.py:135
  77.3 0.7 pad_maximum_fusion.3
  78.1 3.4 %collective-permute-start.3 = (bf16[2,128,512]{1,2,0:T(8,128)(2,1)}, bf16[2,128,512]{1,2,0:T(8,128)(2,1)}, u32[]{:S(2)}, u32[]{:S(2)}) collective-permute-start(bf16[2,128,512]{1,2,0:T(8,128)(2,1)} %pad_maximum_fusion.3), channel_id=1, source_target_pairs={{0,4},{4,8},{8,12},{12,16},{16,20},{20,24},{24,28},{1,5},{5,9},{9,... | collective-permute-start | bytes 786440 | tf_op jit(solution)/shard_map/ppermute | solution.py:20
  81.5 1.3 convolution_multiply_fusion
  82.8 1.0 copy-done.3
  83.8 0.4 fusion.57
  84.2 0.2 copy.59
  84.4 0.9 copy.61
  85.2 0.2 copy.58
  85.4 0.2 copy.60
  85.6 0.1 copy.73
  85.7 4.5 %convolution_bitcast_fusion = f32[2,128,4,128]{1,3,2,0:T(8,128)} fusion(bf16[2,128,4,128]{1,3,2,0:T(8,128)(2,1)} %copy.61, bf16[2,128,4,128]{1,3,2,0:T(8,128)(2,1)S(1)} %copy.60, f32[2,4,128]{2,1,0:T(4,128)S(1)} %fusion.57, f32[2,4,128,256]{3,2,1,0:T(8,128)} %copy-done.3, pred[2,128,256]{2,1,0:T(8,128)(4,1)} %fusion.31), kind=kOutput, calls=%fused_computation.18 | convolution fusion | flops 69469440 | bytes 2166784 | tf_op jit(solution)/shard_map/ngqk,nkgd->nqgd/dot_general | solution.py:44
  90.2 33.5 %collective-permute-done.3 = bf16[2,128,512]{1,2,0:T(8,128)(2,1)} collective-permute-done((bf16[2,128,512]{1,2,0:T(8,128)(2,1)}, bf16[2,128,512]{1,2,0:T(8,128)(2,1)}, u32[]{:S(2)}, u32[]{:S(2)}) %collective-permute-start.3) | collective-permute-done | bytes 262176 | tf_op jit(solution)/shard_map/ppermute | solution.py:20
  123.8 1.0 fusion.56
  124.7 0.1 copy.57
  124.9 1.2 convolution_multiply_fusion.1
  126.1 0.3 fusion.58
  126.4 0.3 convolution_bitcast_fusion.1
  126.7 0.1 pad_maximum_fusion.1
  126.8 1.2 copy.68
  128.0 2.1 %copy.81 = f32[48,8,4,128]{3,1,2,0:T(8,128)} copy(f32[48,8,4,128]{3,2,1,0:T(4,128)} %bitcast.90) | data formatting | bytes 1572864
  130.0 0.7 broadcast_in_dim.124
  130.7 0.7 broadcast_in_dim.131
  131.4 9.5 %shard_map.73 = bf16[384,512]{1,0:T(8,128)(2,1)} custom-call(bf16[384,1536]{1,0:T(8,128)(2,1)} %convolution_convert_fusion.q_ref, bf16[16,2,128,512]{3,2,1,0:T(8,128)(2,1)} %all-to-all-done.1.k_ref.v_ref, bf16[16,2,128,512]{3,2,1,0:T(8,128)(2,1)} %all-to-all-done.1.k_ref.v_ref, f32[3,1,2048]{2,1,0:T(1,128)} %bitcast.104, f32[384,512]{1,0:T(8,128)} %bitcast.89, ...), custom_call_target="tpu_custom_call" | custom-call | flops 1610612736 | bytes 5767168 | tf_op jit(solution)/shard_map/pallas_call | solution.py:71
  140.8 2.2 %fusion.59 = f32[384,2560]{1,0:T(8,128)S(1)} fusion(bf16[384,512]{1,0:T(8,128)(2,1)} %shard_map.73, bf16[512,2560]{1,0:T(8,128)(2,1)S(1)} %copy-done), kind=kOutput, calls=%fused_computation.121 | convolution fusion | flops 1006632960 | bytes 6946816 | tf_op jit(solution)/shard_map/dot_general | solution.py:189
  143.0 1.9 %copy-done.1 = f32[384,2560]{1,0:T(8,128)} copy-done((f32[384,2560]{1,0:T(8,128)}, f32[384,2560]{1,0:T(8,128)S(1)}, u32[]{:S(2)}) %copy-start.1) | copy-done | bytes 3932184
  144.9 1.1 fusion.13
  146.0 2.9 %collective-permute-done.4 = bf16[2,96,2560]{2,1,0:T(8,128)(2,1)} collective-permute-done((bf16[2,96,2560]{2,1,0:T(8,128)(2,1)}, bf16[2,96,2560]{2,1,0:T(8,128)(2,1)}, u32[]{:S(2)}, u32[]{:S(2)}) %collective-permute-start.4) | collective-permute-done | bytes 983072 | tf_op jit(solution)/shard_map/ppermute | solution.py:203
  148.9 2.0 %bitcast_add_fusion = f32[2,96,2560]{2,1,0:T(8,128)S(1)} fusion(bf16[2,96,2560]{2,1,0:T(8,128)(2,1)} %collective-permute-done.4, f32[2,2,96,2560]{3,2,1,0:T(8,128)} %bitcast.85, s32[]{:T(128)S(6)} %select_n.166), kind=kLoop, calls=%fused_computation.8 | loop fusion | flops 983040 | bytes 4915204 | tf_op jit(solution)/shard_map/add | solution.py:206
  150.9 1.3 copy-done.2
  152.2 0.1 fusion.23
  152.3 1.6 collective-permute-start.5
  153.8 11.8 %collective-permute-done.5 = bf16[96,2560]{1,0:T(8,128)(2,1)} collective-permute-done((bf16[96,2560]{1,0:T(8,128)(2,1)S(1)}, bf16[96,2560]{1,0:T(8,128)(2,1)}, u32[]{:S(2)}, u32[]{:S(2)}) %collective-permute-start.5) | collective-permute-done | bytes 491552 | tf_op jit(solution)/shard_map/ppermute | solution.py:211
  165.7 2.2 %fusion.14 = bf16[96,2560]{1,0:T(8,128)(2,1)} fusion(bf16[96,2560]{1,0:T(8,128)(2,1)} %collective-permute-done.5, f32[2,96,2560]{2,1,0:T(8,128)} %copy-done.2, s32[]{:T(128)S(6)} %select_n.169), kind=kLoop, calls=%fused_computation.24 | loop fusion | flops 737280 | bytes 1966084 | tf_op jit(solution)/shard_map/convert_element_type | solution.py:190
  (32 shorter events, 0.2 us)
Async XLA Ops:
  0.0 140.8 %copy-start = (bf16[512,2560]{1,0:T(8,128)(2,1)S(1)}, bf16[512,2560]{1,0:T(8,128)(2,1)}, u32[]{:S(2)}) copy-start(bf16[512,2560]{1,0:T(8,128)(2,1)} %param.9) | copy-start | bytes 7864324
  20.5 6.9 %copy-start.5 = (bf16[96,2560]{1,0:T(8,128)(2,1)S(1)}, bf16[96,2560]{1,0:T(8,128)(2,1)}, u32[]{:S(2)}) copy-start(bf16[96,2560]{1,0:T(8,128)(2,1)} %param.7) | copy-start | bytes 1474564
  20.5 11.7 %copy-start.9 = (f32[4]{0:T(128)S(1)}, f32[4]{0:T(128)}, u32[]{:S(2)}) copy-start(f32[4]{0:T(128)} %param.10) | copy-start | bytes 52
  20.5 109.5 %all-to-all-start.1 = ((bf16[16,2,128,512]{3,2,1,0:T(8,128)(2,1)}), bf16[16,2,128,512]{3,2,1,0:T(8,128)(2,1)}, u32[]{:S(2)}, u32[]{:S(2)}) async-start(bf16[16,2,128,512]{3,2,1,0:T(8,128)(2,1)} %gather_fusion.1), calls=%async_computation.1 | async-start | bytes 8388608 | tf_op jit(solution)/shard_map/all_to_all | solution.py:176
  27.5 10.6 %collective-permute-start.2 = (bf16[96,2560]{1,0:T(8,128)(2,1)S(1)}, bf16[96,2560]{1,0:T(8,128)(2,1)}, u32[]{:S(2)}, u32[]{:S(2)}) collective-permute-start(bf16[96,2560]{1,0:T(8,128)(2,1)S(1)} %copy-done.5), channel_id=1, source_target_pairs={{0,3},{1,0},{2,1},{3,2},{4,7},{5,4},{6,5},{7,6},{8,11},{9,8},{10,9... | collective-permute-start | bytes 1474568 | tf_op jit(solution)/shard_map/ppermute | solution.py:95
  27.5 24.2 %collective-permute-start.1 = (bf16[96,2560]{1,0:T(8,128)(2,1)S(1)}, bf16[96,2560]{1,0:T(8,128)(2,1)}, u32[]{:S(2)}, u32[]{:S(2)}) collective-permute-start(bf16[96,2560]{1,0:T(8,128)(2,1)S(1)} %copy-done.5), channel_id=1, source_target_pairs={{0,2},{1,3},{2,0},{3,1},{4,6},{5,7},{6,4},{7,5},{8,10},{9,11},{10,... | collective-permute-start | bytes 1474568 | tf_op jit(solution)/shard_map/ppermute | solution.py:95
  29.1 22.6 %collective-permute-start = (bf16[96,2560]{1,0:T(8,128)(2,1)S(1)}, bf16[96,2560]{1,0:T(8,128)(2,1)}, u32[]{:S(2)}, u32[]{:S(2)}) collective-permute-start(bf16[96,2560]{1,0:T(8,128)(2,1)S(1)} %copy-done.5), channel_id=1, source_target_pairs={{0,1},{1,2},{2,3},{3,0},{4,5},{5,6},{6,7},{7,4},{8,9},{9,10},{10,1... | collective-permute-start | bytes 1474568 | tf_op jit(solution)/shard_map/ppermute | solution.py:95
  75.5 8.2 %copy-start.8 = (pred[2,128,256]{2,1,0:T(8,128)(4,1)S(1)}, pred[2,128,256]{2,1,0:T(8,128)(4,1)}, u32[]{:S(2)}) copy-start(pred[2,128,256]{2,1,0:T(8,128)(4,1)} %fusion.31) | copy-start | bytes 196612
  78.1 45.7 %collective-permute-start.3 = (bf16[2,128,512]{1,2,0:T(8,128)(2,1)}, bf16[2,128,512]{1,2,0:T(8,128)(2,1)}, u32[]{:S(2)}, u32[]{:S(2)}) collective-permute-start(bf16[2,128,512]{1,2,0:T(8,128)(2,1)} %pad_maximum_fusion.3), channel_id=1, source_target_pairs={{0,4},{4,8},{8,12},{12,16},{16,20},{20,24},{24,28},{1,5},{5,9},{9,... | collective-permute-start | bytes 786440 | tf_op jit(solution)/shard_map/ppermute | solution.py:20
  82.8 1.0 copy-start.3
  85.7 40.4 %copy-start.6 = (pred[128,256]{1,0:T(8,128)(4,1)S(1)}, pred[128,256]{1,0:T(8,128)(4,1)}, u32[]{:S(2)}) copy-start(pred[128,256]{1,0:T(8,128)(4,1)} %get-tuple-element.18) | copy-start | bytes 98308
  90.2 36.2 %copy-start.7 = (bf16[1,128,4,128]{1,3,2,0:T(8,128)(2,1)S(1)}, bf16[1,128,4,128]{1,3,2,0:T(8,128)(2,1)}, u32[]{:S(2)}) copy-start(bf16[1,128,4,128]{1,3,2,0:T(8,128)(2,1)} %get-tuple-element.7) | copy-start | bytes 393220
  124.9 1.8 %copy-start.4 = (f32[2,128,4,128]{1,3,2,0:T(8,128)S(1)}, f32[2,128,4,128]{1,3,2,0:T(8,128)}, u32[]{:S(2)}) copy-start(f32[2,128,4,128]{1,3,2,0:T(8,128)} %convolution_bitcast_fusion) | copy-start | bytes 1572868
  143.0 1.9 %copy-start.1 = (f32[384,2560]{1,0:T(8,128)}, f32[384,2560]{1,0:T(8,128)S(1)}, u32[]{:S(2)}) copy-start(f32[384,2560]{1,0:T(8,128)S(1)} %fusion.59) | copy-start | bytes 11796484
  146.0 2.9 %collective-permute-start.4 = (bf16[2,96,2560]{2,1,0:T(8,128)(2,1)}, bf16[2,96,2560]{2,1,0:T(8,128)(2,1)}, u32[]{:S(2)}, u32[]{:S(2)}) collective-permute-start(bf16[2,96,2560]{2,1,0:T(8,128)(2,1)} %fusion.13), channel_id=1, source_target_pairs={{0,1},{1,0},{2,3},{3,2},{4,5},{5,4},{6,7},{7,6},{8,9},{9,8},{10,11... | collective-permute-start | bytes 2949128 | tf_op jit(solution)/shard_map/ppermute | solution.py:203
  150.9 1.3 copy-start.2
  152.3 13.4 %collective-permute-start.5 = (bf16[96,2560]{1,0:T(8,128)(2,1)S(1)}, bf16[96,2560]{1,0:T(8,128)(2,1)}, u32[]{:S(2)}, u32[]{:S(2)}) collective-permute-start(bf16[96,2560]{1,0:T(8,128)(2,1)S(1)} %fusion.23), channel_id=1, source_target_pairs={{0,2},{1,3},{2,0},{3,1},{4,6},{5,7},{6,4},{7,5},{8,10},{9,11},{10,... | collective-permute-start | bytes 1474568 | tf_op jit(solution)/shard_map/ppermute | solution.py:211

commit v10 on v9

--- a/solution.py
+++ b/solution.py
@@ -42,7 +42,7 @@
     )
     probs = softmax_rows(scores, allowed[:, None])
     return jnp.einsum(
-        "ngqk,nkgd->nqgd", probs, window_values, preferred_element_type=jnp.float32
+        "ngqk,nkgd->ngqd", probs, window_values, preferred_element_type=jnp.float32
     )
 
 
@@ -60,7 +60,7 @@
         weights = jnp.exp((scores - peak) * (HD ** (-0.5)))
         scale = 1.0 / jnp.sum(weights, axis=-1, keepdims=True)
         far = jnp.dot(weights.astype(jnp.bfloat16), values, preferred_element_type=jnp.float32)
-        o_ref[rows, :] = (mix * (far * scale) + (1.0 - mix) * near_ref[rows, :]).astype(o_ref.dtype)
+        o_ref[rows, :] = (mix * (far * scale) + (1.0 - mix) * near_ref[block, 0]).astype(o_ref.dtype)
 
 
 def far_attention(projected, fetched, bias, near_out, mixing):
@@ -76,7 +76,7 @@
             pl.BlockSpec((pool, 1, BLK, HD), lambda h: (0, 0, 0, h)),
             pl.BlockSpec((pool, 1, BLK, HD), lambda h: (0, 1, 0, h)),
             pl.BlockSpec((blocks, 1, pool * BLK), lambda h: (0, 0, 0)),
-            pl.BlockSpec((rows, HD), lambda h: (0, h)),
+            pl.BlockSpec((blocks, 1, BLK, HD), lambda h: (0, h, 0, 0)),
             pl.BlockSpec((1, HD), lambda h: (0, h)),
         ],
         out_specs=pl.BlockSpec((rows, HD), lambda h: (0, h)),
@@ -135,7 +135,7 @@
         jnp.concatenate([before[1][None], value_blocks[:1]], axis=1),
         first_row[:1] - BLK,
     )
-    near_out = jnp.concatenate([opening, later], axis=0).reshape(local_rows, groups, HD)
+    near_out = jnp.concatenate([opening, later], axis=0)
     blocks_here = retrieved.shape[0]
     entries = blocks_here * TOPB
     local_blocks = memory.shape[1] // BLK
@@ -184,10 +184,13 @@
     )
     mixing = jnp.repeat(jax.nn.sigmoid(gate_logit), HD).reshape(1, groups * HD)
     attended = far_attention(
-        projected_flat, fetched, bias, near_out.reshape(local_rows, groups * HD), mixing
+        projected_flat, fetched, bias, near_out, mixing
     )
     partial = jnp.dot(attended, output_weight, preferred_element_type=jnp.float32)
-    return reduce_over_tp(partial).astype(jnp.bfloat16)
+    half = partial.shape[1] // 2
+    return jnp.concatenate(
+        [reduce_over_tp(partial[:, :half]), reduce_over_tp(partial[:, half:])], axis=1
+    ).astype(jnp.bfloat16)
 
 
 def reduce_over_tp(partial):

time: 169 us -> 165 us (0.976)
  waiting for transfers between devices: 66.3 us -> 62.1 us
    unnamed x22, local copies, waits for them, and re-layouts: 6.34 us -> 3.19 us
    ppermute x1 -> x2, waiting for transfers between devices: 2.89 us -> 0.02 us  [reduce_over_tp(): lax.ppermute(other.astype(jnp.bfloat16), 'tp', [(t, t ^ 1) for t in range...]
    convert_element_type x1 -> x0, other arithmetic: 2.22 us -> none  [local(): return reduce_over_tp(partial).astype(jnp.bfloat16)]
    concatenate x1 -> x2, other arithmetic: 0.05 us -> 1.75 us  [the longest x1 0.94 us: local(): near_out = jnp.concatenate([opening, later], axis=0)]
    ppermute x1 -> x2, waiting for transfers between devices: 11.8 us -> 11 us  [reduce_over_tp(): lax.ppermute(outgoing.astype(jnp.bfloat16), 'tp', pairs).astype(jnp.float32)]
  transfers between devices with their start and end apart: 7 -> 9, of which waited for: 5 -> 5; matrix products, arithmetic and copies ran while one was open for 27% -> 30% of each run, Pallas kernels for 0% -> 0%
where the time goes in v10:
time: 165 us; the launch traced here: 164 us
  waiting for transfers between devices  62.1 us (38%)
  local copies, waits for them, and re-layouts  37.9 us (23%)
  matrix products  16.8 us (10%)
  starting transfers between devices  15 us (9%)
  other arithmetic  12.8 us (8%)
  blocking collectives  10 us (6%)
  Pallas kernels  9.47 us (6%)
    ppermute x1, waiting for transfers between devices, from_behind(): lax.ppermute(value, axis, [(source, source + steps) for source in range(i...  33.1 us
    ppermute x3, waiting for transfers between devices, gather_tp(): lax.ppermute(part, 'tp', [(t, (t + shift) % count) for t in range(count)])  18 us
    ppermute x2, waiting for transfers between devices, reduce_over_tp(): lax.ppermute(outgoing.astype(jnp.bfloat16), 'tp', pairs).astype(jnp.float32)  11 us
    all_to_all x1, blocking collectives, local(): lax.all_to_all(wanted_ids, 'mem', split_axis=0, concat_axis=0, tiled=True)  10 us
    pallas_call x1, Pallas kernels, far_attention(): pl.pallas_call(far_kernel, grid=(groups,), in_specs=[pl.BlockSpec((rows,...  9.47 us
    dot_general x1, matrix products, local(): jnp.dot(gather_tp(tokens), input_weight, preferred_element_type=jnp.float32)  8.14 us
    all_to_all x1, starting transfers between devices, local(): lax.all_to_all(picked, 'mem', split_axis=0, concat_axis=0, tiled=True)  6.94 us
    gather x1, local copies, waits for them, and re-layouts, local(): jnp.take(local_store, lax.all_to_all(wanted_ids, 'mem', split_axis=0, con...  6.17 us
  transfers between devices with their start and end apart: 9, of which 5 were waited for; matrix products, arithmetic and copies ran while one was open for 30% of the time, Pallas kernels for 0%

profile of v10, /device:TPU:16, one launch (start us, length us, event | category | flops | bytes accessed | tf_op | source)
XLA Modules:
  0.0 164.3 jit_solution(9273137826484094813)
XLA Ops:
  0.0 0.9 eq.70
  0.9 0.9 select_reduce_fusion.2
  1.8 0.7 compare_reduce_fusion
  2.5 0.2 convert_reduce_fusion.1
  2.7 0.2 convert_reduce_fusion
  2.9 0.1 select_reduce_fusion.3
  3.0 0.1 copy.50
  3.1 10.0 %all_to_all.14 = s32[8,1,2]{2,1,0:T(1,128)S(1)} all-to-all(s32[8,1,2]{2,1,0:T(1,128)S(1)} %copy.50), channel_id=1, replica_groups=mesh['mem'=8,'tp'=4] {'mem'}, dimensions={0} | all-to-all | bytes 128 | tf_op jit(solution)/shard_map/all_to_all | solution.py:170
  13.1 0.5 broadcast.442
  13.6 0.7 reduce.26
  14.3 0.1 reshape.386
  14.4 6.2 %gather_fusion.1 = bf16[16,2,128,512]{3,2,1,0:T(8,128)(2,1)} fusion(bf16[2,32,128,512]{3,2,1,0:T(8,128)(2,1)} %bitcast.94, s32[1024]{0:T(1024)S(1)} %pad_clamp_fusion), kind=kCustom, calls=%fused_computation.1 | custom fusion | bytes 8388672 | tf_op jit(solution)/shard_map/jit(_take)/gather | solution.py:168
  20.5 6.9 %all-to-all-start.1 = ((bf16[16,2,128,512]{3,2,1,0:T(8,128)(2,1)}), bf16[16,2,128,512]{3,2,1,0:T(8,128)(2,1)}, u32[]{:S(2)}, u32[]{:S(2)}) async-start(bf16[16,2,128,512]{3,2,1,0:T(8,128)(2,1)} %gather_fusion.1), calls=%async_computation.1 | async-start | bytes 8388608 | tf_op jit(solution)/shard_map/all_to_all | solution.py:176
  27.5 1.6 collective-permute-start.1
  29.1 0.2 collective-permute-start
  29.3 2.8 %scatter_fusion = pred[3,16]{1,0:T(4,128)(4,1)S(1)} fusion(pred[3,16]{1,0:T(4,128)(4,1)S(1)} %broadcast_in_dim.120, s32[48]{0:T(128)S(1)} %fusion.45, pred[48]{0:T(512)(128)(4,1)S(1)} %broadcast.407), kind=kCustom, calls=%fused_computation.2 | custom fusion | bytes 528 | tf_op jit(solution)/shard_map/scatter | solution.py:180
  32.2 0.1 slice_add_fusion
  32.3 0.7 fusion.34
  33.0 0.7 fusion.30
  33.7 4.3 %collective-permute-done.2 = bf16[96,2560]{1,0:T(8,128)(2,1)} collective-permute-done((bf16[96,2560]{1,0:T(8,128)(2,1)S(1)}, bf16[96,2560]{1,0:T(8,128)(2,1)}, u32[]{:S(2)}, u32[]{:S(2)}) %collective-permute-start.2) | collective-permute-done | bytes 491552 | tf_op jit(solution)/shard_map/ppermute | solution.py:95
  38.0 13.6 %collective-permute-done.1 = bf16[96,2560]{1,0:T(8,128)(2,1)} collective-permute-done((bf16[96,2560]{1,0:T(8,128)(2,1)S(1)}, bf16[96,2560]{1,0:T(8,128)(2,1)}, u32[]{:S(2)}, u32[]{:S(2)}) %collective-permute-start.1) | collective-permute-done | bytes 491552 | tf_op jit(solution)/shard_map/ppermute | solution.py:95
  51.7 2.9 %pad_maximum_fusion = bf16[4,96,2560]{2,1,0:T(8,128)(2,1)} fusion(bf16[1,96,2560]{2,1,0:T(8,128)(2,1)} %bitcast.3, bf16[1,96,2560]{2,1,0:T(8,128)(2,1)} %bitcast.2, bf16[1,96,2560]{2,1,0:T(8,128)(2,1)} %bitcast.1, bf16[1,96,2560]{2,1,0:T(8,128)(2,1)S(1)} %bitcast.104), kind=kLoop, calls=%fused_computation.6 | loop fusion | flops 2949120 | bytes 3932160 | tf_op jit(solution)/shard_map/stack | solution.py:99
  54.6 3.5 %gather_fusion = bf16[4,96,2560]{2,1,0:T(8,128)(2,1)} fusion(bf16[4,96,2560]{2,1,0:T(8,128)(2,1)} %pad_maximum_fusion, s32[1024]{0:T(1024)S(1)} %pad_clamp_fusion.1), kind=kCustom, calls=%fused_computation | custom fusion | bytes 3932176 | tf_op jit(solution)/shard_map/jit(_take)/gather | solution.py:99
  58.1 8.1 %convolution_convert_fusion.q_ref = bf16[384,1536]{1,0:T(8,128)(2,1)} fusion(bf16[384,2560]{1,0:T(8,128)(2,1)} %bitcast.95, bf16[2560,1536]{1,0:T(8,128)(2,1)} %param.8), kind=kOutput, calls=%fused_computation.5 | convolution fusion | flops 3020488704 | bytes 11010048 | tf_op jit(solution)/shard_map/dot_general | solution.py:109
  66.2 2.4 %copy.51 = bf16[384,1536]{0,1:T(8,128)(2,1)} copy(bf16[384,1536]{1,0:T(8,128)(2,1)} %convolution_convert_fusion.q_ref) | data formatting | bytes 2359296 | tf_op jit(solution)/shard_map/convert_element_type | solution.py:114
  68.6 2.2 %fusion.57 = (bf16[256,4,1,128]{0,3,2,1:T(8,128)(2,1)}, bf16[256,4,1,128]{0,3,2,1:T(8,128)(2,1)}, bf16[256,4,1,128]{0,3,2,1:T(8,128)(2,1)}, bf16[256,4,1,128]{0,3,2,1:T(8,128)(2,1)S(1)}, bf16[256,4,1,128]{0,3,2,1:T(8,128)(2,1)S(1)}) fusion(bf16[384,4,3,128]{0,3,2,1:T(8,128)(2,1)} %bitcast.87), kind=kLoop, calls=%fused_computation.122 | loop fusion | bytes 2621440 | tf_op jit(solution)/shard_map/slice | solution.py:127
  70.8 1.1 copy.57
  71.9 1.8 %copy.59 = bf16[256,4,1,128]{3,0,1,2:T(8,128)(2,1)} copy(bf16[256,4,1,128]{0,3,2,1:T(8,128)(2,1)} %get-tuple-element.14) | data formatting | bytes 524288 | tf_op jit(solution)/shard_map/slice | solution.py:128
  73.7 1.8 %copy.58 = bf16[256,4,1,128]{3,0,1,2:T(8,128)(2,1)} copy(bf16[256,4,1,128]{0,3,2,1:T(8,128)(2,1)} %get-tuple-element.15) | data formatting | bytes 524288 | tf_op jit(solution)/shard_map/slice | solution.py:128
  75.5 1.8 %fusion.56 = (bf16[128,4,1,128]{0,3,2,1:T(8,128)(2,1)S(1)}, bf16[128,4,1,128]{0,3,2,1:T(8,128)(2,1)}, bf16[128,4,1,128]{0,3,2,1:T(8,128)(2,1)S(1)}, bf16[128,4,1,128]{0,3,2,1:T(8,128)(2,1)S(1)}) fusion(bf16[384,4,3,128]{0,3,2,1:T(8,128)(2,1)} %bitcast.88), kind=kLoop, calls=%fused_computation.121 | loop fusion | bytes 1048576 | tf_op jit(solution)/shard_map/slice | solution.py:135
  77.4 0.7 pad_maximum_fusion.5
  78.1 3.5 %collective-permute-start.3 = (bf16[2,128,512]{1,2,0:T(8,128)(2,1)}, bf16[2,128,512]{1,2,0:T(8,128)(2,1)}, u32[]{:S(2)}, u32[]{:S(2)}) collective-permute-start(bf16[2,128,512]{1,2,0:T(8,128)(2,1)} %pad_maximum_fusion.5), channel_id=1, source_target_pairs={{0,4},{4,8},{8,12},{12,16},{16,20},{20,24},{24,28},{1,5},{5,9},{9,... | collective-permute-start | bytes 786440 | tf_op jit(solution)/shard_map/ppermute | solution.py:20
  81.6 1.3 convolution_multiply_fusion
  83.0 1.0 copy-done.3
  84.0 0.4 fusion.59
  84.4 0.8 copy.64
  85.2 0.9 copy.63
  86.1 0.1 copy.72
  86.2 0.8 copy.73
  87.0 3.7 %fusion.14 = f32[2,4,128,128]{3,2,1,0:T(8,128)S(1)} fusion(f32[2,4,128]{2,1,0:T(4,128)S(1)} %fusion.59, f32[2,4,128,256]{3,2,1,0:T(8,128)} %copy-done.3, pred[2,128,256]{2,1,0:T(8,128)(4,1)} %fusion.30, bf16[2,128,4,128]{3,1,0,2:T(8,128)(2,1)} %bitcast.105, bf16[2,128,4,128]{3,1,0,2:T(8,128)(2,1)} %bitcast.106), kind=kOutput, calls=%fused_computation.28 | convolution fusion | flops 69469440 | bytes 2166784 | tf_op jit(solution)/shard_map/ngqk,nkgd->ngqd/dot_general | solution.py:44
  90.7 33.1 %collective-permute-done.3 = bf16[2,128,512]{1,2,0:T(8,128)(2,1)} collective-permute-done((bf16[2,128,512]{1,2,0:T(8,128)(2,1)}, bf16[2,128,512]{1,2,0:T(8,128)(2,1)}, u32[]{:S(2)}, u32[]{:S(2)}) %collective-permute-start.3) | collective-permute-done | bytes 262176 | tf_op jit(solution)/shard_map/ppermute | solution.py:20
  123.8 1.6 fusion.58
  125.4 1.0 copy.54
  126.4 0.8 copy.56
  127.2 1.2 convolution_multiply_fusion.1
  128.4 1.1 fusion.60
  129.5 0.3 convolution_bitcast_fusion
  129.8 0.9 pad_maximum_fusion.1.near_ref
  130.8 0.7 broadcast_in_dim.124
  131.4 0.7 broadcast_in_dim.131
  132.1 9.5 %shard_map.73 = bf16[384,512]{1,0:T(8,128)(2,1)} custom-call(bf16[384,1536]{1,0:T(8,128)(2,1)} %convolution_convert_fusion.q_ref, bf16[16,2,128,512]{3,2,1,0:T(8,128)(2,1)} %all-to-all-done.1.k_ref.v_ref, bf16[16,2,128,512]{3,2,1,0:T(8,128)(2,1)} %all-to-all-done.1.k_ref.v_ref, f32[3,1,2048]{2,1,0:T(1,128)} %bitcast.108, ...), custom_call_target="tpu_custom_call" | custom-call | flops 1610612736 | bytes 5767168 | tf_op jit(solution)/shard_map/pallas_call | solution.py:71
  141.6 2.2 %fusion.61 = f32[384,2560]{1,0:T(8,128)S(1)} fusion(bf16[384,512]{1,0:T(8,128)(2,1)} %shard_map.73, bf16[512,2560]{1,0:T(8,128)(2,1)S(1)} %copy-done), kind=kOutput, calls=%fused_computation.126 | convolution fusion | flops 1006632960 | bytes 6946816 | tf_op jit(solution)/shard_map/dot_general | solution.py:189
  143.7 1.5 fusion.55
  145.3 1.3 copy-done.2
  146.6 0.1 collective-permute-start.6
  146.7 1.4 fusion.19
  148.2 0.5 collective-permute-start.4
  148.7 1.4 bitcast_add_fusion
  150.2 1.6 collective-permute-start.7
  151.7 0.1 bitcast_add_fusion.1
  151.9 0.6 collective-permute-start.5
  152.5 6.6 %collective-permute-done.7 = bf16[96,1280]{1,0:T(8,128)(2,1)S(1)} collective-permute-done((bf16[96,1280]{1,0:T(8,128)(2,1)S(1)}, bf16[96,1280]{1,0:T(8,128)(2,1)S(1)}, u32[]{:S(2)}, u32[]{:S(2)}) %collective-permute-start.7) | collective-permute-done | bytes 245792 | tf_op jit(solution)/shard_map/ppermute | solution.py:214
  159.1 4.4 %collective-permute-done.5 = bf16[96,1280]{1,0:T(8,128)(2,1)S(1)} collective-permute-done((bf16[96,1280]{1,0:T(8,128)(2,1)S(1)}, bf16[96,1280]{1,0:T(8,128)(2,1)S(1)}, u32[]{:S(2)}, u32[]{:S(2)}) %collective-permute-start.5) | collective-permute-done | bytes 245792 | tf_op jit(solution)/shard_map/ppermute | solution.py:214
  163.5 0.8 pad_maximum_fusion.4
  (40 shorter events, 0.4 us)
Async XLA Ops:
  0.0 141.6 %copy-start = (bf16[512,2560]{1,0:T(8,128)(2,1)S(1)}, bf16[512,2560]{1,0:T(8,128)(2,1)}, u32[]{:S(2)}) copy-start(bf16[512,2560]{1,0:T(8,128)(2,1)} %param.9) | copy-start | bytes 7864324
  20.5 6.9 %copy-start.5 = (bf16[96,2560]{1,0:T(8,128)(2,1)S(1)}, bf16[96,2560]{1,0:T(8,128)(2,1)}, u32[]{:S(2)}) copy-start(bf16[96,2560]{1,0:T(8,128)(2,1)} %param.7) | copy-start | bytes 1474564
  20.5 11.7 %copy-start.9 = (f32[4]{0:T(128)S(1)}, f32[4]{0:T(128)}, u32[]{:S(2)}) copy-start(f32[4]{0:T(128)} %param.10) | copy-start | bytes 52
  20.5 110.2 %all-to-all-start.1 = ((bf16[16,2,128,512]{3,2,1,0:T(8,128)(2,1)}), bf16[16,2,128,512]{3,2,1,0:T(8,128)(2,1)}, u32[]{:S(2)}, u32[]{:S(2)}) async-start(bf16[16,2,128,512]{3,2,1,0:T(8,128)(2,1)} %gather_fusion.1), calls=%async_computation.1 | async-start | bytes 8388608 | tf_op jit(solution)/shard_map/all_to_all | solution.py:176
  27.5 10.6 %collective-permute-start.2 = (bf16[96,2560]{1,0:T(8,128)(2,1)S(1)}, bf16[96,2560]{1,0:T(8,128)(2,1)}, u32[]{:S(2)}, u32[]{:S(2)}) collective-permute-start(bf16[96,2560]{1,0:T(8,128)(2,1)S(1)} %copy-done.5), channel_id=1, source_target_pairs={{0,3},{1,0},{2,1},{3,2},{4,7},{5,4},{6,5},{7,6},{8,11},{9,8},{10,9... | collective-permute-start | bytes 1474568 | tf_op jit(solution)/shard_map/ppermute | solution.py:95
  27.5 24.2 %collective-permute-start.1 = (bf16[96,2560]{1,0:T(8,128)(2,1)S(1)}, bf16[96,2560]{1,0:T(8,128)(2,1)}, u32[]{:S(2)}, u32[]{:S(2)}) collective-permute-start(bf16[96,2560]{1,0:T(8,128)(2,1)S(1)} %copy-done.5), channel_id=1, source_target_pairs={{0,2},{1,3},{2,0},{3,1},{4,6},{5,7},{6,4},{7,5},{8,10},{9,11},{10,... | collective-permute-start | bytes 1474568 | tf_op jit(solution)/shard_map/ppermute | solution.py:95
  29.1 22.6 %collective-permute-start = (bf16[96,2560]{1,0:T(8,128)(2,1)S(1)}, bf16[96,2560]{1,0:T(8,128)(2,1)}, u32[]{:S(2)}, u32[]{:S(2)}) collective-permute-start(bf16[96,2560]{1,0:T(8,128)(2,1)S(1)} %copy-done.5), channel_id=1, source_target_pairs={{0,1},{1,2},{2,3},{3,0},{4,5},{5,6},{6,7},{7,4},{8,9},{9,10},{10,1... | collective-permute-start | bytes 1474568 | tf_op jit(solution)/shard_map/ppermute | solution.py:95
  75.5 8.4 %copy-start.8 = (pred[2,128,256]{2,1,0:T(8,128)(4,1)S(1)}, pred[2,128,256]{2,1,0:T(8,128)(4,1)}, u32[]{:S(2)}) copy-start(pred[2,128,256]{2,1,0:T(8,128)(4,1)} %fusion.30) | copy-start | bytes 196612
  78.1 45.7 %collective-permute-start.3 = (bf16[2,128,512]{1,2,0:T(8,128)(2,1)}, bf16[2,128,512]{1,2,0:T(8,128)(2,1)}, u32[]{:S(2)}, u32[]{:S(2)}) collective-permute-start(bf16[2,128,512]{1,2,0:T(8,128)(2,1)} %pad_maximum_fusion.5), channel_id=1, source_target_pairs={{0,4},{4,8},{8,12},{12,16},{16,20},{20,24},{24,28},{1,5},{5,9},{9,... | collective-permute-start | bytes 786440 | tf_op jit(solution)/shard_map/ppermute | solution.py:20
  83.0 1.0 copy-start.3
  83.9 2.1 %copy-start.4 = (bf16[128,4,1,128]{0,3,2,1:T(8,128)(2,1)S(1)}, bf16[128,4,1,128]{0,3,2,1:T(8,128)(2,1)}, u32[]{:S(2)}) copy-start(bf16[128,4,1,128]{0,3,2,1:T(8,128)(2,1)} %get-tuple-element.10) | copy-start | bytes 393220
  127.2 2.3 %copy-start.6 = (bf16[128,4,1,128]{3,0,1,2:T(8,128)(2,1)S(1)}, bf16[128,4,1,128]{3,0,1,2:T(8,128)(2,1)}, u32[]{:S(2)}) copy-start(bf16[128,4,1,128]{3,0,1,2:T(8,128)(2,1)} %copy.73) | copy-start | bytes 393220
  127.2 2.3 %copy-start.7 = (bf16[1,128,4,128]{3,1,2,0:T(8,128)(2,1)S(1)}, bf16[1,128,4,128]{3,1,2,0:T(8,128)(2,1)}, u32[]{:S(2)}) copy-start(bf16[1,128,4,128]{3,1,2,0:T(8,128)(2,1)} %copy.56) | copy-start | bytes 393220
  145.3 1.3 copy-start.2
  146.6 2.1 %collective-permute-start.6 = (bf16[2,96,1280]{2,1,0:T(8,128)(2,1)S(1)}, bf16[2,96,1280]{2,1,0:T(8,128)(2,1)}, u32[]{:S(2)}, u32[]{:S(2)}) collective-permute-start(bf16[2,96,1280]{2,1,0:T(8,128)(2,1)S(1)} %fusion.20), channel_id=1, source_target_pairs={{0,1},{1,0},{2,3},{3,2},{4,5},{5,4},{6,7},{7,6},{8,9},{9,8},{10,11... | collective-permute-start | bytes 1474568 | tf_op jit(solution)/shard_map/ppermute | solution.py:206
  146.7 5.0 %copy-start.1 = (f32[384,1280]{1,0:T(8,128)S(1)}, f32[384,1280]{1,0:T(8,128)}, u32[]{:S(2)}) copy-start(f32[384,1280]{1,0:T(8,128)} %get-tuple-element.7) | copy-start | bytes 5898244
  148.2 3.6 %collective-permute-start.4 = (bf16[2,96,1280]{2,1,0:T(8,128)(2,1)S(1)}, bf16[2,96,1280]{2,1,0:T(8,128)(2,1)S(1)}, u32[]{:S(2)}, u32[]{:S(2)}) collective-permute-start(bf16[2,96,1280]{2,1,0:T(8,128)(2,1)S(1)} %fusion.19), channel_id=1, source_target_pairs={{0,1},{1,0},{2,3},{3,2},{4,5},{5,4},{6,7},{7,6},{8,9},{9,8},{10,11... | collective-permute-start | bytes 1474568 | tf_op jit(solution)/shard_map/ppermute | solution.py:206
  150.2 8.9 %collective-permute-start.7 = (bf16[96,1280]{1,0:T(8,128)(2,1)S(1)}, bf16[96,1280]{1,0:T(8,128)(2,1)S(1)}, u32[]{:S(2)}, u32[]{:S(2)}) collective-permute-start(bf16[96,1280]{1,0:T(8,128)(2,1)S(1)} %fusion.33), channel_id=1, source_target_pairs={{0,2},{1,3},{2,0},{3,1},{4,6},{5,7},{6,4},{7,5},{8,10},{9,11},{10,... | collective-permute-start | bytes 737288 | tf_op jit(solution)/shard_map/ppermute | solution.py:214
  151.9 11.6 %collective-permute-start.5 = (bf16[96,1280]{1,0:T(8,128)(2,1)S(1)}, bf16[96,1280]{1,0:T(8,128)(2,1)S(1)}, u32[]{:S(2)}, u32[]{:S(2)}) collective-permute-start(bf16[96,1280]{1,0:T(8,128)(2,1)S(1)} %fusion.32), channel_id=1, source_target_pairs={{0,2},{1,3},{2,0},{3,1},{4,6},{5,7},{6,4},{7,5},{8,10},{9,11},{10,... | collective-permute-start | bytes 737288 | tf_op jit(solution)/shard_map/ppermute | solution.py:214

commit v11 on v10

--- a/solution.py
+++ b/solution.py
@@ -46,24 +46,55 @@
     )
 
 
-def far_kernel(q_ref, k_ref, v_ref, bias_ref, near_ref, mix_ref, o_ref):
+def far_kernel(
+    q_ref, k0_ref, v0_ref, bk_ref, bv_ref, k_ref, v_ref, bias_ref, near_ref, start_ref, mix_ref, o_ref
+):
     pool = k_ref.shape[0]
     keys = k_ref[:, 0].reshape(pool * BLK, HD)
     values = v_ref[:, 0].reshape(pool * BLK, HD)
     mix = mix_ref[...]
+    contract = (((1,), (1,)), ((), ()))
+    first_query = q_ref[0:BLK, :]
+    query_index = lax.broadcasted_iota(jnp.int32, (BLK, BLK), 0)
+    key_index = lax.broadcasted_iota(jnp.int32, (BLK, BLK), 1)
+    allow_before = (key_index > query_index) & (start_ref[...] > 0.5)
+    allow_local = key_index <= query_index
+    score_before = lax.dot_general(
+        first_query, bk_ref[0], contract, preferred_element_type=jnp.float32
+    ) * (HD ** (-0.5))
+    score_local = lax.dot_general(
+        first_query, k0_ref[...], contract, preferred_element_type=jnp.float32
+    ) * (HD ** (-0.5))
+    near_peak = jnp.maximum(
+        jnp.max(jnp.where(allow_before, score_before, NEG_FILL), axis=-1, keepdims=True),
+        jnp.max(jnp.where(allow_local, score_local, NEG_FILL), axis=-1, keepdims=True),
+    )
+    weight_before = jnp.where(allow_before, jnp.exp(score_before - near_peak), 0.0)
+    weight_local = jnp.where(allow_local, jnp.exp(score_local - near_peak), 0.0)
+    near_total = jnp.sum(weight_before, axis=-1, keepdims=True) + jnp.sum(
+        weight_local, axis=-1, keepdims=True
+    )
+    first_near = jnp.dot(
+        (weight_before / near_total).astype(jnp.bfloat16), bv_ref[0],
+        preferred_element_type=jnp.float32,
+    ) + jnp.dot(
+        (weight_local / near_total).astype(jnp.bfloat16), v0_ref[...],
+        preferred_element_type=jnp.float32,
+    )
     for block in range(q_ref.shape[0] // BLK):
         rows = slice(block * BLK, (block + 1) * BLK)
         scores = lax.dot_general(
-            q_ref[rows, :], keys, (((1,), (1,)), ((), ())), preferred_element_type=jnp.float32
+            q_ref[rows, :], keys, contract, preferred_element_type=jnp.float32
         ) + bias_ref[block]
         peak = jnp.max(scores, axis=-1, keepdims=True)
         weights = jnp.exp((scores - peak) * (HD ** (-0.5)))
         scale = 1.0 / jnp.sum(weights, axis=-1, keepdims=True)
         far = jnp.dot(weights.astype(jnp.bfloat16), values, preferred_element_type=jnp.float32)
-        o_ref[rows, :] = (mix * (far * scale) + (1.0 - mix) * near_ref[block, 0]).astype(o_ref.dtype)
-
-
-def far_attention(projected, fetched, bias, near_out, mixing):
+        near = first_near if block == 0 else near_ref[block - 1, 0]
+        o_ref[rows, :] = (mix * (far * scale) + (1.0 - mix) * near).astype(o_ref.dtype)
+
+
+def far_attention(projected, before, fetched, bias, later, start, mixing):
     rows = projected.shape[0]
     blocks = rows // BLK
     pool = fetched.shape[0]
@@ -73,20 +104,25 @@
         grid=(groups,),
         in_specs=[
             pl.BlockSpec((rows, HD), lambda h: (0, h * 3)),
+            pl.BlockSpec((BLK, HD), lambda h: (0, h * 3 + 1)),
+            pl.BlockSpec((BLK, HD), lambda h: (0, h * 3 + 2)),
+            pl.BlockSpec((1, BLK, HD), lambda h: (0, 0, h)),
+            pl.BlockSpec((1, BLK, HD), lambda h: (1, 0, h)),
             pl.BlockSpec((pool, 1, BLK, HD), lambda h: (0, 0, 0, h)),
             pl.BlockSpec((pool, 1, BLK, HD), lambda h: (0, 1, 0, h)),
             pl.BlockSpec((blocks, 1, pool * BLK), lambda h: (0, 0, 0)),
-            pl.BlockSpec((blocks, 1, BLK, HD), lambda h: (0, h, 0, 0)),
+            pl.BlockSpec((blocks - 1, 1, BLK, HD), lambda h: (0, h, 0, 0)),
+            pl.BlockSpec((1, BLK), lambda h: (0, 0)),
             pl.BlockSpec((1, HD), lambda h: (0, h)),
         ],
         out_specs=pl.BlockSpec((rows, HD), lambda h: (0, h)),
         out_shape=jax.ShapeDtypeStruct((rows, groups * HD), jnp.bfloat16),
         cost_estimate=pl.CostEstimate(
-            flops=groups * blocks * 4 * BLK * pool * BLK * HD,
-            transcendentals=groups * blocks * BLK * pool * BLK,
+            flops=groups * (blocks * pool + 2) * 4 * BLK * BLK * HD,
+            transcendentals=groups * (blocks * pool + 2) * BLK * BLK,
             bytes_accessed=fetched.size * 2 + rows * groups * HD * 8,
         ),
-    )(projected, fetched, fetched, bias, near_out, mixing)
+    )(projected, projected, projected, before, before, fetched, fetched, bias, later, start, mixing)
 
 def gather_tp(part):
     count = lax.axis_size("tp")
@@ -117,7 +153,7 @@
     key_rows = projected[:, :, 1]
     value_rows = projected[:, :, 2]
     last_rows = jnp.stack([key_rows[-BLK:], value_rows[-BLK:]]).reshape(2, BLK, groups * HD)
-    before = from_behind(last_rows, "mem", 1).reshape(2, BLK, groups, HD)
+    before = from_behind(last_rows, "mem", 1)
     blocks_here = local_rows // BLK
     query_blocks = queries.reshape(blocks_here, BLK, groups, HD)
     key_blocks = key_rows.reshape(blocks_here, BLK, groups, HD)
@@ -129,13 +165,6 @@
         jnp.concatenate([value_blocks[:-1], value_blocks[1:]], axis=1),
         first_row[1:] - BLK,
     )
-    opening = near_part(
-        query_blocks[:1],
-        jnp.concatenate([before[0][None], key_blocks[:1]], axis=1),
-        jnp.concatenate([before[1][None], value_blocks[:1]], axis=1),
-        first_row[:1] - BLK,
-    )
-    near_out = jnp.concatenate([opening, later], axis=0)
     blocks_here = retrieved.shape[0]
     entries = blocks_here * TOPB
     local_blocks = memory.shape[1] // BLK
@@ -165,14 +194,15 @@
         ),
         axis=2,
     )
-    picked = jnp.take(
-        local_store,
-        lax.all_to_all(wanted_ids, "mem", split_axis=0, concat_axis=0, tiled=True).reshape(
-            holder_count * CAP
-        ),
-        axis=1,
-        mode="clip",
-    ).transpose(1, 0, 2, 3)
+    asked = lax.all_to_all(wanted_ids, "mem", split_axis=0, concat_axis=0, tiled=True).reshape(
+        holder_count * CAP
+    )
+    picked = jnp.stack(
+        [
+            lax.dynamic_index_in_dim(local_store, jnp.clip(asked[slot], 0, local_blocks - 1), 1, False)
+            for slot in range(holder_count * CAP)
+        ]
+    )
     fetched = lax.all_to_all(picked, "mem", split_axis=0, concat_axis=0, tiled=True)
     pool = holder_count * CAP
     row_of = entry_order // TOPB
@@ -184,7 +214,13 @@
     )
     mixing = jnp.repeat(jax.nn.sigmoid(gate_logit), HD).reshape(1, groups * HD)
     attended = far_attention(
-        projected_flat, fetched, bias, near_out, mixing
+        projected_flat,
+        before,
+        fetched,
+        bias,
+        later,
+        jnp.full((1, BLK), jnp.where(lax.axis_index("mem") > 0, 1.0, 0.0), jnp.float32),
+        mixing,
     )
     partial = jnp.dot(attended, output_weight, preferred_element_type=jnp.float32)
     half = partial.shape[1] // 2

time: 165 us -> 192 us (1.16)
  local copies, waits for them, and re-layouts: 37.9 us -> 53.9 us
  between operations: 0.33 us -> 10.3 us
    unnamed x22 -> x29, local copies, waits for them, and re-layouts: 3.19 us -> 27.3 us
    gather x1 -> x0, local copies, waits for them, and re-layouts: 6.17 us -> none  [local(): jnp.take(local_store, lax.all_to_all(wanted_ids, 'mem', split_axis=0, con...]
    slice x4 -> x2, local copies, waits for them, and re-layouts: 5.26 us -> 1.7 us  [the longest x1 0.99 us: local(): key_rows[-BLK:]]
    ppermute x1, waiting for transfers between devices: 33.1 us -> 35.1 us  [from_behind(): lax.ppermute(value, axis, [(source, source + steps) for source in range(i...]
    dot_general x2 -> x1, matrix products: 3.99 us -> 4.38 us  [near_part(): jnp.einsum('ngqk,nkgd->ngqd', probs, window_values, preferred_element_typ...]
  transfers between devices with their start and end apart: 9 -> 9, of which waited for: 5 -> 6; matrix products, arithmetic and copies ran while one was open for 30% -> 21% of each run, Pallas kernels for 0% -> 0%
where the time goes in v11:
time: 192 us; the launch traced here: 191 us
  waiting for transfers between devices  62.4 us (32%)
  local copies, waits for them, and re-layouts  53.9 us (28%)
  matrix products  16.1 us (8%)
  starting transfers between devices  16 us (8%)
  other arithmetic  11 us (6%)
  Pallas kernels  11 us (6%)
  between operations  10.3 us (5%)
  blocking collectives  10 us (5%)
    ppermute x1, waiting for transfers between devices, from_behind(): lax.ppermute(value, axis, [(source, source + steps) for source in range(i...  35.1 us
    unnamed x29, local copies, waits for them, and re-layouts  27.3 us
    ppermute x3, waiting for transfers between devices, gather_tp(): lax.ppermute(part, 'tp', [(t, (t + shift) % count) for t in range(count)])  16.2 us
    pallas_call x1, Pallas kernels, far_attention(): pl.pallas_call(far_kernel, grid=(groups,), in_specs=[pl.BlockSpec((rows,...  11 us
    ppermute x2, waiting for transfers between devices, reduce_over_tp(): lax.ppermute(outgoing.astype(jnp.bfloat16), 'tp', pairs).astype(jnp.float32)  11 us
    all_to_all x1, blocking collectives, local(): lax.all_to_all(wanted_ids, 'mem', split_axis=0, concat_axis=0, tiled=True)  10 us
    dot_general x1, matrix products, local(): jnp.dot(gather_tp(tokens), input_weight, preferred_element_type=jnp.float32)  8.14 us
    all_to_all x1, starting transfers between devices, local(): lax.all_to_all(picked, 'mem', split_axis=0, concat_axis=0, tiled=True)  6.94 us
  transfers between devices with their start and end apart: 9, of which 6 were waited for; matrix products, arithmetic and copies ran while one was open for 21% of the time, Pallas kernels for 0%

profile of v11, /device:TPU:16, one launch (start us, length us, event | category | flops | bytes accessed | tf_op | source)
XLA Modules:
  0.0 190.8 jit_solution(11840297195922731993)
XLA Ops:
  0.0 0.9 eq.70
  0.9 0.9 select_reduce_fusion.1
  1.8 0.7 compare_reduce_fusion
  2.7 0.2 convert_reduce_fusion
  3.1 10.0 %all_to_all.14 = s32[8,1,2]{2,1,0:T(1,128)S(1)} all-to-all(s32[8,1,2]{2,1,0:T(1,128)S(1)} %copy.94), channel_id=1, replica_groups=mesh['mem'=8,'tp'=4] {'mem'}, dimensions={0} | all-to-all | bytes 128 | tf_op jit(solution)/shard_map/all_to_all | solution.py:197
  13.1 0.5 broadcast.399
  13.6 0.7 reduce.22
  14.4 0.7 fusion.42
  25.1 1.7 bitcast_dynamic-update-slice_fusion.15
  26.7 1.7 bitcast_dynamic-update-slice_fusion.14
  28.4 1.7 bitcast_dynamic-update-slice_fusion.13
  30.1 1.7 bitcast_dynamic-update-slice_fusion.12
  31.8 1.7 bitcast_dynamic-update-slice_fusion.11
  33.5 1.7 bitcast_dynamic-update-slice_fusion.10
  35.1 1.7 bitcast_dynamic-update-slice_fusion.9
  36.8 1.7 bitcast_dynamic-update-slice_fusion.8
  38.5 1.7 bitcast_dynamic-update-slice_fusion.7
  40.2 1.7 bitcast_dynamic-update-slice_fusion.6
  41.8 1.7 bitcast_dynamic-update-slice_fusion.5
  43.5 1.7 bitcast_dynamic-update-slice_fusion.4
  45.2 1.7 bitcast_dynamic-update-slice_fusion.3
  46.9 1.7 bitcast_dynamic-update-slice_fusion.2
  48.5 1.7 bitcast_dynamic-update-slice_fusion.1
  50.2 1.7 bitcast_dynamic-update-slice_fusion
  51.9 6.9 %all-to-all-start.1 = ((bf16[16,2,128,512]{3,2,1,0:T(8,128)(2,1)}), bf16[16,2,128,512]{3,2,1,0:T(8,128)(2,1)}, u32[]{:S(2)}, u32[]{:S(2)}) async-start(bf16[16,2,128,512]{3,2,1,0:T(8,128)(2,1)} %bitcast_dynamic-update-slice_fusion), calls=%async_computation.1 | async-start | bytes 8388608 | tf_op jit(solution)/shard_map/all_to_all | solution.py:206
  58.8 1.6 collective-permute-start.1
  60.4 1.4 collective-permute-start.2
  61.8 2.8 %scatter_fusion = pred[3,16]{1,0:T(4,128)(4,1)S(1)} fusion(pred[3,16]{1,0:T(4,128)(4,1)S(1)} %broadcast_in_dim.93, s32[48]{0:T(128)S(1)} %fusion.32, pred[48]{0:T(512)(128)(4,1)S(1)} %broadcast.369), kind=kCustom, calls=%fused_computation.1 | custom fusion | bytes 528 | tf_op jit(solution)/shard_map/scatter | solution.py:210
  64.9 0.7 fusion.19
  65.7 6.2 %collective-permute-done = bf16[96,2560]{1,0:T(8,128)(2,1)} collective-permute-done((bf16[96,2560]{1,0:T(8,128)(2,1)S(1)}, bf16[96,2560]{1,0:T(8,128)(2,1)}, u32[]{:S(2)}, u32[]{:S(2)}) %collective-permute-start) | collective-permute-done | bytes 491552 | tf_op jit(solution)/shard_map/ppermute | solution.py:131
  71.8 1.2 collective-permute-done.1
  73.0 8.9 %collective-permute-done.2 = bf16[96,2560]{1,0:T(8,128)(2,1)} collective-permute-done((bf16[96,2560]{1,0:T(8,128)(2,1)S(1)}, bf16[96,2560]{1,0:T(8,128)(2,1)}, u32[]{:S(2)}, u32[]{:S(2)}) %collective-permute-start.2) | collective-permute-done | bytes 491552 | tf_op jit(solution)/shard_map/ppermute | solution.py:131
  81.9 2.9 %pad_maximum_fusion = bf16[4,96,2560]{2,1,0:T(8,128)(2,1)} fusion(bf16[1,96,2560]{2,1,0:T(8,128)(2,1)} %bitcast.3, bf16[1,96,2560]{2,1,0:T(8,128)(2,1)} %bitcast.2, bf16[1,96,2560]{2,1,0:T(8,128)(2,1)} %bitcast.1, bf16[1,96,2560]{2,1,0:T(8,128)(2,1)S(1)} %bitcast.177), kind=kLoop, calls=%fused_computation.4 | loop fusion | flops 2949120 | bytes 3932160 | tf_op jit(solution)/shard_map/stack | solution.py:135
  84.8 3.5 %gather_fusion = bf16[4,96,2560]{2,1,0:T(8,128)(2,1)} fusion(bf16[4,96,2560]{2,1,0:T(8,128)(2,1)} %pad_maximum_fusion, s32[1024]{0:T(1024)S(1)} %pad_clamp_fusion), kind=kCustom, calls=%fused_computation | custom fusion | bytes 3932176 | tf_op jit(solution)/shard_map/jit(_take)/gather | solution.py:135
  88.3 8.1 %convolution_convert_fusion.q_ref.k0_ref.v0_ref = bf16[384,1536]{1,0:T(8,128)(2,1)} fusion(bf16[384,2560]{1,0:T(8,128)(2,1)} %bitcast.171, bf16[2560,1536]{1,0:T(8,128)(2,1)} %param.8), kind=kOutput, calls=%fused_computation.3 | convolution fusion | flops 3020488704 | bytes 11010048 | tf_op jit(solution)/shard_map/dot_general | solution.py:145
  96.4 2.4 %copy.91 = bf16[384,1536]{0,1:T(8,128)(2,1)} copy(bf16[384,1536]{1,0:T(8,128)(2,1)} %convolution_convert_fusion.q_ref.k0_ref.v0_ref) | data formatting | bytes 2359296 | tf_op jit(solution)/shard_map/convert_element_type | solution.py:150
  98.8 2.1 %fusion.40 = (bf16[256,4,1,128]{0,3,2,1:T(8,128)(2,1)}, bf16[256,4,1,128]{0,3,2,1:T(8,128)(2,1)S(1)}, bf16[256,4,1,128]{0,3,2,1:T(8,128)(2,1)S(1)}, bf16[256,4,1...) fusion(bf16[384,4,3,128]{0,3,2,1:T(8,128)(2,1)} %bitcast.149), kind=kLoop, calls=%fused_computation.110 | loop fusion | bytes 2621440 | tf_op jit(solution)/shard_map/slice | solution.py:163
  101.0 1.8 copy.111
  102.8 1.8 copy.112
  104.6 0.8 copy.113
  105.4 1.0 fusion.41
  106.6 0.7 pad_maximum_fusion.4
  107.4 3.4 %collective-permute-start.3 = (bf16[2,128,512]{2,1,0:T(8,128)(2,1)}, bf16[2,128,512]{2,1,0:T(8,128)(2,1)S(1)}, u32[]{:S(2)}, u32[]{:S(2)}) collective-permute-start(bf16[2,128,512]{2,1,0:T(8,128)(2,1)} %pad_maximum_fusion.4), channel_id=1, source_target_pairs={{0,4},{4,8},{8,12},{12,16},{16,20},{20,24},{24,28},{1,5},{5,9},{9,... | collective-permute-start | bytes 786440 | tf_op jit(solution)/shard_map/ppermute | solution.py:20
  110.7 1.4 convolution_multiply_fusion
  112.2 1.0 copy-done.4
  113.1 1.3 fusion.43
  114.4 0.9 copy.117
  115.5 4.4 %fusion.9.near_ref = f32[2,4,128,128]{3,2,1,0:T(8,128)} fusion(f32[2,4,128]{2,1,0:T(4,128)S(1)} %fusion.43, f32[2,4,128,256]{3,2,1,0:T(8,128)} %copy-done.4, pred[2,128,256]{2,1,0:T(8,128)(4,1)} %fusion.19, bf16[2,128,4,128]{3,1,0,2:T(8,128)(2,1)S(1)} %bitcast.179, bf16[2,128,4,128]{3,1,0,2:T(8,128)(2,1)} %bitcast.178), kind=kOutput, calls=%fused_computation.18 | convolution fusion | flops 69469440 | bytes 2166784 | tf_op jit(solution)/shard_map/ngqk,nkgd->ngqd/dot_general | solution.py:44
  119.8 35.1 %collective-permute-done.3.bk_ref.bv_ref = bf16[2,128,512]{2,1,0:T(8,128)(2,1)S(1)} collective-permute-done((bf16[2,128,512]{2,1,0:T(8,128)(2,1)}, bf16[2,128,512]{2,1,0:T(8,128)(2,1)S(1)}, u32[]{:S(2)}, u32[]{:S(2)}) %collective-permute-start.3) | collective-permute-done | bytes 262176 | tf_op jit(solution)/shard_map/ppermute | solution.py:20
  155.0 0.7 broadcast_in_dim.97
  155.7 0.6 broadcast_in_dim.101.start_ref
  156.3 0.7 broadcast_in_dim.102
  156.9 11.0 %shard_map.73 = bf16[384,512]{1,0:T(8,128)(2,1)} custom-call(bf16[384,1536]{1,0:T(8,128)(2,1)} %convolution_convert_fusion.q_ref.k0_ref.v0_ref, bf16[384,1536]{1,0:T(8,128)(2,1)} %convolution_convert_fusion.q_ref.k0_ref.v0_ref, bf16[384,1536]{1,0:T(8,128)(2,1)} %convolution_convert_fusion.q_ref.k0_ref.v0_ref, bf16[2,128,512]{2,1,0:T(8,128)(2,1)} %copy-done.3, ...), custom_call_target="tpu_custom_call" | custom-call | flops 1677721600 | bytes 5767168 | tf_op jit(solution)/shard_map/pallas_call | solution.py:102
  168.0 2.2 %fusion.44 = f32[384,2560]{1,0:T(8,128)S(1)} fusion(bf16[384,512]{1,0:T(8,128)(2,1)} %shard_map.73, bf16[512,2560]{1,0:T(8,128)(2,1)S(1)} %copy-done), kind=kOutput, calls=%fused_computation.114 | convolution fusion | flops 1006632960 | bytes 6946816 | tf_op jit(solution)/shard_map/dot_general | solution.py:225
  170.2 1.5 fusion.39
  171.7 1.3 copy-done.2
  173.2 1.4 fusion.15
  174.6 0.5 collective-permute-start.6
  175.1 1.4 bitcast_add_fusion.1
  176.6 1.6 collective-permute-start.5
  178.3 0.6 collective-permute-start.7
  178.9 6.6 %collective-permute-done.5 = bf16[96,1280]{1,0:T(8,128)(2,1)S(1)} collective-permute-done((bf16[96,1280]{1,0:T(8,128)(2,1)S(1)}, bf16[96,1280]{1,0:T(8,128)(2,1)S(1)}, u32[]{:S(2)}, u32[]{:S(2)}) %collective-permute-start.5) | collective-permute-done | bytes 245792 | tf_op jit(solution)/shard_map/ppermute | solution.py:250
  185.5 4.4 %collective-permute-done.7 = bf16[96,1280]{1,0:T(8,128)(2,1)S(1)} collective-permute-done((bf16[96,1280]{1,0:T(8,128)(2,1)S(1)}, bf16[96,1280]{1,0:T(8,128)(2,1)S(1)}, u32[]{:S(2)}, u32[]{:S(2)}) %collective-permute-start.7) | collective-permute-done | bytes 245792 | tf_op jit(solution)/shard_map/ppermute | solution.py:250
  190.0 0.8 pad_maximum_fusion.3
  (43 shorter events, 1.5 us)
Async XLA Ops:
  0.0 168.0 %copy-start = (bf16[512,2560]{1,0:T(8,128)(2,1)S(1)}, bf16[512,2560]{1,0:T(8,128)(2,1)}, u32[]{:S(2)}) copy-start(bf16[512,2560]{1,0:T(8,128)(2,1)} %param.9) | copy-start | bytes 7864324
  51.9 6.9 %copy-start.5 = (bf16[96,2560]{1,0:T(8,128)(2,1)S(1)}, bf16[96,2560]{1,0:T(8,128)(2,1)}, u32[]{:S(2)}) copy-start(bf16[96,2560]{1,0:T(8,128)(2,1)} %param.7) | copy-start | bytes 1474564
  51.9 12.9 %copy-start.6 = (f32[4]{0:T(128)S(1)}, f32[4]{0:T(128)}, u32[]{:S(2)}) copy-start(f32[4]{0:T(128)} %param.10) | copy-start | bytes 52
  51.9 103.1 %all-to-all-start.1 = ((bf16[16,2,128,512]{3,2,1,0:T(8,128)(2,1)}), bf16[16,2,128,512]{3,2,1,0:T(8,128)(2,1)}, u32[]{:S(2)}, u32[]{:S(2)}) async-start(bf16[16,2,128,512]{3,2,1,0:T(8,128)(2,1)} %bitcast_dynamic-update-slice_fusion), calls=%async_computation.1 | async-start | bytes 8388608 | tf_op jit(solution)/shard_map/all_to_all | solution.py:206
  58.8 13.0 %collective-permute-start = (bf16[96,2560]{1,0:T(8,128)(2,1)S(1)}, bf16[96,2560]{1,0:T(8,128)(2,1)}, u32[]{:S(2)}, u32[]{:S(2)}) collective-permute-start(bf16[96,2560]{1,0:T(8,128)(2,1)S(1)} %copy-done.5), channel_id=1, source_target_pairs={{0,1},{1,2},{2,3},{3,0},{4,5},{5,6},{6,7},{7,4},{8,9},{9,10},{10,1... | collective-permute-start | bytes 1474568 | tf_op jit(solution)/shard_map/ppermute | solution.py:131
  58.8 14.2 %collective-permute-start.1 = (bf16[96,2560]{1,0:T(8,128)(2,1)S(1)}, bf16[96,2560]{1,0:T(8,128)(2,1)}, u32[]{:S(2)}, u32[]{:S(2)}) collective-permute-start(bf16[96,2560]{1,0:T(8,128)(2,1)S(1)} %copy-done.5), channel_id=1, source_target_pairs={{0,2},{1,3},{2,0},{3,1},{4,6},{5,7},{6,4},{7,5},{8,10},{9,11},{10,... | collective-permute-start | bytes 1474568 | tf_op jit(solution)/shard_map/ppermute | solution.py:131
  60.4 21.5 %collective-permute-start.2 = (bf16[96,2560]{1,0:T(8,128)(2,1)S(1)}, bf16[96,2560]{1,0:T(8,128)(2,1)}, u32[]{:S(2)}, u32[]{:S(2)}) collective-permute-start(bf16[96,2560]{1,0:T(8,128)(2,1)S(1)} %copy-done.5), channel_id=1, source_target_pairs={{0,3},{1,0},{2,1},{3,2},{4,7},{5,4},{6,5},{7,6},{8,11},{9,8},{10,9... | collective-permute-start | bytes 1474568 | tf_op jit(solution)/shard_map/ppermute | solution.py:131
  107.4 47.6 %collective-permute-start.3 = (bf16[2,128,512]{2,1,0:T(8,128)(2,1)}, bf16[2,128,512]{2,1,0:T(8,128)(2,1)S(1)}, u32[]{:S(2)}, u32[]{:S(2)}) collective-permute-start(bf16[2,128,512]{2,1,0:T(8,128)(2,1)} %pad_maximum_fusion.4), channel_id=1, source_target_pairs={{0,4},{4,8},{8,12},{12,16},{16,20},{20,24},{24,28},{1,5},{5,9},{9,... | collective-permute-start | bytes 786440 | tf_op jit(solution)/shard_map/ppermute | solution.py:20
  112.2 1.0 copy-start.4
  155.0 2.0 %copy-start.3 = (bf16[2,128,512]{2,1,0:T(8,128)(2,1)}, bf16[2,128,512]{2,1,0:T(8,128)(2,1)S(1)}, u32[]{:S(2)}) copy-start(bf16[2,128,512]{2,1,0:T(8,128)(2,1)S(1)} %collective-permute-done.3.bk_ref.bv_ref) | copy-start | bytes 786436
  171.7 1.3 copy-start.2
  173.0 2.1 %collective-permute-start.4 = (bf16[2,96,1280]{2,1,0:T(8,128)(2,1)S(1)}, bf16[2,96,1280]{2,1,0:T(8,128)(2,1)}, u32[]{:S(2)}, u32[]{:S(2)}) collective-permute-start(bf16[2,96,1280]{2,1,0:T(8,128)(2,1)S(1)} %fusion.14), channel_id=1, source_target_pairs={{0,1},{1,0},{2,3},{3,2},{4,5},{5,4},{6,7},{7,6},{8,9},{9,8},{10,11... | collective-permute-start | bytes 1474568 | tf_op jit(solution)/shard_map/ppermute | solution.py:242
  173.2 5.0 %copy-start.1 = (f32[384,1280]{1,0:T(8,128)S(1)}, f32[384,1280]{1,0:T(8,128)}, u32[]{:S(2)}) copy-start(f32[384,1280]{1,0:T(8,128)} %get-tuple-element.8) | copy-start | bytes 5898244
  174.6 3.6 %collective-permute-start.6 = (bf16[2,96,1280]{2,1,0:T(8,128)(2,1)S(1)}, bf16[2,96,1280]{2,1,0:T(8,128)(2,1)S(1)}, u32[]{:S(2)}, u32[]{:S(2)}) collective-permute-start(bf16[2,96,1280]{2,1,0:T(8,128)(2,1)S(1)} %fusion.15), channel_id=1, source_target_pairs={{0,1},{1,0},{2,3},{3,2},{4,5},{5,4},{6,7},{7,6},{8,9},{9,8},{10,11... | collective-permute-start | bytes 1474568 | tf_op jit(solution)/shard_map/ppermute | solution.py:242
  176.6 8.9 %collective-permute-start.5 = (bf16[96,1280]{1,0:T(8,128)(2,1)S(1)}, bf16[96,1280]{1,0:T(8,128)(2,1)S(1)}, u32[]{:S(2)}, u32[]{:S(2)}) collective-permute-start(bf16[96,1280]{1,0:T(8,128)(2,1)S(1)} %fusion.20), channel_id=1, source_target_pairs={{0,2},{1,3},{2,0},{3,1},{4,6},{5,7},{6,4},{7,5},{8,10},{9,11},{10,... | collective-permute-start | bytes 737288 | tf_op jit(solution)/shard_map/ppermute | solution.py:250
  178.3 11.6 %collective-permute-start.7 = (bf16[96,1280]{1,0:T(8,128)(2,1)S(1)}, bf16[96,1280]{1,0:T(8,128)(2,1)S(1)}, u32[]{:S(2)}, u32[]{:S(2)}) collective-permute-start(bf16[96,1280]{1,0:T(8,128)(2,1)S(1)} %fusion.21), channel_id=1, source_target_pairs={{0,2},{1,3},{2,0},{3,1},{4,6},{5,7},{6,4},{7,5},{8,10},{9,11},{10,... | collective-permute-start | bytes 737288 | tf_op jit(solution)/shard_map/ppermute | solution.py:250

commit v12 on v11

--- a/solution.py
+++ b/solution.py
@@ -194,15 +194,14 @@
         ),
         axis=2,
     )
-    asked = lax.all_to_all(wanted_ids, "mem", split_axis=0, concat_axis=0, tiled=True).reshape(
-        holder_count * CAP
-    )
-    picked = jnp.stack(
-        [
-            lax.dynamic_index_in_dim(local_store, jnp.clip(asked[slot], 0, local_blocks - 1), 1, False)
-            for slot in range(holder_count * CAP)
-        ]
-    )
+    picked = jnp.take(
+        local_store,
+        lax.all_to_all(wanted_ids, "mem", split_axis=0, concat_axis=0, tiled=True).reshape(
+            holder_count * CAP
+        ),
+        axis=1,
+        mode="clip",
+    ).transpose(1, 0, 2, 3)
     fetched = lax.all_to_all(picked, "mem", split_axis=0, concat_axis=0, tiled=True)
     pool = holder_count * CAP
     row_of = entry_order // TOPB

time: 192 us -> 160 us (0.83)
  local copies, waits for them, and re-layouts: 53.9 us -> 33.2 us
  between operations: 10.3 us -> 0.29 us
    unnamed x29 -> x16, local copies, waits for them, and re-layouts: 27.3 us -> 2.26 us
    gather x0 -> x1, local copies, waits for them, and re-layouts: none -> 6.17 us  [local(): jnp.take(local_store, lax.all_to_all(wanted_ids, 'mem', split_axis=0, con...]
  transfers between devices with their start and end apart: 9 -> 9, of which waited for: 6 -> 6; matrix products, arithmetic and copies ran while one was open for 21% -> 26% of each run, Pallas kernels for 0% -> 0%
where the time goes in v12:
time: 160 us; the launch traced here: 159 us
  waiting for transfers between devices  61.4 us (38%)
  local copies, waits for them, and re-layouts  33.2 us (21%)
  starting transfers between devices  16.3 us (10%)
  matrix products  16.1 us (10%)
  other arithmetic  11.1 us (7%)
  Pallas kernels  11 us (7%)
  blocking collectives  10 us (6%)
    ppermute x1, waiting for transfers between devices, from_behind(): lax.ppermute(value, axis, [(source, source + steps) for source in range(i...  33.4 us
    ppermute x3, waiting for transfers between devices, gather_tp(): lax.ppermute(part, 'tp', [(t, (t + shift) % count) for t in range(count)])  17 us
    pallas_call x1, Pallas kernels, far_attention(): pl.pallas_call(far_kernel, grid=(groups,), in_specs=[pl.BlockSpec((rows,...  11 us
    ppermute x2, waiting for transfers between devices, reduce_over_tp(): lax.ppermute(outgoing.astype(jnp.bfloat16), 'tp', pairs).astype(jnp.float32)  11 us
    all_to_all x1, blocking collectives, local(): lax.all_to_all(wanted_ids, 'mem', split_axis=0, concat_axis=0, tiled=True)  10 us
    dot_general x1, matrix products, local(): jnp.dot(gather_tp(tokens), input_weight, preferred_element_type=jnp.float32)  8.14 us
    all_to_all x1, starting transfers between devices, local(): lax.all_to_all(picked, 'mem', split_axis=0, concat_axis=0, tiled=True)  6.94 us
    gather x1, local copies, waits for them, and re-layouts, local(): jnp.take(local_store, lax.all_to_all(wanted_ids, 'mem', split_axis=0, con...  6.17 us
  transfers between devices with their start and end apart: 9, of which 6 were waited for; matrix products, arithmetic and copies ran while one was open for 26% of the time, Pallas kernels for 0%

profile of v12, /device:TPU:16, one launch (start us, length us, event | category | flops | bytes accessed | tf_op | source)
XLA Modules:
  0.0 159.5 jit_solution(4553901929945657281)
XLA Ops:
  0.0 0.9 eq.70
  0.9 0.9 select_reduce_fusion.1
  1.8 0.2 convert_reduce_fusion.1
  2.0 0.7 compare_reduce_fusion
  2.7 0.2 convert_reduce_fusion
  2.9 0.1 select_reduce_fusion.2
  3.0 0.1 copy.46
  3.1 10.0 %all_to_all.14 = s32[8,1,2]{2,1,0:T(1,128)S(1)} all-to-all(s32[8,1,2]{2,1,0:T(1,128)S(1)} %copy.46), channel_id=1, replica_groups=mesh['mem'=8,'tp'=4] {'mem'}, dimensions={0} | all-to-all | bytes 128 | tf_op jit(solution)/shard_map/all_to_all | solution.py:199
  13.1 0.5 broadcast.403
  13.6 0.7 reduce.22
  14.3 0.1 reshape.307
  14.4 6.2 %gather_fusion.1 = bf16[16,2,128,512]{3,2,1,0:T(8,128)(2,1)} fusion(bf16[2,32,128,512]{3,2,1,0:T(8,128)(2,1)} %bitcast.76, s32[1024]{0:T(1024)S(1)} %pad_clamp_fusion), kind=kCustom, calls=%fused_computation.1 | custom fusion | bytes 8388672 | tf_op jit(solution)/shard_map/jit(_take)/gather | solution.py:197
  20.5 6.9 %all-to-all-start.1 = ((bf16[16,2,128,512]{3,2,1,0:T(8,128)(2,1)}), bf16[16,2,128,512]{3,2,1,0:T(8,128)(2,1)}, u32[]{:S(2)}, u32[]{:S(2)}) async-start(bf16[16,2,128,512]{3,2,1,0:T(8,128)(2,1)} %gather_fusion.1), calls=%async_computation.1 | async-start | bytes 8388608 | tf_op jit(solution)/shard_map/all_to_all | solution.py:205
  27.5 0.0 collective-permute-start
  27.5 1.7 %collective-permute-start.2 = (bf16[96,2560]{1,0:T(8,128)(2,1)S(1)}, bf16[96,2560]{1,0:T(8,128)(2,1)}, u32[]{:S(2)}, u32[]{:S(2)}) collective-permute-start(bf16[96,2560]{1,0:T(8,128)(2,1)S(1)} %copy-done.5), channel_id=1, source_target_pairs={{0,3},{1,0},{2,1},{3,2},{4,7},{5,4},{6,5},{7,6},{8,11},{9,8},{10,9... | collective-permute-start | bytes 1474568 | tf_op jit(solution)/shard_map/ppermute | solution.py:131
  29.2 1.5 collective-permute-start.1
  30.8 2.8 %scatter_fusion = pred[3,16]{1,0:T(4,128)(4,1)S(1)} fusion(pred[3,16]{1,0:T(4,128)(4,1)S(1)} %broadcast_in_dim.98, s32[48]{0:T(128)S(1)} %fusion.32, pred[48]{0:T(512)(128)(4,1)S(1)} %broadcast.369), kind=kCustom, calls=%fused_computation.2 | custom fusion | bytes 528 | tf_op jit(solution)/shard_map/scatter | solution.py:209
  33.7 0.1 slice_add_fusion
  33.8 0.1 fusion.22
  33.9 0.7 fusion.19
  34.6 4.6 %collective-permute-done = bf16[96,2560]{1,0:T(8,128)(2,1)} collective-permute-done((bf16[96,2560]{1,0:T(8,128)(2,1)S(1)}, bf16[96,2560]{1,0:T(8,128)(2,1)}, u32[]{:S(2)}, u32[]{:S(2)}) %collective-permute-start) | collective-permute-done | bytes 491552 | tf_op jit(solution)/shard_map/ppermute | solution.py:131
  39.2 1.6 collective-permute-done.2
  40.8 10.8 %collective-permute-done.1 = bf16[96,2560]{1,0:T(8,128)(2,1)} collective-permute-done((bf16[96,2560]{1,0:T(8,128)(2,1)S(1)}, bf16[96,2560]{1,0:T(8,128)(2,1)}, u32[]{:S(2)}, u32[]{:S(2)}) %collective-permute-start.1) | collective-permute-done | bytes 491552 | tf_op jit(solution)/shard_map/ppermute | solution.py:131
  51.6 2.9 %pad_maximum_fusion = bf16[4,96,2560]{2,1,0:T(8,128)(2,1)} fusion(bf16[1,96,2560]{2,1,0:T(8,128)(2,1)} %bitcast.3, bf16[1,96,2560]{2,1,0:T(8,128)(2,1)} %bitcast.2, bf16[1,96,2560]{2,1,0:T(8,128)(2,1)} %bitcast.1, bf16[1,96,2560]{2,1,0:T(8,128)(2,1)S(1)} %bitcast.83), kind=kLoop, calls=%fused_computation.5 | loop fusion | flops 2949120 | bytes 3932160 | tf_op jit(solution)/shard_map/stack | solution.py:135
  54.6 3.5 %gather_fusion = bf16[4,96,2560]{2,1,0:T(8,128)(2,1)} fusion(bf16[4,96,2560]{2,1,0:T(8,128)(2,1)} %pad_maximum_fusion, s32[1024]{0:T(1024)S(1)} %pad_clamp_fusion.1), kind=kCustom, calls=%fused_computation | custom fusion | bytes 3932176 | tf_op jit(solution)/shard_map/jit(_take)/gather | solution.py:135
  58.0 8.1 %convolution_convert_fusion.q_ref.k0_ref.v0_ref = bf16[384,1536]{1,0:T(8,128)(2,1)} fusion(bf16[384,2560]{1,0:T(8,128)(2,1)} %bitcast.77, bf16[2560,1536]{1,0:T(8,128)(2,1)} %param.8), kind=kOutput, calls=%fused_computation.4 | convolution fusion | flops 3020488704 | bytes 11010048 | tf_op jit(solution)/shard_map/dot_general | solution.py:145
  66.2 2.4 %copy.43 = bf16[384,1536]{0,1:T(8,128)(2,1)} copy(bf16[384,1536]{1,0:T(8,128)(2,1)} %convolution_convert_fusion.q_ref.k0_ref.v0_ref) | data formatting | bytes 2359296 | tf_op jit(solution)/shard_map/convert_element_type | solution.py:150
  68.6 1.0 fusion.41
  69.6 0.1 copy.59
  69.7 0.8 copy.60
  70.5 2.2 %fusion.40 = (bf16[256,4,1,128]{0,3,2,1:T(8,128)(2,1)}, bf16[256,4,1,128]{0,3,2,1:T(8,128)(2,1)S(1)}, bf16[256,4,1,128]{0,3,2,1:T(8,128)(2,1)S(1)}, bf16[256,4,1...) fusion(bf16[384,4,3,128]{0,3,2,1:T(8,128)(2,1)} %bitcast.71), kind=kLoop, calls=%fused_computation.96 | loop fusion | bytes 2621440 | tf_op jit(solution)/shard_map/slice | solution.py:163
  72.6 1.8 %copy.47 = bf16[256,4,1,128]{3,0,1,2:T(8,128)(2,1)} copy(bf16[256,4,1,128]{0,3,2,1:T(8,128)(2,1)} %get-tuple-element.9) | data formatting | bytes 524288 | tf_op jit(solution)/shard_map/slice | solution.py:163
  74.4 1.8 %copy.49 = bf16[256,4,1,128]{3,0,1,2:T(8,128)(2,1)} copy(bf16[256,4,1,128]{0,3,2,1:T(8,128)(2,1)} %get-tuple-element.12) | data formatting | bytes 524288 | tf_op jit(solution)/shard_map/slice | solution.py:164
  76.2 0.8 copy.48
  77.0 1.7 %pad_maximum_fusion.4 = bf16[2,128,512]{2,1,0:T(8,128)(2,1)} fusion(bf16[1,128,512]{2,1,0:T(8,128)(2,1)} %copy.60, bf16[1,128,512]{2,1,0:T(8,128)(2,1)S(1)} %copy.59), kind=kLoop, calls=%fused_computation.33 | loop fusion | flops 131072 | bytes 524288 | tf_op jit(solution)/shard_map/stack | solution.py:155
  78.7 3.4 %collective-permute-start.3 = (bf16[2,128,512]{2,1,0:T(8,128)(2,1)}, bf16[2,128,512]{2,1,0:T(8,128)(2,1)S(1)}, u32[]{:S(2)}, u32[]{:S(2)}) collective-permute-start(bf16[2,128,512]{2,1,0:T(8,128)(2,1)} %pad_maximum_fusion.4), channel_id=1, source_target_pairs={{0,4},{4,8},{8,12},{12,16},{16,20},{20,24},{24,28},{1,5},{5,9},{9,... | collective-permute-start | bytes 786440 | tf_op jit(solution)/shard_map/ppermute | solution.py:20
  82.0 1.4 convolution_multiply_fusion
  83.5 1.0 copy-done.4
  84.4 0.4 fusion.42
  84.8 0.8 copy.54
  85.7 0.2 copy.53
  85.9 4.4 %fusion.9.near_ref = f32[2,4,128,128]{3,2,1,0:T(8,128)} fusion(f32[2,4,128]{2,1,0:T(4,128)S(1)} %fusion.42, f32[2,4,128,256]{3,2,1,0:T(8,128)} %copy-done.4, pred[2,128,256]{2,1,0:T(8,128)(4,1)} %fusion.19, bf16[2,128,4,128]{3,1,0,2:T(8,128)(2,1)} %bitcast.84, bf16[2,128,4,128]{3,1,0,2:T(8,128)(2,1)S(1)} %bitcast.85), kind=kOutput, calls=%fused_computation.19 | convolution fusion | flops 69469440 | bytes 2166784 | tf_op jit(solution)/shard_map/ngqk,nkgd->ngqd/dot_general | solution.py:44
  90.2 33.4 %collective-permute-done.3.bk_ref.bv_ref = bf16[2,128,512]{2,1,0:T(8,128)(2,1)S(1)} collective-permute-done((bf16[2,128,512]{2,1,0:T(8,128)(2,1)}, bf16[2,128,512]{2,1,0:T(8,128)(2,1)S(1)}, u32[]{:S(2)}, u32[]{:S(2)}) %collective-permute-start.3) | collective-permute-done | bytes 262176 | tf_op jit(solution)/shard_map/ppermute | solution.py:20
  123.7 0.0 all-to-all-done.1.k_ref.v_ref
  123.7 0.6 broadcast_in_dim.106.start_ref
  124.3 0.7 broadcast_in_dim.107
  124.9 0.7 broadcast_in_dim.102
  125.6 11.0 %shard_map.73 = bf16[384,512]{1,0:T(8,128)(2,1)} custom-call(bf16[384,1536]{1,0:T(8,128)(2,1)} %convolution_convert_fusion.q_ref.k0_ref.v0_ref, bf16[384,1536]{1,0:T(8,128)(2,1)} %convolution_convert_fusion.q_ref.k0_ref.v0_ref, bf16[384,1536]{1,0:T(8,128)(2,1)} %convolution_convert_fusion.q_ref.k0_ref.v0_ref, bf16[2,128,512]{2,1,0:T(8,128)(2,1)} %copy-done.3, ...), custom_call_target="tpu_custom_call" | custom-call | flops 1677721600 | bytes 5767168 | tf_op jit(solution)/shard_map/pallas_call | solution.py:102
  136.7 2.2 %fusion.43 = f32[384,2560]{1,0:T(8,128)S(1)} fusion(bf16[384,512]{1,0:T(8,128)(2,1)} %shard_map.73, bf16[512,2560]{1,0:T(8,128)(2,1)S(1)} %copy-done), kind=kOutput, calls=%fused_computation.99 | convolution fusion | flops 1006632960 | bytes 6946816 | tf_op jit(solution)/shard_map/dot_general | solution.py:224
  138.8 1.5 fusion.39
  140.4 1.3 copy-done.2
  141.7 0.1 fusion.14
  141.7 0.1 collective-permute-start.4
  141.9 1.4 fusion.15
  143.3 0.5 collective-permute-start.6
  143.8 0.0 collective-permute-done.4
  143.8 1.4 bitcast_add_fusion.1
  145.3 1.6 collective-permute-start.5
  146.8 0.0 collective-permute-done.6
  146.9 0.1 bitcast_add_fusion
  147.0 0.6 collective-permute-start.7
  147.6 6.6 %collective-permute-done.5 = bf16[96,1280]{1,0:T(8,128)(2,1)S(1)} collective-permute-done((bf16[96,1280]{1,0:T(8,128)(2,1)S(1)}, bf16[96,1280]{1,0:T(8,128)(2,1)S(1)}, u32[]{:S(2)}, u32[]{:S(2)}) %collective-permute-start.5) | collective-permute-done | bytes 245792 | tf_op jit(solution)/shard_map/ppermute | solution.py:249
  154.2 4.4 %collective-permute-done.7 = bf16[96,1280]{1,0:T(8,128)(2,1)S(1)} collective-permute-done((bf16[96,1280]{1,0:T(8,128)(2,1)S(1)}, bf16[96,1280]{1,0:T(8,128)(2,1)S(1)}, u32[]{:S(2)}, u32[]{:S(2)}) %collective-permute-start.7) | collective-permute-done | bytes 245792 | tf_op jit(solution)/shard_map/ppermute | solution.py:249
  158.6 0.8 pad_maximum_fusion.3
  (30 shorter events, 0.3 us)
Async XLA Ops:
  0.0 136.7 %copy-start = (bf16[512,2560]{1,0:T(8,128)(2,1)S(1)}, bf16[512,2560]{1,0:T(8,128)(2,1)}, u32[]{:S(2)}) copy-start(bf16[512,2560]{1,0:T(8,128)(2,1)} %param.9) | copy-start | bytes 7864324
  20.5 6.9 %copy-start.5 = (bf16[96,2560]{1,0:T(8,128)(2,1)S(1)}, bf16[96,2560]{1,0:T(8,128)(2,1)}, u32[]{:S(2)}) copy-start(bf16[96,2560]{1,0:T(8,128)(2,1)} %param.7) | copy-start | bytes 1474564
  20.5 13.2 %copy-start.7 = (f32[4]{0:T(128)S(1)}, f32[4]{0:T(128)}, u32[]{:S(2)}) copy-start(f32[4]{0:T(128)} %param.10) | copy-start | bytes 52
  20.5 103.1 %all-to-all-start.1 = ((bf16[16,2,128,512]{3,2,1,0:T(8,128)(2,1)}), bf16[16,2,128,512]{3,2,1,0:T(8,128)(2,1)}, u32[]{:S(2)}, u32[]{:S(2)}) async-start(bf16[16,2,128,512]{3,2,1,0:T(8,128)(2,1)} %gather_fusion.1), calls=%async_computation.1 | async-start | bytes 8388608 | tf_op jit(solution)/shard_map/all_to_all | solution.py:205
  27.5 11.7 %collective-permute-start = (bf16[96,2560]{1,0:T(8,128)(2,1)S(1)}, bf16[96,2560]{1,0:T(8,128)(2,1)}, u32[]{:S(2)}, u32[]{:S(2)}) collective-permute-start(bf16[96,2560]{1,0:T(8,128)(2,1)S(1)} %copy-done.5), channel_id=1, source_target_pairs={{0,1},{1,2},{2,3},{3,0},{4,5},{5,6},{6,7},{7,4},{8,9},{9,10},{10,1... | collective-permute-start | bytes 1474568 | tf_op jit(solution)/shard_map/ppermute | solution.py:131
  27.5 13.3 %collective-permute-start.2 = (bf16[96,2560]{1,0:T(8,128)(2,1)S(1)}, bf16[96,2560]{1,0:T(8,128)(2,1)}, u32[]{:S(2)}, u32[]{:S(2)}) collective-permute-start(bf16[96,2560]{1,0:T(8,128)(2,1)S(1)} %copy-done.5), channel_id=1, source_target_pairs={{0,3},{1,0},{2,1},{3,2},{4,7},{5,4},{6,5},{7,6},{8,11},{9,8},{10,9... | collective-permute-start | bytes 1474568 | tf_op jit(solution)/shard_map/ppermute | solution.py:131
  29.2 22.4 %collective-permute-start.1 = (bf16[96,2560]{1,0:T(8,128)(2,1)S(1)}, bf16[96,2560]{1,0:T(8,128)(2,1)}, u32[]{:S(2)}, u32[]{:S(2)}) collective-permute-start(bf16[96,2560]{1,0:T(8,128)(2,1)S(1)} %copy-done.5), channel_id=1, source_target_pairs={{0,2},{1,3},{2,0},{3,1},{4,6},{5,7},{6,4},{7,5},{8,10},{9,11},{10,... | collective-permute-start | bytes 1474568 | tf_op jit(solution)/shard_map/ppermute | solution.py:131
  77.0 7.4 %copy-start.6 = (pred[2,128,256]{2,1,0:T(8,128)(4,1)S(1)}, pred[2,128,256]{2,1,0:T(8,128)(4,1)}, u32[]{:S(2)}) copy-start(pred[2,128,256]{2,1,0:T(8,128)(4,1)} %fusion.19) | copy-start | bytes 196612
  78.7 45.0 %collective-permute-start.3 = (bf16[2,128,512]{2,1,0:T(8,128)(2,1)}, bf16[2,128,512]{2,1,0:T(8,128)(2,1)S(1)}, u32[]{:S(2)}, u32[]{:S(2)}) collective-permute-start(bf16[2,128,512]{2,1,0:T(8,128)(2,1)} %pad_maximum_fusion.4), channel_id=1, source_target_pairs={{0,4},{4,8},{8,12},{12,16},{16,20},{20,24},{24,28},{1,5},{5,9},{9,... | collective-permute-start | bytes 786440 | tf_op jit(solution)/shard_map/ppermute | solution.py:20
  83.5 1.0 copy-start.4
  123.6 2.0 %copy-start.3 = (bf16[2,128,512]{2,1,0:T(8,128)(2,1)}, bf16[2,128,512]{2,1,0:T(8,128)(2,1)S(1)}, u32[]{:S(2)}) copy-start(bf16[2,128,512]{2,1,0:T(8,128)(2,1)S(1)} %collective-permute-done.3.bk_ref.bv_ref) | copy-start | bytes 786436
  140.4 1.3 copy-start.2
  141.7 2.1 %collective-permute-start.4 = (bf16[2,96,1280]{2,1,0:T(8,128)(2,1)S(1)}, bf16[2,96,1280]{2,1,0:T(8,128)(2,1)}, u32[]{:S(2)}, u32[]{:S(2)}) collective-permute-start(bf16[2,96,1280]{2,1,0:T(8,128)(2,1)S(1)} %fusion.14), channel_id=1, source_target_pairs={{0,1},{1,0},{2,3},{3,2},{4,5},{5,4},{6,7},{7,6},{8,9},{9,8},{10,11... | collective-permute-start | bytes 1474568 | tf_op jit(solution)/shard_map/ppermute | solution.py:241
  141.8 5.0 %copy-start.1 = (f32[384,1280]{1,0:T(8,128)S(1)}, f32[384,1280]{1,0:T(8,128)}, u32[]{:S(2)}) copy-start(f32[384,1280]{1,0:T(8,128)} %get-tuple-element.8) | copy-start | bytes 5898244
  143.3 3.6 %collective-permute-start.6 = (bf16[2,96,1280]{2,1,0:T(8,128)(2,1)S(1)}, bf16[2,96,1280]{2,1,0:T(8,128)(2,1)S(1)}, u32[]{:S(2)}, u32[]{:S(2)}) collective-permute-start(bf16[2,96,1280]{2,1,0:T(8,128)(2,1)S(1)} %fusion.15), channel_id=1, source_target_pairs={{0,1},{1,0},{2,3},{3,2},{4,5},{5,4},{6,7},{7,6},{8,9},{9,8},{10,11... | collective-permute-start | bytes 1474568 | tf_op jit(solution)/shard_map/ppermute | solution.py:241
  145.3 8.9 %collective-permute-start.5 = (bf16[96,1280]{1,0:T(8,128)(2,1)S(1)}, bf16[96,1280]{1,0:T(8,128)(2,1)S(1)}, u32[]{:S(2)}, u32[]{:S(2)}) collective-permute-start(bf16[96,1280]{1,0:T(8,128)(2,1)S(1)} %fusion.20), channel_id=1, source_target_pairs={{0,2},{1,3},{2,0},{3,1},{4,6},{5,7},{6,4},{7,5},{8,10},{9,11},{10,... | collective-permute-start | bytes 737288 | tf_op jit(solution)/shard_map/ppermute | solution.py:249
  147.0 11.6 %collective-permute-start.7 = (bf16[96,1280]{1,0:T(8,128)(2,1)S(1)}, bf16[96,1280]{1,0:T(8,128)(2,1)S(1)}, u32[]{:S(2)}, u32[]{:S(2)}) collective-permute-start(bf16[96,1280]{1,0:T(8,128)(2,1)S(1)} %fusion.21), channel_id=1, source_target_pairs={{0,2},{1,3},{2,0},{3,1},{4,6},{5,7},{6,4},{7,5},{8,10},{9,11},{10,... | collective-permute-start | bytes 737288 | tf_op jit(solution)/shard_map/ppermute | solution.py:249

commit v13 on v12

--- a/solution.py
+++ b/solution.py
@@ -222,9 +222,9 @@
         mixing,
     )
     partial = jnp.dot(attended, output_weight, preferred_element_type=jnp.float32)
-    half = partial.shape[1] // 2
+    width = partial.shape[1] // 4
     return jnp.concatenate(
-        [reduce_over_tp(partial[:, :half]), reduce_over_tp(partial[:, half:])], axis=1
+        [reduce_over_tp(partial[:, k * width:(k + 1) * width]) for k in range(4)], axis=1
     ).astype(jnp.bfloat16)
 
 

time: 160 us -> 156 us (0.975)
  local copies, waits for them, and re-layouts: 33.2 us -> 29.3 us
  starting transfers between devices: 16.3 us -> 19.1 us
  waiting for transfers between devices: 61.4 us -> 59.3 us
    ppermute x2 -> x4, waiting for transfers between devices: 11 us -> 8.68 us  [reduce_over_tp(): lax.ppermute(outgoing.astype(jnp.bfloat16), 'tp', pairs).astype(jnp.float32)]
    ppermute x2 -> x4, starting transfers between devices: 2.16 us -> 4.31 us  [reduce_over_tp(): lax.ppermute(outgoing.astype(jnp.bfloat16), 'tp', pairs).astype(jnp.float32)]
  transfers between devices with their start and end apart: 9 -> 13, of which waited for: 6 -> 9; matrix products, arithmetic and copies ran while one was open for 26% -> 25% of each run, Pallas kernels for 0% -> 0%
where the time goes in v13:
time: 156 us; the launch traced here: 155 us
  waiting for transfers between devices  59.3 us (38%)
  local copies, waits for them, and re-layouts  29.3 us (19%)
  starting transfers between devices  19.1 us (12%)
  matrix products  16.1 us (10%)
  Pallas kernels  11 us (7%)
  blocking collectives  10 us (6%)
  other arithmetic  9.74 us (6%)
    ppermute x1, waiting for transfers between devices, from_behind(): lax.ppermute(value, axis, [(source, source + steps) for source in range(i...  33.4 us
    ppermute x3, waiting for transfers between devices, gather_tp(): lax.ppermute(part, 'tp', [(t, (t + shift) % count) for t in range(count)])  17 us
    pallas_call x1, Pallas kernels, far_attention(): pl.pallas_call(far_kernel, grid=(groups,), in_specs=[pl.BlockSpec((rows,...  11 us
    all_to_all x1, blocking collectives, local(): lax.all_to_all(wanted_ids, 'mem', split_axis=0, concat_axis=0, tiled=True)  10 us
    ppermute x4, waiting for transfers between devices, reduce_over_tp(): lax.ppermute(outgoing.astype(jnp.bfloat16), 'tp', pairs).astype(jnp.float32)  8.68 us
    dot_general x1, matrix products, local(): jnp.dot(gather_tp(tokens), input_weight, preferred_element_type=jnp.float32)  8.14 us
    all_to_all x1, starting transfers between devices, local(): lax.all_to_all(picked, 'mem', split_axis=0, concat_axis=0, tiled=True)  6.94 us
    gather x1, local copies, waits for them, and re-layouts, local(): jnp.take(local_store, lax.all_to_all(wanted_ids, 'mem', split_axis=0, con...  6.17 us
  transfers between devices with their start and end apart: 13, of which 9 were waited for; matrix products, arithmetic and copies ran while one was open for 25% of the time, Pallas kernels for 0%

profile of v13, /device:TPU:16, one launch (start us, length us, event | category | flops | bytes accessed | tf_op | source)
XLA Modules:
  0.0 155.0 jit_solution(3042142840458295563)
XLA Ops:
  0.0 0.9 eq.74
  0.9 0.9 select_reduce_fusion.1
  1.8 0.2 convert_reduce_fusion.1
  2.0 0.7 compare_reduce_fusion
  2.7 0.2 convert_reduce_fusion
  2.9 0.1 select_reduce_fusion.2
  3.0 0.1 copy.52
  3.1 10.0 %all_to_all.14 = s32[8,1,2]{2,1,0:T(1,128)S(1)} all-to-all(s32[8,1,2]{2,1,0:T(1,128)S(1)} %copy.52), channel_id=1, replica_groups=mesh['mem'=8,'tp'=4] {'mem'}, dimensions={0} | all-to-all | bytes 128 | tf_op jit(solution)/shard_map/all_to_all | solution.py:199
  13.1 0.5 broadcast.403
  13.6 0.7 reduce.22
  14.3 0.1 reshape.319
  14.4 6.2 %gather_fusion.1 = bf16[16,2,128,512]{3,2,1,0:T(8,128)(2,1)} fusion(bf16[2,32,128,512]{3,2,1,0:T(8,128)(2,1)} %bitcast.110, s32[1024]{0:T(1024)S(1)} %pad_clamp_fusion), kind=kCustom, calls=%fused_computation.1 | custom fusion | bytes 8388672 | tf_op jit(solution)/shard_map/jit(_take)/gather | solution.py:197
  20.5 6.9 %all-to-all-start.1 = ((bf16[16,2,128,512]{3,2,1,0:T(8,128)(2,1)}), bf16[16,2,128,512]{3,2,1,0:T(8,128)(2,1)}, u32[]{:S(2)}, u32[]{:S(2)}) async-start(bf16[16,2,128,512]{3,2,1,0:T(8,128)(2,1)} %gather_fusion.1), calls=%async_computation.1 | async-start | bytes 8388608 | tf_op jit(solution)/shard_map/all_to_all | solution.py:205
  27.5 0.0 collective-permute-start
  27.5 1.7 %collective-permute-start.2 = (bf16[96,2560]{1,0:T(8,128)(2,1)S(1)}, bf16[96,2560]{1,0:T(8,128)(2,1)}, u32[]{:S(2)}, u32[]{:S(2)}) collective-permute-start(bf16[96,2560]{1,0:T(8,128)(2,1)S(1)} %copy-done.3), channel_id=1, source_target_pairs={{0,3},{1,0},{2,1},{3,2},{4,7},{5,4},{6,5},{7,6},{8,11},{9,8},{10,9... | collective-permute-start | bytes 1474568 | tf_op jit(solution)/shard_map/ppermute | solution.py:131
  29.2 1.5 collective-permute-start.1
  30.8 2.8 %scatter_fusion = pred[3,16]{1,0:T(4,128)(4,1)S(1)} fusion(pred[3,16]{1,0:T(4,128)(4,1)S(1)} %broadcast_in_dim.98, s32[48]{0:T(128)S(1)} %fusion.38, pred[48]{0:T(512)(128)(4,1)S(1)} %broadcast.369), kind=kCustom, calls=%fused_computation.2 | custom fusion | bytes 528 | tf_op jit(solution)/shard_map/scatter | solution.py:209
  33.7 0.1 slice_add_fusion
  33.8 0.1 fusion.24
  33.9 0.7 fusion.15
  34.7 4.6 %collective-permute-done = bf16[96,2560]{1,0:T(8,128)(2,1)} collective-permute-done((bf16[96,2560]{1,0:T(8,128)(2,1)S(1)}, bf16[96,2560]{1,0:T(8,128)(2,1)}, u32[]{:S(2)}, u32[]{:S(2)}) %collective-permute-start) | collective-permute-done | bytes 491552 | tf_op jit(solution)/shard_map/ppermute | solution.py:131
  39.2 1.6 %collective-permute-done.2 = bf16[96,2560]{1,0:T(8,128)(2,1)} collective-permute-done((bf16[96,2560]{1,0:T(8,128)(2,1)S(1)}, bf16[96,2560]{1,0:T(8,128)(2,1)}, u32[]{:S(2)}, u32[]{:S(2)}) %collective-permute-start.2) | collective-permute-done | bytes 491552 | tf_op jit(solution)/shard_map/ppermute | solution.py:131
  40.8 10.8 %collective-permute-done.1 = bf16[96,2560]{1,0:T(8,128)(2,1)} collective-permute-done((bf16[96,2560]{1,0:T(8,128)(2,1)S(1)}, bf16[96,2560]{1,0:T(8,128)(2,1)}, u32[]{:S(2)}, u32[]{:S(2)}) %collective-permute-start.1) | collective-permute-done | bytes 491552 | tf_op jit(solution)/shard_map/ppermute | solution.py:131
  51.6 2.9 %pad_maximum_fusion = bf16[4,96,2560]{2,1,0:T(8,128)(2,1)} fusion(bf16[1,96,2560]{2,1,0:T(8,128)(2,1)} %bitcast.3, bf16[1,96,2560]{2,1,0:T(8,128)(2,1)} %bitcast.2, bf16[1,96,2560]{2,1,0:T(8,128)(2,1)} %bitcast.1, bf16[1,96,2560]{2,1,0:T(8,128)(2,1)S(1)} %bitcast.117), kind=kLoop, calls=%fused_computation.5 | loop fusion | flops 2949120 | bytes 3932160 | tf_op jit(solution)/shard_map/stack | solution.py:135
  54.6 3.5 %gather_fusion = bf16[4,96,2560]{2,1,0:T(8,128)(2,1)} fusion(bf16[4,96,2560]{2,1,0:T(8,128)(2,1)} %pad_maximum_fusion, s32[1024]{0:T(1024)S(1)} %pad_clamp_fusion.1), kind=kCustom, calls=%fused_computation | custom fusion | bytes 3932176 | tf_op jit(solution)/shard_map/jit(_take)/gather | solution.py:135
  58.0 8.1 %convolution_convert_fusion.q_ref.k0_ref.v0_ref = bf16[384,1536]{1,0:T(8,128)(2,1)} fusion(bf16[384,2560]{1,0:T(8,128)(2,1)} %bitcast.111, bf16[2560,1536]{1,0:T(8,128)(2,1)} %param.8), kind=kOutput, calls=%fused_computation.4 | convolution fusion | flops 3020488704 | bytes 11010048 | tf_op jit(solution)/shard_map/dot_general | solution.py:145
  66.2 2.4 %copy.49 = bf16[384,1536]{0,1:T(8,128)(2,1)} copy(bf16[384,1536]{1,0:T(8,128)(2,1)} %convolution_convert_fusion.q_ref.k0_ref.v0_ref) | data formatting | bytes 2359296 | tf_op jit(solution)/shard_map/convert_element_type | solution.py:150
  68.6 1.0 fusion.47
  69.6 0.1 copy.67
  69.7 0.8 copy.68
  70.5 2.2 %fusion.46 = (bf16[256,4,1,128]{0,3,2,1:T(8,128)(2,1)}, bf16[256,4,1,128]{0,3,2,1:T(8,128)(2,1)S(1)}, bf16[256,4,1,128]{0,3,2,1:T(8,128)(2,1)S(1)}, bf16[256,4,1...) fusion(bf16[384,4,3,128]{0,3,2,1:T(8,128)(2,1)} %bitcast.101), kind=kLoop, calls=%fused_computation.110 | loop fusion | bytes 2621440 | tf_op jit(solution)/shard_map/slice | solution.py:163
  72.6 1.8 %copy.53 = bf16[256,4,1,128]{3,0,1,2:T(8,128)(2,1)} copy(bf16[256,4,1,128]{0,3,2,1:T(8,128)(2,1)} %get-tuple-element.11) | data formatting | bytes 524288 | tf_op jit(solution)/shard_map/slice | solution.py:163
  74.4 1.8 %copy.55 = bf16[256,4,1,128]{3,0,1,2:T(8,128)(2,1)} copy(bf16[256,4,1,128]{0,3,2,1:T(8,128)(2,1)} %get-tuple-element.14) | data formatting | bytes 524288 | tf_op jit(solution)/shard_map/slice | solution.py:164
  76.2 0.8 copy.54
  77.0 1.7 %pad_maximum_fusion.4 = bf16[2,128,512]{2,1,0:T(8,128)(2,1)} fusion(bf16[1,128,512]{2,1,0:T(8,128)(2,1)} %copy.68, bf16[1,128,512]{2,1,0:T(8,128)(2,1)S(1)} %copy.67), kind=kLoop, calls=%fused_computation.29 | loop fusion | flops 131072 | bytes 524288 | tf_op jit(solution)/shard_map/stack | solution.py:155
  78.7 3.4 %collective-permute-start.3 = (bf16[2,128,512]{2,1,0:T(8,128)(2,1)}, bf16[2,128,512]{2,1,0:T(8,128)(2,1)S(1)}, u32[]{:S(2)}, u32[]{:S(2)}) collective-permute-start(bf16[2,128,512]{2,1,0:T(8,128)(2,1)} %pad_maximum_fusion.4), channel_id=1, source_target_pairs={{0,4},{4,8},{8,12},{12,16},{16,20},{20,24},{24,28},{1,5},{5,9},{9,... | collective-permute-start | bytes 786440 | tf_op jit(solution)/shard_map/ppermute | solution.py:20
  82.0 1.4 convolution_multiply_fusion
  83.5 1.0 copy-done.2
  84.4 0.4 fusion.48
  84.8 0.8 copy.60
  85.7 0.2 copy.59
  85.9 4.4 %fusion.9.near_ref = f32[2,4,128,128]{3,2,1,0:T(8,128)} fusion(f32[2,4,128]{2,1,0:T(4,128)S(1)} %fusion.48, f32[2,4,128,256]{3,2,1,0:T(8,128)} %copy-done.2, pred[2,128,256]{2,1,0:T(8,128)(4,1)} %fusion.15, bf16[2,128,4,128]{3,1,0,2:T(8,128)(2,1)} %bitcast.118, bf16[2,128,4,128]{3,1,0,2:T(8,128)(2,1)S(1)} %bitcast.119), kind=kOutput, calls=%fused_computation.15 | convolution fusion | flops 69469440 | bytes 2166784 | tf_op jit(solution)/shard_map/ngqk,nkgd->ngqd/dot_general | solution.py:44
  90.2 33.4 %collective-permute-done.3.bk_ref.bv_ref = bf16[2,128,512]{2,1,0:T(8,128)(2,1)S(1)} collective-permute-done((bf16[2,128,512]{2,1,0:T(8,128)(2,1)}, bf16[2,128,512]{2,1,0:T(8,128)(2,1)S(1)}, u32[]{:S(2)}, u32[]{:S(2)}) %collective-permute-start.3) | collective-permute-done | bytes 262176 | tf_op jit(solution)/shard_map/ppermute | solution.py:20
  123.7 0.0 all-to-all-done.1.k_ref.v_ref
  123.7 0.6 broadcast_in_dim.106.start_ref
  124.3 0.7 broadcast_in_dim.107
  124.9 0.7 broadcast_in_dim.102
  125.6 11.0 %shard_map.73 = bf16[384,512]{1,0:T(8,128)(2,1)} custom-call(bf16[384,1536]{1,0:T(8,128)(2,1)} %convolution_convert_fusion.q_ref.k0_ref.v0_ref, bf16[384,1536]{1,0:T(8,128)(2,1)} %convolution_convert_fusion.q_ref.k0_ref.v0_ref, bf16[384,1536]{1,0:T(8,128)(2,1)} %convolution_convert_fusion.q_ref.k0_ref.v0_ref, bf16[2,128,512]{2,1,0:T(8,128)(2,1)} %copy-done.1, ...), custom_call_target="tpu_custom_call" | custom-call | flops 1677721600 | bytes 5767168 | tf_op jit(solution)/shard_map/pallas_call | solution.py:102
  136.7 2.2 %fusion.49 = f32[384,2560]{1,0:T(8,128)S(1)} fusion(bf16[384,512]{1,0:T(8,128)(2,1)} %shard_map.73, bf16[512,2560]{1,0:T(8,128)(2,1)S(1)} %copy-done), kind=kOutput, calls=%fused_computation.113 | convolution fusion | flops 1006632960 | bytes 6946816 | tf_op jit(solution)/shard_map/dot_general | solution.py:224
  138.8 0.3 fusion.45
  139.2 0.1 collective-permute-start.6
  139.3 0.5 collective-permute-start.8
  139.9 0.1 collective-permute-start.4
  140.0 0.5 collective-permute-start.10
  140.5 0.2 collective-permute-done.6
  140.8 1.6 %collective-permute-start.7 = (bf16[96,640]{1,0:T(8,128)(2,1)S(1)}, bf16[96,640]{1,0:T(8,128)(2,1)S(1)}, u32[]{:S(2)}, u32[]{:S(2)}) collective-permute-start(bf16[96,640]{1,0:T(8,128)(2,1)S(1)} %fusion.26), channel_id=1, source_target_pairs={{0,2},{1,3},{2,0},{3,1},{4,6},{5,7},{6,4},{7,5},{8,10},{9,11},{10,... | collective-permute-start | bytes 368648 | tf_op jit(solution)/shard_map/ppermute | solution.py:249
  142.5 0.6 collective-permute-start.9
  143.1 1.6 %collective-permute-start.5 = (bf16[96,640]{1,0:T(8,128)(2,1)S(1)}, bf16[96,640]{1,0:T(8,128)(2,1)S(1)}, u32[]{:S(2)}, u32[]{:S(2)}) collective-permute-start(bf16[96,640]{1,0:T(8,128)(2,1)S(1)} %fusion.25), channel_id=1, source_target_pairs={{0,2},{1,3},{2,0},{3,1},{4,6},{5,7},{6,4},{7,5},{8,10},{9,11},{10,... | collective-permute-start | bytes 368648 | tf_op jit(solution)/shard_map/ppermute | solution.py:249
  144.8 0.6 collective-permute-start.11
  145.4 1.7 %collective-permute-done.7 = bf16[96,640]{1,0:T(8,128)(2,1)S(1)} collective-permute-done((bf16[96,640]{1,0:T(8,128)(2,1)S(1)}, bf16[96,640]{1,0:T(8,128)(2,1)S(1)}, u32[]{:S(2)}, u32[]{:S(2)}) %collective-permute-start.7) | collective-permute-done | bytes 122912 | tf_op jit(solution)/shard_map/ppermute | solution.py:249
  147.1 2.6 %collective-permute-done.9 = bf16[96,640]{1,0:T(8,128)(2,1)S(1)} collective-permute-done((bf16[96,640]{1,0:T(8,128)(2,1)S(1)}, bf16[96,640]{1,0:T(8,128)(2,1)S(1)}, u32[]{:S(2)}, u32[]{:S(2)}) %collective-permute-start.9) | collective-permute-done | bytes 122912 | tf_op jit(solution)/shard_map/ppermute | solution.py:249
  149.7 2.6 %collective-permute-done.5 = bf16[96,640]{1,0:T(8,128)(2,1)S(1)} collective-permute-done((bf16[96,640]{1,0:T(8,128)(2,1)S(1)}, bf16[96,640]{1,0:T(8,128)(2,1)S(1)}, u32[]{:S(2)}, u32[]{:S(2)}) %collective-permute-start.5) | collective-permute-done | bytes 122912 | tf_op jit(solution)/shard_map/ppermute | solution.py:249
  152.3 1.8 %collective-permute-done.11 = bf16[96,640]{1,0:T(8,128)(2,1)S(1)} collective-permute-done((bf16[96,640]{1,0:T(8,128)(2,1)S(1)}, bf16[96,640]{1,0:T(8,128)(2,1)S(1)}, u32[]{:S(2)}, u32[]{:S(2)}) %collective-permute-start.11) | collective-permute-done | bytes 122912 | tf_op jit(solution)/shard_map/ppermute | solution.py:249
  154.2 0.8 pad_maximum_fusion.3
  (42 shorter events, 0.6 us)
Async XLA Ops:
  0.0 136.7 %copy-start = (bf16[512,2560]{1,0:T(8,128)(2,1)S(1)}, bf16[512,2560]{1,0:T(8,128)(2,1)}, u32[]{:S(2)}) copy-start(bf16[512,2560]{1,0:T(8,128)(2,1)} %param.9) | copy-start | bytes 7864324
  20.5 6.9 %copy-start.3 = (bf16[96,2560]{1,0:T(8,128)(2,1)S(1)}, bf16[96,2560]{1,0:T(8,128)(2,1)}, u32[]{:S(2)}) copy-start(bf16[96,2560]{1,0:T(8,128)(2,1)} %param.7) | copy-start | bytes 1474564
  20.5 13.2 %copy-start.5 = (f32[4]{0:T(128)S(1)}, f32[4]{0:T(128)}, u32[]{:S(2)}) copy-start(f32[4]{0:T(128)} %param.10) | copy-start | bytes 52
  20.5 103.1 %all-to-all-start.1 = ((bf16[16,2,128,512]{3,2,1,0:T(8,128)(2,1)}), bf16[16,2,128,512]{3,2,1,0:T(8,128)(2,1)}, u32[]{:S(2)}, u32[]{:S(2)}) async-start(bf16[16,2,128,512]{3,2,1,0:T(8,128)(2,1)} %gather_fusion.1), calls=%async_computation.1 | async-start | bytes 8388608 | tf_op jit(solution)/shard_map/all_to_all | solution.py:205
  27.5 11.7 %collective-permute-start = (bf16[96,2560]{1,0:T(8,128)(2,1)S(1)}, bf16[96,2560]{1,0:T(8,128)(2,1)}, u32[]{:S(2)}, u32[]{:S(2)}) collective-permute-start(bf16[96,2560]{1,0:T(8,128)(2,1)S(1)} %copy-done.3), channel_id=1, source_target_pairs={{0,1},{1,2},{2,3},{3,0},{4,5},{5,6},{6,7},{7,4},{8,9},{9,10},{10,1... | collective-permute-start | bytes 1474568 | tf_op jit(solution)/shard_map/ppermute | solution.py:131
  27.5 13.3 %collective-permute-start.2 = (bf16[96,2560]{1,0:T(8,128)(2,1)S(1)}, bf16[96,2560]{1,0:T(8,128)(2,1)}, u32[]{:S(2)}, u32[]{:S(2)}) collective-permute-start(bf16[96,2560]{1,0:T(8,128)(2,1)S(1)} %copy-done.3), channel_id=1, source_target_pairs={{0,3},{1,0},{2,1},{3,2},{4,7},{5,4},{6,5},{7,6},{8,11},{9,8},{10,9... | collective-permute-start | bytes 1474568 | tf_op jit(solution)/shard_map/ppermute | solution.py:131
  29.2 22.4 %collective-permute-start.1 = (bf16[96,2560]{1,0:T(8,128)(2,1)S(1)}, bf16[96,2560]{1,0:T(8,128)(2,1)}, u32[]{:S(2)}, u32[]{:S(2)}) collective-permute-start(bf16[96,2560]{1,0:T(8,128)(2,1)S(1)} %copy-done.3), channel_id=1, source_target_pairs={{0,2},{1,3},{2,0},{3,1},{4,6},{5,7},{6,4},{7,5},{8,10},{9,11},{10,... | collective-permute-start | bytes 1474568 | tf_op jit(solution)/shard_map/ppermute | solution.py:131
  77.0 7.4 %copy-start.4 = (pred[2,128,256]{2,1,0:T(8,128)(4,1)S(1)}, pred[2,128,256]{2,1,0:T(8,128)(4,1)}, u32[]{:S(2)}) copy-start(pred[2,128,256]{2,1,0:T(8,128)(4,1)} %fusion.15) | copy-start | bytes 196612
  78.7 45.0 %collective-permute-start.3 = (bf16[2,128,512]{2,1,0:T(8,128)(2,1)}, bf16[2,128,512]{2,1,0:T(8,128)(2,1)S(1)}, u32[]{:S(2)}, u32[]{:S(2)}) collective-permute-start(bf16[2,128,512]{2,1,0:T(8,128)(2,1)} %pad_maximum_fusion.4), channel_id=1, source_target_pairs={{0,4},{4,8},{8,12},{12,16},{16,20},{20,24},{24,28},{1,5},{5,9},{9,... | collective-permute-start | bytes 786440 | tf_op jit(solution)/shard_map/ppermute | solution.py:20
  83.5 1.0 copy-start.2
  123.6 2.0 %copy-start.1 = (bf16[2,128,512]{2,1,0:T(8,128)(2,1)}, bf16[2,128,512]{2,1,0:T(8,128)(2,1)S(1)}, u32[]{:S(2)}) copy-start(bf16[2,128,512]{2,1,0:T(8,128)(2,1)S(1)} %collective-permute-done.3.bk_ref.bv_ref) | copy-start | bytes 786436
  139.2 1.6 %collective-permute-start.6 = (bf16[2,96,640]{2,1,0:T(8,128)(2,1)S(1)}, bf16[2,96,640]{2,1,0:T(8,128)(2,1)S(1)}, u32[]{:S(2)}, u32[]{:S(2)}) collective-permute-start(bf16[2,96,640]{2,1,0:T(8,128)(2,1)S(1)} %fusion.17), channel_id=1, source_target_pairs={{0,1},{1,0},{2,3},{3,2},{4,5},{5,4},{6,7},{7,6},{8,9},{9,8},{10,11... | collective-permute-start | bytes 737288 | tf_op jit(solution)/shard_map/ppermute | solution.py:241
  139.3 3.1 %collective-permute-start.8 = (bf16[2,96,640]{2,1,0:T(8,128)(2,1)S(1)}, bf16[2,96,640]{2,1,0:T(8,128)(2,1)S(1)}, u32[]{:S(2)}, u32[]{:S(2)}) collective-permute-start(bf16[2,96,640]{2,1,0:T(8,128)(2,1)S(1)} %fusion.18), channel_id=1, source_target_pairs={{0,1},{1,0},{2,3},{3,2},{4,5},{5,4},{6,7},{7,6},{8,9},{9,8},{10,11... | collective-permute-start | bytes 737288 | tf_op jit(solution)/shard_map/ppermute | solution.py:241
  139.9 3.2 %collective-permute-start.4 = (bf16[2,96,640]{2,1,0:T(8,128)(2,1)S(1)}, bf16[2,96,640]{2,1,0:T(8,128)(2,1)S(1)}, u32[]{:S(2)}, u32[]{:S(2)}) collective-permute-start(bf16[2,96,640]{2,1,0:T(8,128)(2,1)S(1)} %fusion.16), channel_id=1, source_target_pairs={{0,1},{1,0},{2,3},{3,2},{4,5},{5,4},{6,7},{7,6},{8,9},{9,8},{10,11... | collective-permute-start | bytes 737288 | tf_op jit(solution)/shard_map/ppermute | solution.py:241
  140.0 4.7 %collective-permute-start.10 = (bf16[2,96,640]{2,1,0:T(8,128)(2,1)S(1)}, bf16[2,96,640]{2,1,0:T(8,128)(2,1)S(1)}, u32[]{:S(2)}, u32[]{:S(2)}) collective-permute-start(bf16[2,96,640]{2,1,0:T(8,128)(2,1)S(1)} %fusion.19), channel_id=1, source_target_pairs={{0,1},{1,0},{2,3},{3,2},{4,5},{5,4},{6,7},{7,6},{8,9},{9,8},{10,11... | collective-permute-start | bytes 737288 | tf_op jit(solution)/shard_map/ppermute | solution.py:241
  140.8 6.2 %collective-permute-start.7 = (bf16[96,640]{1,0:T(8,128)(2,1)S(1)}, bf16[96,640]{1,0:T(8,128)(2,1)S(1)}, u32[]{:S(2)}, u32[]{:S(2)}) collective-permute-start(bf16[96,640]{1,0:T(8,128)(2,1)S(1)} %fusion.26), channel_id=1, source_target_pairs={{0,2},{1,3},{2,0},{3,1},{4,6},{5,7},{6,4},{7,5},{8,10},{9,11},{10,... | collective-permute-start | bytes 368648 | tf_op jit(solution)/shard_map/ppermute | solution.py:249
  142.5 7.2 %collective-permute-start.9 = (bf16[96,640]{1,0:T(8,128)(2,1)S(1)}, bf16[96,640]{1,0:T(8,128)(2,1)S(1)}, u32[]{:S(2)}, u32[]{:S(2)}) collective-permute-start(bf16[96,640]{1,0:T(8,128)(2,1)S(1)} %fusion.27), channel_id=1, source_target_pairs={{0,2},{1,3},{2,0},{3,1},{4,6},{5,7},{6,4},{7,5},{8,10},{9,11},{10,... | collective-permute-start | bytes 368648 | tf_op jit(solution)/shard_map/ppermute | solution.py:249
  143.1 9.2 %collective-permute-start.5 = (bf16[96,640]{1,0:T(8,128)(2,1)S(1)}, bf16[96,640]{1,0:T(8,128)(2,1)S(1)}, u32[]{:S(2)}, u32[]{:S(2)}) collective-permute-start(bf16[96,640]{1,0:T(8,128)(2,1)S(1)} %fusion.25), channel_id=1, source_target_pairs={{0,2},{1,3},{2,0},{3,1},{4,6},{5,7},{6,4},{7,5},{8,10},{9,11},{10,... | collective-permute-start | bytes 368648 | tf_op jit(solution)/shard_map/ppermute | solution.py:249
  144.8 9.3 %collective-permute-start.11 = (bf16[96,640]{1,0:T(8,128)(2,1)S(1)}, bf16[96,640]{1,0:T(8,128)(2,1)S(1)}, u32[]{:S(2)}, u32[]{:S(2)}) collective-permute-start(bf16[96,640]{1,0:T(8,128)(2,1)S(1)} %fusion.28), channel_id=1, source_target_pairs={{0,2},{1,3},{2,0},{3,1},{4,6},{5,7},{6,4},{7,5},{8,10},{9,11},{10,... | collective-permute-start | bytes 368648 | tf_op jit(solution)/shard_map/ppermute | solution.py:249

commit v14 on v13

--- a/solution.py
+++ b/solution.py
@@ -222,9 +222,13 @@
         mixing,
     )
     partial = jnp.dot(attended, output_weight, preferred_element_type=jnp.float32)
-    width = partial.shape[1] // 4
+    width = 4 * HD
     return jnp.concatenate(
-        [reduce_over_tp(partial[:, k * width:(k + 1) * width]) for k in range(4)], axis=1
+        [
+            reduce_over_tp(partial[:, k * width:(k + 1) * width])
+            for k in range(partial.shape[1] // width)
+        ],
+        axis=1,
     ).astype(jnp.bfloat16)
 
 

time: 156 us -> 157 us (level)
  starting transfers between devices: 19.1 us -> 21 us
  waiting for transfers between devices: 59.3 us -> 57.5 us
    ppermute x4 -> x5, starting transfers between devices: 4.31 us -> 5.92 us  [reduce_over_tp(): lax.ppermute(outgoing.astype(jnp.bfloat16), 'tp', pairs).astype(jnp.float32)]
    ppermute x4 -> x5, waiting for transfers between devices: 8.68 us -> 7.12 us  [reduce_over_tp(): lax.ppermute(outgoing.astype(jnp.bfloat16), 'tp', pairs).astype(jnp.float32)]
  transfers between devices with their start and end apart: 13 -> 15, of which waited for: 9 -> 8; matrix products, arithmetic and copies ran while one was open for 25% -> 25% of each run, Pallas kernels for 0% -> 0%
where the time goes in v14:
time: 157 us; the launch traced here: 156 us
  waiting for transfers between devices  57.5 us (37%)
  local copies, waits for them, and re-layouts  30.4 us (19%)
  starting transfers between devices  21 us (13%)
  matrix products  16.1 us (10%)
  Pallas kernels  11 us (7%)
  blocking collectives  10 us (6%)
  other arithmetic  9.63 us (6%)
    ppermute x1, waiting for transfers between devices, from_behind(): lax.ppermute(value, axis, [(source, source + steps) for source in range(i...  33.2 us
    ppermute x3, waiting for transfers between devices, gather_tp(): lax.ppermute(part, 'tp', [(t, (t + shift) % count) for t in range(count)])  17 us
    pallas_call x1, Pallas kernels, far_attention(): pl.pallas_call(far_kernel, grid=(groups,), in_specs=[pl.BlockSpec((rows,...  11 us
    all_to_all x1, blocking collectives, local(): lax.all_to_all(wanted_ids, 'mem', split_axis=0, concat_axis=0, tiled=True)  10 us
    dot_general x1, matrix products, local(): jnp.dot(gather_tp(tokens), input_weight, preferred_element_type=jnp.float32)  8.14 us
    ppermute x5, waiting for transfers between devices, reduce_over_tp(): lax.ppermute(outgoing.astype(jnp.bfloat16), 'tp', pairs).astype(jnp.float32)  7.12 us
    all_to_all x1, starting transfers between devices, local(): lax.all_to_all(picked, 'mem', split_axis=0, concat_axis=0, tiled=True)  6.94 us
    gather x1, local copies, waits for them, and re-layouts, local(): jnp.take(local_store, lax.all_to_all(wanted_ids, 'mem', split_axis=0, con...  6.17 us
  transfers between devices with their start and end apart: 15, of which 8 were waited for; matrix products, arithmetic and copies ran while one was open for 25% of the time, Pallas kernels for 0%

profile of v14, /device:TPU:16, one launch (start us, length us, event | category | flops | bytes accessed | tf_op | source)
XLA Modules:
  0.0 156.1 jit_solution(9463384384250026571)
XLA Ops:
  0.0 0.9 eq.76
  0.9 0.9 select_reduce_fusion.1
  1.8 0.2 convert_reduce_fusion.1
  2.0 0.7 compare_reduce_fusion
  2.7 0.2 convert_reduce_fusion
  2.9 0.1 select_reduce_fusion.2
  3.0 0.1 copy.55
  3.1 10.0 %all_to_all.14 = s32[8,1,2]{2,1,0:T(1,128)S(1)} all-to-all(s32[8,1,2]{2,1,0:T(1,128)S(1)} %copy.55), channel_id=1, replica_groups=mesh['mem'=8,'tp'=4] {'mem'}, dimensions={0} | all-to-all | bytes 128 | tf_op jit(solution)/shard_map/all_to_all | solution.py:199
  13.1 0.5 broadcast.403
  13.6 0.7 reduce.22
  14.3 0.1 reshape.325
  14.4 6.2 %gather_fusion.1 = bf16[16,2,128,512]{3,2,1,0:T(8,128)(2,1)} fusion(bf16[2,32,128,512]{3,2,1,0:T(8,128)(2,1)} %bitcast.137, s32[1024]{0:T(1024)S(1)} %pad_clamp_fusion), kind=kCustom, calls=%fused_computation.1 | custom fusion | bytes 8388672 | tf_op jit(solution)/shard_map/jit(_take)/gather | solution.py:197
  20.5 6.9 %all-to-all-start.1 = ((bf16[16,2,128,512]{3,2,1,0:T(8,128)(2,1)}), bf16[16,2,128,512]{3,2,1,0:T(8,128)(2,1)}, u32[]{:S(2)}, u32[]{:S(2)}) async-start(bf16[16,2,128,512]{3,2,1,0:T(8,128)(2,1)} %gather_fusion.1), calls=%async_computation.1 | async-start | bytes 8388608 | tf_op jit(solution)/shard_map/all_to_all | solution.py:205
  27.5 1.7 %collective-permute-start.2 = (bf16[96,2560]{1,0:T(8,128)(2,1)S(1)}, bf16[96,2560]{1,0:T(8,128)(2,1)}, u32[]{:S(2)}, u32[]{:S(2)}) collective-permute-start(bf16[96,2560]{1,0:T(8,128)(2,1)S(1)} %copy-done.3), channel_id=1, source_target_pairs={{0,3},{1,0},{2,1},{3,2},{4,7},{5,4},{6,5},{7,6},{8,11},{9,8},{10,9... | collective-permute-start | bytes 1474568 | tf_op jit(solution)/shard_map/ppermute | solution.py:131
  29.2 1.5 collective-permute-start.1
  30.8 2.8 %scatter_fusion = pred[3,16]{1,0:T(4,128)(4,1)S(1)} fusion(pred[3,16]{1,0:T(4,128)(4,1)S(1)} %broadcast_in_dim.98, s32[48]{0:T(128)S(1)} %fusion.46, pred[48]{0:T(512)(128)(4,1)S(1)} %broadcast.369), kind=kCustom, calls=%fused_computation.2 | custom fusion | bytes 528 | tf_op jit(solution)/shard_map/scatter | solution.py:209
  33.7 0.1 slice_add_fusion
  33.8 0.1 fusion.26
  33.9 0.7 fusion.15
  34.7 4.6 %collective-permute-done = bf16[96,2560]{1,0:T(8,128)(2,1)} collective-permute-done((bf16[96,2560]{1,0:T(8,128)(2,1)S(1)}, bf16[96,2560]{1,0:T(8,128)(2,1)}, u32[]{:S(2)}, u32[]{:S(2)}) %collective-permute-start) | collective-permute-done | bytes 491552 | tf_op jit(solution)/shard_map/ppermute | solution.py:131
  39.2 1.6 %collective-permute-done.2 = bf16[96,2560]{1,0:T(8,128)(2,1)} collective-permute-done((bf16[96,2560]{1,0:T(8,128)(2,1)S(1)}, bf16[96,2560]{1,0:T(8,128)(2,1)}, u32[]{:S(2)}, u32[]{:S(2)}) %collective-permute-start.2) | collective-permute-done | bytes 491552 | tf_op jit(solution)/shard_map/ppermute | solution.py:131
  40.8 10.8 %collective-permute-done.1 = bf16[96,2560]{1,0:T(8,128)(2,1)} collective-permute-done((bf16[96,2560]{1,0:T(8,128)(2,1)S(1)}, bf16[96,2560]{1,0:T(8,128)(2,1)}, u32[]{:S(2)}, u32[]{:S(2)}) %collective-permute-start.1) | collective-permute-done | bytes 491552 | tf_op jit(solution)/shard_map/ppermute | solution.py:131
  51.6 2.9 %pad_maximum_fusion = bf16[4,96,2560]{2,1,0:T(8,128)(2,1)} fusion(bf16[1,96,2560]{2,1,0:T(8,128)(2,1)} %bitcast.3, bf16[1,96,2560]{2,1,0:T(8,128)(2,1)} %bitcast.2, bf16[1,96,2560]{2,1,0:T(8,128)(2,1)} %bitcast.1, bf16[1,96,2560]{2,1,0:T(8,128)(2,1)S(1)} %bitcast.144), kind=kLoop, calls=%fused_computation.5 | loop fusion | flops 2949120 | bytes 3932160 | tf_op jit(solution)/shard_map/stack | solution.py:135
  54.6 3.5 %gather_fusion = bf16[4,96,2560]{2,1,0:T(8,128)(2,1)} fusion(bf16[4,96,2560]{2,1,0:T(8,128)(2,1)} %pad_maximum_fusion, s32[1024]{0:T(1024)S(1)} %pad_clamp_fusion.1), kind=kCustom, calls=%fused_computation | custom fusion | bytes 3932176 | tf_op jit(solution)/shard_map/jit(_take)/gather | solution.py:135
  58.0 8.1 %convolution_convert_fusion.q_ref.k0_ref.v0_ref = bf16[384,1536]{1,0:T(8,128)(2,1)} fusion(bf16[384,2560]{1,0:T(8,128)(2,1)} %bitcast.138, bf16[2560,1536]{1,0:T(8,128)(2,1)} %param.8), kind=kOutput, calls=%fused_computation.4 | convolution fusion | flops 3020488704 | bytes 11010048 | tf_op jit(solution)/shard_map/dot_general | solution.py:145
  66.2 2.4 %copy.52 = bf16[384,1536]{0,1:T(8,128)(2,1)} copy(bf16[384,1536]{1,0:T(8,128)(2,1)} %convolution_convert_fusion.q_ref.k0_ref.v0_ref) | data formatting | bytes 2359296 | tf_op jit(solution)/shard_map/convert_element_type | solution.py:150
  68.6 1.0 fusion.55
  69.6 0.1 copy.71
  69.7 0.8 copy.72
  70.5 2.2 %fusion.54 = (bf16[256,4,1,128]{0,3,2,1:T(8,128)(2,1)}, bf16[256,4,1,128]{0,3,2,1:T(8,128)(2,1)S(1)}, bf16[256,4,1,128]{0,3,2,1:T(8,128)(2,1)S(1)}, bf16[256,4,1...) fusion(bf16[384,4,3,128]{0,3,2,1:T(8,128)(2,1)} %bitcast.126), kind=kLoop, calls=%fused_computation.121 | loop fusion | bytes 2621440 | tf_op jit(solution)/shard_map/slice | solution.py:163
  72.6 1.8 %copy.56 = bf16[256,4,1,128]{3,0,1,2:T(8,128)(2,1)} copy(bf16[256,4,1,128]{0,3,2,1:T(8,128)(2,1)} %get-tuple-element.12) | data formatting | bytes 524288 | tf_op jit(solution)/shard_map/slice | solution.py:163
  74.4 1.8 %copy.58 = bf16[256,4,1,128]{3,0,1,2:T(8,128)(2,1)} copy(bf16[256,4,1,128]{0,3,2,1:T(8,128)(2,1)} %get-tuple-element.15) | data formatting | bytes 524288 | tf_op jit(solution)/shard_map/slice | solution.py:164
  76.2 0.8 copy.57
  77.0 1.7 %pad_maximum_fusion.3 = bf16[2,128,512]{2,1,0:T(8,128)(2,1)} fusion(bf16[1,128,512]{2,1,0:T(8,128)(2,1)} %copy.72, bf16[1,128,512]{2,1,0:T(8,128)(2,1)S(1)} %copy.71), kind=kLoop, calls=%fused_computation.30 | loop fusion | flops 131072 | bytes 524288 | tf_op jit(solution)/shard_map/stack | solution.py:155
  78.7 3.5 %collective-permute-start.3 = (bf16[2,128,512]{2,1,0:T(8,128)(2,1)}, bf16[2,128,512]{2,1,0:T(8,128)(2,1)S(1)}, u32[]{:S(2)}, u32[]{:S(2)}) collective-permute-start(bf16[2,128,512]{2,1,0:T(8,128)(2,1)} %pad_maximum_fusion.3), channel_id=1, source_target_pairs={{0,4},{4,8},{8,12},{12,16},{16,20},{20,24},{24,28},{1,5},{5,9},{9,... | collective-permute-start | bytes 786440 | tf_op jit(solution)/shard_map/ppermute | solution.py:20
  82.2 1.4 convolution_multiply_fusion
  83.7 1.0 copy-done.2
  84.6 0.4 fusion.56
  85.0 0.8 copy.63
  85.9 0.2 copy.62
  86.0 4.4 %fusion.9.near_ref = f32[2,4,128,128]{3,2,1,0:T(8,128)} fusion(f32[2,4,128]{2,1,0:T(4,128)S(1)} %fusion.56, f32[2,4,128,256]{3,2,1,0:T(8,128)} %copy-done.2, pred[2,128,256]{2,1,0:T(8,128)(4,1)} %fusion.15, bf16[2,128,4,128]{3,1,0,2:T(8,128)(2,1)} %bitcast.145, bf16[2,128,4,128]{3,1,0,2:T(8,128)(2,1)S(1)} %bitcast.146), kind=kOutput, calls=%fused_computation.15 | convolution fusion | flops 69469440 | bytes 2166784 | tf_op jit(solution)/shard_map/ngqk,nkgd->ngqd/dot_general | solution.py:44
  90.4 33.2 %collective-permute-done.3.bk_ref.bv_ref = bf16[2,128,512]{2,1,0:T(8,128)(2,1)S(1)} collective-permute-done((bf16[2,128,512]{2,1,0:T(8,128)(2,1)}, bf16[2,128,512]{2,1,0:T(8,128)(2,1)S(1)}, u32[]{:S(2)}, u32[]{:S(2)}) %collective-permute-start.3) | collective-permute-done | bytes 262176 | tf_op jit(solution)/shard_map/ppermute | solution.py:20
  123.7 0.6 broadcast_in_dim.106.start_ref
  124.3 0.7 broadcast_in_dim.107
  124.9 0.7 broadcast_in_dim.102
  125.6 11.0 %shard_map.73 = bf16[384,512]{1,0:T(8,128)(2,1)} custom-call(bf16[384,1536]{1,0:T(8,128)(2,1)} %convolution_convert_fusion.q_ref.k0_ref.v0_ref, bf16[384,1536]{1,0:T(8,128)(2,1)} %convolution_convert_fusion.q_ref.k0_ref.v0_ref, bf16[384,1536]{1,0:T(8,128)(2,1)} %convolution_convert_fusion.q_ref.k0_ref.v0_ref, bf16[2,128,512]{2,1,0:T(8,128)(2,1)} %copy-done.1, ...), custom_call_target="tpu_custom_call" | custom-call | flops 1677721600 | bytes 5767168 | tf_op jit(solution)/shard_map/pallas_call | solution.py:102
  136.7 2.2 %fusion.57 = f32[384,2560]{1,0:T(8,128)S(1)} fusion(bf16[384,512]{1,0:T(8,128)(2,1)} %shard_map.73, bf16[512,2560]{1,0:T(8,128)(2,1)S(1)} %copy-done), kind=kOutput, calls=%fused_computation.124 | convolution fusion | flops 1006632960 | bytes 6946816 | tf_op jit(solution)/shard_map/dot_general | solution.py:224
  138.8 0.6 fusion.53
  139.5 0.1 collective-permute-start.4
  139.6 0.5 collective-permute-start.6
  140.1 0.1 collective-permute-start.8
  140.2 0.5 collective-permute-start.12
  140.7 0.1 collective-permute-start.10
  140.9 0.2 collective-permute-done.4
  141.1 1.6 %collective-permute-start.5 = (bf16[96,512]{1,0:T(8,128)(2,1)S(1)}, bf16[96,512]{1,0:T(8,128)(2,1)S(1)}, u32[]{:S(2)}, u32[]{:S(2)}) collective-permute-start(bf16[96,512]{1,0:T(8,128)(2,1)S(1)} %fusion.27), channel_id=1, source_target_pairs={{0,2},{1,3},{2,0},{3,1},{4,6},{5,7},{6,4},{7,5},{8,10},{9,11},{10,... | collective-permute-start | bytes 294920 | tf_op jit(solution)/shard_map/ppermute | solution.py:253
  142.8 0.6 collective-permute-start.7
  143.5 1.6 %collective-permute-start.9 = (bf16[96,512]{1,0:T(8,128)(2,1)S(1)}, bf16[96,512]{1,0:T(8,128)(2,1)S(1)}, u32[]{:S(2)}, u32[]{:S(2)}) collective-permute-start(bf16[96,512]{1,0:T(8,128)(2,1)S(1)} %fusion.29), channel_id=1, source_target_pairs={{0,2},{1,3},{2,0},{3,1},{4,6},{5,7},{6,4},{7,5},{8,10},{9,11},{10,... | collective-permute-start | bytes 294920 | tf_op jit(solution)/shard_map/ppermute | solution.py:253
  145.1 0.6 collective-permute-start.13
  145.8 1.6 %collective-permute-start.11 = (bf16[96,512]{1,0:T(8,128)(2,1)S(1)}, bf16[96,512]{1,0:T(8,128)(2,1)S(1)}, u32[]{:S(2)}, u32[]{:S(2)}) collective-permute-start(bf16[96,512]{1,0:T(8,128)(2,1)S(1)} %fusion.30), channel_id=1, source_target_pairs={{0,2},{1,3},{2,0},{3,1},{4,6},{5,7},{6,4},{7,5},{8,10},{9,11},{10,... | collective-permute-start | bytes 294920 | tf_op jit(solution)/shard_map/ppermute | solution.py:253
  147.4 1.5 collective-permute-done.7
  148.9 2.1 %collective-permute-done.9 = bf16[96,512]{1,0:T(8,128)(2,1)S(1)} collective-permute-done((bf16[96,512]{1,0:T(8,128)(2,1)S(1)}, bf16[96,512]{1,0:T(8,128)(2,1)S(1)}, u32[]{:S(2)}, u32[]{:S(2)}) %collective-permute-start.9) | collective-permute-done | bytes 98336 | tf_op jit(solution)/shard_map/ppermute | solution.py:253
  151.0 3.5 %collective-permute-done.11 = bf16[96,512]{1,0:T(8,128)(2,1)S(1)} collective-permute-done((bf16[96,512]{1,0:T(8,128)(2,1)S(1)}, bf16[96,512]{1,0:T(8,128)(2,1)S(1)}, u32[]{:S(2)}, u32[]{:S(2)}) %collective-permute-start.11) | collective-permute-done | bytes 98336 | tf_op jit(solution)/shard_map/ppermute | solution.py:253
  154.6 0.8 copy-done.5
  155.4 0.7 fusion.36
  (51 shorter events, 0.7 us)
Async XLA Ops:
  0.0 136.7 %copy-start = (bf16[512,2560]{1,0:T(8,128)(2,1)S(1)}, bf16[512,2560]{1,0:T(8,128)(2,1)}, u32[]{:S(2)}) copy-start(bf16[512,2560]{1,0:T(8,128)(2,1)} %param.9) | copy-start | bytes 7864324
  20.5 6.9 %copy-start.3 = (bf16[96,2560]{1,0:T(8,128)(2,1)S(1)}, bf16[96,2560]{1,0:T(8,128)(2,1)}, u32[]{:S(2)}) copy-start(bf16[96,2560]{1,0:T(8,128)(2,1)} %param.7) | copy-start | bytes 1474564
  20.5 13.2 %copy-start.6 = (f32[4]{0:T(128)S(1)}, f32[4]{0:T(128)}, u32[]{:S(2)}) copy-start(f32[4]{0:T(128)} %param.10) | copy-start | bytes 52
  20.5 103.1 %all-to-all-start.1 = ((bf16[16,2,128,512]{3,2,1,0:T(8,128)(2,1)}), bf16[16,2,128,512]{3,2,1,0:T(8,128)(2,1)}, u32[]{:S(2)}, u32[]{:S(2)}) async-start(bf16[16,2,128,512]{3,2,1,0:T(8,128)(2,1)} %gather_fusion.1), calls=%async_computation.1 | async-start | bytes 8388608 | tf_op jit(solution)/shard_map/all_to_all | solution.py:205
  27.5 11.7 %collective-permute-start = (bf16[96,2560]{1,0:T(8,128)(2,1)S(1)}, bf16[96,2560]{1,0:T(8,128)(2,1)}, u32[]{:S(2)}, u32[]{:S(2)}) collective-permute-start(bf16[96,2560]{1,0:T(8,128)(2,1)S(1)} %copy-done.3), channel_id=1, source_target_pairs={{0,1},{1,2},{2,3},{3,0},{4,5},{5,6},{6,7},{7,4},{8,9},{9,10},{10,1... | collective-permute-start | bytes 1474568 | tf_op jit(solution)/shard_map/ppermute | solution.py:131
  27.5 13.3 %collective-permute-start.2 = (bf16[96,2560]{1,0:T(8,128)(2,1)S(1)}, bf16[96,2560]{1,0:T(8,128)(2,1)}, u32[]{:S(2)}, u32[]{:S(2)}) collective-permute-start(bf16[96,2560]{1,0:T(8,128)(2,1)S(1)} %copy-done.3), channel_id=1, source_target_pairs={{0,3},{1,0},{2,1},{3,2},{4,7},{5,4},{6,5},{7,6},{8,11},{9,8},{10,9... | collective-permute-start | bytes 1474568 | tf_op jit(solution)/shard_map/ppermute | solution.py:131
  29.2 22.4 %collective-permute-start.1 = (bf16[96,2560]{1,0:T(8,128)(2,1)S(1)}, bf16[96,2560]{1,0:T(8,128)(2,1)}, u32[]{:S(2)}, u32[]{:S(2)}) collective-permute-start(bf16[96,2560]{1,0:T(8,128)(2,1)S(1)} %copy-done.3), channel_id=1, source_target_pairs={{0,2},{1,3},{2,0},{3,1},{4,6},{5,7},{6,4},{7,5},{8,10},{9,11},{10,... | collective-permute-start | bytes 1474568 | tf_op jit(solution)/shard_map/ppermute | solution.py:131
  77.0 7.6 %copy-start.4 = (pred[2,128,256]{2,1,0:T(8,128)(4,1)S(1)}, pred[2,128,256]{2,1,0:T(8,128)(4,1)}, u32[]{:S(2)}) copy-start(pred[2,128,256]{2,1,0:T(8,128)(4,1)} %fusion.15) | copy-start | bytes 196612
  78.7 45.0 %collective-permute-start.3 = (bf16[2,128,512]{2,1,0:T(8,128)(2,1)}, bf16[2,128,512]{2,1,0:T(8,128)(2,1)S(1)}, u32[]{:S(2)}, u32[]{:S(2)}) collective-permute-start(bf16[2,128,512]{2,1,0:T(8,128)(2,1)} %pad_maximum_fusion.3), channel_id=1, source_target_pairs={{0,4},{4,8},{8,12},{12,16},{16,20},{20,24},{24,28},{1,5},{5,9},{9,... | collective-permute-start | bytes 786440 | tf_op jit(solution)/shard_map/ppermute | solution.py:20
  83.6 1.0 copy-start.2
  123.6 2.0 %copy-start.1 = (bf16[2,128,512]{2,1,0:T(8,128)(2,1)}, bf16[2,128,512]{2,1,0:T(8,128)(2,1)S(1)}, u32[]{:S(2)}) copy-start(bf16[2,128,512]{2,1,0:T(8,128)(2,1)S(1)} %collective-permute-done.3.bk_ref.bv_ref) | copy-start | bytes 786436
  139.5 1.5 collective-permute-start.4
  139.6 3.1 %collective-permute-start.6 = (bf16[2,96,512]{2,1,0:T(8,128)(2,1)S(1)}, bf16[2,96,512]{2,1,0:T(8,128)(2,1)S(1)}, u32[]{:S(2)}, u32[]{:S(2)}) collective-permute-start(bf16[2,96,512]{2,1,0:T(8,128)(2,1)S(1)} %fusion.17), channel_id=1, source_target_pairs={{0,1},{1,0},{2,3},{3,2},{4,5},{5,4},{6,7},{7,6},{8,9},{9,8},{10,11... | collective-permute-start | bytes 589832 | tf_op jit(solution)/shard_map/ppermute | solution.py:245
  140.1 3.3 %collective-permute-start.8 = (bf16[2,96,512]{2,1,0:T(8,128)(2,1)S(1)}, bf16[2,96,512]{2,1,0:T(8,128)(2,1)S(1)}, u32[]{:S(2)}, u32[]{:S(2)}) collective-permute-start(bf16[2,96,512]{2,1,0:T(8,128)(2,1)S(1)} %fusion.18), channel_id=1, source_target_pairs={{0,1},{1,0},{2,3},{3,2},{4,5},{5,4},{6,7},{7,6},{8,9},{9,8},{10,11... | collective-permute-start | bytes 589832 | tf_op jit(solution)/shard_map/ppermute | solution.py:245
  140.2 4.8 %collective-permute-start.12 = (bf16[2,96,512]{2,1,0:T(8,128)(2,1)S(1)}, bf16[2,96,512]{2,1,0:T(8,128)(2,1)S(1)}, u32[]{:S(2)}, u32[]{:S(2)}) collective-permute-start(bf16[2,96,512]{2,1,0:T(8,128)(2,1)S(1)} %fusion.20), channel_id=1, source_target_pairs={{0,1},{1,0},{2,3},{3,2},{4,5},{5,4},{6,7},{7,6},{8,9},{9,8},{10,11... | collective-permute-start | bytes 589832 | tf_op jit(solution)/shard_map/ppermute | solution.py:245
  140.7 5.0 %collective-permute-start.10 = (bf16[2,96,512]{2,1,0:T(8,128)(2,1)S(1)}, bf16[2,96,512]{2,1,0:T(8,128)(2,1)S(1)}, u32[]{:S(2)}, u32[]{:S(2)}) collective-permute-start(bf16[2,96,512]{2,1,0:T(8,128)(2,1)S(1)} %fusion.19), channel_id=1, source_target_pairs={{0,1},{1,0},{2,3},{3,2},{4,5},{5,4},{6,7},{7,6},{8,9},{9,8},{10,11... | collective-permute-start | bytes 589832 | tf_op jit(solution)/shard_map/ppermute | solution.py:245
  141.1 6.3 %collective-permute-start.5 = (bf16[96,512]{1,0:T(8,128)(2,1)S(1)}, bf16[96,512]{1,0:T(8,128)(2,1)S(1)}, u32[]{:S(2)}, u32[]{:S(2)}) collective-permute-start(bf16[96,512]{1,0:T(8,128)(2,1)S(1)} %fusion.27), channel_id=1, source_target_pairs={{0,2},{1,3},{2,0},{3,1},{4,6},{5,7},{6,4},{7,5},{8,10},{9,11},{10,... | collective-permute-start | bytes 294920 | tf_op jit(solution)/shard_map/ppermute | solution.py:253
  142.8 6.1 %collective-permute-start.7 = (bf16[96,512]{1,0:T(8,128)(2,1)S(1)}, bf16[96,512]{1,0:T(8,128)(2,1)S(1)}, u32[]{:S(2)}, u32[]{:S(2)}) collective-permute-start(bf16[96,512]{1,0:T(8,128)(2,1)S(1)} %fusion.28), channel_id=1, source_target_pairs={{0,2},{1,3},{2,0},{3,1},{4,6},{5,7},{6,4},{7,5},{8,10},{9,11},{10,... | collective-permute-start | bytes 294920 | tf_op jit(solution)/shard_map/ppermute | solution.py:253
  143.5 7.6 %collective-permute-start.9 = (bf16[96,512]{1,0:T(8,128)(2,1)S(1)}, bf16[96,512]{1,0:T(8,128)(2,1)S(1)}, u32[]{:S(2)}, u32[]{:S(2)}) collective-permute-start(bf16[96,512]{1,0:T(8,128)(2,1)S(1)} %fusion.29), channel_id=1, source_target_pairs={{0,2},{1,3},{2,0},{3,1},{4,6},{5,7},{6,4},{7,5},{8,10},{9,11},{10,... | collective-permute-start | bytes 294920 | tf_op jit(solution)/shard_map/ppermute | solution.py:253
  145.1 9.5 %collective-permute-start.13 = (bf16[96,512]{1,0:T(8,128)(2,1)S(1)}, bf16[96,512]{1,0:T(8,128)(2,1)S(1)}, u32[]{:S(2)}, u32[]{:S(2)}) collective-permute-start(bf16[96,512]{1,0:T(8,128)(2,1)S(1)} %fusion.31), channel_id=1, source_target_pairs={{0,2},{1,3},{2,0},{3,1},{4,6},{5,7},{6,4},{7,5},{8,10},{9,11},{10,... | collective-permute-start | bytes 294920 | tf_op jit(solution)/shard_map/ppermute | solution.py:253
  145.8 8.8 %collective-permute-start.11 = (bf16[96,512]{1,0:T(8,128)(2,1)S(1)}, bf16[96,512]{1,0:T(8,128)(2,1)S(1)}, u32[]{:S(2)}, u32[]{:S(2)}) collective-permute-start(bf16[96,512]{1,0:T(8,128)(2,1)S(1)} %fusion.30), channel_id=1, source_target_pairs={{0,2},{1,3},{2,0},{3,1},{4,6},{5,7},{6,4},{7,5},{8,10},{9,11},{10,... | collective-permute-start | bytes 294920 | tf_op jit(solution)/shard_map/ppermute | solution.py:253
  154.6 0.8 copy-start.5

commit v15 on v11

--- a/solution.py
+++ b/solution.py
@@ -197,12 +197,15 @@
     asked = lax.all_to_all(wanted_ids, "mem", split_axis=0, concat_axis=0, tiled=True).reshape(
         holder_count * CAP
     )
-    picked = jnp.stack(
-        [
-            lax.dynamic_index_in_dim(local_store, jnp.clip(asked[slot], 0, local_blocks - 1), 1, False)
-            for slot in range(holder_count * CAP)
-        ]
-    )
+    chooser = (
+        asked[:, None] == lax.broadcasted_iota(jnp.int32, (holder_count * CAP, local_blocks), 1)
+    ).astype(jnp.bfloat16)
+    picked = jnp.einsum(
+        "sb,pbx->spx",
+        chooser,
+        local_store.reshape(2, local_blocks, BLK * groups * HD),
+        preferred_element_type=jnp.float32,
+    ).astype(jnp.bfloat16).reshape(holder_count * CAP, 2, BLK, groups * HD)
     fetched = lax.all_to_all(picked, "mem", split_axis=0, concat_axis=0, tiled=True)
     pool = holder_count * CAP
     row_of = entry_order // TOPB
@@ -223,9 +226,9 @@
         mixing,
     )
     partial = jnp.dot(attended, output_weight, preferred_element_type=jnp.float32)
-    half = partial.shape[1] // 2
+    width = partial.shape[1] // 4
     return jnp.concatenate(
-        [reduce_over_tp(partial[:, :half]), reduce_over_tp(partial[:, half:])], axis=1
+        [reduce_over_tp(partial[:, k * width:(k + 1) * width]) for k in range(4)], axis=1
     ).astype(jnp.bfloat16)
 
 

time: 192 us -> 165 us (0.86)
  local copies, waits for them, and re-layouts: 53.9 us -> 38.3 us
  blocking collectives: 10 us -> 0 us
  between operations: 10.3 us -> 0.33 us
  starting transfers between devices: 16 us -> 24.6 us
  matrix products: 16.1 us -> 20.8 us
  waiting for transfers between devices: 62.4 us -> 58.9 us
    unnamed x29 -> x11, local copies, waits for them, and re-layouts: 27.3 us -> 2.51 us
    all_to_all x1 -> x0, blocking collectives: 10 us -> none  [local(): lax.all_to_all(wanted_ids, 'mem', split_axis=0, concat_axis=0, tiled=True)]
    another operation x1, local copies, waits for them, and re-layouts: 1.68 us -> 10.6 us  [local(): local_store.reshape(2, local_blocks, BLK * groups * HD)]
    all_to_all x0 -> x1, starting transfers between devices: none -> 6.14 us  [local(): lax.all_to_all(wanted_ids, 'mem', split_axis=0, concat_axis=0, tiled=True)]
    dot_general x0 -> x1, matrix products: none -> 4.68 us  [local(): jnp.einsum('sb,pbx->spx', chooser, local_store.reshape(2, local_blocks, B...]
    reshape x1, local copies, waits for them, and re-layouts: 0.08 us -> 2.43 us  [local(): picked = jnp.einsum('sb,pbx->spx', chooser, local_store.reshape(2, local_...]
    ppermute x2 -> x4, waiting for transfers between devices: 11 us -> 8.68 us  [reduce_over_tp(): lax.ppermute(outgoing.astype(jnp.bfloat16), 'tp', pairs).astype(jnp.float32)]
    ppermute x1, waiting for transfers between devices: 35.1 us -> 33 us  [from_behind(): lax.ppermute(value, axis, [(source, source + steps) for source in range(i...]
  transfers between devices with their start and end apart: 9 -> 14, of which waited for: 6 -> 9; matrix products, arithmetic and copies ran while one was open for 21% -> 30% of each run, Pallas kernels for 0% -> 0%
where the time goes in v15:
time: 165 us
  waiting for transfers between devices  58.9 us (36%)
  local copies, waits for them, and re-layouts  38.3 us (23%)
  starting transfers between devices  24.6 us (15%)
  matrix products  20.8 us (13%)
  Pallas kernels  11 us (7%)
  other arithmetic  10.6 us (6%)
    ppermute x1, waiting for transfers between devices, from_behind(): lax.ppermute(value, axis, [(source, source + steps) for source in range(i...  33 us
    ppermute x3, waiting for transfers between devices, gather_tp(): lax.ppermute(part, 'tp', [(t, (t + shift) % count) for t in range(count)])  17 us
    pallas_call x1, Pallas kernels, far_attention(): pl.pallas_call(far_kernel, grid=(groups,), in_specs=[pl.BlockSpec((rows,...  11 us
    another operation x1, local copies, waits for them, and re-layouts, local(): local_store.reshape(2, local_blocks, BLK * groups * HD)  10.6 us
    ppermute x4, waiting for transfers between devices, reduce_over_tp(): lax.ppermute(outgoing.astype(jnp.bfloat16), 'tp', pairs).astype(jnp.float32)  8.68 us
    dot_general x1, matrix products, local(): jnp.dot(gather_tp(tokens), input_weight, preferred_element_type=jnp.float32)  8.14 us
    all_to_all x1, starting transfers between devices, local(): lax.all_to_all(wanted_ids, 'mem', split_axis=0, concat_axis=0, tiled=True)  6.14 us
    all_to_all x1, starting transfers between devices, local(): lax.all_to_all(picked, 'mem', split_axis=0, concat_axis=0, tiled=True)  6.13 us
  transfers between devices with their start and end apart: 14, of which 9 were waited for; matrix products, arithmetic and copies ran while one was open for 30% of the time, Pallas kernels for 0%

profile of v15, /device:TPU:16, one launch (start us, length us, event | category | flops | bytes accessed | tf_op | source)
XLA Modules:
  0.0 164.5 jit_solution(10970730514343825870)
XLA Ops:
  0.0 0.9 eq.84
  0.9 0.9 select_reduce_fusion.1
  1.8 0.2 convert_reduce_fusion.1
  2.0 0.7 compare_reduce_fusion
  2.7 0.2 convert_reduce_fusion
  2.9 0.1 select_reduce_fusion.2
  3.0 0.7 copy.55
  3.7 6.1 %all-to-all-start = ((s32[8,1,2]{2,1,0:T(1,128)}), s32[8,1,2]{2,1,0:T(1,128)S(1)}, u32[]{:S(2)}, u32[]{:S(2)}) async-start(s32[8,1,2]{2,1,0:T(1,128)} %copy.55), calls=%async_computation | async-start | bytes 8192 | tf_op jit(solution)/shard_map/all_to_all | solution.py:197
  9.8 10.6 %reshape_reshape.6 = bf16[2,32,65536]{2,1,0:T(8,128)(2,1)} reshape(bf16[2,4096,512]{2,1,0:T(8,128)(2,1)} %param.11) | data formatting | bytes 16777216 | tf_op jit(solution)/shard_map/reshape;reshape | solution.py:206
  20.4 0.5 broadcast.399
  20.9 0.7 reduce.22
  21.5 0.1 eq.98
  21.6 4.7 %convolution_convert_fusion = bf16[16,2,65536]{2,0,1:T(8,128)(2,1)S(1)} fusion(bf16[2,32,65536]{2,1,0:T(8,128)(2,1)} %reshape_reshape.6, s32[16]{0:T(128)S(1)} %eq.98), kind=kOutput, calls=%fused_computation.3 | convolution fusion | flops 136315392 | bytes 12582976 | tf_op jit(solution)/shard_map/sb,pbx->spx/dot_general | solution.py:203
  26.3 1.5 copy.80
  27.9 2.4 %copy.73 = bf16[16,2,128,512]{3,2,1,0:T(8,128)(2,1)} copy(bf16[16,2,128,512]{3,2,0,1:T(8,128)(2,1)S(1)} %bitcast.110) | data formatting | bytes 8388608 | tf_op jit(solution)/shard_map/reshape | solution.py:208
  30.3 6.1 %all-to-all-start.1 = ((bf16[16,2,128,512]{3,2,1,0:T(8,128)(2,1)}), bf16[16,2,128,512]{3,2,1,0:T(8,128)(2,1)}, u32[]{:S(2)}, u32[]{:S(2)}) async-start(bf16[16,2,128,512]{3,2,1,0:T(8,128)(2,1)} %copy.73), calls=%async_computation.1 | async-start | bytes 8388608 | tf_op jit(solution)/shard_map/all_to_all | solution.py:209
  36.4 1.7 %collective-permute-start.2 = (bf16[96,2560]{1,0:T(8,128)(2,1)S(1)}, bf16[96,2560]{1,0:T(8,128)(2,1)}, u32[]{:S(2)}, u32[]{:S(2)}) collective-permute-start(bf16[96,2560]{1,0:T(8,128)(2,1)S(1)} %copy-done.3), channel_id=1, source_target_pairs={{0,3},{1,0},{2,1},{3,2},{4,7},{5,4},{6,5},{7,6},{8,11},{9,8},{10,9... | collective-permute-start | bytes 1474568 | tf_op jit(solution)/shard_map/ppermute | solution.py:131
  38.2 1.5 collective-permute-start.1
  39.7 2.8 %scatter_fusion = pred[3,16]{1,0:T(4,128)(4,1)S(1)} fusion(pred[3,16]{1,0:T(4,128)(4,1)S(1)} %broadcast_in_dim.93, s32[48]{0:T(128)S(1)} %fusion.41, pred[48]{0:T(512)(128)(4,1)S(1)} %broadcast.369), kind=kCustom, calls=%fused_computation.1 | custom fusion | bytes 528 | tf_op jit(solution)/shard_map/scatter | solution.py:213
  42.8 0.1 fusion.24
  42.9 0.7 fusion.15
  43.6 4.6 %collective-permute-done = bf16[96,2560]{1,0:T(8,128)(2,1)} collective-permute-done((bf16[96,2560]{1,0:T(8,128)(2,1)S(1)}, bf16[96,2560]{1,0:T(8,128)(2,1)}, u32[]{:S(2)}, u32[]{:S(2)}) %collective-permute-start) | collective-permute-done | bytes 491552 | tf_op jit(solution)/shard_map/ppermute | solution.py:131
  48.2 1.6 collective-permute-done.2
  49.8 10.8 %collective-permute-done.1 = bf16[96,2560]{1,0:T(8,128)(2,1)} collective-permute-done((bf16[96,2560]{1,0:T(8,128)(2,1)S(1)}, bf16[96,2560]{1,0:T(8,128)(2,1)}, u32[]{:S(2)}, u32[]{:S(2)}) %collective-permute-start.1) | collective-permute-done | bytes 491552 | tf_op jit(solution)/shard_map/ppermute | solution.py:131
  60.6 2.9 %pad_maximum_fusion = bf16[4,96,2560]{2,1,0:T(8,128)(2,1)} fusion(bf16[1,96,2560]{2,1,0:T(8,128)(2,1)} %bitcast.3, bf16[1,96,2560]{2,1,0:T(8,128)(2,1)} %bitcast.2, bf16[1,96,2560]{2,1,0:T(8,128)(2,1)} %bitcast.1, bf16[1,96,2560]{2,1,0:T(8,128)(2,1)S(1)} %bitcast.127), kind=kLoop, calls=%fused_computation.5 | loop fusion | flops 2949120 | bytes 3932160 | tf_op jit(solution)/shard_map/stack | solution.py:135
  63.5 3.5 %gather_fusion = bf16[4,96,2560]{2,1,0:T(8,128)(2,1)} fusion(bf16[4,96,2560]{2,1,0:T(8,128)(2,1)} %pad_maximum_fusion, s32[1024]{0:T(1024)S(1)} %pad_clamp_fusion), kind=kCustom, calls=%fused_computation | custom fusion | bytes 3932176 | tf_op jit(solution)/shard_map/jit(_take)/gather | solution.py:135
  67.0 8.1 %convolution_convert_fusion.1.q_ref.k0_ref.v0_ref = bf16[384,1536]{1,0:T(8,128)(2,1)} fusion(bf16[384,2560]{1,0:T(8,128)(2,1)} %bitcast.121, bf16[2560,1536]{1,0:T(8,128)(2,1)} %param.8), kind=kOutput, calls=%fused_computation.4 | convolution fusion | flops 3020488704 | bytes 11010048 | tf_op jit(solution)/shard_map/dot_general | solution.py:145
  75.1 2.4 %copy.52 = bf16[384,1536]{0,1:T(8,128)(2,1)} copy(bf16[384,1536]{1,0:T(8,128)(2,1)} %convolution_convert_fusion.1.q_ref.k0_ref.v0_ref) | data formatting | bytes 2359296 | tf_op jit(solution)/shard_map/convert_element_type | solution.py:150
  77.5 1.0 fusion.50
  78.5 0.1 copy.71
  78.6 0.8 copy.72
  79.4 2.2 %fusion.49 = (bf16[256,4,1,128]{0,3,2,1:T(8,128)(2,1)}, bf16[256,4,1,128]{0,3,2,1:T(8,128)(2,1)S(1)}, bf16[256,4,1,128]{0,3,2,1:T(8,128)(2,1)S(1)}, bf16[256,4,1...) fusion(bf16[384,4,3,128]{0,3,2,1:T(8,128)(2,1)} %bitcast.112), kind=kLoop, calls=%fused_computation.112 | loop fusion | bytes 2621440 | tf_op jit(solution)/shard_map/slice | solution.py:163
  81.6 1.8 %copy.57 = bf16[256,4,1,128]{3,0,1,2:T(8,128)(2,1)} copy(bf16[256,4,1,128]{0,3,2,1:T(8,128)(2,1)} %get-tuple-element.11) | data formatting | bytes 524288 | tf_op jit(solution)/shard_map/slice | solution.py:163
  83.3 1.8 %copy.59 = bf16[256,4,1,128]{3,0,1,2:T(8,128)(2,1)} copy(bf16[256,4,1,128]{0,3,2,1:T(8,128)(2,1)} %get-tuple-element.14) | data formatting | bytes 524288 | tf_op jit(solution)/shard_map/slice | solution.py:164
  85.1 0.8 copy.58
  86.0 1.6 pad_maximum_fusion.4
  87.6 3.5 %collective-permute-start.3 = (bf16[2,128,512]{2,1,0:T(8,128)(2,1)}, bf16[2,128,512]{2,1,0:T(8,128)(2,1)S(1)}, u32[]{:S(2)}, u32[]{:S(2)}) collective-permute-start(bf16[2,128,512]{2,1,0:T(8,128)(2,1)} %pad_maximum_fusion.4), channel_id=1, source_target_pairs={{0,4},{4,8},{8,12},{12,16},{16,20},{20,24},{24,28},{1,5},{5,9},{9,... | collective-permute-start | bytes 786440 | tf_op jit(solution)/shard_map/ppermute | solution.py:20
  91.1 1.4 convolution_multiply_fusion
  92.6 1.0 copy-done.2
  93.5 1.3 fusion.51
  94.8 0.9 copy.64
  95.7 0.2 copy.63
  95.9 4.4 %fusion.9.near_ref = f32[2,4,128,128]{3,2,1,0:T(8,128)} fusion(f32[2,4,128]{2,1,0:T(4,128)S(1)} %fusion.51, f32[2,4,128,256]{3,2,1,0:T(8,128)} %copy-done.2, pred[2,128,256]{2,1,0:T(8,128)(4,1)} %fusion.15, bf16[2,128,4,128]{3,1,0,2:T(8,128)(2,1)} %bitcast.128, bf16[2,128,4,128]{3,1,0,2:T(8,128)(2,1)S(1)} %bitcast.129), kind=kOutput, calls=%fused_computation.15 | convolution fusion | flops 69469440 | bytes 2166784 | tf_op jit(solution)/shard_map/ngqk,nkgd->ngqd/dot_general | solution.py:44
  100.2 33.0 %collective-permute-done.3.bk_ref.bv_ref = bf16[2,128,512]{2,1,0:T(8,128)(2,1)S(1)} collective-permute-done((bf16[2,128,512]{2,1,0:T(8,128)(2,1)}, bf16[2,128,512]{2,1,0:T(8,128)(2,1)S(1)}, u32[]{:S(2)}, u32[]{:S(2)}) %collective-permute-start.3) | collective-permute-done | bytes 262176 | tf_op jit(solution)/shard_map/ppermute | solution.py:20
  133.2 0.6 broadcast_in_dim.101.start_ref
  133.8 0.7 broadcast_in_dim.102
  134.5 0.7 broadcast_in_dim.97
  135.2 11.0 %shard_map.73 = bf16[384,512]{1,0:T(8,128)(2,1)} custom-call(bf16[384,1536]{1,0:T(8,128)(2,1)} %convolution_convert_fusion.1.q_ref.k0_ref.v0_ref, bf16[384,1536]{1,0:T(8,128)(2,1)} %convolution_convert_fusion.1.q_ref.k0_ref.v0_ref, bf16[384,1536]{1,0:T(8,128)(2,1)} %convolution_convert_fusion.1.q_ref.k0_ref.v0_ref, bf16[2,128,512]{2,1,0:T(8,128)(2,1)} %copy-done.1, ...), custom_call_target="tpu_custom_call" | custom-call | flops 1677721600 | bytes 5767168 | tf_op jit(solution)/shard_map/pallas_call | solution.py:102
  146.2 2.2 %fusion.52 = f32[384,2560]{1,0:T(8,128)S(1)} fusion(bf16[384,512]{1,0:T(8,128)(2,1)} %shard_map.73, bf16[512,2560]{1,0:T(8,128)(2,1)S(1)} %copy-done), kind=kOutput, calls=%fused_computation.115 | convolution fusion | flops 1006632960 | bytes 6946816 | tf_op jit(solution)/shard_map/dot_general | solution.py:228
  148.4 0.3 fusion.48
  148.7 0.1 collective-permute-start.6
  148.8 0.5 collective-permute-start.8
  149.4 0.1 collective-permute-start.4
  149.5 0.5 collective-permute-start.10
  150.1 0.2 collective-permute-done.6
  150.4 1.6 collective-permute-start.7
  152.0 0.6 collective-permute-start.9
  152.7 1.6 collective-permute-start.5
  154.4 0.6 collective-permute-start.11
  154.9 1.7 %collective-permute-done.7 = bf16[96,640]{1,0:T(8,128)(2,1)S(1)} collective-permute-done((bf16[96,640]{1,0:T(8,128)(2,1)S(1)}, bf16[96,640]{1,0:T(8,128)(2,1)S(1)}, u32[]{:S(2)}, u32[]{:S(2)}) %collective-permute-start.7) | collective-permute-done | bytes 122912 | tf_op jit(solution)/shard_map/ppermute | solution.py:253
  156.6 2.6 %collective-permute-done.9 = bf16[96,640]{1,0:T(8,128)(2,1)S(1)} collective-permute-done((bf16[96,640]{1,0:T(8,128)(2,1)S(1)}, bf16[96,640]{1,0:T(8,128)(2,1)S(1)}, u32[]{:S(2)}, u32[]{:S(2)}) %collective-permute-start.9) | collective-permute-done | bytes 122912 | tf_op jit(solution)/shard_map/ppermute | solution.py:253
  159.3 2.6 %collective-permute-done.5 = bf16[96,640]{1,0:T(8,128)(2,1)S(1)} collective-permute-done((bf16[96,640]{1,0:T(8,128)(2,1)S(1)}, bf16[96,640]{1,0:T(8,128)(2,1)S(1)}, u32[]{:S(2)}, u32[]{:S(2)}) %collective-permute-start.5) | collective-permute-done | bytes 122912 | tf_op jit(solution)/shard_map/ppermute | solution.py:253
  161.9 1.8 %collective-permute-done.11 = bf16[96,640]{1,0:T(8,128)(2,1)S(1)} collective-permute-done((bf16[96,640]{1,0:T(8,128)(2,1)S(1)}, bf16[96,640]{1,0:T(8,128)(2,1)S(1)}, u32[]{:S(2)}, u32[]{:S(2)}) %collective-permute-start.11) | collective-permute-done | bytes 122912 | tf_op jit(solution)/shard_map/ppermute | solution.py:253
  163.7 0.8 pad_maximum_fusion.3
  (43 shorter events, 0.7 us)
Async XLA Ops:
  0.0 146.2 %copy-start = (bf16[512,2560]{1,0:T(8,128)(2,1)S(1)}, bf16[512,2560]{1,0:T(8,128)(2,1)}, u32[]{:S(2)}) copy-start(bf16[512,2560]{1,0:T(8,128)(2,1)} %param.9) | copy-start | bytes 7864324
  3.7 16.7 %all-to-all-start = ((s32[8,1,2]{2,1,0:T(1,128)}), s32[8,1,2]{2,1,0:T(1,128)S(1)}, u32[]{:S(2)}, u32[]{:S(2)}) async-start(s32[8,1,2]{2,1,0:T(1,128)} %copy.55), calls=%async_computation | async-start | bytes 8192 | tf_op jit(solution)/shard_map/all_to_all | solution.py:197
  30.3 6.1 %copy-start.3 = (bf16[96,2560]{1,0:T(8,128)(2,1)S(1)}, bf16[96,2560]{1,0:T(8,128)(2,1)}, u32[]{:S(2)}) copy-start(bf16[96,2560]{1,0:T(8,128)(2,1)} %param.7) | copy-start | bytes 1474564
  30.3 12.4 %copy-start.4 = (f32[4]{0:T(128)S(1)}, f32[4]{0:T(128)}, u32[]{:S(2)}) copy-start(f32[4]{0:T(128)} %param.10) | copy-start | bytes 52
  30.3 102.9 %all-to-all-start.1 = ((bf16[16,2,128,512]{3,2,1,0:T(8,128)(2,1)}), bf16[16,2,128,512]{3,2,1,0:T(8,128)(2,1)}, u32[]{:S(2)}, u32[]{:S(2)}) async-start(bf16[16,2,128,512]{3,2,1,0:T(8,128)(2,1)} %copy.73), calls=%async_computation.1 | async-start | bytes 8388608 | tf_op jit(solution)/shard_map/all_to_all | solution.py:209
  36.4 11.7 %collective-permute-start = (bf16[96,2560]{1,0:T(8,128)(2,1)S(1)}, bf16[96,2560]{1,0:T(8,128)(2,1)}, u32[]{:S(2)}, u32[]{:S(2)}) collective-permute-start(bf16[96,2560]{1,0:T(8,128)(2,1)S(1)} %copy-done.3), channel_id=1, source_target_pairs={{0,1},{1,2},{2,3},{3,0},{4,5},{5,6},{6,7},{7,4},{8,9},{9,10},{10,1... | collective-permute-start | bytes 1474568 | tf_op jit(solution)/shard_map/ppermute | solution.py:131
  36.4 13.3 %collective-permute-start.2 = (bf16[96,2560]{1,0:T(8,128)(2,1)S(1)}, bf16[96,2560]{1,0:T(8,128)(2,1)}, u32[]{:S(2)}, u32[]{:S(2)}) collective-permute-start(bf16[96,2560]{1,0:T(8,128)(2,1)S(1)} %copy-done.3), channel_id=1, source_target_pairs={{0,3},{1,0},{2,1},{3,2},{4,7},{5,4},{6,5},{7,6},{8,11},{9,8},{10,9... | collective-permute-start | bytes 1474568 | tf_op jit(solution)/shard_map/ppermute | solution.py:131
  38.2 22.4 %collective-permute-start.1 = (bf16[96,2560]{1,0:T(8,128)(2,1)S(1)}, bf16[96,2560]{1,0:T(8,128)(2,1)}, u32[]{:S(2)}, u32[]{:S(2)}) collective-permute-start(bf16[96,2560]{1,0:T(8,128)(2,1)S(1)} %copy-done.3), channel_id=1, source_target_pairs={{0,2},{1,3},{2,0},{3,1},{4,6},{5,7},{6,4},{7,5},{8,10},{9,11},{10,... | collective-permute-start | bytes 1474568 | tf_op jit(solution)/shard_map/ppermute | solution.py:131
  87.6 45.6 %collective-permute-start.3 = (bf16[2,128,512]{2,1,0:T(8,128)(2,1)}, bf16[2,128,512]{2,1,0:T(8,128)(2,1)S(1)}, u32[]{:S(2)}, u32[]{:S(2)}) collective-permute-start(bf16[2,128,512]{2,1,0:T(8,128)(2,1)} %pad_maximum_fusion.4), channel_id=1, source_target_pairs={{0,4},{4,8},{8,12},{12,16},{16,20},{20,24},{24,28},{1,5},{5,9},{9,... | collective-permute-start | bytes 786440 | tf_op jit(solution)/shard_map/ppermute | solution.py:20
  92.5 1.0 copy-start.2
  133.2 2.0 %copy-start.1 = (bf16[2,128,512]{2,1,0:T(8,128)(2,1)}, bf16[2,128,512]{2,1,0:T(8,128)(2,1)S(1)}, u32[]{:S(2)}) copy-start(bf16[2,128,512]{2,1,0:T(8,128)(2,1)S(1)} %collective-permute-done.3.bk_ref.bv_ref) | copy-start | bytes 786436
  148.7 1.6 collective-permute-start.6
  148.8 3.1 %collective-permute-start.8 = (bf16[2,96,640]{2,1,0:T(8,128)(2,1)S(1)}, bf16[2,96,640]{2,1,0:T(8,128)(2,1)S(1)}, u32[]{:S(2)}, u32[]{:S(2)}) collective-permute-start(bf16[2,96,640]{2,1,0:T(8,128)(2,1)S(1)} %fusion.18), channel_id=1, source_target_pairs={{0,1},{1,0},{2,3},{3,2},{4,5},{5,4},{6,7},{7,6},{8,9},{9,8},{10,11... | collective-permute-start | bytes 737288 | tf_op jit(solution)/shard_map/ppermute | solution.py:245
  149.4 3.2 %collective-permute-start.4 = (bf16[2,96,640]{2,1,0:T(8,128)(2,1)S(1)}, bf16[2,96,640]{2,1,0:T(8,128)(2,1)S(1)}, u32[]{:S(2)}, u32[]{:S(2)}) collective-permute-start(bf16[2,96,640]{2,1,0:T(8,128)(2,1)S(1)} %fusion.16), channel_id=1, source_target_pairs={{0,1},{1,0},{2,3},{3,2},{4,5},{5,4},{6,7},{7,6},{8,9},{9,8},{10,11... | collective-permute-start | bytes 737288 | tf_op jit(solution)/shard_map/ppermute | solution.py:245
  149.5 4.7 %collective-permute-start.10 = (bf16[2,96,640]{2,1,0:T(8,128)(2,1)S(1)}, bf16[2,96,640]{2,1,0:T(8,128)(2,1)S(1)}, u32[]{:S(2)}, u32[]{:S(2)}) collective-permute-start(bf16[2,96,640]{2,1,0:T(8,128)(2,1)S(1)} %fusion.19), channel_id=1, source_target_pairs={{0,1},{1,0},{2,3},{3,2},{4,5},{5,4},{6,7},{7,6},{8,9},{9,8},{10,11... | collective-permute-start | bytes 737288 | tf_op jit(solution)/shard_map/ppermute | solution.py:245
  150.4 6.2 %collective-permute-start.7 = (bf16[96,640]{1,0:T(8,128)(2,1)S(1)}, bf16[96,640]{1,0:T(8,128)(2,1)S(1)}, u32[]{:S(2)}, u32[]{:S(2)}) collective-permute-start(bf16[96,640]{1,0:T(8,128)(2,1)S(1)} %fusion.26), channel_id=1, source_target_pairs={{0,2},{1,3},{2,0},{3,1},{4,6},{5,7},{6,4},{7,5},{8,10},{9,11},{10,... | collective-permute-start | bytes 368648 | tf_op jit(solution)/shard_map/ppermute | solution.py:253
  152.0 7.2 %collective-permute-start.9 = (bf16[96,640]{1,0:T(8,128)(2,1)S(1)}, bf16[96,640]{1,0:T(8,128)(2,1)S(1)}, u32[]{:S(2)}, u32[]{:S(2)}) collective-permute-start(bf16[96,640]{1,0:T(8,128)(2,1)S(1)} %fusion.27), channel_id=1, source_target_pairs={{0,2},{1,3},{2,0},{3,1},{4,6},{5,7},{6,4},{7,5},{8,10},{9,11},{10,... | collective-permute-start | bytes 368648 | tf_op jit(solution)/shard_map/ppermute | solution.py:253
  152.7 9.2 %collective-permute-start.5 = (bf16[96,640]{1,0:T(8,128)(2,1)S(1)}, bf16[96,640]{1,0:T(8,128)(2,1)S(1)}, u32[]{:S(2)}, u32[]{:S(2)}) collective-permute-start(bf16[96,640]{1,0:T(8,128)(2,1)S(1)} %fusion.25), channel_id=1, source_target_pairs={{0,2},{1,3},{2,0},{3,1},{4,6},{5,7},{6,4},{7,5},{8,10},{9,11},{10,... | collective-permute-start | bytes 368648 | tf_op jit(solution)/shard_map/ppermute | solution.py:253
  154.4 9.3 %collective-permute-start.11 = (bf16[96,640]{1,0:T(8,128)(2,1)S(1)}, bf16[96,640]{1,0:T(8,128)(2,1)S(1)}, u32[]{:S(2)}, u32[]{:S(2)}) collective-permute-start(bf16[96,640]{1,0:T(8,128)(2,1)S(1)} %fusion.28), channel_id=1, source_target_pairs={{0,2},{1,3},{2,0},{3,1},{4,6},{5,7},{6,4},{7,5},{8,10},{9,11},{10,... | collective-permute-start | bytes 368648 | tf_op jit(solution)/shard_map/ppermute | solution.py:253

commit v16 on v13

--- a/solution.py
+++ b/solution.py
@@ -47,11 +47,13 @@
 
 
 def far_kernel(
-    q_ref, k0_ref, v0_ref, bk_ref, bv_ref, k_ref, v_ref, bias_ref, near_ref, start_ref, mix_ref, o_ref
+    q_ref, k0_ref, v0_ref, bk_ref, bv_ref, k_ref, kb_ref, v_ref, vb_ref, bias_ref, near_ref, start_ref, mix_ref, o_ref
 ):
-    pool = k_ref.shape[0]
-    keys = k_ref[:, 0].reshape(pool * BLK, HD)
-    values = v_ref[:, 0].reshape(pool * BLK, HD)
+    span = k_ref.shape[0] * BLK
+    keys = k_ref[:, 0].reshape(span, HD)
+    values = v_ref[:, 0].reshape(span, HD)
+    keys_b = kb_ref[:, 0].reshape(span, HD)
+    values_b = vb_ref[:, 0].reshape(span, HD)
     mix = mix_ref[...]
     contract = (((1,), (1,)), ((), ()))
     first_query = q_ref[0:BLK, :]
@@ -83,21 +85,32 @@
     )
     for block in range(q_ref.shape[0] // BLK):
         rows = slice(block * BLK, (block + 1) * BLK)
+        query = q_ref[rows, :]
         scores = lax.dot_general(
-            q_ref[rows, :], keys, contract, preferred_element_type=jnp.float32
-        ) + bias_ref[block]
-        peak = jnp.max(scores, axis=-1, keepdims=True)
+            query, keys, contract, preferred_element_type=jnp.float32
+        ) + bias_ref[block, :, 0:span]
+        scores_b = lax.dot_general(
+            query, keys_b, contract, preferred_element_type=jnp.float32
+        ) + bias_ref[block, :, span:2 * span]
+        peak = jnp.maximum(
+            jnp.max(scores, axis=-1, keepdims=True), jnp.max(scores_b, axis=-1, keepdims=True)
+        )
         weights = jnp.exp((scores - peak) * (HD ** (-0.5)))
-        scale = 1.0 / jnp.sum(weights, axis=-1, keepdims=True)
-        far = jnp.dot(weights.astype(jnp.bfloat16), values, preferred_element_type=jnp.float32)
+        weights_b = jnp.exp((scores_b - peak) * (HD ** (-0.5)))
+        scale = 1.0 / (
+            jnp.sum(weights, axis=-1, keepdims=True) + jnp.sum(weights_b, axis=-1, keepdims=True)
+        )
+        far = jnp.dot(
+            weights.astype(jnp.bfloat16), values, preferred_element_type=jnp.float32
+        ) + jnp.dot(weights_b.astype(jnp.bfloat16), values_b, preferred_element_type=jnp.float32)
         near = first_near if block == 0 else near_ref[block - 1, 0]
         o_ref[rows, :] = (mix * (far * scale) + (1.0 - mix) * near).astype(o_ref.dtype)
 
 
-def far_attention(projected, before, fetched, bias, later, start, mixing):
+def far_attention(projected, before, fetched, fetched_b, bias, later, start, mixing):
     rows = projected.shape[0]
     blocks = rows // BLK
-    pool = fetched.shape[0]
+    pool = fetched.shape[0] * 2
     groups = fetched.shape[3] // HD
     return pl.pallas_call(
         far_kernel,
@@ -108,8 +121,10 @@
             pl.BlockSpec((BLK, HD), lambda h: (0, h * 3 + 2)),
             pl.BlockSpec((1, BLK, HD), lambda h: (0, 0, h)),
             pl.BlockSpec((1, BLK, HD), lambda h: (1, 0, h)),
-            pl.BlockSpec((pool, 1, BLK, HD), lambda h: (0, 0, 0, h)),
-            pl.BlockSpec((pool, 1, BLK, HD), lambda h: (0, 1, 0, h)),
+            pl.BlockSpec((pool // 2, 1, BLK, HD), lambda h: (0, 0, 0, h)),
+            pl.BlockSpec((pool // 2, 1, BLK, HD), lambda h: (0, 0, 0, h)),
+            pl.BlockSpec((pool // 2, 1, BLK, HD), lambda h: (0, 1, 0, h)),
+            pl.BlockSpec((pool // 2, 1, BLK, HD), lambda h: (0, 1, 0, h)),
             pl.BlockSpec((blocks, 1, pool * BLK), lambda h: (0, 0, 0)),
             pl.BlockSpec((blocks - 1, 1, BLK, HD), lambda h: (0, h, 0, 0)),
             pl.BlockSpec((1, BLK), lambda h: (0, 0)),
@@ -120,9 +135,12 @@
         cost_estimate=pl.CostEstimate(
             flops=groups * (blocks * pool + 2) * 4 * BLK * BLK * HD,
             transcendentals=groups * (blocks * pool + 2) * BLK * BLK,
-            bytes_accessed=fetched.size * 2 + rows * groups * HD * 8,
+            bytes_accessed=fetched.size * 4 + rows * groups * HD * 8,
         ),
-    )(projected, projected, projected, before, before, fetched, fetched, bias, later, start, mixing)
+    )(
+        projected, projected, projected, before, before,
+        fetched, fetched_b, fetched, fetched_b, bias, later, start, mixing,
+    )
 
 def gather_tp(part):
     count = lax.axis_size("tp")
@@ -194,19 +212,21 @@
         ),
         axis=2,
     )
-    picked = jnp.take(
-        local_store,
-        lax.all_to_all(wanted_ids, "mem", split_axis=0, concat_axis=0, tiled=True).reshape(
-            holder_count * CAP
-        ),
-        axis=1,
-        mode="clip",
-    ).transpose(1, 0, 2, 3)
-    fetched = lax.all_to_all(picked, "mem", split_axis=0, concat_axis=0, tiled=True)
+    asked = lax.all_to_all(wanted_ids, "mem", split_axis=0, concat_axis=0, tiled=True)
+    halves = [
+        lax.all_to_all(
+            jnp.take(local_store, asked[:, part], axis=1, mode="clip").transpose(1, 0, 2, 3),
+            "mem",
+            split_axis=0,
+            concat_axis=0,
+            tiled=True,
+        )
+        for part in range(CAP)
+    ]
     pool = holder_count * CAP
     row_of = entry_order // TOPB
     member = (
-        jnp.zeros((blocks_here, pool), jnp.bool_).at[row_of, holder * CAP + slot_of].set(True)
+        jnp.zeros((blocks_here, pool), jnp.bool_).at[row_of, slot_of * holder_count + holder].set(True)
     )
     bias = jnp.where(jnp.repeat(member, BLK, axis=1), 0.0, NEG_FILL).reshape(
         blocks_here, 1, pool * BLK
@@ -215,7 +235,8 @@
     attended = far_attention(
         projected_flat,
         before,
-        fetched,
+        halves[0],
+        halves[1],
         bias,
         later,
         jnp.full((1, BLK), jnp.where(lax.axis_index("mem") > 0, 1.0, 0.0), jnp.float32),

time: 156 us -> 161 us (1.032)
  starting transfers between devices: 19.1 us -> 26.6 us
  waiting for transfers between devices: 59.3 us -> 53.3 us
  local copies, waits for them, and re-layouts: 29.3 us -> 33.5 us
    all_to_all x1 -> x2, waiting for transfers between devices: 0.01 us -> 32.2 us  [local(): lax.all_to_all(jnp.take(local_store, asked[:, part], axis=1, mode='clip')...]
    ppermute x1, waiting for transfers between devices: 33.4 us -> 12.2 us  [from_behind(): lax.ppermute(value, axis, [(source, source + steps) for source in range(i...]
    ppermute x3, waiting for transfers between devices: 17 us -> 0.01 us  [gather_tp(): lax.ppermute(part, 'tp', [(t, (t + shift) % count) for t in range(count)])]
    all_to_all x1 -> x2, starting transfers between devices: 6.94 us -> 14.4 us  [local(): lax.all_to_all(jnp.take(local_store, asked[:, part], axis=1, mode='clip')...]
    gather x1 -> x2, local copies, waits for them, and re-layouts: 6.17 us -> 10.7 us  [local(): jnp.take(local_store, asked[:, part], axis=1, mode='clip')]
  transfers between devices with their start and end apart: 13 -> 14, of which waited for: 9 -> 7; matrix products, arithmetic and copies ran while one was open for 25% -> 27% of each run, Pallas kernels for 0% -> 0%
where the time goes in v16:
time: 161 us; the launch traced here: 160 us
  waiting for transfers between devices  53.3 us (33%)
  local copies, waits for them, and re-layouts  33.5 us (21%)
  starting transfers between devices  26.6 us (17%)
  matrix products  16.1 us (10%)
  Pallas kernels  10.9 us (7%)
  blocking collectives  10 us (6%)
  other arithmetic  9.04 us (6%)
    all_to_all x2, waiting for transfers between devices, local(): lax.all_to_all(jnp.take(local_store, asked[:, part], axis=1, mode='clip')...  32.2 us
    all_to_all x2, starting transfers between devices, local(): lax.all_to_all(jnp.take(local_store, asked[:, part], axis=1, mode='clip')...  14.4 us
    ppermute x1, waiting for transfers between devices, from_behind(): lax.ppermute(value, axis, [(source, source + steps) for source in range(i...  12.2 us
    pallas_call x1, Pallas kernels, far_attention(): pl.pallas_call(far_kernel, grid=(groups,), in_specs=[pl.BlockSpec((rows,...  10.9 us
    gather x2, local copies, waits for them, and re-layouts, local(): jnp.take(local_store, asked[:, part], axis=1, mode='clip')  10.7 us
    all_to_all x1, blocking collectives, local(): lax.all_to_all(wanted_ids, 'mem', split_axis=0, concat_axis=0, tiled=True)  10 us
    ppermute x4, waiting for transfers between devices, reduce_over_tp(): lax.ppermute(outgoing.astype(jnp.bfloat16), 'tp', pairs).astype(jnp.float32)  8.68 us
    dot_general x1, matrix products, local(): jnp.dot(gather_tp(tokens), input_weight, preferred_element_type=jnp.float32)  8.07 us
  transfers between devices with their start and end apart: 14, of which 7 were waited for; matrix products, arithmetic and copies ran while one was open for 27% of the time, Pallas kernels for 0%

profile of v16, /device:TPU:16, one launch (start us, length us, event | category | flops | bytes accessed | tf_op | source)
XLA Modules:
  0.0 159.8 jit_solution(2616155017762038846)
XLA Ops:
  0.0 0.9 eq.74
  0.9 0.9 select_reduce_fusion.1
  1.8 0.2 convert_reduce_fusion.1
  2.0 0.7 compare_reduce_fusion
  2.7 0.2 convert_reduce_fusion
  2.9 0.1 select_reduce_fusion.2
  3.0 0.1 copy.51
  3.1 10.0 %all_to_all.22 = s32[8,1,2]{2,1,0:T(1,128)S(1)} all-to-all(s32[8,1,2]{2,1,0:T(1,128)S(1)} %copy.51), channel_id=1, replica_groups=mesh['mem'=8,'tp'=4] {'mem'}, dimensions={0} | all-to-all | bytes 128 | tf_op jit(solution)/shard_map/all_to_all | solution.py:215
  13.1 0.1 copy.52
  13.2 5.4 %gather_fusion.1 = bf16[8,2,128,512]{3,2,1,0:T(8,128)(2,1)} fusion(bf16[2,32,128,512]{3,2,1,0:T(8,128)(2,1)} %bitcast.115, s32[1024]{0:T(1024)S(1)} %pad_clamp_fusion.1), kind=kCustom, calls=%fused_computation.1 | custom fusion | bytes 4194336 | tf_op jit(solution)/shard_map/jit(_take)/gather | solution.py:218
  18.6 6.7 %all-to-all-start.1 = ((bf16[8,2,128,512]{3,2,1,0:T(8,128)(2,1)}), bf16[8,2,128,512]{3,2,1,0:T(8,128)(2,1)}, u32[]{:S(2)}, u32[]{:S(2)}) async-start(bf16[8,2,128,512]{3,2,1,0:T(8,128)(2,1)} %gather_fusion.1), calls=%async_computation.1 | async-start | bytes 4194304 | tf_op jit(solution)/shard_map/all_to_all | solution.py:217
  25.3 1.7 %collective-permute-start.2 = (bf16[96,2560]{1,0:T(8,128)(2,1)S(1)}, bf16[96,2560]{1,0:T(8,128)(2,1)}, u32[]{:S(2)}, u32[]{:S(2)}) collective-permute-start(bf16[96,2560]{1,0:T(8,128)(2,1)S(1)} %copy-done.3), channel_id=1, source_target_pairs={{0,3},{1,0},{2,1},{3,2},{4,7},{5,4},{6,5},{7,6},{8,11},{9,8},{10,9... | collective-permute-start | bytes 1474568 | tf_op jit(solution)/shard_map/ppermute | solution.py:149
  27.0 1.5 collective-permute-start.1
  28.6 2.8 %scatter_fusion = pred[3,16]{1,0:T(4,128)(4,1)S(1)} fusion(pred[3,16]{1,0:T(4,128)(4,1)S(1)} %broadcast_in_dim.96, s32[48]{0:T(128)S(1)} %fusion.38, pred[48]{0:T(512)(128)(4,1)S(1)} %broadcast.371), kind=kCustom, calls=%fused_computation.3 | custom fusion | bytes 528 | tf_op jit(solution)/shard_map/scatter | solution.py:229
  31.5 0.1 slice_add_fusion
  31.5 5.4 %gather_fusion.2 = bf16[8,2,128,512]{3,2,1,0:T(8,128)(2,1)} fusion(bf16[2,32,128,512]{3,2,1,0:T(8,128)(2,1)} %bitcast.116, s32[1024]{0:T(1024)S(1)} %pad_clamp_fusion), kind=kCustom, calls=%fused_computation.2 | custom fusion | bytes 4194336 | tf_op jit(solution)/shard_map/jit(_take)/gather | solution.py:218
  36.9 32.2 %all-to-all-done.1.k_ref.v_ref = bf16[8,2,128,512]{3,2,1,0:T(8,128)(2,1)} async-done(((bf16[8,2,128,512]{3,2,1,0:T(8,128)(2,1)}), bf16[8,2,128,512]{3,2,1,0:T(8,128)(2,1)}, u32[]{:S(2)}, u32[]{:S(2)}) %all-to-all-start.1) | async-done | bytes 2097184 | tf_op jit(solution)/shard_map/all_to_all | solution.py:217
  69.1 7.6 %all-to-all-start.2 = ((bf16[8,2,128,512]{3,2,1,0:T(8,128)(2,1)}), bf16[8,2,128,512]{3,2,1,0:T(8,128)(2,1)}, u32[]{:S(2)}, u32[]{:S(2)}) async-start(bf16[8,2,128,512]{3,2,1,0:T(8,128)(2,1)} %gather_fusion.2), calls=%async_computation.2 | async-start | bytes 4194304 | tf_op jit(solution)/shard_map/all_to_all | solution.py:217
  76.9 0.1 fusion.24
  77.0 0.7 fusion.15
  77.7 0.0 collective-permute-done.1
  77.7 2.9 %pad_maximum_fusion = bf16[4,96,2560]{2,1,0:T(8,128)(2,1)} fusion(bf16[1,96,2560]{2,1,0:T(8,128)(2,1)} %bitcast.3, bf16[1,96,2560]{2,1,0:T(8,128)(2,1)} %bitcast.2, bf16[1,96,2560]{2,1,0:T(8,128)(2,1)} %bitcast.1, bf16[1,96,2560]{2,1,0:T(8,128)(2,1)S(1)} %bitcast.123), kind=kLoop, calls=%fused_computation.6 | loop fusion | flops 2949120 | bytes 3932160 | tf_op jit(solution)/shard_map/stack | solution.py:153
  80.6 3.6 %gather_fusion = bf16[4,96,2560]{2,1,0:T(8,128)(2,1)} fusion(bf16[4,96,2560]{2,1,0:T(8,128)(2,1)} %pad_maximum_fusion, s32[1024]{0:T(1024)S(1)} %pad_clamp_fusion.2), kind=kCustom, calls=%fused_computation | custom fusion | bytes 3932176 | tf_op jit(solution)/shard_map/jit(_take)/gather | solution.py:153
  84.1 8.1 %convolution_convert_fusion.q_ref.k0_ref.v0_ref = bf16[384,1536]{1,0:T(8,128)(2,1)} fusion(bf16[384,2560]{1,0:T(8,128)(2,1)} %bitcast.117, bf16[2560,1536]{1,0:T(8,128)(2,1)} %param.8), kind=kOutput, calls=%fused_computation.5 | convolution fusion | flops 3020488704 | bytes 11010048 | tf_op jit(solution)/shard_map/dot_general | solution.py:163
  92.2 2.4 %copy.48 = bf16[384,1536]{0,1:T(8,128)(2,1)} copy(bf16[384,1536]{1,0:T(8,128)(2,1)} %convolution_convert_fusion.q_ref.k0_ref.v0_ref) | data formatting | bytes 2359296 | tf_op jit(solution)/shard_map/convert_element_type | solution.py:168
  94.6 1.0 fusion.47
  95.6 0.1 copy.67
  95.7 0.8 copy.68
  96.5 2.2 %fusion.46 = (bf16[256,4,1,128]{0,3,2,1:T(8,128)(2,1)}, bf16[256,4,1,128]{0,3,2,1:T(8,128)(2,1)S(1)}, bf16[256,4,1,128]{0,3,2,1:T(8,128)(2,1)S(1)}, bf16[256,4,1...) fusion(bf16[384,4,3,128]{0,3,2,1:T(8,128)(2,1)} %bitcast.106), kind=kLoop, calls=%fused_computation.114 | loop fusion | bytes 2621440 | tf_op jit(solution)/shard_map/slice | solution.py:181
  98.7 1.8 %copy.53 = bf16[256,4,1,128]{3,0,1,2:T(8,128)(2,1)} copy(bf16[256,4,1,128]{0,3,2,1:T(8,128)(2,1)} %get-tuple-element.11) | data formatting | bytes 524288 | tf_op jit(solution)/shard_map/slice | solution.py:181
  100.4 1.8 %copy.55 = bf16[256,4,1,128]{3,0,1,2:T(8,128)(2,1)} copy(bf16[256,4,1,128]{0,3,2,1:T(8,128)(2,1)} %get-tuple-element.14) | data formatting | bytes 524288 | tf_op jit(solution)/shard_map/slice | solution.py:182
  102.2 0.8 copy.54
  103.1 1.7 %pad_maximum_fusion.4 = bf16[2,128,512]{2,1,0:T(8,128)(2,1)} fusion(bf16[1,128,512]{2,1,0:T(8,128)(2,1)} %copy.68, bf16[1,128,512]{2,1,0:T(8,128)(2,1)S(1)} %copy.67), kind=kLoop, calls=%fused_computation.30 | loop fusion | flops 131072 | bytes 524288 | tf_op jit(solution)/shard_map/stack | solution.py:173
  104.7 3.4 %collective-permute-start.3 = (bf16[2,128,512]{2,1,0:T(8,128)(2,1)}, bf16[2,128,512]{2,1,0:T(8,128)(2,1)S(1)}, u32[]{:S(2)}, u32[]{:S(2)}) collective-permute-start(bf16[2,128,512]{2,1,0:T(8,128)(2,1)} %pad_maximum_fusion.4), channel_id=1, source_target_pairs={{0,4},{4,8},{8,12},{12,16},{16,20},{20,24},{24,28},{1,5},{5,9},{9,... | collective-permute-start | bytes 786440 | tf_op jit(solution)/shard_map/ppermute | solution.py:20
  108.1 1.4 convolution_multiply_fusion
  109.5 1.0 copy-done.2
  110.5 0.4 fusion.48
  110.9 0.9 copy.60
  111.8 0.2 copy.59
  112.0 4.5 %fusion.9.near_ref = f32[2,4,128,128]{3,2,1,0:T(8,128)} fusion(f32[2,4,128]{2,1,0:T(4,128)S(1)} %fusion.48, f32[2,4,128,256]{3,2,1,0:T(8,128)} %copy-done.2, pred[2,128,256]{2,1,0:T(8,128)(4,1)} %fusion.15, bf16[2,128,4,128]{3,1,0,2:T(8,128)(2,1)} %bitcast.124, bf16[2,128,4,128]{3,1,0,2:T(8,128)(2,1)S(1)} %bitcast.125), kind=kOutput, calls=%fused_computation.16 | convolution fusion | flops 69469440 | bytes 2166784 | tf_op jit(solution)/shard_map/ngqk,nkgd->ngqd/dot_general | solution.py:44
  116.4 12.2 %collective-permute-done.3.bk_ref.bv_ref = bf16[2,128,512]{2,1,0:T(8,128)(2,1)S(1)} collective-permute-done((bf16[2,128,512]{2,1,0:T(8,128)(2,1)}, bf16[2,128,512]{2,1,0:T(8,128)(2,1)S(1)}, u32[]{:S(2)}, u32[]{:S(2)}) %collective-permute-start.3) | collective-permute-done | bytes 262176 | tf_op jit(solution)/shard_map/ppermute | solution.py:20
  128.7 0.0 all-to-all-done.2.kb_ref.vb_ref
  128.7 0.6 broadcast_in_dim.104.start_ref
  129.3 0.6 broadcast_in_dim.105
  130.0 0.7 broadcast_in_dim.100
  130.6 10.9 %shard_map.73 = bf16[384,512]{1,0:T(8,128)(2,1)} custom-call(bf16[384,1536]{1,0:T(8,128)(2,1)} %convolution_convert_fusion.q_ref.k0_ref.v0_ref, bf16[384,1536]{1,0:T(8,128)(2,1)} %convolution_convert_fusion.q_ref.k0_ref.v0_ref, bf16[384,1536]{1,0:T(8,128)(2,1)} %convolution_convert_fusion.q_ref.k0_ref.v0_ref, bf16[2,128,512]{2,1,0:T(8,128)(2,1)} %copy-done.1, ...), custom_call_target="tpu_custom_call" | custom-call | flops 1677721600 | bytes 5767168 | tf_op jit(solution)/shard_map/pallas_call | solution.py:115
  141.5 2.2 %fusion.49 = f32[384,2560]{1,0:T(8,128)S(1)} fusion(bf16[384,512]{1,0:T(8,128)(2,1)} %shard_map.73, bf16[512,2560]{1,0:T(8,128)(2,1)S(1)} %copy-done), kind=kOutput, calls=%fused_computation.117 | convolution fusion | flops 1006632960 | bytes 6946816 | tf_op jit(solution)/shard_map/dot_general | solution.py:245
  143.7 0.3 fusion.45
  144.0 0.1 collective-permute-start.6
  144.1 0.5 collective-permute-start.8
  144.7 0.1 collective-permute-start.4
  144.8 0.5 collective-permute-start.10
  145.4 0.2 collective-permute-done.6
  145.7 1.6 collective-permute-start.7
  147.3 0.0 collective-permute-done.8
  147.3 0.6 collective-permute-start.9
  147.9 0.0 collective-permute-done.4
  148.0 1.6 collective-permute-start.5
  149.7 0.6 collective-permute-start.11
  150.2 1.7 %collective-permute-done.7 = bf16[96,640]{1,0:T(8,128)(2,1)S(1)} collective-permute-done((bf16[96,640]{1,0:T(8,128)(2,1)S(1)}, bf16[96,640]{1,0:T(8,128)(2,1)S(1)}, u32[]{:S(2)}, u32[]{:S(2)}) %collective-permute-start.7) | collective-permute-done | bytes 122912 | tf_op jit(solution)/shard_map/ppermute | solution.py:270
  151.9 2.6 %collective-permute-done.9 = bf16[96,640]{1,0:T(8,128)(2,1)S(1)} collective-permute-done((bf16[96,640]{1,0:T(8,128)(2,1)S(1)}, bf16[96,640]{1,0:T(8,128)(2,1)S(1)}, u32[]{:S(2)}, u32[]{:S(2)}) %collective-permute-start.9) | collective-permute-done | bytes 122912 | tf_op jit(solution)/shard_map/ppermute | solution.py:270
  154.6 2.6 %collective-permute-done.5 = bf16[96,640]{1,0:T(8,128)(2,1)S(1)} collective-permute-done((bf16[96,640]{1,0:T(8,128)(2,1)S(1)}, bf16[96,640]{1,0:T(8,128)(2,1)S(1)}, u32[]{:S(2)}, u32[]{:S(2)}) %collective-permute-start.5) | collective-permute-done | bytes 122912 | tf_op jit(solution)/shard_map/ppermute | solution.py:270
  157.2 1.8 %collective-permute-done.11 = bf16[96,640]{1,0:T(8,128)(2,1)S(1)} collective-permute-done((bf16[96,640]{1,0:T(8,128)(2,1)S(1)}, bf16[96,640]{1,0:T(8,128)(2,1)S(1)}, u32[]{:S(2)}, u32[]{:S(2)}) %collective-permute-start.11) | collective-permute-done | bytes 122912 | tf_op jit(solution)/shard_map/ppermute | solution.py:270
  159.0 0.8 pad_maximum_fusion.3
  (45 shorter events, 0.6 us)
Async XLA Ops:
  0.0 141.5 %copy-start = (bf16[512,2560]{1,0:T(8,128)(2,1)S(1)}, bf16[512,2560]{1,0:T(8,128)(2,1)}, u32[]{:S(2)}) copy-start(bf16[512,2560]{1,0:T(8,128)(2,1)} %param.9) | copy-start | bytes 7864324
  18.6 6.7 %copy-start.3 = (bf16[96,2560]{1,0:T(8,128)(2,1)S(1)}, bf16[96,2560]{1,0:T(8,128)(2,1)}, u32[]{:S(2)}) copy-start(bf16[96,2560]{1,0:T(8,128)(2,1)} %param.7) | copy-start | bytes 1474564
  18.6 50.5 %all-to-all-start.1 = ((bf16[8,2,128,512]{3,2,1,0:T(8,128)(2,1)}), bf16[8,2,128,512]{3,2,1,0:T(8,128)(2,1)}, u32[]{:S(2)}, u32[]{:S(2)}) async-start(bf16[8,2,128,512]{3,2,1,0:T(8,128)(2,1)} %gather_fusion.1), calls=%async_computation.1 | async-start | bytes 4194304 | tf_op jit(solution)/shard_map/all_to_all | solution.py:217
  25.3 52.4 %collective-permute-start = (bf16[96,2560]{1,0:T(8,128)(2,1)S(1)}, bf16[96,2560]{1,0:T(8,128)(2,1)}, u32[]{:S(2)}, u32[]{:S(2)}) collective-permute-start(bf16[96,2560]{1,0:T(8,128)(2,1)S(1)} %copy-done.3), channel_id=1, source_target_pairs={{0,1},{1,2},{2,3},{3,0},{4,5},{5,6},{6,7},{7,4},{8,9},{9,10},{10,1... | collective-permute-start | bytes 1474568 | tf_op jit(solution)/shard_map/ppermute | solution.py:149
  25.3 52.4 %collective-permute-start.2 = (bf16[96,2560]{1,0:T(8,128)(2,1)S(1)}, bf16[96,2560]{1,0:T(8,128)(2,1)}, u32[]{:S(2)}, u32[]{:S(2)}) collective-permute-start(bf16[96,2560]{1,0:T(8,128)(2,1)S(1)} %copy-done.3), channel_id=1, source_target_pairs={{0,3},{1,0},{2,1},{3,2},{4,7},{5,4},{6,5},{7,6},{8,11},{9,8},{10,9... | collective-permute-start | bytes 1474568 | tf_op jit(solution)/shard_map/ppermute | solution.py:149
  27.0 50.7 %collective-permute-start.1 = (bf16[96,2560]{1,0:T(8,128)(2,1)S(1)}, bf16[96,2560]{1,0:T(8,128)(2,1)}, u32[]{:S(2)}, u32[]{:S(2)}) collective-permute-start(bf16[96,2560]{1,0:T(8,128)(2,1)S(1)} %copy-done.3), channel_id=1, source_target_pairs={{0,2},{1,3},{2,0},{3,1},{4,6},{5,7},{6,4},{7,5},{8,10},{9,11},{10,... | collective-permute-start | bytes 1474568 | tf_op jit(solution)/shard_map/ppermute | solution.py:149
  36.9 39.8 %copy-start.5 = (f32[4]{0:T(128)S(1)}, f32[4]{0:T(128)}, u32[]{:S(2)}) copy-start(f32[4]{0:T(128)} %param.10) | copy-start | bytes 52
  69.1 59.6 %all-to-all-start.2 = ((bf16[8,2,128,512]{3,2,1,0:T(8,128)(2,1)}), bf16[8,2,128,512]{3,2,1,0:T(8,128)(2,1)}, u32[]{:S(2)}, u32[]{:S(2)}) async-start(bf16[8,2,128,512]{3,2,1,0:T(8,128)(2,1)} %gather_fusion.2), calls=%async_computation.2 | async-start | bytes 4194304 | tf_op jit(solution)/shard_map/all_to_all | solution.py:217
  103.1 7.5 %copy-start.4 = (pred[2,128,256]{2,1,0:T(8,128)(4,1)S(1)}, pred[2,128,256]{2,1,0:T(8,128)(4,1)}, u32[]{:S(2)}) copy-start(pred[2,128,256]{2,1,0:T(8,128)(4,1)} %fusion.15) | copy-start | bytes 196612
  104.7 24.0 %collective-permute-start.3 = (bf16[2,128,512]{2,1,0:T(8,128)(2,1)}, bf16[2,128,512]{2,1,0:T(8,128)(2,1)S(1)}, u32[]{:S(2)}, u32[]{:S(2)}) collective-permute-start(bf16[2,128,512]{2,1,0:T(8,128)(2,1)} %pad_maximum_fusion.4), channel_id=1, source_target_pairs={{0,4},{4,8},{8,12},{12,16},{16,20},{20,24},{24,28},{1,5},{5,9},{9,... | collective-permute-start | bytes 786440 | tf_op jit(solution)/shard_map/ppermute | solution.py:20
  109.5 1.0 copy-start.2
  128.7 2.0 %copy-start.1 = (bf16[2,128,512]{2,1,0:T(8,128)(2,1)}, bf16[2,128,512]{2,1,0:T(8,128)(2,1)S(1)}, u32[]{:S(2)}) copy-start(bf16[2,128,512]{2,1,0:T(8,128)(2,1)S(1)} %collective-permute-done.3.bk_ref.bv_ref) | copy-start | bytes 786436
  144.0 1.6 collective-permute-start.6
  144.1 3.1 %collective-permute-start.8 = (bf16[2,96,640]{2,1,0:T(8,128)(2,1)S(1)}, bf16[2,96,640]{2,1,0:T(8,128)(2,1)S(1)}, u32[]{:S(2)}, u32[]{:S(2)}) collective-permute-start(bf16[2,96,640]{2,1,0:T(8,128)(2,1)S(1)} %fusion.18), channel_id=1, source_target_pairs={{0,1},{1,0},{2,3},{3,2},{4,5},{5,4},{6,7},{7,6},{8,9},{9,8},{10,11... | collective-permute-start | bytes 737288 | tf_op jit(solution)/shard_map/ppermute | solution.py:262
  144.7 3.2 %collective-permute-start.4 = (bf16[2,96,640]{2,1,0:T(8,128)(2,1)S(1)}, bf16[2,96,640]{2,1,0:T(8,128)(2,1)S(1)}, u32[]{:S(2)}, u32[]{:S(2)}) collective-permute-start(bf16[2,96,640]{2,1,0:T(8,128)(2,1)S(1)} %fusion.16), channel_id=1, source_target_pairs={{0,1},{1,0},{2,3},{3,2},{4,5},{5,4},{6,7},{7,6},{8,9},{9,8},{10,11... | collective-permute-start | bytes 737288 | tf_op jit(solution)/shard_map/ppermute | solution.py:262
  144.8 4.7 %collective-permute-start.10 = (bf16[2,96,640]{2,1,0:T(8,128)(2,1)S(1)}, bf16[2,96,640]{2,1,0:T(8,128)(2,1)S(1)}, u32[]{:S(2)}, u32[]{:S(2)}) collective-permute-start(bf16[2,96,640]{2,1,0:T(8,128)(2,1)S(1)} %fusion.19), channel_id=1, source_target_pairs={{0,1},{1,0},{2,3},{3,2},{4,5},{5,4},{6,7},{7,6},{8,9},{9,8},{10,11... | collective-permute-start | bytes 737288 | tf_op jit(solution)/shard_map/ppermute | solution.py:262
  145.7 6.2 %collective-permute-start.7 = (bf16[96,640]{1,0:T(8,128)(2,1)S(1)}, bf16[96,640]{1,0:T(8,128)(2,1)S(1)}, u32[]{:S(2)}, u32[]{:S(2)}) collective-permute-start(bf16[96,640]{1,0:T(8,128)(2,1)S(1)} %fusion.26), channel_id=1, source_target_pairs={{0,2},{1,3},{2,0},{3,1},{4,6},{5,7},{6,4},{7,5},{8,10},{9,11},{10,... | collective-permute-start | bytes 368648 | tf_op jit(solution)/shard_map/ppermute | solution.py:270
  147.3 7.2 %collective-permute-start.9 = (bf16[96,640]{1,0:T(8,128)(2,1)S(1)}, bf16[96,640]{1,0:T(8,128)(2,1)S(1)}, u32[]{:S(2)}, u32[]{:S(2)}) collective-permute-start(bf16[96,640]{1,0:T(8,128)(2,1)S(1)} %fusion.27), channel_id=1, source_target_pairs={{0,2},{1,3},{2,0},{3,1},{4,6},{5,7},{6,4},{7,5},{8,10},{9,11},{10,... | collective-permute-start | bytes 368648 | tf_op jit(solution)/shard_map/ppermute | solution.py:270
  148.0 9.2 %collective-permute-start.5 = (bf16[96,640]{1,0:T(8,128)(2,1)S(1)}, bf16[96,640]{1,0:T(8,128)(2,1)S(1)}, u32[]{:S(2)}, u32[]{:S(2)}) collective-permute-start(bf16[96,640]{1,0:T(8,128)(2,1)S(1)} %fusion.25), channel_id=1, source_target_pairs={{0,2},{1,3},{2,0},{3,1},{4,6},{5,7},{6,4},{7,5},{8,10},{9,11},{10,... | collective-permute-start | bytes 368648 | tf_op jit(solution)/shard_map/ppermute | solution.py:270
  149.7 9.3 %collective-permute-start.11 = (bf16[96,640]{1,0:T(8,128)(2,1)S(1)}, bf16[96,640]{1,0:T(8,128)(2,1)S(1)}, u32[]{:S(2)}, u32[]{:S(2)}) collective-permute-start(bf16[96,640]{1,0:T(8,128)(2,1)S(1)} %fusion.28), channel_id=1, source_target_pairs={{0,2},{1,3},{2,0},{3,1},{4,6},{5,7},{6,4},{7,5},{8,10},{9,11},{10,... | collective-permute-start | bytes 368648 | tf_op jit(solution)/shard_map/ppermute | solution.py:270

commit v17 on v14

--- a/solution.py
+++ b/solution.py
@@ -221,12 +221,17 @@
         jnp.full((1, BLK), jnp.where(lax.axis_index("mem") > 0, 1.0, 0.0), jnp.float32),
         mixing,
     )
-    partial = jnp.dot(attended, output_weight, preferred_element_type=jnp.float32)
-    width = 4 * HD
+    width = output_weight.shape[1] // 4
     return jnp.concatenate(
         [
-            reduce_over_tp(partial[:, k * width:(k + 1) * width])
-            for k in range(partial.shape[1] // width)
+            reduce_over_tp(
+                jnp.dot(
+                    attended,
+                    output_weight[:, k * width:(k + 1) * width],
+                    preferred_element_type=jnp.float32,
+                )
+            )
+            for k in range(4)
         ],
         axis=1,
     ).astype(jnp.bfloat16)

time: 157 us -> 157 us (level)
  waiting for transfers between devices: 57.5 us -> 74.6 us
  local copies, waits for them, and re-layouts: 30.4 us -> 19.7 us
  other arithmetic: 9.63 us -> 7.37 us
  matrix products: 16.1 us -> 14 us
  starting transfers between devices: 21 us -> 19.2 us
    ppermute x1, waiting for transfers between devices: 33.2 us -> 48.8 us  [from_behind(): lax.ppermute(value, axis, [(source, source + steps) for source in range(i...]
    slice x2, local copies, waits for them, and re-layouts: 3.94 us -> 1.99 us  [local(): query_blocks[1:]]
    dot_general x1 -> x4, matrix products: 2.17 us -> 3.91 us  [local(): jnp.dot(attended, output_weight[:, k * width:(k + 1) * width], preferred_...]
    dot_general x1, matrix products: 4.38 us -> 2.71 us  [near_part(): jnp.einsum('ngqk,nkgd->ngqd', probs, window_values, preferred_element_typ...]
    convert_element_type x1, local copies, waits for them, and re-layouts: 2.39 us -> 0.74 us  [local(): projected_flat = projected.astype(jnp.bfloat16)]
    another operation x1, other arithmetic: 2.91 us -> 1.27 us  [gather_tp(): jnp.stack(arrived)]
    slice x1, local copies, waits for them, and re-layouts: 1.79 us -> 0.17 us  [local(): key_blocks[1:]]
    ppermute x5 -> x4, starting transfers between devices: 5.92 us -> 4.31 us  [reduce_over_tp(): lax.ppermute(outgoing.astype(jnp.bfloat16), 'tp', pairs).astype(jnp.float32)]
  transfers between devices with their start and end apart: 15 -> 13, of which waited for: 8 -> 9; matrix products, arithmetic and copies ran while one was open for 25% -> 15% of each run, Pallas kernels for 0% -> 0%
where the time goes in v17:
time: 157 us; the launch traced here: 156 us
  waiting for transfers between devices  74.6 us (48%)
  local copies, waits for them, and re-layouts  19.7 us (13%)
  starting transfers between devices  19.2 us (12%)
  matrix products  14 us (9%)
  Pallas kernels  11.2 us (7%)
  blocking collectives  10 us (6%)
  other arithmetic  7.37 us (5%)
    ppermute x1, waiting for transfers between devices, from_behind(): lax.ppermute(value, axis, [(source, source + steps) for source in range(i...  48.8 us
    ppermute x3, waiting for transfers between devices, gather_tp(): lax.ppermute(part, 'tp', [(t, (t + shift) % count) for t in range(count)])  16.9 us
    pallas_call x1, Pallas kernels, far_attention(): pl.pallas_call(far_kernel, grid=(groups,), in_specs=[pl.BlockSpec((rows,...  11.2 us
    all_to_all x1, blocking collectives, local(): lax.all_to_all(wanted_ids, 'mem', split_axis=0, concat_axis=0, tiled=True)  10 us
    ppermute x4, waiting for transfers between devices, reduce_over_tp(): lax.ppermute(outgoing.astype(jnp.bfloat16), 'tp', pairs).astype(jnp.float32)  8.68 us
    dot_general x1, matrix products, local(): jnp.dot(gather_tp(tokens), input_weight, preferred_element_type=jnp.float32)  7.03 us
    all_to_all x1, starting transfers between devices, local(): lax.all_to_all(picked, 'mem', split_axis=0, concat_axis=0, tiled=True)  6.94 us
    gather x1, local copies, waits for them, and re-layouts, local(): jnp.take(local_store, lax.all_to_all(wanted_ids, 'mem', split_axis=0, con...  6.17 us
  transfers between devices with their start and end apart: 13, of which 9 were waited for; matrix products, arithmetic and copies ran while one was open for 15% of the time, Pallas kernels for 0%

profile of v17, /device:TPU:16, one launch (start us, length us, event | category | flops | bytes accessed | tf_op | source)
XLA Modules:
  0.0 156.4 jit_solution(5929711537044687375)
XLA Ops:
  0.0 0.8 eq.74
  0.8 0.9 select_reduce_fusion.1
  1.6 0.2 convert_reduce_fusion.1
  1.8 0.7 compare_reduce_fusion
  2.5 0.2 convert_reduce_fusion
  2.7 0.1 select_reduce_fusion.2
  2.8 0.1 copy.54
  2.9 10.0 %all_to_all.14 = s32[8,1,2]{2,1,0:T(1,128)S(1)} all-to-all(s32[8,1,2]{2,1,0:T(1,128)S(1)} %copy.54), channel_id=1, replica_groups=mesh['mem'=8,'tp'=4] {'mem'}, dimensions={0} | all-to-all | bytes 128 | tf_op jit(solution)/shard_map/all_to_all | solution.py:199
  13.0 0.5 broadcast.403
  13.5 0.7 reduce.22
  14.1 0.1 reshape.319
  14.2 6.2 %gather_fusion.1 = bf16[16,2,128,512]{3,2,1,0:T(8,128)(2,1)} fusion(bf16[2,32,128,512]{3,2,1,0:T(8,128)(2,1)} %bitcast.112, s32[1024]{0:T(1024)S(1)} %pad_clamp_fusion), kind=kCustom, calls=%fused_computation.1 | custom fusion | bytes 8388672 | tf_op jit(solution)/shard_map/jit(_take)/gather | solution.py:197
  20.4 6.9 %all-to-all-start.1 = ((bf16[16,2,128,512]{3,2,1,0:T(8,128)(2,1)}), bf16[16,2,128,512]{3,2,1,0:T(8,128)(2,1)}, u32[]{:S(2)}, u32[]{:S(2)}) async-start(bf16[16,2,128,512]{3,2,1,0:T(8,128)(2,1)} %gather_fusion.1), calls=%async_computation.1 | async-start | bytes 8388608 | tf_op jit(solution)/shard_map/all_to_all | solution.py:205
  27.3 1.7 %collective-permute-start.2 = (bf16[96,2560]{1,0:T(8,128)(2,1)S(1)}, bf16[96,2560]{1,0:T(8,128)(2,1)S(1)}, u32[]{:S(2)}, u32[]{:S(2)}) collective-permute-start(bf16[96,2560]{1,0:T(8,128)(2,1)S(1)} %copy-done.4), channel_id=1, source_target_pairs={{0,3},{1,0},{2,1},{3,2},{4,7},{5,4},{6,5},{7,6},{8,11},{9,8},{10,9... | collective-permute-start | bytes 1474568 | tf_op jit(solution)/shard_map/ppermute | solution.py:131
  29.1 1.5 collective-permute-start.1
  30.6 2.8 %scatter_fusion = pred[3,16]{1,0:T(4,128)(4,1)S(1)} fusion(pred[3,16]{1,0:T(4,128)(4,1)S(1)} %broadcast_in_dim.98, s32[48]{0:T(128)S(1)} %fusion.46, pred[48]{0:T(512)(128)(4,1)S(1)} %broadcast.369), kind=kCustom, calls=%fused_computation.2 | custom fusion | bytes 528 | tf_op jit(solution)/shard_map/scatter | solution.py:209
  33.5 0.1 slice_add_fusion
  33.7 0.1 fusion.32
  33.8 0.7 fusion.23
  34.5 4.5 %collective-permute-done = bf16[96,2560]{1,0:T(8,128)(2,1)S(1)} collective-permute-done((bf16[96,2560]{1,0:T(8,128)(2,1)S(1)}, bf16[96,2560]{1,0:T(8,128)(2,1)S(1)}, u32[]{:S(2)}, u32[]{:S(2)}) %collective-permute-start) | collective-permute-done | bytes 491552 | tf_op jit(solution)/shard_map/ppermute | solution.py:131
  39.0 1.7 %collective-permute-done.2 = bf16[96,2560]{1,0:T(8,128)(2,1)S(1)} collective-permute-done((bf16[96,2560]{1,0:T(8,128)(2,1)S(1)}, bf16[96,2560]{1,0:T(8,128)(2,1)S(1)}, u32[]{:S(2)}, u32[]{:S(2)}) %collective-permute-start.2) | collective-permute-done | bytes 491552 | tf_op jit(solution)/shard_map/ppermute | solution.py:131
  40.7 10.7 %collective-permute-done.1 = bf16[96,2560]{1,0:T(8,128)(2,1)S(1)} collective-permute-done((bf16[96,2560]{1,0:T(8,128)(2,1)S(1)}, bf16[96,2560]{1,0:T(8,128)(2,1)S(1)}, u32[]{:S(2)}, u32[]{:S(2)}) %collective-permute-start.1) | collective-permute-done | bytes 491552 | tf_op jit(solution)/shard_map/ppermute | solution.py:131
  51.4 0.8 copy-done.5
  52.2 1.3 pad_maximum_fusion
  53.4 2.0 %gather_fusion = bf16[4,96,2560]{2,1,0:T(8,128)(2,1)} fusion(bf16[4,96,2560]{2,1,0:T(8,128)(2,1)S(1)} %pad_maximum_fusion, s32[1024]{0:T(1024)S(1)} %pad_clamp_fusion.1), kind=kCustom, calls=%fused_computation | custom fusion | bytes 3932176 | tf_op jit(solution)/shard_map/jit(_take)/gather | solution.py:135
  55.5 7.0 %convolution_convert_fusion.q_ref.k0_ref.v0_ref = bf16[384,1536]{1,0:T(8,128)(2,1)S(1)} fusion(bf16[384,2560]{1,0:T(8,128)(2,1)} %bitcast.113, bf16[2560,1536]{1,0:T(8,128)(2,1)} %param.8), kind=kOutput, calls=%fused_computation.4 | convolution fusion | flops 3020488704 | bytes 11010048 | tf_op jit(solution)/shard_map/dot_general | solution.py:145
  62.5 0.7 copy.51
  63.3 0.1 copy.69
  63.4 0.8 copy.70
  64.2 0.8 fusion.53
  65.0 1.1 copy.55
  66.2 0.2 copy.57
  66.4 0.2 copy.56
  66.6 0.9 pad_maximum_fusion.4
  67.5 3.4 %collective-permute-start.3 = (bf16[2,128,512]{2,1,0:T(8,128)(2,1)S(1)}, bf16[2,128,512]{2,1,0:T(8,128)(2,1)S(1)}, u32[]{:S(2)}, u32[]{:S(2)}) collective-permute-start(bf16[2,128,512]{2,1,0:T(8,128)(2,1)S(1)} %pad_maximum_fusion.4), channel_id=1, source_target_pairs={{0,4},{4,8},{8,12},{12,16},{16,20},{20,24},{24,28},{1,5},{5,9},{9,... | collective-permute-start | bytes 786440 | tf_op jit(solution)/shard_map/ppermute | solution.py:20
  70.9 0.3 convolution_multiply_fusion
  71.2 0.4 fusion.55
  71.6 0.2 copy.62
  71.8 0.2 copy.61
  72.0 2.7 %fusion.17.near_ref = f32[2,4,128,128]{3,2,1,0:T(8,128)} fusion(f32[2,4,128]{2,1,0:T(4,128)S(1)} %fusion.55, f32[2,4,128,256]{3,2,1,0:T(8,128)S(1)} %convolution_multiply_fusion, pred[2,128,256]{2,1,0:T(8,128)(4,1)S(1)} %copy-done.6, bf16[2,128,4,128]{3,1,0,2:T(8,128)(2,1)S(1)} %bitcast.123, bf16[2,128,4,128]{3,1,0,2:T(8,128)(2,1)S(1)} %bitcast.124), kind=kOutput, calls=%fused_computation.23 | convolution fusion | flops 69469440 | bytes 2166784 | tf_op jit(solution)/shard_map/ngqk,nkgd->ngqd/dot_general | solution.py:44
  74.7 48.8 %collective-permute-done.3.bk_ref.bv_ref = bf16[2,128,512]{2,1,0:T(8,128)(2,1)S(1)} collective-permute-done((bf16[2,128,512]{2,1,0:T(8,128)(2,1)S(1)}, bf16[2,128,512]{2,1,0:T(8,128)(2,1)S(1)}, u32[]{:S(2)}, u32[]{:S(2)}) %collective-permute-start.3) | collective-permute-done | bytes 262176 | tf_op jit(solution)/shard_map/ppermute | solution.py:20
  123.5 0.5 broadcast_in_dim.106.start_ref
  124.0 0.7 broadcast_in_dim.107
  124.7 0.7 broadcast_in_dim.102
  125.4 11.2 %shard_map.73 = bf16[384,512]{1,0:T(8,128)(2,1)} custom-call(bf16[384,1536]{1,0:T(8,128)(2,1)} %copy-done, bf16[384,1536]{1,0:T(8,128)(2,1)} %copy-done, bf16[384,1536]{1,0:T(8,128)(2,1)} %copy-done, bf16[2,128,512]{2,1,0:T(8,128)(2,1)} %copy-done.3, bf16[2,128,512]{2,1,0:T(8,128)(2,1)} %copy-done.3, bf16[16,2,128,512]{3,2,1,0:T(8,128)(2,1)} %all-to-all-done.1.k_ref.v_ref, ...), custom_call_target="tpu_custom_call" | custom-call | flops 1677721600 | bytes 5767168 | tf_op jit(solution)/shard_map/pallas_call | solution.py:102
  136.5 0.0 copy-start.1
  136.6 1.5 fusion.9
  138.1 1.5 fusion.11
  139.6 0.5 fusion.13
  140.0 0.5 fusion.15
  140.6 0.1 collective-permute-start.10
  140.7 0.5 collective-permute-start.8
  141.3 0.1 collective-permute-start.6
  141.4 0.5 collective-permute-start.4
  141.9 0.2 collective-permute-done.10
  142.2 1.6 %collective-permute-start.11 = (bf16[96,640]{1,0:T(8,128)(2,1)S(1)}, bf16[96,640]{1,0:T(8,128)(2,1)S(1)}, u32[]{:S(2)}, u32[]{:S(2)}) collective-permute-start(bf16[96,640]{1,0:T(8,128)(2,1)S(1)} %fusion.36), channel_id=1, source_target_pairs={{0,2},{1,3},{2,0},{3,1},{4,6},{5,7},{6,4},{7,5},{8,10},{9,11},{10,... | collective-permute-start | bytes 368648 | tf_op jit(solution)/shard_map/ppermute | solution.py:258
  143.9 0.6 collective-permute-start.9
  144.5 1.6 %collective-permute-start.7 = (bf16[96,640]{1,0:T(8,128)(2,1)S(1)}, bf16[96,640]{1,0:T(8,128)(2,1)S(1)}, u32[]{:S(2)}, u32[]{:S(2)}) collective-permute-start(bf16[96,640]{1,0:T(8,128)(2,1)S(1)} %fusion.34), channel_id=1, source_target_pairs={{0,2},{1,3},{2,0},{3,1},{4,6},{5,7},{6,4},{7,5},{8,10},{9,11},{10,... | collective-permute-start | bytes 368648 | tf_op jit(solution)/shard_map/ppermute | solution.py:258
  146.2 0.6 collective-permute-start.5
  146.8 1.7 %collective-permute-done.11 = bf16[96,640]{1,0:T(8,128)(2,1)S(1)} collective-permute-done((bf16[96,640]{1,0:T(8,128)(2,1)S(1)}, bf16[96,640]{1,0:T(8,128)(2,1)S(1)}, u32[]{:S(2)}, u32[]{:S(2)}) %collective-permute-start.11) | collective-permute-done | bytes 122912 | tf_op jit(solution)/shard_map/ppermute | solution.py:258
  148.5 2.6 %collective-permute-done.9 = bf16[96,640]{1,0:T(8,128)(2,1)S(1)} collective-permute-done((bf16[96,640]{1,0:T(8,128)(2,1)S(1)}, bf16[96,640]{1,0:T(8,128)(2,1)S(1)}, u32[]{:S(2)}, u32[]{:S(2)}) %collective-permute-start.9) | collective-permute-done | bytes 122912 | tf_op jit(solution)/shard_map/ppermute | solution.py:258
  151.1 2.6 %collective-permute-done.7 = bf16[96,640]{1,0:T(8,128)(2,1)S(1)} collective-permute-done((bf16[96,640]{1,0:T(8,128)(2,1)S(1)}, bf16[96,640]{1,0:T(8,128)(2,1)S(1)}, u32[]{:S(2)}, u32[]{:S(2)}) %collective-permute-start.7) | collective-permute-done | bytes 122912 | tf_op jit(solution)/shard_map/ppermute | solution.py:258
  153.7 1.8 %collective-permute-done.5 = bf16[96,640]{1,0:T(8,128)(2,1)S(1)} collective-permute-done((bf16[96,640]{1,0:T(8,128)(2,1)S(1)}, bf16[96,640]{1,0:T(8,128)(2,1)S(1)}, u32[]{:S(2)}, u32[]{:S(2)}) %collective-permute-start.5) | collective-permute-done | bytes 122912 | tf_op jit(solution)/shard_map/ppermute | solution.py:258
  155.6 0.8 pad_maximum_fusion.3
  (48 shorter events, 0.7 us)
Async XLA Ops:
  20.4 6.9 %copy-start.4 = (bf16[96,2560]{1,0:T(8,128)(2,1)S(1)}, bf16[96,2560]{1,0:T(8,128)(2,1)}, u32[]{:S(2)}) copy-start(bf16[96,2560]{1,0:T(8,128)(2,1)} %param.7) | copy-start | bytes 1474564
  20.4 13.2 %copy-start.7 = (f32[4]{0:T(128)S(1)}, f32[4]{0:T(128)}, u32[]{:S(2)}) copy-start(f32[4]{0:T(128)} %param.10) | copy-start | bytes 52
  20.4 103.1 %all-to-all-start.1 = ((bf16[16,2,128,512]{3,2,1,0:T(8,128)(2,1)}), bf16[16,2,128,512]{3,2,1,0:T(8,128)(2,1)}, u32[]{:S(2)}, u32[]{:S(2)}) async-start(bf16[16,2,128,512]{3,2,1,0:T(8,128)(2,1)} %gather_fusion.1), calls=%async_computation.1 | async-start | bytes 8388608 | tf_op jit(solution)/shard_map/all_to_all | solution.py:205
  27.3 11.6 %collective-permute-start = (bf16[96,2560]{1,0:T(8,128)(2,1)S(1)}, bf16[96,2560]{1,0:T(8,128)(2,1)S(1)}, u32[]{:S(2)}, u32[]{:S(2)}) collective-permute-start(bf16[96,2560]{1,0:T(8,128)(2,1)S(1)} %copy-done.4), channel_id=1, source_target_pairs={{0,1},{1,2},{2,3},{3,0},{4,5},{5,6},{6,7},{7,4},{8,9},{9,10},{10,1... | collective-permute-start | bytes 1474568 | tf_op jit(solution)/shard_map/ppermute | solution.py:131
  27.3 13.3 %collective-permute-start.2 = (bf16[96,2560]{1,0:T(8,128)(2,1)S(1)}, bf16[96,2560]{1,0:T(8,128)(2,1)S(1)}, u32[]{:S(2)}, u32[]{:S(2)}) collective-permute-start(bf16[96,2560]{1,0:T(8,128)(2,1)S(1)} %copy-done.4), channel_id=1, source_target_pairs={{0,3},{1,0},{2,1},{3,2},{4,7},{5,4},{6,5},{7,6},{8,11},{9,8},{10,9... | collective-permute-start | bytes 1474568 | tf_op jit(solution)/shard_map/ppermute | solution.py:131
  29.1 22.3 %collective-permute-start.1 = (bf16[96,2560]{1,0:T(8,128)(2,1)S(1)}, bf16[96,2560]{1,0:T(8,128)(2,1)S(1)}, u32[]{:S(2)}, u32[]{:S(2)}) collective-permute-start(bf16[96,2560]{1,0:T(8,128)(2,1)S(1)} %copy-done.4), channel_id=1, source_target_pairs={{0,2},{1,3},{2,0},{3,1},{4,6},{5,7},{6,4},{7,5},{8,10},{9,11},{10,... | collective-permute-start | bytes 1474568 | tf_op jit(solution)/shard_map/ppermute | solution.py:131
  51.4 0.8 copy-start.5
  62.5 2.5 %copy-start = (bf16[384,1536]{1,0:T(8,128)(2,1)}, bf16[384,1536]{1,0:T(8,128)(2,1)S(1)}, u32[]{:S(2)}) copy-start(bf16[384,1536]{1,0:T(8,128)(2,1)S(1)} %convolution_convert_fusion.q_ref.k0_ref.v0_ref) | copy-start | bytes 3538948
  65.0 6.1 %copy-start.6 = (pred[2,128,256]{2,1,0:T(8,128)(4,1)S(1)}, pred[2,128,256]{2,1,0:T(8,128)(4,1)}, u32[]{:S(2)}) copy-start(pred[2,128,256]{2,1,0:T(8,128)(4,1)} %fusion.23) | copy-start | bytes 196612
  67.5 56.0 %collective-permute-start.3 = (bf16[2,128,512]{2,1,0:T(8,128)(2,1)S(1)}, bf16[2,128,512]{2,1,0:T(8,128)(2,1)S(1)}, u32[]{:S(2)}, u32[]{:S(2)}) collective-permute-start(bf16[2,128,512]{2,1,0:T(8,128)(2,1)S(1)} %pad_maximum_fusion.4), channel_id=1, source_target_pairs={{0,4},{4,8},{8,12},{12,16},{16,20},{20,24},{24,28},{1,5},{5,9},{9,... | collective-permute-start | bytes 786440 | tf_op jit(solution)/shard_map/ppermute | solution.py:20
  123.5 1.9 %copy-start.3 = (bf16[2,128,512]{2,1,0:T(8,128)(2,1)}, bf16[2,128,512]{2,1,0:T(8,128)(2,1)S(1)}, u32[]{:S(2)}) copy-start(bf16[2,128,512]{2,1,0:T(8,128)(2,1)S(1)} %collective-permute-done.3.bk_ref.bv_ref) | copy-start | bytes 786436
  125.4 11.2 %copy-start.2 = (bf16[512,2560]{1,0:T(8,128)(2,1)S(1)}, bf16[512,2560]{1,0:T(8,128)(2,1)}, u32[]{:S(2)}) copy-start(bf16[512,2560]{1,0:T(8,128)(2,1)} %param.9) | copy-start | bytes 7864324
  136.5 3.0 %copy-start.1 = (bf16[384,512]{1,0:T(8,128)(2,1)S(1)}, bf16[384,512]{1,0:T(8,128)(2,1)}, u32[]{:S(2)}) copy-start(bf16[384,512]{1,0:T(8,128)(2,1)} %shard_map.73) | copy-start | bytes 1179652
  140.6 1.6 %collective-permute-start.10 = (bf16[2,96,640]{2,1,0:T(8,128)(2,1)S(1)}, bf16[2,96,640]{2,1,0:T(8,128)(2,1)S(1)}, u32[]{:S(2)}, u32[]{:S(2)}) collective-permute-start(bf16[2,96,640]{2,1,0:T(8,128)(2,1)S(1)} %fusion.27), channel_id=1, source_target_pairs={{0,1},{1,0},{2,3},{3,2},{4,5},{5,4},{6,7},{7,6},{8,9},{9,8},{10,11... | collective-permute-start | bytes 737288 | tf_op jit(solution)/shard_map/ppermute | solution.py:250
  140.7 3.1 %collective-permute-start.8 = (bf16[2,96,640]{2,1,0:T(8,128)(2,1)S(1)}, bf16[2,96,640]{2,1,0:T(8,128)(2,1)S(1)}, u32[]{:S(2)}, u32[]{:S(2)}) collective-permute-start(bf16[2,96,640]{2,1,0:T(8,128)(2,1)S(1)} %fusion.26), channel_id=1, source_target_pairs={{0,1},{1,0},{2,3},{3,2},{4,5},{5,4},{6,7},{7,6},{8,9},{9,8},{10,11... | collective-permute-start | bytes 737288 | tf_op jit(solution)/shard_map/ppermute | solution.py:250
  141.3 3.2 %collective-permute-start.6 = (bf16[2,96,640]{2,1,0:T(8,128)(2,1)S(1)}, bf16[2,96,640]{2,1,0:T(8,128)(2,1)S(1)}, u32[]{:S(2)}, u32[]{:S(2)}) collective-permute-start(bf16[2,96,640]{2,1,0:T(8,128)(2,1)S(1)} %fusion.25), channel_id=1, source_target_pairs={{0,1},{1,0},{2,3},{3,2},{4,5},{5,4},{6,7},{7,6},{8,9},{9,8},{10,11... | collective-permute-start | bytes 737288 | tf_op jit(solution)/shard_map/ppermute | solution.py:250
  141.4 4.7 %collective-permute-start.4 = (bf16[2,96,640]{2,1,0:T(8,128)(2,1)S(1)}, bf16[2,96,640]{2,1,0:T(8,128)(2,1)S(1)}, u32[]{:S(2)}, u32[]{:S(2)}) collective-permute-start(bf16[2,96,640]{2,1,0:T(8,128)(2,1)S(1)} %fusion.24), channel_id=1, source_target_pairs={{0,1},{1,0},{2,3},{3,2},{4,5},{5,4},{6,7},{7,6},{8,9},{9,8},{10,11... | collective-permute-start | bytes 737288 | tf_op jit(solution)/shard_map/ppermute | solution.py:250
  142.2 6.2 %collective-permute-start.11 = (bf16[96,640]{1,0:T(8,128)(2,1)S(1)}, bf16[96,640]{1,0:T(8,128)(2,1)S(1)}, u32[]{:S(2)}, u32[]{:S(2)}) collective-permute-start(bf16[96,640]{1,0:T(8,128)(2,1)S(1)} %fusion.36), channel_id=1, source_target_pairs={{0,2},{1,3},{2,0},{3,1},{4,6},{5,7},{6,4},{7,5},{8,10},{9,11},{10,... | collective-permute-start | bytes 368648 | tf_op jit(solution)/shard_map/ppermute | solution.py:258
  143.9 7.2 %collective-permute-start.9 = (bf16[96,640]{1,0:T(8,128)(2,1)S(1)}, bf16[96,640]{1,0:T(8,128)(2,1)S(1)}, u32[]{:S(2)}, u32[]{:S(2)}) collective-permute-start(bf16[96,640]{1,0:T(8,128)(2,1)S(1)} %fusion.35), channel_id=1, source_target_pairs={{0,2},{1,3},{2,0},{3,1},{4,6},{5,7},{6,4},{7,5},{8,10},{9,11},{10,... | collective-permute-start | bytes 368648 | tf_op jit(solution)/shard_map/ppermute | solution.py:258
  144.5 9.2 %collective-permute-start.7 = (bf16[96,640]{1,0:T(8,128)(2,1)S(1)}, bf16[96,640]{1,0:T(8,128)(2,1)S(1)}, u32[]{:S(2)}, u32[]{:S(2)}) collective-permute-start(bf16[96,640]{1,0:T(8,128)(2,1)S(1)} %fusion.34), channel_id=1, source_target_pairs={{0,2},{1,3},{2,0},{3,1},{4,6},{5,7},{6,4},{7,5},{8,10},{9,11},{10,... | collective-permute-start | bytes 368648 | tf_op jit(solution)/shard_map/ppermute | solution.py:258
  146.2 9.3 %collective-permute-start.5 = (bf16[96,640]{1,0:T(8,128)(2,1)S(1)}, bf16[96,640]{1,0:T(8,128)(2,1)S(1)}, u32[]{:S(2)}, u32[]{:S(2)}) collective-permute-start(bf16[96,640]{1,0:T(8,128)(2,1)S(1)} %fusion.33), channel_id=1, source_target_pairs={{0,2},{1,3},{2,0},{3,1},{4,6},{5,7},{6,4},{7,5},{8,10},{9,11},{10,... | collective-permute-start | bytes 368648 | tf_op jit(solution)/shard_map/ppermute | solution.py:258

commit v18 on v15

--- a/solution.py
+++ b/solution.py
@@ -197,15 +197,10 @@
     asked = lax.all_to_all(wanted_ids, "mem", split_axis=0, concat_axis=0, tiled=True).reshape(
         holder_count * CAP
     )
-    chooser = (
-        asked[:, None] == lax.broadcasted_iota(jnp.int32, (holder_count * CAP, local_blocks), 1)
-    ).astype(jnp.bfloat16)
-    picked = jnp.einsum(
-        "sb,pbx->spx",
-        chooser,
-        local_store.reshape(2, local_blocks, BLK * groups * HD),
-        preferred_element_type=jnp.float32,
-    ).astype(jnp.bfloat16).reshape(holder_count * CAP, 2, BLK, groups * HD)
+    rows_wanted = jnp.stack([asked, asked + local_blocks], axis=1).reshape(holder_count * CAP * 2)
+    picked = jnp.take(
+        memory.reshape(2 * local_blocks, BLK, groups * HD), rows_wanted, axis=0, mode="clip"
+    ).reshape(holder_count * CAP, 2, BLK, groups * HD)
     fetched = lax.all_to_all(picked, "mem", split_axis=0, concat_axis=0, tiled=True)
     pool = holder_count * CAP
     row_of = entry_order // TOPB

time: 165 us -> 156 us (0.945)
  blocking collectives: 0 us -> 10 us
  local copies, waits for them, and re-layouts: 38.3 us -> 29.5 us
  starting transfers between devices: 24.6 us -> 19.1 us
  matrix products: 20.8 us -> 16.1 us
    another operation x1 -> x2, local copies, waits for them, and re-layouts: 10.6 us -> 0.17 us  [local(): jnp.stack([asked, asked + local_blocks], axis=1)]
    all_to_all x0 -> x1, blocking collectives: none -> 10 us  [local(): lax.all_to_all(wanted_ids, 'mem', split_axis=0, concat_axis=0, tiled=True)]
    gather x0 -> x1, local copies, waits for them, and re-layouts: none -> 6.17 us  [local(): jnp.take(memory.reshape(2 * local_blocks, BLK, groups * HD), rows_wanted,...]
    all_to_all x1 -> x0, starting transfers between devices: 6.14 us -> none  [local(): lax.all_to_all(wanted_ids, 'mem', split_axis=0, concat_axis=0, tiled=True)]
    dot_general x1 -> x0, matrix products: 4.68 us -> none  [local(): jnp.einsum('sb,pbx->spx', chooser, local_store.reshape(2, local_blocks, B...]
    reshape x1 -> x0, local copies, waits for them, and re-layouts: 2.43 us -> none  [local(): picked = jnp.einsum('sb,pbx->spx', chooser, local_store.reshape(2, local_...]
  transfers between devices with their start and end apart: 14 -> 13, of which waited for: 9 -> 9; matrix products, arithmetic and copies ran while one was open for 30% -> 25% of each run, Pallas kernels for 0% -> 0%
where the time goes in v18:
time: 156 us; the launch traced here: 155 us
  waiting for transfers between devices  59.3 us (38%)
  local copies, waits for them, and re-layouts  29.5 us (19%)
  starting transfers between devices  19.1 us (12%)
  matrix products  16.1 us (10%)
  Pallas kernels  11 us (7%)
  blocking collectives  10 us (6%)
  other arithmetic  9.76 us (6%)
    ppermute x1, waiting for transfers between devices, from_behind(): lax.ppermute(value, axis, [(source, source + steps) for source in range(i...  33.4 us
    ppermute x3, waiting for transfers between devices, gather_tp(): lax.ppermute(part, 'tp', [(t, (t + shift) % count) for t in range(count)])  17 us
    pallas_call x1, Pallas kernels, far_attention(): pl.pallas_call(far_kernel, grid=(groups,), in_specs=[pl.BlockSpec((rows,...  11 us
    all_to_all x1, blocking collectives, local(): lax.all_to_all(wanted_ids, 'mem', split_axis=0, concat_axis=0, tiled=True)  10 us
    ppermute x4, waiting for transfers between devices, reduce_over_tp(): lax.ppermute(outgoing.astype(jnp.bfloat16), 'tp', pairs).astype(jnp.float32)  8.68 us
    dot_general x1, matrix products, local(): jnp.dot(gather_tp(tokens), input_weight, preferred_element_type=jnp.float32)  8.14 us
    all_to_all x1, starting transfers between devices, local(): lax.all_to_all(picked, 'mem', split_axis=0, concat_axis=0, tiled=True)  6.94 us
    gather x1, local copies, waits for them, and re-layouts, local(): jnp.take(memory.reshape(2 * local_blocks, BLK, groups * HD), rows_wanted,...  6.17 us
  transfers between devices with their start and end apart: 13, of which 9 were waited for; matrix products, arithmetic and copies ran while one was open for 25% of the time, Pallas kernels for 0%

profile of v18, /device:TPU:16, one launch (start us, length us, event | category | flops | bytes accessed | tf_op | source)
XLA Modules:
  0.0 155.2 jit_solution(9246533641367942371)
XLA Ops:
  0.0 0.9 eq.74
  0.9 0.9 select_reduce_fusion.1
  1.8 0.2 convert_reduce_fusion.1
  2.0 0.7 compare_reduce_fusion
  2.7 0.2 convert_reduce_fusion
  2.9 0.1 select_reduce_fusion.2
  3.0 0.1 copy.55
  3.1 10.0 %all_to_all.14 = s32[8,1,2]{2,1,0:T(1,128)S(1)} all-to-all(s32[8,1,2]{2,1,0:T(1,128)S(1)} %copy.55), channel_id=1, replica_groups=mesh['mem'=8,'tp'=4] {'mem'}, dimensions={0} | all-to-all | bytes 128 | tf_op jit(solution)/shard_map/all_to_all | solution.py:197
  13.1 0.5 broadcast.415
  13.6 0.7 reduce.22
  14.3 0.1 stack_reshape.3
  14.4 0.1 copy.56
  14.5 0.1 reshape.335
  14.6 6.2 %gather_fusion.1 = bf16[32,128,512]{2,1,0:T(8,128)(2,1)} fusion(bf16[64,128,512]{2,1,0:T(8,128)(2,1)} %bitcast.112, s32[1024]{0:T(1024)S(1)} %pad_clamp_fusion), kind=kCustom, calls=%fused_computation.1 | custom fusion | bytes 8388736 | tf_op jit(solution)/shard_map/jit(_take)/gather | solution.py:201
  20.7 6.9 %all-to-all-start.1 = ((bf16[16,2,128,512]{3,2,1,0:T(8,128)(2,1)}), bf16[16,2,128,512]{3,2,1,0:T(8,128)(2,1)}, u32[]{:S(2)}, u32[]{:S(2)}) async-start(bf16[16,2,128,512]{3,2,1,0:T(8,128)(2,1)} %bitcast.101), calls=%async_computation.1 | async-start | bytes 8388608 | tf_op jit(solution)/shard_map/all_to_all | solution.py:204
  27.7 1.7 %collective-permute-start.2 = (bf16[96,2560]{1,0:T(8,128)(2,1)S(1)}, bf16[96,2560]{1,0:T(8,128)(2,1)}, u32[]{:S(2)}, u32[]{:S(2)}) collective-permute-start(bf16[96,2560]{1,0:T(8,128)(2,1)S(1)} %copy-done.3), channel_id=1, source_target_pairs={{0,3},{1,0},{2,1},{3,2},{4,7},{5,4},{6,5},{7,6},{8,11},{9,8},{10,9... | collective-permute-start | bytes 1474568 | tf_op jit(solution)/shard_map/ppermute | solution.py:131
  29.4 1.5 collective-permute-start.1
  31.0 2.8 %scatter_fusion = pred[3,16]{1,0:T(4,128)(4,1)S(1)} fusion(pred[3,16]{1,0:T(4,128)(4,1)S(1)} %broadcast_in_dim.98, s32[48]{0:T(128)S(1)} %fusion.38, pred[48]{0:T(512)(128)(4,1)S(1)} %broadcast.380), kind=kCustom, calls=%fused_computation.2 | custom fusion | bytes 528 | tf_op jit(solution)/shard_map/scatter | solution.py:208
  33.9 0.1 slice_add_fusion
  34.0 0.1 fusion.24
  34.1 0.7 fusion.15
  34.9 4.6 %collective-permute-done = bf16[96,2560]{1,0:T(8,128)(2,1)} collective-permute-done((bf16[96,2560]{1,0:T(8,128)(2,1)S(1)}, bf16[96,2560]{1,0:T(8,128)(2,1)}, u32[]{:S(2)}, u32[]{:S(2)}) %collective-permute-start) | collective-permute-done | bytes 491552 | tf_op jit(solution)/shard_map/ppermute | solution.py:131
  39.4 1.6 %collective-permute-done.2 = bf16[96,2560]{1,0:T(8,128)(2,1)} collective-permute-done((bf16[96,2560]{1,0:T(8,128)(2,1)S(1)}, bf16[96,2560]{1,0:T(8,128)(2,1)}, u32[]{:S(2)}, u32[]{:S(2)}) %collective-permute-start.2) | collective-permute-done | bytes 491552 | tf_op jit(solution)/shard_map/ppermute | solution.py:131
  41.0 10.8 %collective-permute-done.1 = bf16[96,2560]{1,0:T(8,128)(2,1)} collective-permute-done((bf16[96,2560]{1,0:T(8,128)(2,1)S(1)}, bf16[96,2560]{1,0:T(8,128)(2,1)}, u32[]{:S(2)}, u32[]{:S(2)}) %collective-permute-start.1) | collective-permute-done | bytes 491552 | tf_op jit(solution)/shard_map/ppermute | solution.py:131
  51.8 2.9 %pad_maximum_fusion = bf16[4,96,2560]{2,1,0:T(8,128)(2,1)} fusion(bf16[1,96,2560]{2,1,0:T(8,128)(2,1)} %bitcast.3, bf16[1,96,2560]{2,1,0:T(8,128)(2,1)} %bitcast.2, bf16[1,96,2560]{2,1,0:T(8,128)(2,1)} %bitcast.1, bf16[1,96,2560]{2,1,0:T(8,128)(2,1)S(1)} %bitcast.119), kind=kLoop, calls=%fused_computation.5 | loop fusion | flops 2949120 | bytes 3932160 | tf_op jit(solution)/shard_map/stack | solution.py:135
  54.8 3.5 %gather_fusion = bf16[4,96,2560]{2,1,0:T(8,128)(2,1)} fusion(bf16[4,96,2560]{2,1,0:T(8,128)(2,1)} %pad_maximum_fusion, s32[1024]{0:T(1024)S(1)} %pad_clamp_fusion.1), kind=kCustom, calls=%fused_computation | custom fusion | bytes 3932176 | tf_op jit(solution)/shard_map/jit(_take)/gather | solution.py:135
  58.2 8.1 %convolution_convert_fusion.q_ref.k0_ref.v0_ref = bf16[384,1536]{1,0:T(8,128)(2,1)} fusion(bf16[384,2560]{1,0:T(8,128)(2,1)} %bitcast.113, bf16[2560,1536]{1,0:T(8,128)(2,1)} %param.8), kind=kOutput, calls=%fused_computation.4 | convolution fusion | flops 3020488704 | bytes 11010048 | tf_op jit(solution)/shard_map/dot_general | solution.py:145
  66.4 2.4 %copy.52 = bf16[384,1536]{0,1:T(8,128)(2,1)} copy(bf16[384,1536]{1,0:T(8,128)(2,1)} %convolution_convert_fusion.q_ref.k0_ref.v0_ref) | data formatting | bytes 2359296 | tf_op jit(solution)/shard_map/convert_element_type | solution.py:150
  68.8 1.0 fusion.47
  69.8 0.1 copy.71
  69.9 0.8 copy.72
  70.7 2.2 %fusion.46 = (bf16[256,4,1,128]{0,3,2,1:T(8,128)(2,1)}, bf16[256,4,1,128]{0,3,2,1:T(8,128)(2,1)S(1)}, bf16[256,4,1,128]{0,3,2,1:T(8,128)(2,1)S(1)}, bf16[256,4,1...) fusion(bf16[384,4,3,128]{0,3,2,1:T(8,128)(2,1)} %bitcast.103), kind=kLoop, calls=%fused_computation.112 | loop fusion | bytes 2621440 | tf_op jit(solution)/shard_map/slice | solution.py:163
  72.8 1.8 %copy.57 = bf16[256,4,1,128]{3,0,1,2:T(8,128)(2,1)} copy(bf16[256,4,1,128]{0,3,2,1:T(8,128)(2,1)} %get-tuple-element.11) | data formatting | bytes 524288 | tf_op jit(solution)/shard_map/slice | solution.py:163
  74.6 1.8 %copy.59 = bf16[256,4,1,128]{3,0,1,2:T(8,128)(2,1)} copy(bf16[256,4,1,128]{0,3,2,1:T(8,128)(2,1)} %get-tuple-element.14) | data formatting | bytes 524288 | tf_op jit(solution)/shard_map/slice | solution.py:164
  76.4 0.8 copy.58
  77.2 1.7 %pad_maximum_fusion.4 = bf16[2,128,512]{2,1,0:T(8,128)(2,1)} fusion(bf16[1,128,512]{2,1,0:T(8,128)(2,1)} %copy.72, bf16[1,128,512]{2,1,0:T(8,128)(2,1)S(1)} %copy.71), kind=kLoop, calls=%fused_computation.29 | loop fusion | flops 131072 | bytes 524288 | tf_op jit(solution)/shard_map/stack | solution.py:155
  78.9 3.4 %collective-permute-start.3 = (bf16[2,128,512]{2,1,0:T(8,128)(2,1)}, bf16[2,128,512]{2,1,0:T(8,128)(2,1)S(1)}, u32[]{:S(2)}, u32[]{:S(2)}) collective-permute-start(bf16[2,128,512]{2,1,0:T(8,128)(2,1)} %pad_maximum_fusion.4), channel_id=1, source_target_pairs={{0,4},{4,8},{8,12},{12,16},{16,20},{20,24},{24,28},{1,5},{5,9},{9,... | collective-permute-start | bytes 786440 | tf_op jit(solution)/shard_map/ppermute | solution.py:20
  82.3 1.4 convolution_multiply_fusion
  83.7 1.0 copy-done.2
  84.6 0.4 fusion.48
  85.0 0.8 copy.64
  85.9 0.2 copy.63
  86.1 4.4 %fusion.9.near_ref = f32[2,4,128,128]{3,2,1,0:T(8,128)} fusion(f32[2,4,128]{2,1,0:T(4,128)S(1)} %fusion.48, f32[2,4,128,256]{3,2,1,0:T(8,128)} %copy-done.2, pred[2,128,256]{2,1,0:T(8,128)(4,1)} %fusion.15, bf16[2,128,4,128]{3,1,0,2:T(8,128)(2,1)} %bitcast.120, bf16[2,128,4,128]{3,1,0,2:T(8,128)(2,1)S(1)} %bitcast.121), kind=kOutput, calls=%fused_computation.15 | convolution fusion | flops 69469440 | bytes 2166784 | tf_op jit(solution)/shard_map/ngqk,nkgd->ngqd/dot_general | solution.py:44
  90.5 33.4 %collective-permute-done.3.bk_ref.bv_ref = bf16[2,128,512]{2,1,0:T(8,128)(2,1)S(1)} collective-permute-done((bf16[2,128,512]{2,1,0:T(8,128)(2,1)}, bf16[2,128,512]{2,1,0:T(8,128)(2,1)S(1)}, u32[]{:S(2)}, u32[]{:S(2)}) %collective-permute-start.3) | collective-permute-done | bytes 262176 | tf_op jit(solution)/shard_map/ppermute | solution.py:20
  123.9 0.6 broadcast_in_dim.106.start_ref
  124.5 0.7 broadcast_in_dim.107
  125.1 0.7 broadcast_in_dim.102
  125.8 11.0 %shard_map.73 = bf16[384,512]{1,0:T(8,128)(2,1)} custom-call(bf16[384,1536]{1,0:T(8,128)(2,1)} %convolution_convert_fusion.q_ref.k0_ref.v0_ref, bf16[384,1536]{1,0:T(8,128)(2,1)} %convolution_convert_fusion.q_ref.k0_ref.v0_ref, bf16[384,1536]{1,0:T(8,128)(2,1)} %convolution_convert_fusion.q_ref.k0_ref.v0_ref, bf16[2,128,512]{2,1,0:T(8,128)(2,1)} %copy-done.1, ...), custom_call_target="tpu_custom_call" | custom-call | flops 1677721600 | bytes 5767168 | tf_op jit(solution)/shard_map/pallas_call | solution.py:102
  136.9 2.2 %fusion.49 = f32[384,2560]{1,0:T(8,128)S(1)} fusion(bf16[384,512]{1,0:T(8,128)(2,1)} %shard_map.73, bf16[512,2560]{1,0:T(8,128)(2,1)S(1)} %copy-done), kind=kOutput, calls=%fused_computation.115 | convolution fusion | flops 1006632960 | bytes 6946816 | tf_op jit(solution)/shard_map/dot_general | solution.py:223
  139.0 0.3 fusion.45
  139.4 0.1 collective-permute-start.6
  139.5 0.5 collective-permute-start.8
  140.1 0.1 collective-permute-start.4
  140.2 0.5 collective-permute-start.10
  140.7 0.2 collective-permute-done.6
  141.0 1.6 %collective-permute-start.7 = (bf16[96,640]{1,0:T(8,128)(2,1)S(1)}, bf16[96,640]{1,0:T(8,128)(2,1)S(1)}, u32[]{:S(2)}, u32[]{:S(2)}) collective-permute-start(bf16[96,640]{1,0:T(8,128)(2,1)S(1)} %fusion.26), channel_id=1, source_target_pairs={{0,2},{1,3},{2,0},{3,1},{4,6},{5,7},{6,4},{7,5},{8,10},{9,11},{10,... | collective-permute-start | bytes 368648 | tf_op jit(solution)/shard_map/ppermute | solution.py:248
  142.7 0.6 collective-permute-start.9
  143.3 1.6 %collective-permute-start.5 = (bf16[96,640]{1,0:T(8,128)(2,1)S(1)}, bf16[96,640]{1,0:T(8,128)(2,1)S(1)}, u32[]{:S(2)}, u32[]{:S(2)}) collective-permute-start(bf16[96,640]{1,0:T(8,128)(2,1)S(1)} %fusion.25), channel_id=1, source_target_pairs={{0,2},{1,3},{2,0},{3,1},{4,6},{5,7},{6,4},{7,5},{8,10},{9,11},{10,... | collective-permute-start | bytes 368648 | tf_op jit(solution)/shard_map/ppermute | solution.py:248
  145.0 0.6 collective-permute-start.11
  145.6 1.7 %collective-permute-done.7 = bf16[96,640]{1,0:T(8,128)(2,1)S(1)} collective-permute-done((bf16[96,640]{1,0:T(8,128)(2,1)S(1)}, bf16[96,640]{1,0:T(8,128)(2,1)S(1)}, u32[]{:S(2)}, u32[]{:S(2)}) %collective-permute-start.7) | collective-permute-done | bytes 122912 | tf_op jit(solution)/shard_map/ppermute | solution.py:248
  147.3 2.6 %collective-permute-done.9 = bf16[96,640]{1,0:T(8,128)(2,1)S(1)} collective-permute-done((bf16[96,640]{1,0:T(8,128)(2,1)S(1)}, bf16[96,640]{1,0:T(8,128)(2,1)S(1)}, u32[]{:S(2)}, u32[]{:S(2)}) %collective-permute-start.9) | collective-permute-done | bytes 122912 | tf_op jit(solution)/shard_map/ppermute | solution.py:248
  149.9 2.6 %collective-permute-done.5 = bf16[96,640]{1,0:T(8,128)(2,1)S(1)} collective-permute-done((bf16[96,640]{1,0:T(8,128)(2,1)S(1)}, bf16[96,640]{1,0:T(8,128)(2,1)S(1)}, u32[]{:S(2)}, u32[]{:S(2)}) %collective-permute-start.5) | collective-permute-done | bytes 122912 | tf_op jit(solution)/shard_map/ppermute | solution.py:248
  152.5 1.8 %collective-permute-done.11 = bf16[96,640]{1,0:T(8,128)(2,1)S(1)} collective-permute-done((bf16[96,640]{1,0:T(8,128)(2,1)S(1)}, bf16[96,640]{1,0:T(8,128)(2,1)S(1)}, u32[]{:S(2)}, u32[]{:S(2)}) %collective-permute-start.11) | collective-permute-done | bytes 122912 | tf_op jit(solution)/shard_map/ppermute | solution.py:248
  154.4 0.8 pad_maximum_fusion.3
  (46 shorter events, 0.6 us)
Async XLA Ops:
  0.0 136.9 %copy-start = (bf16[512,2560]{1,0:T(8,128)(2,1)S(1)}, bf16[512,2560]{1,0:T(8,128)(2,1)}, u32[]{:S(2)}) copy-start(bf16[512,2560]{1,0:T(8,128)(2,1)} %param.9) | copy-start | bytes 7864324
  20.7 6.9 %copy-start.3 = (bf16[96,2560]{1,0:T(8,128)(2,1)S(1)}, bf16[96,2560]{1,0:T(8,128)(2,1)}, u32[]{:S(2)}) copy-start(bf16[96,2560]{1,0:T(8,128)(2,1)} %param.7) | copy-start | bytes 1474564
  20.7 13.2 %copy-start.5 = (f32[4]{0:T(128)S(1)}, f32[4]{0:T(128)}, u32[]{:S(2)}) copy-start(f32[4]{0:T(128)} %param.10) | copy-start | bytes 52
  20.7 103.1 %all-to-all-start.1 = ((bf16[16,2,128,512]{3,2,1,0:T(8,128)(2,1)}), bf16[16,2,128,512]{3,2,1,0:T(8,128)(2,1)}, u32[]{:S(2)}, u32[]{:S(2)}) async-start(bf16[16,2,128,512]{3,2,1,0:T(8,128)(2,1)} %bitcast.101), calls=%async_computation.1 | async-start | bytes 8388608 | tf_op jit(solution)/shard_map/all_to_all | solution.py:204
  27.7 11.7 %collective-permute-start = (bf16[96,2560]{1,0:T(8,128)(2,1)S(1)}, bf16[96,2560]{1,0:T(8,128)(2,1)}, u32[]{:S(2)}, u32[]{:S(2)}) collective-permute-start(bf16[96,2560]{1,0:T(8,128)(2,1)S(1)} %copy-done.3), channel_id=1, source_target_pairs={{0,1},{1,2},{2,3},{3,0},{4,5},{5,6},{6,7},{7,4},{8,9},{9,10},{10,1... | collective-permute-start | bytes 1474568 | tf_op jit(solution)/shard_map/ppermute | solution.py:131
  27.7 13.3 %collective-permute-start.2 = (bf16[96,2560]{1,0:T(8,128)(2,1)S(1)}, bf16[96,2560]{1,0:T(8,128)(2,1)}, u32[]{:S(2)}, u32[]{:S(2)}) collective-permute-start(bf16[96,2560]{1,0:T(8,128)(2,1)S(1)} %copy-done.3), channel_id=1, source_target_pairs={{0,3},{1,0},{2,1},{3,2},{4,7},{5,4},{6,5},{7,6},{8,11},{9,8},{10,9... | collective-permute-start | bytes 1474568 | tf_op jit(solution)/shard_map/ppermute | solution.py:131
  29.4 22.4 %collective-permute-start.1 = (bf16[96,2560]{1,0:T(8,128)(2,1)S(1)}, bf16[96,2560]{1,0:T(8,128)(2,1)}, u32[]{:S(2)}, u32[]{:S(2)}) collective-permute-start(bf16[96,2560]{1,0:T(8,128)(2,1)S(1)} %copy-done.3), channel_id=1, source_target_pairs={{0,2},{1,3},{2,0},{3,1},{4,6},{5,7},{6,4},{7,5},{8,10},{9,11},{10,... | collective-permute-start | bytes 1474568 | tf_op jit(solution)/shard_map/ppermute | solution.py:131
  77.2 7.4 %copy-start.4 = (pred[2,128,256]{2,1,0:T(8,128)(4,1)S(1)}, pred[2,128,256]{2,1,0:T(8,128)(4,1)}, u32[]{:S(2)}) copy-start(pred[2,128,256]{2,1,0:T(8,128)(4,1)} %fusion.15) | copy-start | bytes 196612
  78.9 45.0 %collective-permute-start.3 = (bf16[2,128,512]{2,1,0:T(8,128)(2,1)}, bf16[2,128,512]{2,1,0:T(8,128)(2,1)S(1)}, u32[]{:S(2)}, u32[]{:S(2)}) collective-permute-start(bf16[2,128,512]{2,1,0:T(8,128)(2,1)} %pad_maximum_fusion.4), channel_id=1, source_target_pairs={{0,4},{4,8},{8,12},{12,16},{16,20},{20,24},{24,28},{1,5},{5,9},{9,... | collective-permute-start | bytes 786440 | tf_op jit(solution)/shard_map/ppermute | solution.py:20
  83.7 1.0 copy-start.2
  123.9 2.0 %copy-start.1 = (bf16[2,128,512]{2,1,0:T(8,128)(2,1)}, bf16[2,128,512]{2,1,0:T(8,128)(2,1)S(1)}, u32[]{:S(2)}) copy-start(bf16[2,128,512]{2,1,0:T(8,128)(2,1)S(1)} %collective-permute-done.3.bk_ref.bv_ref) | copy-start | bytes 786436
  139.4 1.6 %collective-permute-start.6 = (bf16[2,96,640]{2,1,0:T(8,128)(2,1)S(1)}, bf16[2,96,640]{2,1,0:T(8,128)(2,1)S(1)}, u32[]{:S(2)}, u32[]{:S(2)}) collective-permute-start(bf16[2,96,640]{2,1,0:T(8,128)(2,1)S(1)} %fusion.17), channel_id=1, source_target_pairs={{0,1},{1,0},{2,3},{3,2},{4,5},{5,4},{6,7},{7,6},{8,9},{9,8},{10,11... | collective-permute-start | bytes 737288 | tf_op jit(solution)/shard_map/ppermute | solution.py:240
  139.5 3.1 %collective-permute-start.8 = (bf16[2,96,640]{2,1,0:T(8,128)(2,1)S(1)}, bf16[2,96,640]{2,1,0:T(8,128)(2,1)S(1)}, u32[]{:S(2)}, u32[]{:S(2)}) collective-permute-start(bf16[2,96,640]{2,1,0:T(8,128)(2,1)S(1)} %fusion.18), channel_id=1, source_target_pairs={{0,1},{1,0},{2,3},{3,2},{4,5},{5,4},{6,7},{7,6},{8,9},{9,8},{10,11... | collective-permute-start | bytes 737288 | tf_op jit(solution)/shard_map/ppermute | solution.py:240
  140.1 3.2 %collective-permute-start.4 = (bf16[2,96,640]{2,1,0:T(8,128)(2,1)S(1)}, bf16[2,96,640]{2,1,0:T(8,128)(2,1)S(1)}, u32[]{:S(2)}, u32[]{:S(2)}) collective-permute-start(bf16[2,96,640]{2,1,0:T(8,128)(2,1)S(1)} %fusion.16), channel_id=1, source_target_pairs={{0,1},{1,0},{2,3},{3,2},{4,5},{5,4},{6,7},{7,6},{8,9},{9,8},{10,11... | collective-permute-start | bytes 737288 | tf_op jit(solution)/shard_map/ppermute | solution.py:240
  140.2 4.7 %collective-permute-start.10 = (bf16[2,96,640]{2,1,0:T(8,128)(2,1)S(1)}, bf16[2,96,640]{2,1,0:T(8,128)(2,1)S(1)}, u32[]{:S(2)}, u32[]{:S(2)}) collective-permute-start(bf16[2,96,640]{2,1,0:T(8,128)(2,1)S(1)} %fusion.19), channel_id=1, source_target_pairs={{0,1},{1,0},{2,3},{3,2},{4,5},{5,4},{6,7},{7,6},{8,9},{9,8},{10,11... | collective-permute-start | bytes 737288 | tf_op jit(solution)/shard_map/ppermute | solution.py:240
  141.0 6.2 %collective-permute-start.7 = (bf16[96,640]{1,0:T(8,128)(2,1)S(1)}, bf16[96,640]{1,0:T(8,128)(2,1)S(1)}, u32[]{:S(2)}, u32[]{:S(2)}) collective-permute-start(bf16[96,640]{1,0:T(8,128)(2,1)S(1)} %fusion.26), channel_id=1, source_target_pairs={{0,2},{1,3},{2,0},{3,1},{4,6},{5,7},{6,4},{7,5},{8,10},{9,11},{10,... | collective-permute-start | bytes 368648 | tf_op jit(solution)/shard_map/ppermute | solution.py:248
  142.7 7.2 %collective-permute-start.9 = (bf16[96,640]{1,0:T(8,128)(2,1)S(1)}, bf16[96,640]{1,0:T(8,128)(2,1)S(1)}, u32[]{:S(2)}, u32[]{:S(2)}) collective-permute-start(bf16[96,640]{1,0:T(8,128)(2,1)S(1)} %fusion.27), channel_id=1, source_target_pairs={{0,2},{1,3},{2,0},{3,1},{4,6},{5,7},{6,4},{7,5},{8,10},{9,11},{10,... | collective-permute-start | bytes 368648 | tf_op jit(solution)/shard_map/ppermute | solution.py:248
  143.3 9.2 %collective-permute-start.5 = (bf16[96,640]{1,0:T(8,128)(2,1)S(1)}, bf16[96,640]{1,0:T(8,128)(2,1)S(1)}, u32[]{:S(2)}, u32[]{:S(2)}) collective-permute-start(bf16[96,640]{1,0:T(8,128)(2,1)S(1)} %fusion.25), channel_id=1, source_target_pairs={{0,2},{1,3},{2,0},{3,1},{4,6},{5,7},{6,4},{7,5},{8,10},{9,11},{10,... | collective-permute-start | bytes 368648 | tf_op jit(solution)/shard_map/ppermute | solution.py:248
  145.0 9.3 %collective-permute-start.11 = (bf16[96,640]{1,0:T(8,128)(2,1)S(1)}, bf16[96,640]{1,0:T(8,128)(2,1)S(1)}, u32[]{:S(2)}, u32[]{:S(2)}) collective-permute-start(bf16[96,640]{1,0:T(8,128)(2,1)S(1)} %fusion.28), channel_id=1, source_target_pairs={{0,2},{1,3},{2,0},{3,1},{4,6},{5,7},{6,4},{7,5},{8,10},{9,11},{10,... | collective-permute-start | bytes 368648 | tf_op jit(solution)/shard_map/ppermute | solution.py:248

commit v19 on v18

--- a/solution.py
+++ b/solution.py
@@ -124,6 +124,36 @@
         ),
     )(projected, projected, projected, before, before, fetched, fetched, bias, later, start, mixing)
 
+def pick_kernel(ids_ref, mem_ref, out_ref, sems):
+    copies = []
+    for slot in range(out_ref.shape[0]):
+        for part in range(2):
+            copy = pltpu.make_async_copy(
+                mem_ref.at[part, pl.ds(ids_ref[slot] * BLK, BLK)],
+                out_ref.at[slot, part],
+                sems.at[slot, part],
+            )
+            copy.start()
+            copies.append(copy)
+    for copy in copies:
+        copy.wait()
+
+
+def pick_blocks(ids, memory):
+    count = ids.shape[0]
+    return pl.pallas_call(
+        pick_kernel,
+        grid_spec=pltpu.PrefetchScalarGridSpec(
+            num_scalar_prefetch=1,
+            grid=(1,),
+            in_specs=[pl.BlockSpec(memory_space=pl.ANY)],
+            out_specs=pl.BlockSpec(memory_space=pl.ANY),
+            scratch_shapes=[pltpu.SemaphoreType.DMA((count, 2))],
+        ),
+        out_shape=jax.ShapeDtypeStruct((count, 2, BLK, memory.shape[2]), memory.dtype),
+    )(ids, memory)
+
+
 def gather_tp(part):
     count = lax.axis_size("tp")
     me = lax.axis_index("tp")
@@ -197,10 +227,7 @@
     asked = lax.all_to_all(wanted_ids, "mem", split_axis=0, concat_axis=0, tiled=True).reshape(
         holder_count * CAP
     )
-    rows_wanted = jnp.stack([asked, asked + local_blocks], axis=1).reshape(holder_count * CAP * 2)
-    picked = jnp.take(
-        memory.reshape(2 * local_blocks, BLK, groups * HD), rows_wanted, axis=0, mode="clip"
-    ).reshape(holder_count * CAP, 2, BLK, groups * HD)
+    picked = pick_blocks(jnp.clip(asked, 0, local_blocks - 1), memory)
     fetched = lax.all_to_all(picked, "mem", split_axis=0, concat_axis=0, tiled=True)
     pool = holder_count * CAP
     row_of = entry_order // TOPB

time: 156 us -> 278 us (1.78)
  Pallas kernels: 11 us -> 140 us
  local copies, waits for them, and re-layouts: 29.5 us -> 23.2 us
    pallas_call x0 -> x1, Pallas kernels: none -> 129 us  [pick_blocks(): pl.pallas_call(pick_kernel, grid_spec=pltpu.PrefetchScalarGridSpec(num_sc...]
    gather x1 -> x0, local copies, waits for them, and re-layouts: 6.17 us -> none  [local(): jnp.take(memory.reshape(2 * local_blocks, BLK, groups * HD), rows_wanted,...]
  transfers between devices with their start and end apart: 13 -> 13, of which waited for: 9 -> 9; matrix products, arithmetic and copies ran while one was open for 25% -> 14% of each run, Pallas kernels for 0% -> 0%
where the time goes in v19:
time: 278 us; the launch traced here: 277 us
  Pallas kernels  140 us (50%)
  waiting for transfers between devices  59.3 us (21%)
  local copies, waits for them, and re-layouts  23.2 us (8%)
  starting transfers between devices  19.2 us (7%)
  matrix products  16.1 us (6%)
  blocking collectives  10 us (4%)
  other arithmetic  9.09 us (3%)
    pallas_call x1, Pallas kernels, pick_blocks(): pl.pallas_call(pick_kernel, grid_spec=pltpu.PrefetchScalarGridSpec(num_sc...  129 us
    ppermute x1, waiting for transfers between devices, from_behind(): lax.ppermute(value, axis, [(source, source + steps) for source in range(i...  33.4 us
    ppermute x3, waiting for transfers between devices, gather_tp(): lax.ppermute(part, 'tp', [(t, (t + shift) % count) for t in range(count)])  17 us
    pallas_call x1, Pallas kernels, far_attention(): pl.pallas_call(far_kernel, grid=(groups,), in_specs=[pl.BlockSpec((rows,...  11 us
    all_to_all x1, blocking collectives, local(): lax.all_to_all(wanted_ids, 'mem', split_axis=0, concat_axis=0, tiled=True)  10 us
    ppermute x4, waiting for transfers between devices, reduce_over_tp(): lax.ppermute(outgoing.astype(jnp.bfloat16), 'tp', pairs).astype(jnp.float32)  8.68 us
    dot_general x1, matrix products, local(): jnp.dot(gather_tp(tokens), input_weight, preferred_element_type=jnp.float32)  8.14 us
    all_to_all x1, starting transfers between devices, local(): lax.all_to_all(picked, 'mem', split_axis=0, concat_axis=0, tiled=True)  6.95 us
  transfers between devices with their start and end apart: 13, of which 9 were waited for; matrix products, arithmetic and copies ran while one was open for 14% of the time, Pallas kernels for 0%

profile of v19, /device:TPU:16, one launch (start us, length us, event | category | flops | bytes accessed | tf_op | source)
XLA Modules:
  0.0 277.3 jit_solution(2440252765517062439)
XLA Ops:
  0.0 0.9 eq.74
  0.9 0.9 select_reduce_fusion.1
  1.8 0.2 convert_reduce_fusion.1
  2.0 0.7 compare_reduce_fusion
  2.7 0.2 convert_reduce_fusion
  2.9 0.1 select_reduce_fusion.2
  3.0 0.1 copy.52
  3.1 10.0 %all_to_all.14 = s32[8,1,2]{2,1,0:T(1,128)S(1)} all-to-all(s32[8,1,2]{2,1,0:T(1,128)S(1)} %copy.52), channel_id=1, replica_groups=mesh['mem'=8,'tp'=4] {'mem'}, dimensions={0} | all-to-all | bytes 128 | tf_op jit(solution)/shard_map/all_to_all | solution.py:227
  13.1 0.6 min.12.ids_ref
  13.7 129.1 %shard_map.73 = bf16[16,2,128,512]{3,2,1,0:T(8,128)(2,1)} custom-call(s32[16]{0:T(128)} %min.12.ids_ref, bf16[2,4096,512]{2,1,0:T(8,128)(2,1)} %mem_ref.1), custom_call_target="tpu_custom_call" | custom-call | tf_op jit(solution)/shard_map/pallas_call | solution.py:144
  142.8 0.0 copy-start.3
  142.8 0.0 copy-start.5
  142.9 6.9 %all-to-all-start.1 = ((bf16[16,2,128,512]{3,2,1,0:T(8,128)(2,1)}), bf16[16,2,128,512]{3,2,1,0:T(8,128)(2,1)}, u32[]{:S(2)}, u32[]{:S(2)}) async-start(bf16[16,2,128,512]{3,2,1,0:T(8,128)(2,1)} %shard_map.73), calls=%async_computation.1 | async-start | bytes 8388608 | tf_op jit(solution)/shard_map/all_to_all | solution.py:231
  149.8 0.0 collective-permute-start
  149.8 1.7 collective-permute-start.2
  151.6 1.5 collective-permute-start.1
  153.1 2.8 %scatter_fusion = pred[3,16]{1,0:T(4,128)(4,1)S(1)} fusion(pred[3,16]{1,0:T(4,128)(4,1)S(1)} %broadcast_in_dim.93, s32[48]{0:T(128)S(1)} %fusion.38, pred[48]{0:T(512)(128)(4,1)S(1)} %broadcast.373), kind=kCustom, calls=%fused_computation.1 | custom fusion | bytes 528 | tf_op jit(solution)/shard_map/scatter | solution.py:235
  156.0 0.1 slice_add_fusion
  156.2 0.1 fusion.24
  156.3 0.7 fusion.15
  157.0 4.6 %collective-permute-done = bf16[96,2560]{1,0:T(8,128)(2,1)} collective-permute-done((bf16[96,2560]{1,0:T(8,128)(2,1)S(1)}, bf16[96,2560]{1,0:T(8,128)(2,1)}, u32[]{:S(2)}, u32[]{:S(2)}) %collective-permute-start) | collective-permute-done | bytes 491552 | tf_op jit(solution)/shard_map/ppermute | solution.py:161
  161.6 1.6 collective-permute-done.2
  163.1 10.8 %collective-permute-done.1 = bf16[96,2560]{1,0:T(8,128)(2,1)} collective-permute-done((bf16[96,2560]{1,0:T(8,128)(2,1)S(1)}, bf16[96,2560]{1,0:T(8,128)(2,1)}, u32[]{:S(2)}, u32[]{:S(2)}) %collective-permute-start.1) | collective-permute-done | bytes 491552 | tf_op jit(solution)/shard_map/ppermute | solution.py:161
  174.0 2.9 %pad_maximum_fusion = bf16[4,96,2560]{2,1,0:T(8,128)(2,1)} fusion(bf16[1,96,2560]{2,1,0:T(8,128)(2,1)} %bitcast.3, bf16[1,96,2560]{2,1,0:T(8,128)(2,1)} %bitcast.2, bf16[1,96,2560]{2,1,0:T(8,128)(2,1)} %bitcast.1, bf16[1,96,2560]{2,1,0:T(8,128)(2,1)S(1)} %bitcast.115), kind=kLoop, calls=%fused_computation.4 | loop fusion | flops 2949120 | bytes 3932160 | tf_op jit(solution)/shard_map/stack | solution.py:165
  176.9 3.5 %gather_fusion = bf16[4,96,2560]{2,1,0:T(8,128)(2,1)} fusion(bf16[4,96,2560]{2,1,0:T(8,128)(2,1)} %pad_maximum_fusion, s32[1024]{0:T(1024)S(1)} %pad_clamp_fusion), kind=kCustom, calls=%fused_computation | custom fusion | bytes 3932176 | tf_op jit(solution)/shard_map/jit(_take)/gather | solution.py:165
  180.4 8.1 %convolution_convert_fusion.q_ref.k0_ref.v0_ref = bf16[384,1536]{1,0:T(8,128)(2,1)} fusion(bf16[384,2560]{1,0:T(8,128)(2,1)} %bitcast.109, bf16[2560,1536]{1,0:T(8,128)(2,1)} %param.8), kind=kOutput, calls=%fused_computation.3 | convolution fusion | flops 3020488704 | bytes 11010048 | tf_op jit(solution)/shard_map/dot_general | solution.py:175
  188.5 2.4 copy.49
  190.9 1.0 fusion.47
  191.9 0.1 copy.67
  192.0 0.8 copy.68
  192.8 2.2 fusion.46
  195.0 1.8 copy.53
  196.7 1.8 copy.55
  198.5 0.8 copy.54
  199.3 1.7 pad_maximum_fusion.4
  201.0 3.4 %collective-permute-start.3 = (bf16[2,128,512]{2,1,0:T(8,128)(2,1)}, bf16[2,128,512]{2,1,0:T(8,128)(2,1)S(1)}, u32[]{:S(2)}, u32[]{:S(2)}) collective-permute-start(bf16[2,128,512]{2,1,0:T(8,128)(2,1)} %pad_maximum_fusion.4), channel_id=1, source_target_pairs={{0,4},{4,8},{8,12},{12,16},{16,20},{20,24},{24,28},{1,5},{5,9},{9,... | collective-permute-start | bytes 786440 | tf_op jit(solution)/shard_map/ppermute | solution.py:20
  204.4 1.4 convolution_multiply_fusion
  205.8 1.0 copy-done.2
  206.8 0.4 fusion.48
  207.2 0.8 copy.60
  208.0 0.2 copy.59
  208.2 4.4 %fusion.9.near_ref = f32[2,4,128,128]{3,2,1,0:T(8,128)} fusion(f32[2,4,128]{2,1,0:T(4,128)S(1)} %fusion.48, f32[2,4,128,256]{3,2,1,0:T(8,128)} %copy-done.2, pred[2,128,256]{2,1,0:T(8,128)(4,1)} %fusion.15, bf16[2,128,4,128]{3,1,0,2:T(8,128)(2,1)} %bitcast.116, bf16[2,128,4,128]{3,1,0,2:T(8,128)(2,1)S(1)} %bitcast.117), kind=kOutput, calls=%fused_computation.14 | convolution fusion | flops 69469440 | bytes 2166784 | tf_op jit(solution)/shard_map/ngqk,nkgd->ngqd/dot_general | solution.py:44
  212.6 33.4 %collective-permute-done.3.bk_ref.bv_ref = bf16[2,128,512]{2,1,0:T(8,128)(2,1)S(1)} collective-permute-done((bf16[2,128,512]{2,1,0:T(8,128)(2,1)}, bf16[2,128,512]{2,1,0:T(8,128)(2,1)S(1)}, u32[]{:S(2)}, u32[]{:S(2)}) %collective-permute-start.3) | collective-permute-done | bytes 262176 | tf_op jit(solution)/shard_map/ppermute | solution.py:20
  246.0 0.6 broadcast_in_dim.101.start_ref
  246.6 0.7 broadcast_in_dim.102
  247.3 0.7 broadcast_in_dim.97
  248.0 11.0 %shard_map.74 = bf16[384,512]{1,0:T(8,128)(2,1)} custom-call(bf16[384,1536]{1,0:T(8,128)(2,1)} %convolution_convert_fusion.q_ref.k0_ref.v0_ref, bf16[384,1536]{1,0:T(8,128)(2,1)} %convolution_convert_fusion.q_ref.k0_ref.v0_ref, bf16[384,1536]{1,0:T(8,128)(2,1)} %convolution_convert_fusion.q_ref.k0_ref.v0_ref, bf16[2,128,512]{2,1,0:T(8,128)(2,1)} %copy-done.1, ...), custom_call_target="tpu_custom_call" | custom-call | flops 1677721600 | bytes 5767168 | tf_op jit(solution)/shard_map/pallas_call | solution.py:102
  259.0 2.2 fusion.49
  261.2 0.3 fusion.45
  261.5 0.1 collective-permute-start.6
  261.6 0.5 collective-permute-start.8
  262.2 0.1 collective-permute-start.4
  262.3 0.5 collective-permute-start.10
  262.9 0.2 collective-permute-done.6
  263.1 1.6 collective-permute-start.7
  264.8 0.6 collective-permute-start.9
  265.4 0.0 collective-permute-done.4
  265.5 1.6 collective-permute-start.5
  267.1 0.6 collective-permute-start.11
  267.7 1.7 collective-permute-done.7
  269.4 2.6 collective-permute-done.9
  272.0 2.6 collective-permute-done.5
  274.7 1.8 collective-permute-done.11
  276.5 0.8 pad_maximum_fusion.3
  (40 shorter events, 0.6 us)
Async XLA Ops:
  0.0 259.0 %copy-start = (bf16[512,2560]{1,0:T(8,128)(2,1)S(1)}, bf16[512,2560]{1,0:T(8,128)(2,1)}, u32[]{:S(2)}) copy-start(bf16[512,2560]{1,0:T(8,128)(2,1)} %param.9) | copy-start | bytes 7864324
  142.8 7.0 %copy-start.3 = (bf16[96,2560]{1,0:T(8,128)(2,1)S(1)}, bf16[96,2560]{1,0:T(8,128)(2,1)}, u32[]{:S(2)}) copy-start(bf16[96,2560]{1,0:T(8,128)(2,1)} %param.7) | copy-start | bytes 1474564
  142.8 13.2 %copy-start.5 = (f32[4]{0:T(128)S(1)}, f32[4]{0:T(128)}, u32[]{:S(2)}) copy-start(f32[4]{0:T(128)} %param.10) | copy-start | bytes 52
  142.9 103.1 %all-to-all-start.1 = ((bf16[16,2,128,512]{3,2,1,0:T(8,128)(2,1)}), bf16[16,2,128,512]{3,2,1,0:T(8,128)(2,1)}, u32[]{:S(2)}, u32[]{:S(2)}) async-start(bf16[16,2,128,512]{3,2,1,0:T(8,128)(2,1)} %shard_map.73), calls=%async_computation.1 | async-start | bytes 8388608 | tf_op jit(solution)/shard_map/all_to_all | solution.py:231
  149.8 11.7 %collective-permute-start = (bf16[96,2560]{1,0:T(8,128)(2,1)S(1)}, bf16[96,2560]{1,0:T(8,128)(2,1)}, u32[]{:S(2)}, u32[]{:S(2)}) collective-permute-start(bf16[96,2560]{1,0:T(8,128)(2,1)S(1)} %copy-done.3), channel_id=1, source_target_pairs={{0,1},{1,2},{2,3},{3,0},{4,5},{5,6},{6,7},{7,4},{8,9},{9,10},{10,1... | collective-permute-start | bytes 1474568 | tf_op jit(solution)/shard_map/ppermute | solution.py:161
  149.8 13.3 %collective-permute-start.2 = (bf16[96,2560]{1,0:T(8,128)(2,1)S(1)}, bf16[96,2560]{1,0:T(8,128)(2,1)}, u32[]{:S(2)}, u32[]{:S(2)}) collective-permute-start(bf16[96,2560]{1,0:T(8,128)(2,1)S(1)} %copy-done.3), channel_id=1, source_target_pairs={{0,3},{1,0},{2,1},{3,2},{4,7},{5,4},{6,5},{7,6},{8,11},{9,8},{10,9... | collective-permute-start | bytes 1474568 | tf_op jit(solution)/shard_map/ppermute | solution.py:161
  151.6 22.4 %collective-permute-start.1 = (bf16[96,2560]{1,0:T(8,128)(2,1)S(1)}, bf16[96,2560]{1,0:T(8,128)(2,1)}, u32[]{:S(2)}, u32[]{:S(2)}) collective-permute-start(bf16[96,2560]{1,0:T(8,128)(2,1)S(1)} %copy-done.3), channel_id=1, source_target_pairs={{0,2},{1,3},{2,0},{3,1},{4,6},{5,7},{6,4},{7,5},{8,10},{9,11},{10,... | collective-permute-start | bytes 1474568 | tf_op jit(solution)/shard_map/ppermute | solution.py:161
  199.3 7.4 %copy-start.4 = (pred[2,128,256]{2,1,0:T(8,128)(4,1)S(1)}, pred[2,128,256]{2,1,0:T(8,128)(4,1)}, u32[]{:S(2)}) copy-start(pred[2,128,256]{2,1,0:T(8,128)(4,1)} %fusion.15) | copy-start | bytes 196612
  201.0 45.0 %collective-permute-start.3 = (bf16[2,128,512]{2,1,0:T(8,128)(2,1)}, bf16[2,128,512]{2,1,0:T(8,128)(2,1)S(1)}, u32[]{:S(2)}, u32[]{:S(2)}) collective-permute-start(bf16[2,128,512]{2,1,0:T(8,128)(2,1)} %pad_maximum_fusion.4), channel_id=1, source_target_pairs={{0,4},{4,8},{8,12},{12,16},{16,20},{20,24},{24,28},{1,5},{5,9},{9,... | collective-permute-start | bytes 786440 | tf_op jit(solution)/shard_map/ppermute | solution.py:20
  205.8 1.0 copy-start.2
  246.0 2.0 copy-start.1
  261.5 1.6 collective-permute-start.6
  261.6 3.1 %collective-permute-start.8 = (bf16[2,96,640]{2,1,0:T(8,128)(2,1)S(1)}, bf16[2,96,640]{2,1,0:T(8,128)(2,1)S(1)}, u32[]{:S(2)}, u32[]{:S(2)}) collective-permute-start(bf16[2,96,640]{2,1,0:T(8,128)(2,1)S(1)} %fusion.18), channel_id=1, source_target_pairs={{0,1},{1,0},{2,3},{3,2},{4,5},{5,4},{6,7},{7,6},{8,9},{9,8},{10,11... | collective-permute-start | bytes 737288 | tf_op jit(solution)/shard_map/ppermute | solution.py:267
  262.2 3.2 %collective-permute-start.4 = (bf16[2,96,640]{2,1,0:T(8,128)(2,1)S(1)}, bf16[2,96,640]{2,1,0:T(8,128)(2,1)S(1)}, u32[]{:S(2)}, u32[]{:S(2)}) collective-permute-start(bf16[2,96,640]{2,1,0:T(8,128)(2,1)S(1)} %fusion.16), channel_id=1, source_target_pairs={{0,1},{1,0},{2,3},{3,2},{4,5},{5,4},{6,7},{7,6},{8,9},{9,8},{10,11... | collective-permute-start | bytes 737288 | tf_op jit(solution)/shard_map/ppermute | solution.py:267
  262.3 4.7 %collective-permute-start.10 = (bf16[2,96,640]{2,1,0:T(8,128)(2,1)S(1)}, bf16[2,96,640]{2,1,0:T(8,128)(2,1)S(1)}, u32[]{:S(2)}, u32[]{:S(2)}) collective-permute-start(bf16[2,96,640]{2,1,0:T(8,128)(2,1)S(1)} %fusion.19), channel_id=1, source_target_pairs={{0,1},{1,0},{2,3},{3,2},{4,5},{5,4},{6,7},{7,6},{8,9},{9,8},{10,11... | collective-permute-start | bytes 737288 | tf_op jit(solution)/shard_map/ppermute | solution.py:267
  263.1 6.2 %collective-permute-start.7 = (bf16[96,640]{1,0:T(8,128)(2,1)S(1)}, bf16[96,640]{1,0:T(8,128)(2,1)S(1)}, u32[]{:S(2)}, u32[]{:S(2)}) collective-permute-start(bf16[96,640]{1,0:T(8,128)(2,1)S(1)} %fusion.26), channel_id=1, source_target_pairs={{0,2},{1,3},{2,0},{3,1},{4,6},{5,7},{6,4},{7,5},{8,10},{9,11},{10,... | collective-permute-start | bytes 368648 | tf_op jit(solution)/shard_map/ppermute | solution.py:275
  264.8 7.2 %collective-permute-start.9 = (bf16[96,640]{1,0:T(8,128)(2,1)S(1)}, bf16[96,640]{1,0:T(8,128)(2,1)S(1)}, u32[]{:S(2)}, u32[]{:S(2)}) collective-permute-start(bf16[96,640]{1,0:T(8,128)(2,1)S(1)} %fusion.27), channel_id=1, source_target_pairs={{0,2},{1,3},{2,0},{3,1},{4,6},{5,7},{6,4},{7,5},{8,10},{9,11},{10,... | collective-permute-start | bytes 368648 | tf_op jit(solution)/shard_map/ppermute | solution.py:275
  265.5 9.2 %collective-permute-start.5 = (bf16[96,640]{1,0:T(8,128)(2,1)S(1)}, bf16[96,640]{1,0:T(8,128)(2,1)S(1)}, u32[]{:S(2)}, u32[]{:S(2)}) collective-permute-start(bf16[96,640]{1,0:T(8,128)(2,1)S(1)} %fusion.25), channel_id=1, source_target_pairs={{0,2},{1,3},{2,0},{3,1},{4,6},{5,7},{6,4},{7,5},{8,10},{9,11},{10,... | collective-permute-start | bytes 368648 | tf_op jit(solution)/shard_map/ppermute | solution.py:275
  267.1 9.3 %collective-permute-start.11 = (bf16[96,640]{1,0:T(8,128)(2,1)S(1)}, bf16[96,640]{1,0:T(8,128)(2,1)S(1)}, u32[]{:S(2)}, u32[]{:S(2)}) collective-permute-start(bf16[96,640]{1,0:T(8,128)(2,1)S(1)} %fusion.28), channel_id=1, source_target_pairs={{0,2},{1,3},{2,0},{3,1},{4,6},{5,7},{6,4},{7,5},{8,10},{9,11},{10,... | collective-permute-start | bytes 368648 | tf_op jit(solution)/shard_map/ppermute | solution.py:275
